TPU v7x, 256 devices: a whole 4x4x8 slice. The times are simulated.
256 devices in a mesh: section: 4 (over x), dp: 32 (over z, y), mp: 2 (over core).
Axes of the slice: x: 4, y: 4, z: 8, core: 2. Of those that a mesh axis runs over, the one named last changes fastest.
Arguments:
- frames: bfloat16 [8192, 2560], P('dp', 'mp'), may hold values from -6 to 6
- frame_count: int32 [32], P('dp'), may hold values from 64 to 256, as said below
- norm_gain: float32 [4, 2560], P('section'), may hold values from 0.5 to 1.5
- weight_in: bfloat16 [4, 2560, 5120], P('section', 'dp', 'mp'), may hold values from -0.125 to 0.125
- weight_out: bfloat16 [4, 5120, 2560], P('section', 'mp', 'dp'), may hold values from -0.15625 to 0.15625
Outputs:
- states: bfloat16 [4, 8192, 2560], P('section', 'dp', 'mp')
Inputs may be any that keep to these rules, and one draw needn't show every extreme that they name: `frame_count`: each entry lies between 64 and 256; one entry equals 256 in every draw.
All inputs are finite; a program needn't handle non-finite values.
Results may differ from a plain program's by a relative error of at most 0.017.
Values may be sent and summed in bfloat16 or wider, within the bound.
No kernel may reach another device: no remote copies, remote signals or barrier semaphores. Data moves between devices by JAX's collectives and lax.ppermute only.
A program may use at most 128 MiB of HBM per device.

v0:
```python
import jax
import jax.numpy as jnp
from jax import lax
from jax.sharding import PartitionSpec as P

MICRO = 4


def passed_along(value, axis, steps):
    count = lax.axis_size(axis)
    first, last = (max(0, -steps), min(count, count - steps))
    return lax.ppermute(value, axis, [(source, source + steps) for source in range(first, last)])


def per_device(frames, frame_count, norm_gain, weight_in, weight_out):
    segment_count = lax.axis_size("section")
    segment_index = lax.axis_index("section")
    full_in, full_out = (
        lax.all_gather(weight_in, "dp", axis=1, tiled=True),
        lax.all_gather(weight_out, "dp", axis=2, tiled=True),
    )
    matrix_in = full_in[0]
    matrix_out = full_out[0]
    gain_row = norm_gain[0]
    pieces = MICRO
    local_rows = frames.shape[0]
    block_rows = local_rows // pieces
    width_local = frames.shape[1]
    live_count = frame_count[0]
    frame_blocks = frames.reshape(pieces, block_rows, width_local)

    def apply_layer(current):
        whole = lax.all_gather(current, "mp", axis=1, tiled=True)
        wide = whole.astype(jnp.float32)
        meansq = jnp.mean(wide * wide, axis=-1, keepdims=True)
        normed = (wide * lax.rsqrt(meansq + 1e-06) * gain_row).astype(jnp.bfloat16)
        hidden = jax.nn.gelu(
            jnp.dot(normed, matrix_in, preferred_element_type=jnp.float32), approximate=False
        ).astype(jnp.bfloat16)
        partial_term = jnp.dot(hidden, matrix_out, preferred_element_type=jnp.float32)
        summed = lax.psum_scatter(
            partial_term.astype(jnp.bfloat16), "mp", scatter_dimension=1, tiled=True
        ).astype(jnp.float32)
        return (current.astype(jnp.float32) + summed).astype(jnp.bfloat16)

    def advance(moment, carry):
        incoming, stored = carry
        position = moment - segment_index
        entry = jnp.minimum(moment, pieces - 1)
        first = lax.dynamic_index_in_dim(frame_blocks, entry, 0, keepdims=False)
        row_ids = entry * block_rows + jnp.arange(block_rows, dtype=jnp.int32)
        first = jnp.where((row_ids < live_count)[:, None], first, jnp.zeros_like(first))
        current = jnp.where(segment_index == 0, first, incoming)
        result = apply_layer(current)
        active = jnp.logical_and(position >= 0, position < pieces)
        target = jnp.clip(position, 0, pieces - 1)
        updated = lax.dynamic_update_index_in_dim(stored, result, target, 0)
        stored = jnp.where(active, updated, stored)
        incoming = passed_along(result, "section", 1)
        return (incoming, stored)

    initial = (
        jnp.zeros((block_rows, width_local), jnp.bfloat16),
        jnp.zeros((pieces, block_rows, width_local), jnp.bfloat16),
    )
    leftover, stored = lax.fori_loop(0, pieces + segment_count - 1, advance, initial)
    return stored.reshape(1, local_rows, width_local)


def solution(mesh):
    in_specs = (
        P("dp", "mp"),
        P("dp"),
        P("section", None),
        P("section", "dp", "mp"),
        P("section", "mp", "dp"),
    )
    out_specs = P("section", "dp", "mp")
    return jax.shard_map(
        per_device, mesh=mesh, in_specs=in_specs, out_specs=out_specs, check_vma=False
    )
```

profile of v0, /device:TPU:1, one launch (start us, length us, event | category | flops | bytes accessed | tf_op | source)
XLA Modules:
  0.0 541.0 jit_solution(16708624841427479918)
XLA Ops:
  6.5 0.7 all-gather.5.cloned.1.call-update
  7.3 0.7 all-gather.3.cloned.1.call-update
  8.0 127.6 %all-gather.5.cloned.1.call-done = bf16[1,2560,2560]{1,2,0:T(8,128)(2,1)} async-done(((bf16[1,2560,80]{1,2,0:T(8,128)(2,1)}), bf16[1,2560,2560]{1,2,0:T(8,128)(2,1)}) %all-gather.5.cloned.1.call-update) | async-done | bytes 13107216 | tf_op jit(solution)/shard_map/all_gather | solution.py:20
  135.6 17.7 %copy.7 = bf16[2560,2560]{1,0:T(8,128)(2,1)} copy(bf16[2560,2560]{0,1:T(8,128)(2,1)} %bitcast.23) | data formatting | bytes 26214400 | tf_op jit(solution)/shard_map/while | solution.py:66
  153.4 104.2 %all-gather.3.cloned.1.call-done = bf16[1,2560,2560]{2,1,0:T(8,128)(2,1)} async-done(((bf16[1,80,2560]{2,1,0:T(8,128)(2,1)}), bf16[1,2560,2560]{2,1,0:T(8,128)(2,1)}) %all-gather.3.cloned.1.call-update) | async-done | bytes 13107216 | tf_op jit(solution)/shard_map/all_gather | solution.py:19
  257.6 276.0 %while.16 = (s32[]{:T(128)}, bf16[64,1280]{1,0:T(8,128)(2,1)S(1)}, bf16[4,64,1280]{2,1,0:T(8,128)(2,1)S(1)}, pred[]{:T(512)}, s32[]{:T(128)}, /*index=5*/bf16[4,...) while((s32[]{:T(128)}, bf16[64,1280]{1,0:T(8,128)(2,1)S(1)}, ...), condition=%wide.region_3.4_spmd, body=%wide.region_0.3_spmd.sunk | while | flops 1690255616 | bytes 31161836 | solution.py:66
  257.7 0.7 add_compare_fusion.2
  258.4 1.0 fusion.99
  259.4 2.7 all_gather.17
  262.3 12.4 %convolution_convert_fusion.2 = bf16[64,2560]{1,0:T(8,128)(2,1)} fusion(bf16[2560,2560]{1,0:T(8,128)(2,1)} %get-tuple-element.338, bf16[2560,2560]{1,0:T(8,128)(2,1)} %get-tuple-element.337, bf16[64,2560]{1,0:T(8,128)(2,1)S(1)} %all_gather.17, f32[2560]{0:T(1024)S(1)} %reduce.2, f32[64]{0:T(128)S(1)} %add_rsqrt_fusion.2), kind=kOutput, calls=%fused_computation.clone.1 | convolution fusion | flops 1689190400 | bytes 26880256 | tf_op jit(solution)/shard_map/while/body/eval_jaxpr/dot_general | solution.py:40
  274.8 10.7 %reduce-scatter.2.cloned.1.call-done = bf16[64,1280]{1,0:T(8,128)(2,1)} async-done(((bf16[64,2560]{1,0:T(8,128)(2,1)}), bf16[64,1280]{1,0:T(8,128)(2,1)}) %reduce-scatter.2.cloned.1.call-update) | async-done | bytes 163856 | tf_op jit(solution)/shard_map/while/body/eval_jaxpr/reduce_scatter | solution.py:41
  285.5 1.0 fusion.101
  286.5 2.8 collective-permute-start
  289.3 3.4 collective-permute-done
  292.7 0.7 add_compare_fusion.2
  293.4 1.0 fusion.99
  294.4 2.6 all_gather.17
  297.3 12.4 %convolution_convert_fusion.2 = bf16[64,2560]{1,0:T(8,128)(2,1)} fusion(bf16[2560,2560]{1,0:T(8,128)(2,1)} %get-tuple-element.338, bf16[2560,2560]{1,0:T(8,128)(2,1)} %get-tuple-element.337, bf16[64,2560]{1,0:T(8,128)(2,1)S(1)} %all_gather.17, f32[2560]{0:T(1024)S(1)} %reduce.2, f32[64]{0:T(128)S(1)} %add_rsqrt_fusion.2), kind=kOutput, calls=%fused_computation.clone.1 | convolution fusion | flops 1689190400 | bytes 26880256 | tf_op jit(solution)/shard_map/while/body/eval_jaxpr/dot_general | solution.py:40
  309.7 15.9 %reduce-scatter.2.cloned.1.call-done = bf16[64,1280]{1,0:T(8,128)(2,1)} async-done(((bf16[64,2560]{1,0:T(8,128)(2,1)}), bf16[64,1280]{1,0:T(8,128)(2,1)}) %reduce-scatter.2.cloned.1.call-update) | async-done | bytes 163856 | tf_op jit(solution)/shard_map/while/body/eval_jaxpr/reduce_scatter | solution.py:41
  325.6 1.0 fusion.101
  326.6 2.9 collective-permute-start
  329.5 3.4 collective-permute-done
  332.9 0.7 add_compare_fusion.2
  333.5 1.0 fusion.99
  334.5 2.6 all_gather.17
  337.4 12.4 %convolution_convert_fusion.2 = bf16[64,2560]{1,0:T(8,128)(2,1)} fusion(bf16[2560,2560]{1,0:T(8,128)(2,1)} %get-tuple-element.338, bf16[2560,2560]{1,0:T(8,128)(2,1)} %get-tuple-element.337, bf16[64,2560]{1,0:T(8,128)(2,1)S(1)} %all_gather.17, f32[2560]{0:T(1024)S(1)} %reduce.2, f32[64]{0:T(128)S(1)} %add_rsqrt_fusion.2), kind=kOutput, calls=%fused_computation.clone.1 | convolution fusion | flops 1689190400 | bytes 26880256 | tf_op jit(solution)/shard_map/while/body/eval_jaxpr/dot_general | solution.py:40
  349.9 15.9 %reduce-scatter.2.cloned.1.call-done = bf16[64,1280]{1,0:T(8,128)(2,1)} async-done(((bf16[64,2560]{1,0:T(8,128)(2,1)}), bf16[64,1280]{1,0:T(8,128)(2,1)}) %reduce-scatter.2.cloned.1.call-update) | async-done | bytes 163856 | tf_op jit(solution)/shard_map/while/body/eval_jaxpr/reduce_scatter | solution.py:41
  365.8 1.0 fusion.101
  366.7 2.9 collective-permute-start
  369.6 3.4 collective-permute-done
  373.0 0.7 add_compare_fusion.2
  373.7 1.0 fusion.99
  374.7 2.6 all_gather.17
  377.6 12.4 %convolution_convert_fusion.2 = bf16[64,2560]{1,0:T(8,128)(2,1)} fusion(bf16[2560,2560]{1,0:T(8,128)(2,1)} %get-tuple-element.338, bf16[2560,2560]{1,0:T(8,128)(2,1)} %get-tuple-element.337, bf16[64,2560]{1,0:T(8,128)(2,1)S(1)} %all_gather.17, f32[2560]{0:T(1024)S(1)} %reduce.2, f32[64]{0:T(128)S(1)} %add_rsqrt_fusion.2), kind=kOutput, calls=%fused_computation.clone.1 | convolution fusion | flops 1689190400 | bytes 26880256 | tf_op jit(solution)/shard_map/while/body/eval_jaxpr/dot_general | solution.py:40
  390.0 15.9 %reduce-scatter.2.cloned.1.call-done = bf16[64,1280]{1,0:T(8,128)(2,1)} async-done(((bf16[64,2560]{1,0:T(8,128)(2,1)}), bf16[64,1280]{1,0:T(8,128)(2,1)}) %reduce-scatter.2.cloned.1.call-update) | async-done | bytes 163856 | tf_op jit(solution)/shard_map/while/body/eval_jaxpr/reduce_scatter | solution.py:41
  405.9 1.0 fusion.101
  406.9 2.9 collective-permute-start
  409.8 3.4 collective-permute-done
  413.2 0.7 add_compare_fusion.2
  413.8 1.0 fusion.99
  414.9 2.6 all_gather.17
  417.5 0.2 fusion.100
  417.7 12.4 %convolution_convert_fusion.2 = bf16[64,2560]{1,0:T(8,128)(2,1)} fusion(bf16[2560,2560]{1,0:T(8,128)(2,1)} %get-tuple-element.338, bf16[2560,2560]{1,0:T(8,128)(2,1)} %get-tuple-element.337, bf16[64,2560]{1,0:T(8,128)(2,1)S(1)} %all_gather.17, f32[2560]{0:T(1024)S(1)} %reduce.2, f32[64]{0:T(128)S(1)} %add_rsqrt_fusion.2), kind=kOutput, calls=%fused_computation.clone.1 | convolution fusion | flops 1689190400 | bytes 26880256 | tf_op jit(solution)/shard_map/while/body/eval_jaxpr/dot_general | solution.py:40
  430.2 15.9 %reduce-scatter.2.cloned.1.call-done = bf16[64,1280]{1,0:T(8,128)(2,1)} async-done(((bf16[64,2560]{1,0:T(8,128)(2,1)}), bf16[64,1280]{1,0:T(8,128)(2,1)}) %reduce-scatter.2.cloned.1.call-update) | async-done | bytes 163856 | tf_op jit(solution)/shard_map/while/body/eval_jaxpr/reduce_scatter | solution.py:41
  446.1 1.0 fusion.101
  447.0 2.9 collective-permute-start
  449.9 3.4 collective-permute-done
  453.3 0.7 add_compare_fusion.2
  454.0 1.0 fusion.99
  455.0 2.6 all_gather.17
  457.9 12.4 %convolution_convert_fusion.2 = bf16[64,2560]{1,0:T(8,128)(2,1)} fusion(bf16[2560,2560]{1,0:T(8,128)(2,1)} %get-tuple-element.338, bf16[2560,2560]{1,0:T(8,128)(2,1)} %get-tuple-element.337, bf16[64,2560]{1,0:T(8,128)(2,1)S(1)} %all_gather.17, f32[2560]{0:T(1024)S(1)} %reduce.2, f32[64]{0:T(128)S(1)} %add_rsqrt_fusion.2), kind=kOutput, calls=%fused_computation.clone.1 | convolution fusion | flops 1689190400 | bytes 26880256 | tf_op jit(solution)/shard_map/while/body/eval_jaxpr/dot_general | solution.py:40
  470.3 15.9 %reduce-scatter.2.cloned.1.call-done = bf16[64,1280]{1,0:T(8,128)(2,1)} async-done(((bf16[64,2560]{1,0:T(8,128)(2,1)}), bf16[64,1280]{1,0:T(8,128)(2,1)}) %reduce-scatter.2.cloned.1.call-update) | async-done | bytes 163856 | tf_op jit(solution)/shard_map/while/body/eval_jaxpr/reduce_scatter | solution.py:41
  486.2 1.0 fusion.101
  487.2 2.9 collective-permute-start
  490.1 3.4 collective-permute-done
  493.5 0.7 add_compare_fusion.2
  494.1 1.0 fusion.99
  495.2 2.6 all_gather.17
  498.0 12.4 %convolution_convert_fusion.2 = bf16[64,2560]{1,0:T(8,128)(2,1)} fusion(bf16[2560,2560]{1,0:T(8,128)(2,1)} %get-tuple-element.338, bf16[2560,2560]{1,0:T(8,128)(2,1)} %get-tuple-element.337, bf16[64,2560]{1,0:T(8,128)(2,1)S(1)} %all_gather.17, f32[2560]{0:T(1024)S(1)} %reduce.2, f32[64]{0:T(128)S(1)} %add_rsqrt_fusion.2), kind=kOutput, calls=%fused_computation.clone.1 | convolution fusion | flops 1689190400 | bytes 26880256 | tf_op jit(solution)/shard_map/while/body/eval_jaxpr/dot_general | solution.py:40
  510.5 15.9 %reduce-scatter.2.cloned.1.call-done = bf16[64,1280]{1,0:T(8,128)(2,1)} async-done(((bf16[64,2560]{1,0:T(8,128)(2,1)}), bf16[64,1280]{1,0:T(8,128)(2,1)}) %reduce-scatter.2.cloned.1.call-update) | async-done | bytes 163856 | tf_op jit(solution)/shard_map/while/body/eval_jaxpr/reduce_scatter | solution.py:41
  526.4 1.0 fusion.101
  527.3 2.9 collective-permute-start
  530.2 3.4 collective-permute-done
  533.6 0.8 copy-done
  (41 shorter events, 1.6 us)
Async XLA Ops:
  6.5 129.1 %all-gather.5.cloned.1.call-start = ((), (), s32[]{:S(2)}) async-start(), calls=%async_computation.2 | async-start | bytes 13516800 | tf_op jit(solution)/shard_map/all_gather | solution.py:20
  7.3 250.3 %all-gather.3.cloned.1.call-start = ((), (), s32[]{:S(2)}) async-start(), calls=%async_computation.1 | async-start | bytes 13516800 | tf_op jit(solution)/shard_map/all_gather | solution.py:19
  135.6 122.0 %copy-start.1 = (f32[1,2560]{1,0:T(1,128)S(1)}, f32[1,2560]{1,0:T(1,128)}, u32[]{:S(2)}) copy-start(f32[1,2560]{1,0:T(1,128)} %param.9) | copy-start | bytes 30724
  257.7 27.8 %reduce-scatter.2.cloned.1.call-start = ((), (), s32[]{:S(2)}) async-start(), calls=%async_computation.3 | async-start | bytes 491520 | tf_op jit(solution)/shard_map/while/body/eval_jaxpr/reduce_scatter | solution.py:41
  286.5 6.3 %collective-permute-start = (bf16[64,1280]{1,0:T(8,128)(2,1)S(1)}, bf16[64,1280]{1,0:T(8,128)(2,1)S(1)}, u32[]{:S(2)}, u32[]{:S(2)}) collective-permute-start(bf16[64,1280]{1,0:T(8,128)(2,1)S(1)} %get-tuple-element.296), channel_id=1, source_target_pairs={{0,64},{64,128},{128,192},{1,65},{65,129},{129,193},{2,66},{66,130... | collective-permute-start | bytes 491528 | tf_op jit(solution)/shard_map/while/body/eval_jaxpr/ppermute | solution.py:12
  292.7 32.9 %reduce-scatter.2.cloned.1.call-start = ((), (), s32[]{:S(2)}) async-start(), calls=%async_computation.3 | async-start | bytes 491520 | tf_op jit(solution)/shard_map/while/body/eval_jaxpr/reduce_scatter | solution.py:41
  326.6 6.3 %collective-permute-start = (bf16[64,1280]{1,0:T(8,128)(2,1)S(1)}, bf16[64,1280]{1,0:T(8,128)(2,1)S(1)}, u32[]{:S(2)}, u32[]{:S(2)}) collective-permute-start(bf16[64,1280]{1,0:T(8,128)(2,1)S(1)} %get-tuple-element.296), channel_id=1, source_target_pairs={{0,64},{64,128},{128,192},{1,65},{65,129},{129,193},{2,66},{66,130... | collective-permute-start | bytes 491528 | tf_op jit(solution)/shard_map/while/body/eval_jaxpr/ppermute | solution.py:12
  332.9 32.9 %reduce-scatter.2.cloned.1.call-start = ((), (), s32[]{:S(2)}) async-start(), calls=%async_computation.3 | async-start | bytes 491520 | tf_op jit(solution)/shard_map/while/body/eval_jaxpr/reduce_scatter | solution.py:41
  366.7 6.3 %collective-permute-start = (bf16[64,1280]{1,0:T(8,128)(2,1)S(1)}, bf16[64,1280]{1,0:T(8,128)(2,1)S(1)}, u32[]{:S(2)}, u32[]{:S(2)}) collective-permute-start(bf16[64,1280]{1,0:T(8,128)(2,1)S(1)} %get-tuple-element.296), channel_id=1, source_target_pairs={{0,64},{64,128},{128,192},{1,65},{65,129},{129,193},{2,66},{66,130... | collective-permute-start | bytes 491528 | tf_op jit(solution)/shard_map/while/body/eval_jaxpr/ppermute | solution.py:12
  373.0 32.9 %reduce-scatter.2.cloned.1.call-start = ((), (), s32[]{:S(2)}) async-start(), calls=%async_computation.3 | async-start | bytes 491520 | tf_op jit(solution)/shard_map/while/body/eval_jaxpr/reduce_scatter | solution.py:41
  406.9 6.3 %collective-permute-start = (bf16[64,1280]{1,0:T(8,128)(2,1)S(1)}, bf16[64,1280]{1,0:T(8,128)(2,1)S(1)}, u32[]{:S(2)}, u32[]{:S(2)}) collective-permute-start(bf16[64,1280]{1,0:T(8,128)(2,1)S(1)} %get-tuple-element.296), channel_id=1, source_target_pairs={{0,64},{64,128},{128,192},{1,65},{65,129},{129,193},{2,66},{66,130... | collective-permute-start | bytes 491528 | tf_op jit(solution)/shard_map/while/body/eval_jaxpr/ppermute | solution.py:12
  413.2 32.9 %reduce-scatter.2.cloned.1.call-start = ((), (), s32[]{:S(2)}) async-start(), calls=%async_computation.3 | async-start | bytes 491520 | tf_op jit(solution)/shard_map/while/body/eval_jaxpr/reduce_scatter | solution.py:41
  447.0 6.3 %collective-permute-start = (bf16[64,1280]{1,0:T(8,128)(2,1)S(1)}, bf16[64,1280]{1,0:T(8,128)(2,1)S(1)}, u32[]{:S(2)}, u32[]{:S(2)}) collective-permute-start(bf16[64,1280]{1,0:T(8,128)(2,1)S(1)} %get-tuple-element.296), channel_id=1, source_target_pairs={{0,64},{64,128},{128,192},{1,65},{65,129},{129,193},{2,66},{66,130... | collective-permute-start | bytes 491528 | tf_op jit(solution)/shard_map/while/body/eval_jaxpr/ppermute | solution.py:12
  453.3 32.9 %reduce-scatter.2.cloned.1.call-start = ((), (), s32[]{:S(2)}) async-start(), calls=%async_computation.3 | async-start | bytes 491520 | tf_op jit(solution)/shard_map/while/body/eval_jaxpr/reduce_scatter | solution.py:41
  487.2 6.3 %collective-permute-start = (bf16[64,1280]{1,0:T(8,128)(2,1)S(1)}, bf16[64,1280]{1,0:T(8,128)(2,1)S(1)}, u32[]{:S(2)}, u32[]{:S(2)}) collective-permute-start(bf16[64,1280]{1,0:T(8,128)(2,1)S(1)} %get-tuple-element.296), channel_id=1, source_target_pairs={{0,64},{64,128},{128,192},{1,65},{65,129},{129,193},{2,66},{66,130... | collective-permute-start | bytes 491528 | tf_op jit(solution)/shard_map/while/body/eval_jaxpr/ppermute | solution.py:12
  493.5 32.9 %reduce-scatter.2.cloned.1.call-start = ((), (), s32[]{:S(2)}) async-start(), calls=%async_computation.3 | async-start | bytes 491520 | tf_op jit(solution)/shard_map/while/body/eval_jaxpr/reduce_scatter | solution.py:41
  527.3 6.3 %collective-permute-start = (bf16[64,1280]{1,0:T(8,128)(2,1)S(1)}, bf16[64,1280]{1,0:T(8,128)(2,1)S(1)}, u32[]{:S(2)}, u32[]{:S(2)}) collective-permute-start(bf16[64,1280]{1,0:T(8,128)(2,1)S(1)} %get-tuple-element.296), channel_id=1, source_target_pairs={{0,64},{64,128},{128,192},{1,65},{65,129},{129,193},{2,66},{66,130... | collective-permute-start | bytes 491528 | tf_op jit(solution)/shard_map/while/body/eval_jaxpr/ppermute | solution.py:12
  533.6 0.8 copy-start
Sparse Core Ops, SparseCore 0:
  9.9 125.6 all-gather.4
  138.2 119.2 all-gather.2
  274.9 10.5 reduce-scatter.1
  309.8 15.7 reduce-scatter.1
  350.0 15.7 reduce-scatter.1
  390.1 15.7 reduce-scatter.1
  430.3 15.7 reduce-scatter.1
  470.4 15.7 reduce-scatter.1
  510.6 15.7 reduce-scatter.1
where the time goes:
time: 543 us; the launch traced here: 541 us
  waiting for transfers between devices  363 us (67%)
  matrix products  86.8 us (16%)
  starting transfers between devices  20.1 us (4%)
  other arithmetic  20 us (4%)
  local copies, waits for them, and re-layouts  18.6 us (3%)
  blocking collectives  18.6 us (3%)
  between operations  13.1 us (2%)
    all_gather x1, waiting for transfers between devices, per_device(): lax.all_gather(weight_out, 'dp', axis=2, tiled=True)  128 us
    reduce_scatter x7, waiting for transfers between devices, apply_layer(): lax.psum_scatter(partial_term.astype(jnp.bfloat16), 'mp', scatter_dimensi...  106 us
    all_gather x1, waiting for transfers between devices, per_device(): lax.all_gather(weight_in, 'dp', axis=1, tiled=True)  104 us
    dot_general x7, matrix products, apply_layer(): jnp.dot(hidden, matrix_out, preferred_element_type=jnp.float32)  86.8 us
    ppermute x7, waiting for transfers between devices, passed_along(): lax.ppermute(value, axis, [(source, source + steps) for source in range(f...  23.9 us
    ppermute x7, starting transfers between devices, passed_along(): lax.ppermute(value, axis, [(source, source + steps) for source in range(f...  20 us
    all_gather x7, blocking collectives, apply_layer(): whole = lax.all_gather(current, 'mp', axis=1, tiled=True)  18.6 us
    while x1, local copies, waits for them, and re-layouts, per_device(): lax.fori_loop(0, pieces + segment_count - 1, advance, initial)  17.7 us
  transfers between devices with their start and end apart: 16, of which 16 were waited for; matrix products, arithmetic and copies ran while one was open for 3% of the time, Pallas kernels for 0%

commit v1 on v0

v1 whole, which is shorter than its diff:
```python
import jax
import jax.numpy as jnp
from jax import lax
from jax.sharding import PartitionSpec as P


def passed_along(value, axis, steps):
    count = lax.axis_size(axis)
    first, last = (max(0, -steps), min(count, count - steps))
    return lax.ppermute(value, axis, [(source, source + steps) for source in range(first, last)])


def per_device(frames, frame_count, norm_gain, weight_in, weight_out):
    segment_count = lax.axis_size("section")
    segment_index = lax.axis_index("section")
    half_index = lax.axis_index("mp")
    matrix_in = lax.all_gather(weight_in[0], "dp", axis=0, tiled=True)
    matrix_out_t = lax.all_gather(weight_out[0].T, "dp", axis=0, tiled=True)
    gain_row = norm_gain[0]
    local_rows, width_local = frames.shape
    live_count = frame_count[0]
    row_ids = jnp.arange(local_rows, dtype=jnp.int32)
    first = jnp.where((row_ids < live_count)[:, None], frames, jnp.zeros_like(frames))

    def apply_layer(current):
        whole = lax.all_gather(current, "mp", axis=1, tiled=True)
        wide = whole.astype(jnp.float32)
        meansq = jnp.mean(wide * wide, axis=-1, keepdims=True)
        normed = (wide * lax.rsqrt(meansq + 1e-06) * gain_row).astype(jnp.bfloat16)
        hidden = jax.nn.gelu(
            jnp.dot(normed, matrix_in, preferred_element_type=jnp.float32), approximate=False
        ).astype(jnp.bfloat16)
        partial_term = lax.dot_general(
            hidden, matrix_out_t, (((1,), (1,)), ((), ())), preferred_element_type=jnp.float32
        ).astype(jnp.bfloat16)
        halves = partial_term.reshape(local_rows, 2, width_local)
        keep = jnp.where(half_index == 0, halves[:, 0], halves[:, 1])
        send = jnp.where(half_index == 0, halves[:, 1], halves[:, 0])
        other = lax.ppermute(send, "mp", [(0, 1), (1, 0)])
        summed = keep.astype(jnp.float32) + other.astype(jnp.float32)
        return (current.astype(jnp.float32) + summed).astype(jnp.bfloat16)

    def advance(moment, carry):
        current, stored = carry
        result = apply_layer(current)
        stored = jnp.where(segment_index == moment, result, stored)
        return (passed_along(result, "section", 1), stored)

    initial = (first, jnp.zeros((local_rows, width_local), jnp.bfloat16))
    leftover, stored = lax.fori_loop(0, segment_count, advance, initial)
    return stored.reshape(1, local_rows, width_local)


def solution(mesh):
    in_specs = (
        P("dp", "mp"),
        P("dp"),
        P("section", None),
        P("section", "dp", "mp"),
        P("section", "mp", "dp"),
    )
    out_specs = P("section", "dp", "mp")
    return jax.shard_map(
        per_device, mesh=mesh, in_specs=in_specs, out_specs=out_specs, check_vma=False
    )
```

time: 543 us -> 538 us (level)
  waiting for transfers between devices: 363 us -> 385 us
  blocking collectives: 18.6 us -> 0 us
  matrix products: 86.8 us -> 74.5 us
  starting transfers between devices: 20.1 us -> 12.3 us
  local copies, waits for them, and re-layouts: 18.6 us -> 24.8 us
  other arithmetic: 20 us -> 25.9 us
    reduce_scatter x7 -> x0, waiting for transfers between devices: 106 us -> none  [apply_layer(): lax.psum_scatter(partial_term.astype(jnp.bfloat16), 'mp', scatter_dimensi...]
    all_gather x2 -> x6, waiting for transfers between devices: 232 us -> 318 us  [the longest x1 126 us: per_device(): matrix_in = lax.all_gather(weight_in[0], 'dp', axis=0, tiled=True)]
    ppermute x7 -> x4, waiting for transfers between devices: 23.9 us -> 56.8 us  [passed_along(): lax.ppermute(value, axis, [(source, source + steps) for source in range(f...]
    all_gather x7 -> x0, blocking collectives: 18.6 us -> none  [apply_layer(): whole = lax.all_gather(current, 'mp', axis=1, tiled=True)]
    slice x0 -> x4, local copies, waits for them, and re-layouts: none -> 16.3 us  [apply_layer(): keep = jnp.where(half_index == 0, halves[:, 0], halves[:, 1])]
    while x1 -> x16, local copies, waits for them, and re-layouts: 17.7 us -> 3.42 us  [per_device(): lax.fori_loop(0, pieces + segment_count - 1, advance, initial)]
    dot_general x7 -> x4, matrix products: 86.8 us -> 74.5 us  [apply_layer(): lax.dot_general(hidden, matrix_out_t, (((1,), (1,)), ((), ())), preferred...]
    ppermute x0 -> x4, waiting for transfers between devices: none -> 8.94 us  [apply_layer(): other = lax.ppermute(send, 'mp', [(0, 1), (1, 0)])]
  transfers between devices with their start and end apart: 16 -> 14, of which waited for: 16 -> 14; matrix products, arithmetic and copies ran while one was open for 3% -> 1% of each run, Pallas kernels for 0% -> 0%
where the time goes in v1:
time: 538 us; the launch traced here: 537 us
  waiting for transfers between devices  385 us (72%)
  matrix products  74.5 us (14%)
  other arithmetic  25.9 us (5%)
  local copies, waits for them, and re-layouts  24.8 us (5%)
  between operations  14.1 us (3%)
  starting transfers between devices  12.3 us (2%)
    all_gather x1, waiting for transfers between devices, per_device(): matrix_in = lax.all_gather(weight_in[0], 'dp', axis=0, tiled=True)  126 us
    all_gather x1, waiting for transfers between devices, per_device(): matrix_out_t = lax.all_gather(weight_out[0].T, 'dp', axis=0, tiled=True)  122 us
    dot_general x4, matrix products, apply_layer(): lax.dot_general(hidden, matrix_out_t, (((1,), (1,)), ((), ())), preferred...  74.5 us
    all_gather x4, waiting for transfers between devices, apply_layer(): whole = lax.all_gather(current, 'mp', axis=1, tiled=True)  70.2 us
    ppermute x4, waiting for transfers between devices, passed_along(): lax.ppermute(value, axis, [(source, source + steps) for source in range(f...  56.8 us
    slice x4, local copies, waits for them, and re-layouts, apply_layer(): keep = jnp.where(half_index == 0, halves[:, 0], halves[:, 1])  16.3 us
    ppermute x4, starting transfers between devices, passed_along(): lax.ppermute(value, axis, [(source, source + steps) for source in range(f...  11.4 us
    select_n x4, other arithmetic, advance(): stored = jnp.where(segment_index == moment, result, stored)  11 us
  transfers between devices with their start and end apart: 14, of which 14 were waited for; matrix products, arithmetic and copies ran while one was open for 1% of the time, Pallas kernels for 0%

profile of v1, /device:TPU:1, one launch (start us, length us, event | category | flops | bytes accessed | tf_op | source)
XLA Modules:
  0.0 536.7 jit_solution(13332952725772248802)
XLA Ops:
  6.5 0.7 all-gather.7.cloned.1.call-update
  7.3 0.0 all-gather.5.cloned.1.call-start
  7.3 0.7 all-gather.5.cloned.1.call-update
  8.7 1.2 broadcast_select_fusion
  9.9 125.7 %all-gather.7.cloned.1.call-done = bf16[1,2560,2560]{2,1,0:T(8,128)(2,1)} async-done(((bf16[1,80,2560]{2,1,0:T(8,128)(2,1)}), bf16[1,2560,2560]{2,1,0:T(8,128)(2,1)}) %all-gather.7.cloned.1.call-update) | async-done | bytes 13107216 | tf_op jit(solution)/shard_map/all_gather | solution.py:17
  135.6 121.9 %all-gather.5.cloned.1.call-done = bf16[2560,2560]{1,0:T(8,128)(2,1)} async-done(((bf16[80,2560]{1,0:T(8,128)(2,1)}), bf16[2560,2560]{1,0:T(8,128)(2,1)}) %all-gather.5.cloned.1.call-update) | async-done | bytes 13107216 | tf_op jit(solution)/shard_map/all_gather | solution.py:18
  257.6 272.3 %while.18 = (s32[]{:T(128)}, bf16[256,1280]{1,0:T(8,128)(2,1)S(1)}, bf16[256,1280]{1,0:T(8,128)(2,1)}, pred[]{:T(512)}, f32[1,2560]{1,0:T(1,128)}, /*index=5*/bf...) while((s32[]{:T(128)}, bf16[256,1280]{1,0:T(8,128)(2,1)S(1)}, ...), condition=%wide.region_2.3_spmd.clone, body=%wide.region_0.2_spmd.clone.sunk | while | flops 6762004992 | bytes 58362168 | solution.py:50
  257.6 0.8 copy-done
  258.4 0.0 all-gather.9.cloned.1.call-update
  258.4 0.7 reduce.2
  259.2 14.0 %all-gather.9.cloned.1.call-done = bf16[256,2560]{1,0:T(8,128)(2,1)} async-done(((bf16[256,1280]{1,0:T(8,128)(2,1)}), bf16[256,2560]{1,0:T(8,128)(2,1)}) %all-gather.9.cloned.1.call-update) | async-done | bytes 1310736 | tf_op jit(solution)/shard_map/while/body/eval_jaxpr/all_gather | solution.py:26
  273.1 1.7 fusion.99
  274.8 18.6 %convolution_convert_fusion.2 = bf16[256,2560]{1,0:T(8,128)(2,1)S(1)} fusion(bf16[2560,2560]{1,0:T(8,128)(2,1)} %get-tuple-element.329, bf16[2560,2560]{1,0:T(8,128)(2,1)} %get-tuple-element.328, bf16[256,2560]{1,0:T(8,128)(2,1)} %all-gather.9.cloned.1.call-done, f32[2560]{0:T(1024)S(1)} %reduce.2, f32[256]{0:T(256)S(1)} %add_rsqrt_fusion.2), kind=kOutput, calls=%fused_computation.1.clone.1 | convolution fusion | flops 6756761600 | bytes 28847104 | tf_op jit(solution)/shard_map/while/body/eval_jaxpr/dot_general | solution.py:33
  293.4 1.2 reshape.40
  294.7 4.1 fusion.100
  298.8 0.0 copy-start.1
  298.8 1.0 select_bitcast_fusion.2
  299.8 0.2 collective-permute-start
  300.0 2.2 collective-permute-done
  302.2 2.6 select_select_fusion.2
  304.8 2.9 collective-permute-start.1
  307.7 14.2 %collective-permute-done.1 = bf16[256,1280]{1,0:T(8,128)(2,1)S(1)} collective-permute-done((bf16[256,1280]{1,0:T(8,128)(2,1)}, bf16[256,1280]{1,0:T(8,128)(2,1)S(1)}, u32[]{:S(2)}, u32[]{:S(2)}) %collective-permute-start.1) | collective-permute-done | bytes 655392 | tf_op jit(solution)/shard_map/while/body/eval_jaxpr/ppermute | solution.py:10
  321.9 0.8 copy-done
  322.8 0.0 all-gather.9.cloned.1.call-update
  322.8 0.7 reduce.2
  323.5 18.7 %all-gather.9.cloned.1.call-done = bf16[256,2560]{1,0:T(8,128)(2,1)} async-done(((bf16[256,1280]{1,0:T(8,128)(2,1)}), bf16[256,2560]{1,0:T(8,128)(2,1)}) %all-gather.9.cloned.1.call-update) | async-done | bytes 1310736 | tf_op jit(solution)/shard_map/while/body/eval_jaxpr/all_gather | solution.py:26
  342.3 1.7 fusion.99
  343.9 18.6 %convolution_convert_fusion.2 = bf16[256,2560]{1,0:T(8,128)(2,1)S(1)} fusion(bf16[2560,2560]{1,0:T(8,128)(2,1)} %get-tuple-element.329, bf16[2560,2560]{1,0:T(8,128)(2,1)} %get-tuple-element.328, bf16[256,2560]{1,0:T(8,128)(2,1)} %all-gather.9.cloned.1.call-done, f32[2560]{0:T(1024)S(1)} %reduce.2, f32[256]{0:T(256)S(1)} %add_rsqrt_fusion.2), kind=kOutput, calls=%fused_computation.1.clone.1 | convolution fusion | flops 6756761600 | bytes 28847104 | tf_op jit(solution)/shard_map/while/body/eval_jaxpr/dot_general | solution.py:33
  362.5 1.2 reshape.40
  363.8 4.1 fusion.100
  367.9 1.0 select_bitcast_fusion.2
  368.9 0.2 collective-permute-start
  369.1 2.2 collective-permute-done
  371.3 2.8 select_select_fusion.2
  374.2 2.9 collective-permute-start.1
  377.0 14.2 %collective-permute-done.1 = bf16[256,1280]{1,0:T(8,128)(2,1)S(1)} collective-permute-done((bf16[256,1280]{1,0:T(8,128)(2,1)}, bf16[256,1280]{1,0:T(8,128)(2,1)S(1)}, u32[]{:S(2)}, u32[]{:S(2)}) %collective-permute-start.1) | collective-permute-done | bytes 655392 | tf_op jit(solution)/shard_map/while/body/eval_jaxpr/ppermute | solution.py:10
  391.2 0.8 copy-done
  392.1 0.0 all-gather.9.cloned.1.call-update
  392.1 0.7 reduce.2
  392.8 18.8 %all-gather.9.cloned.1.call-done = bf16[256,2560]{1,0:T(8,128)(2,1)} async-done(((bf16[256,1280]{1,0:T(8,128)(2,1)}), bf16[256,2560]{1,0:T(8,128)(2,1)}) %all-gather.9.cloned.1.call-update) | async-done | bytes 1310736 | tf_op jit(solution)/shard_map/while/body/eval_jaxpr/all_gather | solution.py:26
  411.6 1.7 fusion.99
  413.2 18.6 %convolution_convert_fusion.2 = bf16[256,2560]{1,0:T(8,128)(2,1)S(1)} fusion(bf16[2560,2560]{1,0:T(8,128)(2,1)} %get-tuple-element.329, bf16[2560,2560]{1,0:T(8,128)(2,1)} %get-tuple-element.328, bf16[256,2560]{1,0:T(8,128)(2,1)} %all-gather.9.cloned.1.call-done, f32[2560]{0:T(1024)S(1)} %reduce.2, f32[256]{0:T(256)S(1)} %add_rsqrt_fusion.2), kind=kOutput, calls=%fused_computation.1.clone.1 | convolution fusion | flops 6756761600 | bytes 28847104 | tf_op jit(solution)/shard_map/while/body/eval_jaxpr/dot_general | solution.py:33
  431.9 1.2 reshape.40
  433.1 4.1 fusion.100
  437.2 1.0 select_bitcast_fusion.2
  438.2 0.2 collective-permute-start
  438.4 2.2 collective-permute-done
  440.7 2.8 select_select_fusion.2
  443.5 2.8 collective-permute-start.1
  446.3 14.2 %collective-permute-done.1 = bf16[256,1280]{1,0:T(8,128)(2,1)S(1)} collective-permute-done((bf16[256,1280]{1,0:T(8,128)(2,1)}, bf16[256,1280]{1,0:T(8,128)(2,1)S(1)}, u32[]{:S(2)}, u32[]{:S(2)}) %collective-permute-start.1) | collective-permute-done | bytes 655392 | tf_op jit(solution)/shard_map/while/body/eval_jaxpr/ppermute | solution.py:10
  460.5 0.8 copy-done
  461.4 0.0 all-gather.9.cloned.1.call-update
  461.4 0.7 reduce.2
  462.1 18.7 %all-gather.9.cloned.1.call-done = bf16[256,2560]{1,0:T(8,128)(2,1)} async-done(((bf16[256,1280]{1,0:T(8,128)(2,1)}), bf16[256,2560]{1,0:T(8,128)(2,1)}) %all-gather.9.cloned.1.call-update) | async-done | bytes 1310736 | tf_op jit(solution)/shard_map/while/body/eval_jaxpr/all_gather | solution.py:26
  480.9 1.7 fusion.99
  482.6 18.6 %convolution_convert_fusion.2 = bf16[256,2560]{1,0:T(8,128)(2,1)S(1)} fusion(bf16[2560,2560]{1,0:T(8,128)(2,1)} %get-tuple-element.329, bf16[2560,2560]{1,0:T(8,128)(2,1)} %get-tuple-element.328, bf16[256,2560]{1,0:T(8,128)(2,1)} %all-gather.9.cloned.1.call-done, f32[2560]{0:T(1024)S(1)} %reduce.2, f32[256]{0:T(256)S(1)} %add_rsqrt_fusion.2), kind=kOutput, calls=%fused_computation.1.clone.1 | convolution fusion | flops 6756761600 | bytes 28847104 | tf_op jit(solution)/shard_map/while/body/eval_jaxpr/dot_general | solution.py:33
  501.2 1.2 reshape.40
  502.4 4.1 fusion.100
  506.5 1.0 select_bitcast_fusion.2
  507.6 0.2 collective-permute-start
  507.8 2.2 collective-permute-done
  510.0 2.8 select_select_fusion.2
  512.8 2.8 collective-permute-start.1
  515.7 14.2 %collective-permute-done.1 = bf16[256,1280]{1,0:T(8,128)(2,1)S(1)} collective-permute-done((bf16[256,1280]{1,0:T(8,128)(2,1)}, bf16[256,1280]{1,0:T(8,128)(2,1)S(1)}, u32[]{:S(2)}, u32[]{:S(2)}) %collective-permute-start.1) | collective-permute-done | bytes 655392 | tf_op jit(solution)/shard_map/while/body/eval_jaxpr/ppermute | solution.py:10
  (22 shorter events, 0.1 us)
Async XLA Ops:
  6.5 129.1 %all-gather.7.cloned.1.call-start = ((), (), s32[]{:S(2)}) async-start(), calls=%async_computation.1 | async-start | bytes 13516800 | tf_op jit(solution)/shard_map/all_gather | solution.py:17
  7.3 250.3 %all-gather.5.cloned.1.call-start = ((), (), s32[]{:S(2)}) async-start(), calls=%async_computation | async-start | bytes 13516800 | tf_op jit(solution)/shard_map/all_gather | solution.py:18
  257.6 0.9 copy-start
  257.6 15.6 %all-gather.9.cloned.1.call-start = ((), (), s32[]{:S(2)}) async-start(), calls=%async_computation.2 | async-start | bytes 1966080 | tf_op jit(solution)/shard_map/while/body/eval_jaxpr/all_gather | solution.py:26
  298.8 3.5 copy-start.1
  299.8 2.4 collective-permute-start
  304.8 17.1 %collective-permute-start.1 = (bf16[256,1280]{1,0:T(8,128)(2,1)}, bf16[256,1280]{1,0:T(8,128)(2,1)S(1)}, u32[]{:S(2)}, u32[]{:S(2)}) collective-permute-start(bf16[256,1280]{1,0:T(8,128)(2,1)} %get-tuple-element.299), channel_id=1, source_target_pairs={{0,64},{64,128},{128,192},{1,65},{65,129},{129,193},{2,66},{66,130... | collective-permute-start | bytes 1966088 | tf_op jit(solution)/shard_map/while/body/eval_jaxpr/ppermute | solution.py:10
  321.9 0.9 copy-start
  321.9 20.4 %all-gather.9.cloned.1.call-start = ((), (), s32[]{:S(2)}) async-start(), calls=%async_computation.2 | async-start | bytes 1966080 | tf_op jit(solution)/shard_map/while/body/eval_jaxpr/all_gather | solution.py:26
  367.9 3.5 copy-start.1
  368.9 2.4 collective-permute-start
  374.2 17.0 %collective-permute-start.1 = (bf16[256,1280]{1,0:T(8,128)(2,1)}, bf16[256,1280]{1,0:T(8,128)(2,1)S(1)}, u32[]{:S(2)}, u32[]{:S(2)}) collective-permute-start(bf16[256,1280]{1,0:T(8,128)(2,1)} %get-tuple-element.299), channel_id=1, source_target_pairs={{0,64},{64,128},{128,192},{1,65},{65,129},{129,193},{2,66},{66,130... | collective-permute-start | bytes 1966088 | tf_op jit(solution)/shard_map/while/body/eval_jaxpr/ppermute | solution.py:10
  391.2 0.9 copy-start
  391.2 20.4 %all-gather.9.cloned.1.call-start = ((), (), s32[]{:S(2)}) async-start(), calls=%async_computation.2 | async-start | bytes 1966080 | tf_op jit(solution)/shard_map/while/body/eval_jaxpr/all_gather | solution.py:26
  437.2 3.5 copy-start.1
  438.2 2.4 collective-permute-start
  443.5 17.0 %collective-permute-start.1 = (bf16[256,1280]{1,0:T(8,128)(2,1)}, bf16[256,1280]{1,0:T(8,128)(2,1)S(1)}, u32[]{:S(2)}, u32[]{:S(2)}) collective-permute-start(bf16[256,1280]{1,0:T(8,128)(2,1)} %get-tuple-element.299), channel_id=1, source_target_pairs={{0,64},{64,128},{128,192},{1,65},{65,129},{129,193},{2,66},{66,130... | collective-permute-start | bytes 1966088 | tf_op jit(solution)/shard_map/while/body/eval_jaxpr/ppermute | solution.py:10
  460.5 0.9 copy-start
  460.5 20.4 %all-gather.9.cloned.1.call-start = ((), (), s32[]{:S(2)}) async-start(), calls=%async_computation.2 | async-start | bytes 1966080 | tf_op jit(solution)/shard_map/while/body/eval_jaxpr/all_gather | solution.py:26
  506.5 3.5 copy-start.1
  507.6 2.4 collective-permute-start
  512.8 17.0 %collective-permute-start.1 = (bf16[256,1280]{1,0:T(8,128)(2,1)}, bf16[256,1280]{1,0:T(8,128)(2,1)S(1)}, u32[]{:S(2)}, u32[]{:S(2)}) collective-permute-start(bf16[256,1280]{1,0:T(8,128)(2,1)} %get-tuple-element.299), channel_id=1, source_target_pairs={{0,64},{64,128},{128,192},{1,65},{65,129},{129,193},{2,66},{66,130... | collective-permute-start | bytes 1966088 | tf_op jit(solution)/shard_map/while/body/eval_jaxpr/ppermute | solution.py:10
Sparse Core Ops, SparseCore 0:
  9.9 125.6 all-gather.6
  138.2 119.2 all-gather.4
  260.2 12.9 all-gather.8
  324.2 17.9 all-gather.8
  393.5 18.0 all-gather.8
  462.8 18.0 all-gather.8

commit v2 on v1

--- a/solution.py
+++ b/solution.py
@@ -23,7 +23,12 @@
     first = jnp.where((row_ids < live_count)[:, None], frames, jnp.zeros_like(frames))
 
     def apply_layer(current):
-        whole = lax.all_gather(current, "mp", axis=1, tiled=True)
+        partner = lax.ppermute(current, "mp", [(0, 1), (1, 0)])
+        whole = jnp.where(
+            half_index == 0,
+            jnp.concatenate([current, partner], axis=1),
+            jnp.concatenate([partner, current], axis=1),
+        )
         wide = whole.astype(jnp.float32)
         meansq = jnp.mean(wide * wide, axis=-1, keepdims=True)
         normed = (wide * lax.rsqrt(meansq + 1e-06) * gain_row).astype(jnp.bfloat16)
@@ -33,9 +38,10 @@
         partial_term = lax.dot_general(
             hidden, matrix_out_t, (((1,), (1,)), ((), ())), preferred_element_type=jnp.float32
         ).astype(jnp.bfloat16)
-        halves = partial_term.reshape(local_rows, 2, width_local)
-        keep = jnp.where(half_index == 0, halves[:, 0], halves[:, 1])
-        send = jnp.where(half_index == 0, halves[:, 1], halves[:, 0])
+        keep = lax.dynamic_slice_in_dim(partial_term, half_index * width_local, width_local, axis=1)
+        send = lax.dynamic_slice_in_dim(
+            partial_term, (1 - half_index) * width_local, width_local, axis=1
+        )
         other = lax.ppermute(send, "mp", [(0, 1), (1, 0)])
         summed = keep.astype(jnp.float32) + other.astype(jnp.float32)
         return (current.astype(jnp.float32) + summed).astype(jnp.bfloat16)

time: 538 us -> 439 us (0.82)
  waiting for transfers between devices: 385 us -> 315 us
  local copies, waits for them, and re-layouts: 24.8 us -> 1.04 us
  other arithmetic: 25.9 us -> 12.2 us
  starting transfers between devices: 12.3 us -> 22.1 us
    all_gather x4 -> x0, waiting for transfers between devices: 70.2 us -> none  [apply_layer(): whole = lax.all_gather(current, 'mp', axis=1, tiled=True)]
    slice x4 -> x0, local copies, waits for them, and re-layouts: 16.3 us -> none  [apply_layer(): keep = jnp.where(half_index == 0, halves[:, 0], halves[:, 1])]
where the time goes in v2:
time: 439 us; the launch traced here: 438 us
  waiting for transfers between devices  315 us (72%)
  matrix products  73.3 us (17%)
  starting transfers between devices  22.1 us (5%)
  between operations  14.1 us (3%)
  other arithmetic  12.2 us (3%)
    all_gather x1, waiting for transfers between devices, per_device(): matrix_in = lax.all_gather(weight_in[0], 'dp', axis=0, tiled=True)  126 us
    all_gather x1, waiting for transfers between devices, per_device(): matrix_out_t = lax.all_gather(weight_out[0].T, 'dp', axis=0, tiled=True)  122 us
    dot_general x4, matrix products, apply_layer(): lax.dot_general(hidden, matrix_out_t, (((1,), (1,)), ((), ())), preferred...  73.3 us
    ppermute x4, waiting for transfers between devices, passed_along(): lax.ppermute(value, axis, [(source, source + steps) for source in range(f...  54.8 us
    ppermute x4, starting transfers between devices, passed_along(): lax.ppermute(value, axis, [(source, source + steps) for source in range(f...  15.6 us
  transfers between devices with their start and end apart: 14, of which 14 were waited for; matrix products, arithmetic and copies ran while one was open for 1% of the time, Pallas kernels for 0%

profile of v2, /device:TPU:1, one launch (start us, length us, event | category | flops | bytes accessed | tf_op | source)
XLA Modules:
  0.0 438.0 jit_solution(9730247414991071577)
XLA Ops:
  6.5 0.0 all-gather.6.cloned.1.call-start
  6.5 0.7 all-gather.6.cloned.1.call-update
  7.3 0.0 all-gather.4.cloned.1.call-start
  7.3 0.7 all-gather.4.cloned.1.call-update
  8.7 1.2 broadcast_select_fusion
  9.9 125.7 %all-gather.6.cloned.1.call-done = bf16[1,2560,2560]{2,1,0:T(8,128)(2,1)} async-done(((bf16[1,80,2560]{2,1,0:T(8,128)(2,1)}), bf16[1,2560,2560]{2,1,0:T(8,128)(2,1)}) %all-gather.6.cloned.1.call-update) | async-done | bytes 13107216 | tf_op jit(solution)/shard_map/all_gather | solution.py:17
  135.6 121.9 %all-gather.4.cloned.1.call-done = bf16[2560,2560]{1,0:T(8,128)(2,1)} async-done(((bf16[80,2560]{1,0:T(8,128)(2,1)}), bf16[2560,2560]{1,0:T(8,128)(2,1)}) %all-gather.4.cloned.1.call-update) | async-done | bytes 13107216 | tf_op jit(solution)/shard_map/all_gather | solution.py:18
  257.6 172.8 %while.18 = (s32[]{:T(128)}, bf16[256,1280]{1,0:T(8,128)(2,1)S(1)}, bf16[256,1280]{1,0:T(8,128)(2,1)S(1)}, pred[]{:T(512)}, f32[1,2560]{1,0:T(1,128)}, /*index=5...) while((s32[]{:T(128)}, bf16[256,1280]{1,0:T(8,128)(2,1)S(1)}, ...), condition=%wide.region_2.3_spmd.clone, body=%wide.region_0.2_spmd.clone.sunk | while | flops 6773146112 | bytes 43288856 | solution.py:56
  257.6 1.0 collective-permute-start
  258.6 0.7 reduce.2
  259.3 1.0 collective-permute-done
  260.3 0.4 fusion.96
  260.8 18.3 %convolution_convert_fusion.2 = bf16[256,2560]{1,0:T(8,128)(2,1)S(1)} fusion(bf16[2560,2560]{1,0:T(8,128)(2,1)} %get-tuple-element.366, bf16[2560,2560]{1,0:T(8,128)(2,1)} %get-tuple-element.365, f32[2560]{0:T(1024)S(1)} %reduce.2, f32[256]{0:T(256)S(1)} %add_rsqrt_fusion.2, bf16[256,1280]{1,0:T(8,128)(2,1)S(1)} %collective-permute-done, ...), kind=kOutput, calls=%fused_computation.1.clone.1 | convolution fusion | flops 6762659840 | bytes 28847104 | tf_op jit(solution)/shard_map/while/body/eval_jaxpr/dot_general | solution.py:38
  279.1 0.1 constant_dynamic-slice_fusion.2
  279.1 0.5 collective-permute-start.1
  279.6 1.9 collective-permute-done.1
  281.5 1.6 select_select_fusion.2
  283.0 3.1 collective-permute-start.2
  286.2 13.7 %collective-permute-done.2 = bf16[256,1280]{1,0:T(8,128)(2,1)S(1)} collective-permute-done((bf16[256,1280]{1,0:T(8,128)(2,1)S(1)}, bf16[256,1280]{1,0:T(8,128)(2,1)S(1)}, u32[]{:S(2)}, u32[]{:S(2)}) %collective-permute-start.2) | collective-permute-done | bytes 655392 | tf_op jit(solution)/shard_map/while/body/eval_jaxpr/ppermute | solution.py:10
  299.9 1.2 collective-permute-start
  301.1 0.7 reduce.2
  301.8 1.0 collective-permute-done
  302.8 0.4 fusion.96
  303.2 18.3 %convolution_convert_fusion.2 = bf16[256,2560]{1,0:T(8,128)(2,1)S(1)} fusion(bf16[2560,2560]{1,0:T(8,128)(2,1)} %get-tuple-element.366, bf16[2560,2560]{1,0:T(8,128)(2,1)} %get-tuple-element.365, f32[2560]{0:T(1024)S(1)} %reduce.2, f32[256]{0:T(256)S(1)} %add_rsqrt_fusion.2, bf16[256,1280]{1,0:T(8,128)(2,1)S(1)} %collective-permute-done, ...), kind=kOutput, calls=%fused_computation.1.clone.1 | convolution fusion | flops 6762659840 | bytes 28847104 | tf_op jit(solution)/shard_map/while/body/eval_jaxpr/dot_general | solution.py:38
  321.6 0.1 constant_dynamic-slice_fusion.2
  321.6 0.5 collective-permute-start.1
  322.1 1.9 collective-permute-done.1
  323.9 1.6 select_select_fusion.2
  325.5 4.1 collective-permute-start.2
  329.7 13.7 %collective-permute-done.2 = bf16[256,1280]{1,0:T(8,128)(2,1)S(1)} collective-permute-done((bf16[256,1280]{1,0:T(8,128)(2,1)S(1)}, bf16[256,1280]{1,0:T(8,128)(2,1)S(1)}, u32[]{:S(2)}, u32[]{:S(2)}) %collective-permute-start.2) | collective-permute-done | bytes 655392 | tf_op jit(solution)/shard_map/while/body/eval_jaxpr/ppermute | solution.py:10
  343.4 1.2 collective-permute-start
  344.6 0.7 reduce.2
  345.3 1.0 collective-permute-done
  346.3 0.4 fusion.96
  346.7 18.3 %convolution_convert_fusion.2 = bf16[256,2560]{1,0:T(8,128)(2,1)S(1)} fusion(bf16[2560,2560]{1,0:T(8,128)(2,1)} %get-tuple-element.366, bf16[2560,2560]{1,0:T(8,128)(2,1)} %get-tuple-element.365, f32[2560]{0:T(1024)S(1)} %reduce.2, f32[256]{0:T(256)S(1)} %add_rsqrt_fusion.2, bf16[256,1280]{1,0:T(8,128)(2,1)S(1)} %collective-permute-done, ...), kind=kOutput, calls=%fused_computation.1.clone.1 | convolution fusion | flops 6762659840 | bytes 28847104 | tf_op jit(solution)/shard_map/while/body/eval_jaxpr/dot_general | solution.py:38
  365.0 0.1 constant_dynamic-slice_fusion.2
  365.1 0.5 collective-permute-start.1
  365.6 1.9 collective-permute-done.1
  367.4 1.6 select_select_fusion.2
  369.0 4.1 collective-permute-start.2
  373.2 13.7 %collective-permute-done.2 = bf16[256,1280]{1,0:T(8,128)(2,1)S(1)} collective-permute-done((bf16[256,1280]{1,0:T(8,128)(2,1)S(1)}, bf16[256,1280]{1,0:T(8,128)(2,1)S(1)}, u32[]{:S(2)}, u32[]{:S(2)}) %collective-permute-start.2) | collective-permute-done | bytes 655392 | tf_op jit(solution)/shard_map/while/body/eval_jaxpr/ppermute | solution.py:10
  386.9 1.2 collective-permute-start
  388.0 0.7 reduce.2
  388.8 1.0 collective-permute-done
  389.8 0.4 fusion.96
  390.2 18.3 %convolution_convert_fusion.2 = bf16[256,2560]{1,0:T(8,128)(2,1)S(1)} fusion(bf16[2560,2560]{1,0:T(8,128)(2,1)} %get-tuple-element.366, bf16[2560,2560]{1,0:T(8,128)(2,1)} %get-tuple-element.365, f32[2560]{0:T(1024)S(1)} %reduce.2, f32[256]{0:T(256)S(1)} %add_rsqrt_fusion.2, bf16[256,1280]{1,0:T(8,128)(2,1)S(1)} %collective-permute-done, ...), kind=kOutput, calls=%fused_computation.1.clone.1 | convolution fusion | flops 6762659840 | bytes 28847104 | tf_op jit(solution)/shard_map/while/body/eval_jaxpr/dot_general | solution.py:38
  408.5 0.1 constant_dynamic-slice_fusion.2
  408.6 0.5 collective-permute-start.1
  409.1 1.9 collective-permute-done.1
  410.9 1.6 select_select_fusion.2
  412.5 4.1 collective-permute-start.2
  416.6 13.7 %collective-permute-done.2 = bf16[256,1280]{1,0:T(8,128)(2,1)S(1)} collective-permute-done((bf16[256,1280]{1,0:T(8,128)(2,1)S(1)}, bf16[256,1280]{1,0:T(8,128)(2,1)S(1)}, u32[]{:S(2)}, u32[]{:S(2)}) %collective-permute-start.2) | collective-permute-done | bytes 655392 | tf_op jit(solution)/shard_map/while/body/eval_jaxpr/ppermute | solution.py:10
  430.3 0.0 copy-start
  430.3 0.8 copy-done
  (6 shorter events, 0.0 us)
Async XLA Ops:
  6.5 129.1 %all-gather.6.cloned.1.call-start = ((), (), s32[]{:S(2)}) async-start(), calls=%async_computation.1 | async-start | bytes 13516800 | tf_op jit(solution)/shard_map/all_gather | solution.py:17
  7.3 250.3 %all-gather.4.cloned.1.call-start = ((), (), s32[]{:S(2)}) async-start(), calls=%async_computation | async-start | bytes 13516800 | tf_op jit(solution)/shard_map/all_gather | solution.py:18
  257.6 2.8 collective-permute-start
  279.1 2.3 collective-permute-start.1
  283.0 16.8 %collective-permute-start.2 = (bf16[256,1280]{1,0:T(8,128)(2,1)S(1)}, bf16[256,1280]{1,0:T(8,128)(2,1)S(1)}, u32[]{:S(2)}, u32[]{:S(2)}) collective-permute-start(bf16[256,1280]{1,0:T(8,128)(2,1)S(1)} %get-tuple-element.332), channel_id=1, source_target_pairs={{0,64},{64,128},{128,192},{1,65},{65,129},{129,193},{2,66},{66,130... | collective-permute-start | bytes 1966088 | tf_op jit(solution)/shard_map/while/body/eval_jaxpr/ppermute | solution.py:10
  299.9 2.9 collective-permute-start
  321.6 2.3 collective-permute-start.1
  325.5 17.8 %collective-permute-start.2 = (bf16[256,1280]{1,0:T(8,128)(2,1)S(1)}, bf16[256,1280]{1,0:T(8,128)(2,1)S(1)}, u32[]{:S(2)}, u32[]{:S(2)}) collective-permute-start(bf16[256,1280]{1,0:T(8,128)(2,1)S(1)} %get-tuple-element.332), channel_id=1, source_target_pairs={{0,64},{64,128},{128,192},{1,65},{65,129},{129,193},{2,66},{66,130... | collective-permute-start | bytes 1966088 | tf_op jit(solution)/shard_map/while/body/eval_jaxpr/ppermute | solution.py:10
  343.4 2.9 collective-permute-start
  365.1 2.3 collective-permute-start.1
  369.0 17.8 %collective-permute-start.2 = (bf16[256,1280]{1,0:T(8,128)(2,1)S(1)}, bf16[256,1280]{1,0:T(8,128)(2,1)S(1)}, u32[]{:S(2)}, u32[]{:S(2)}) collective-permute-start(bf16[256,1280]{1,0:T(8,128)(2,1)S(1)} %get-tuple-element.332), channel_id=1, source_target_pairs={{0,64},{64,128},{128,192},{1,65},{65,129},{129,193},{2,66},{66,130... | collective-permute-start | bytes 1966088 | tf_op jit(solution)/shard_map/while/body/eval_jaxpr/ppermute | solution.py:10
  386.9 2.9 collective-permute-start
  408.6 2.3 collective-permute-start.1
  412.5 17.8 %collective-permute-start.2 = (bf16[256,1280]{1,0:T(8,128)(2,1)S(1)}, bf16[256,1280]{1,0:T(8,128)(2,1)S(1)}, u32[]{:S(2)}, u32[]{:S(2)}) collective-permute-start(bf16[256,1280]{1,0:T(8,128)(2,1)S(1)} %get-tuple-element.332), channel_id=1, source_target_pairs={{0,64},{64,128},{128,192},{1,65},{65,129},{129,193},{2,66},{66,130... | collective-permute-start | bytes 1966088 | tf_op jit(solution)/shard_map/while/body/eval_jaxpr/ppermute | solution.py:10
  430.3 0.8 copy-start
Sparse Core Ops, SparseCore 0:
  9.9 125.6 all-gather.5
  138.2 119.2 all-gather.3

commit v3 on v2

--- a/solution.py
+++ b/solution.py
@@ -2,6 +2,8 @@
 import jax.numpy as jnp
 from jax import lax
 from jax.sharding import PartitionSpec as P
+
+CHUNKS = 4
 
 
 def passed_along(value, axis, steps):
@@ -14,8 +16,14 @@
     segment_count = lax.axis_size("section")
     segment_index = lax.axis_index("section")
     half_index = lax.axis_index("mp")
-    matrix_in = lax.all_gather(weight_in[0], "dp", axis=0, tiled=True)
-    matrix_out_t = lax.all_gather(weight_out[0].T, "dp", axis=0, tiled=True)
+    hidden_local = weight_in.shape[2]
+    piece = hidden_local // CHUNKS
+    chunks = []
+    for index in range(CHUNKS):
+        cols = slice(index * piece, (index + 1) * piece)
+        chunk_in = lax.all_gather(weight_in[0][:, cols], "dp", axis=0, tiled=True)
+        chunk_out = lax.all_gather(weight_out[0][cols, :].T, "dp", axis=0, tiled=True)
+        chunks.append((chunk_in, chunk_out))
     gain_row = norm_gain[0]
     local_rows, width_local = frames.shape
     live_count = frame_count[0]
@@ -32,12 +40,16 @@
         wide = whole.astype(jnp.float32)
         meansq = jnp.mean(wide * wide, axis=-1, keepdims=True)
         normed = (wide * lax.rsqrt(meansq + 1e-06) * gain_row).astype(jnp.bfloat16)
-        hidden = jax.nn.gelu(
-            jnp.dot(normed, matrix_in, preferred_element_type=jnp.float32), approximate=False
-        ).astype(jnp.bfloat16)
-        partial_term = lax.dot_general(
-            hidden, matrix_out_t, (((1,), (1,)), ((), ())), preferred_element_type=jnp.float32
-        ).astype(jnp.bfloat16)
+        total = None
+        for chunk_in, chunk_out in chunks:
+            hidden = jax.nn.gelu(
+                jnp.dot(normed, chunk_in, preferred_element_type=jnp.float32), approximate=False
+            ).astype(jnp.bfloat16)
+            term = lax.dot_general(
+                hidden, chunk_out, (((1,), (1,)), ((), ())), preferred_element_type=jnp.float32
+            )
+            total = term if total is None else total + term
+        partial_term = total.astype(jnp.bfloat16)
         keep = lax.dynamic_slice_in_dim(partial_term, half_index * width_local, width_local, axis=1)
         send = lax.dynamic_slice_in_dim(
             partial_term, (1 - half_index) * width_local, width_local, axis=1
@@ -46,14 +58,16 @@
         summed = keep.astype(jnp.float32) + other.astype(jnp.float32)
         return (current.astype(jnp.float32) + summed).astype(jnp.bfloat16)
 
+    result = apply_layer(first)
+    stored = jnp.where(segment_index == 0, result, jnp.zeros_like(result))
+
     def advance(moment, carry):
-        current, stored = carry
-        result = apply_layer(current)
+        previous, stored = carry
+        result = apply_layer(passed_along(previous, "section", 1))
         stored = jnp.where(segment_index == moment, result, stored)
-        return (passed_along(result, "section", 1), stored)
+        return (result, stored)
 
-    initial = (first, jnp.zeros((local_rows, width_local), jnp.bfloat16))
-    leftover, stored = lax.fori_loop(0, segment_count, advance, initial)
+    leftover, stored = lax.fori_loop(1, segment_count, advance, (result, stored))
     return stored.reshape(1, local_rows, width_local)
 
 

time: 439 us -> 844 us (1.92)
  waiting for transfers between devices: 315 us -> 659 us
  matrix products: 73.3 us -> 129 us
    all_gather x2 -> x8, waiting for transfers between devices: 248 us -> 600 us  [the longest x4 307 us: per_device(): lax.all_gather(weight_out[0][cols, :].T, 'dp', axis=0, tiled=True)]
    dot_general x4 -> x16, matrix products: 73.3 us -> 129 us  [apply_layer(): lax.dot_general(hidden, chunk_out, (((1,), (1,)), ((), ())), preferred_el...]
    ppermute x4 -> x3, waiting for transfers between devices: 54.8 us -> 42 us  [passed_along(): lax.ppermute(value, axis, [(source, source + steps) for source in range(f...]
  transfers between devices with their start and end apart: 14 -> 19, of which waited for: 14 -> 19; matrix products, arithmetic and copies ran while one was open for 1% -> 3% of each run, Pallas kernels for 0% -> 0%
where the time goes in v3:
time: 844 us
  waiting for transfers between devices  659 us (78%)
  matrix products  129 us (15%)
  starting transfers between devices  23.6 us (3%)
  between operations  14.2 us (2%)
  other arithmetic  13.1 us (2%)
    all_gather x4, waiting for transfers between devices, per_device(): lax.all_gather(weight_out[0][cols, :].T, 'dp', axis=0, tiled=True)  307 us
    all_gather x4, waiting for transfers between devices, per_device(): chunk_in = lax.all_gather(weight_in[0][:, cols], 'dp', axis=0, tiled=True)  293 us
    dot_general x16, matrix products, apply_layer(): lax.dot_general(hidden, chunk_out, (((1,), (1,)), ((), ())), preferred_el...  129 us
    ppermute x3, waiting for transfers between devices, passed_along(): lax.ppermute(value, axis, [(source, source + steps) for source in range(f...  42 us
  transfers between devices with their start and end apart: 19, of which 19 were waited for; matrix products, arithmetic and copies ran while one was open for 3% of the time, Pallas kernels for 0%

profile of v3, /device:TPU:1, one launch (start us, length us, event | category | flops | bytes accessed | tf_op | source)
XLA Modules:
  0.0 843.6 jit_solution(11647590530056371370)
XLA Ops:
  6.5 1.9 slice_bitcast_fusion
  8.5 1.8 fusion.578
  10.4 0.7 all-gather.13.cloned.1.call-update
  11.1 0.5 all-gather.15.cloned.1.call-update
  11.7 0.5 all-gather.17.cloned.1.call-update
  12.3 0.5 all-gather.19.cloned.1.call-update
  12.9 0.7 all-gather.21.cloned.1.call-update
  13.6 0.7 all-gather.23.cloned.1.call-update
  15.1 3.3 collective-permute-start.3
  18.5 1.7 collective-permute-done.3
  20.6 0.6 fusion.292
  21.2 68.9 %all-gather.11.cloned.1.call-done = bf16[2560,640]{1,0:T(8,128)(2,1)} async-done(((bf16[80,640]{1,0:T(8,128)(2,1)}), bf16[2560,640]{1,0:T(8,128)(2,1)}) %all-gather.11.cloned.1.call-update) | async-done | bytes 3276816 | tf_op jit(solution)/shard_map/all_gather | solution.py:25
  90.1 79.5 %all-gather.9.cloned.1.call-done = bf16[2560,640]{1,0:T(8,128)(2,1)} async-done(((bf16[80,640]{1,0:T(8,128)(2,1)}), bf16[2560,640]{1,0:T(8,128)(2,1)}) %all-gather.9.cloned.1.call-update) | async-done | bytes 3276816 | tf_op jit(solution)/shard_map/all_gather | solution.py:24
  169.6 7.9 fusion.336
  177.4 71.6 %all-gather.13.cloned.1.call-done = bf16[2560,640]{1,0:T(8,128)(2,1)} async-done(((bf16[80,640]{1,0:T(8,128)(2,1)}), bf16[2560,640]{1,0:T(8,128)(2,1)}) %all-gather.13.cloned.1.call-update) | async-done | bytes 3276816 | tf_op jit(solution)/shard_map/all_gather | solution.py:24
  249.1 79.3 %all-gather.15.cloned.1.call-done = bf16[2560,640]{1,0:T(8,128)(2,1)} async-done(((bf16[80,640]{1,0:T(8,128)(2,1)}), bf16[2560,640]{1,0:T(8,128)(2,1)}) %all-gather.15.cloned.1.call-update) | async-done | bytes 3276816 | tf_op jit(solution)/shard_map/all_gather | solution.py:25
  328.4 8.6 %convolution_add_fusion.5 = f32[256,2560]{1,0:T(8,128)} fusion(f32[256,2560]{1,0:T(8,128)} %fusion.336, bf16[2560,640]{1,0:T(8,128)(2,1)} %all-gather.15.cloned.1.call-done, bf16[256,2560]{1,0:T(8,128)(2,1)S(1)} %fusion.292, bf16[2560,640]{1,0:T(8,128)(2,1)} %all-gather.13.cloned.1.call-done), kind=kOutput, calls=%fused_computation.333 | convolution fusion | flops 1689026560 | bytes 13107200 | tf_op jit(solution)/shard_map/dot_general | solution.py:48
  337.0 70.7 %all-gather.17.cloned.1.call-done = bf16[2560,640]{1,0:T(8,128)(2,1)} async-done(((bf16[80,640]{1,0:T(8,128)(2,1)}), bf16[2560,640]{1,0:T(8,128)(2,1)}) %all-gather.17.cloned.1.call-update) | async-done | bytes 3276816 | tf_op jit(solution)/shard_map/all_gather | solution.py:24
  407.7 79.3 %all-gather.19.cloned.1.call-done = bf16[2560,640]{1,0:T(8,128)(2,1)} async-done(((bf16[80,640]{1,0:T(8,128)(2,1)}), bf16[2560,640]{1,0:T(8,128)(2,1)}) %all-gather.19.cloned.1.call-update) | async-done | bytes 3276816 | tf_op jit(solution)/shard_map/all_gather | solution.py:25
  487.1 8.6 %convolution_add_fusion.4 = f32[256,2560]{1,0:T(8,128)} fusion(f32[256,2560]{1,0:T(8,128)} %convolution_add_fusion.5, bf16[2560,640]{1,0:T(8,128)(2,1)} %all-gather.19.cloned.1.call-done, bf16[256,2560]{1,0:T(8,128)(2,1)S(1)} %fusion.292, bf16[2560,640]{1,0:T(8,128)(2,1)} %all-gather.17.cloned.1.call-done), kind=kOutput, calls=%fused_computation.332 | convolution fusion | flops 1689026560 | bytes 13107200 | tf_op jit(solution)/shard_map/dot_general | solution.py:48
  495.7 70.9 %all-gather.21.cloned.1.call-done = bf16[2560,640]{1,0:T(8,128)(2,1)} async-done(((bf16[80,640]{1,0:T(8,128)(2,1)}), bf16[2560,640]{1,0:T(8,128)(2,1)}) %all-gather.21.cloned.1.call-update) | async-done | bytes 3276816 | tf_op jit(solution)/shard_map/all_gather | solution.py:24
  566.6 79.5 %all-gather.23.cloned.1.call-done = bf16[2560,640]{1,0:T(8,128)(2,1)} async-done(((bf16[80,640]{1,0:T(8,128)(2,1)}), bf16[2560,640]{1,0:T(8,128)(2,1)}) %all-gather.23.cloned.1.call-update) | async-done | bytes 3276816 | tf_op jit(solution)/shard_map/all_gather | solution.py:25
  646.1 7.2 fusion.289
  653.3 4.8 collective-permute-start.4
  658.1 1.7 collective-permute-done.4
  659.8 1.4 broadcast_select_fusion.2
  661.2 175.5 %while.17 = (s32[]{:T(128)}, bf16[256,1280]{1,0:T(8,128)(2,1)}, bf16[256,1280]{1,0:T(8,128)(2,1)}, pred[]{:T(512)}, f32[1,2560]{1,0:T(1,128)S(1)}, /*index=5*/bf...) while((s32[]{:T(128)}, bf16[256,1280]{1,0:T(8,128)(2,1)}, ...), condition=%wide.region_3.4_spmd, body=%wide.region_1.3_spmd.sunk | while | flops 6774784000 | bytes 65571124 | solution.py:70
  661.2 3.1 collective-permute-start
  664.4 14.0 %collective-permute-done = bf16[256,1280]{1,0:T(8,128)(2,1)S(1)} collective-permute-done((bf16[256,1280]{1,0:T(8,128)(2,1)}, bf16[256,1280]{1,0:T(8,128)(2,1)S(1)}, u32[]{:S(2)}, u32[]{:S(2)}) %collective-permute-start) | collective-permute-done | bytes 655392 | tf_op jit(solution)/shard_map/while/body/eval_jaxpr/ppermute | solution.py:12
  678.4 1.2 collective-permute-start.1
  679.6 1.7 collective-permute-done.1
  681.3 0.4 fusion.655
  681.7 0.6 fusion.656
  682.3 7.9 fusion.657
  690.2 8.7 %convolution_add_fusion.8 = f32[256,2560]{1,0:T(8,128)} fusion(f32[256,2560]{1,0:T(8,128)} %fusion.657, bf16[2560,640]{1,0:T(8,128)(2,1)} %get-tuple-element.529, bf16[256,2560]{1,0:T(8,128)(2,1)S(1)} %fusion.656, bf16[2560,640]{1,0:T(8,128)(2,1)} %get-tuple-element.528), kind=kOutput, calls=%fused_computation.2.clone.1 | convolution fusion | flops 1689026560 | bytes 13107200 | tf_op jit(solution)/shard_map/while/body/eval_jaxpr/dot_general | solution.py:48
  698.8 8.6 %convolution_add_fusion.9 = f32[256,2560]{1,0:T(8,128)} fusion(f32[256,2560]{1,0:T(8,128)} %convolution_add_fusion.8, bf16[2560,640]{1,0:T(8,128)(2,1)} %get-tuple-element.531, bf16[256,2560]{1,0:T(8,128)(2,1)S(1)} %fusion.656, bf16[2560,640]{1,0:T(8,128)(2,1)} %get-tuple-element.530), kind=kOutput, calls=%fused_computation.1.clone.1 | convolution fusion | flops 1689026560 | bytes 13107200 | tf_op jit(solution)/shard_map/while/body/eval_jaxpr/dot_general | solution.py:48
  707.5 7.2 fusion.658
  714.8 0.5 collective-permute-start.2
  715.2 1.7 collective-permute-done.2
  717.0 2.5 broadcast_select_fusion.4
  719.4 2.9 collective-permute-start
  722.4 14.0 %collective-permute-done = bf16[256,1280]{1,0:T(8,128)(2,1)S(1)} collective-permute-done((bf16[256,1280]{1,0:T(8,128)(2,1)}, bf16[256,1280]{1,0:T(8,128)(2,1)S(1)}, u32[]{:S(2)}, u32[]{:S(2)}) %collective-permute-start) | collective-permute-done | bytes 655392 | tf_op jit(solution)/shard_map/while/body/eval_jaxpr/ppermute | solution.py:12
  736.4 1.2 collective-permute-start.1
  737.6 1.7 collective-permute-done.1
  739.8 0.6 fusion.656
  740.3 7.9 fusion.657
  748.2 8.6 %convolution_add_fusion.8 = f32[256,2560]{1,0:T(8,128)} fusion(f32[256,2560]{1,0:T(8,128)} %fusion.657, bf16[2560,640]{1,0:T(8,128)(2,1)} %get-tuple-element.529, bf16[256,2560]{1,0:T(8,128)(2,1)S(1)} %fusion.656, bf16[2560,640]{1,0:T(8,128)(2,1)} %get-tuple-element.528), kind=kOutput, calls=%fused_computation.2.clone.1 | convolution fusion | flops 1689026560 | bytes 13107200 | tf_op jit(solution)/shard_map/while/body/eval_jaxpr/dot_general | solution.py:48
  756.9 8.7 %convolution_add_fusion.9 = f32[256,2560]{1,0:T(8,128)} fusion(f32[256,2560]{1,0:T(8,128)} %convolution_add_fusion.8, bf16[2560,640]{1,0:T(8,128)(2,1)} %get-tuple-element.531, bf16[256,2560]{1,0:T(8,128)(2,1)S(1)} %fusion.656, bf16[2560,640]{1,0:T(8,128)(2,1)} %get-tuple-element.530), kind=kOutput, calls=%fused_computation.1.clone.1 | convolution fusion | flops 1689026560 | bytes 13107200 | tf_op jit(solution)/shard_map/while/body/eval_jaxpr/dot_general | solution.py:48
  765.5 7.2 fusion.658
  772.8 0.5 collective-permute-start.2
  773.3 1.7 collective-permute-done.2
  775.0 2.5 broadcast_select_fusion.4
  777.5 4.2 collective-permute-start
  781.7 14.0 %collective-permute-done = bf16[256,1280]{1,0:T(8,128)(2,1)S(1)} collective-permute-done((bf16[256,1280]{1,0:T(8,128)(2,1)}, bf16[256,1280]{1,0:T(8,128)(2,1)S(1)}, u32[]{:S(2)}, u32[]{:S(2)}) %collective-permute-start) | collective-permute-done | bytes 655392 | tf_op jit(solution)/shard_map/while/body/eval_jaxpr/ppermute | solution.py:12
  795.7 1.2 collective-permute-start.1
  796.9 1.7 collective-permute-done.1
  799.0 0.6 fusion.656
  799.6 7.9 fusion.657
  807.5 8.6 %convolution_add_fusion.8 = f32[256,2560]{1,0:T(8,128)} fusion(f32[256,2560]{1,0:T(8,128)} %fusion.657, bf16[2560,640]{1,0:T(8,128)(2,1)} %get-tuple-element.529, bf16[256,2560]{1,0:T(8,128)(2,1)S(1)} %fusion.656, bf16[2560,640]{1,0:T(8,128)(2,1)} %get-tuple-element.528), kind=kOutput, calls=%fused_computation.2.clone.1 | convolution fusion | flops 1689026560 | bytes 13107200 | tf_op jit(solution)/shard_map/while/body/eval_jaxpr/dot_general | solution.py:48
  816.2 8.6 %convolution_add_fusion.9 = f32[256,2560]{1,0:T(8,128)} fusion(f32[256,2560]{1,0:T(8,128)} %convolution_add_fusion.8, bf16[2560,640]{1,0:T(8,128)(2,1)} %get-tuple-element.531, bf16[256,2560]{1,0:T(8,128)(2,1)S(1)} %fusion.656, bf16[2560,640]{1,0:T(8,128)(2,1)} %get-tuple-element.530), kind=kOutput, calls=%fused_computation.1.clone.1 | convolution fusion | flops 1689026560 | bytes 13107200 | tf_op jit(solution)/shard_map/while/body/eval_jaxpr/dot_general | solution.py:48
  824.8 7.2 fusion.658
  832.1 0.5 collective-permute-start.2
  832.5 1.7 collective-permute-done.2
  834.3 2.5 broadcast_select_fusion.4
  (31 shorter events, 2.1 us)
Async XLA Ops:
  6.5 8.5 %copy-start = (bf16[256,1280]{1,0:T(8,128)(2,1)S(1)}, bf16[256,1280]{1,0:T(8,128)(2,1)}, u32[]{:S(2)}) copy-start(bf16[256,1280]{1,0:T(8,128)(2,1)} %param.7) | copy-start | bytes 1966084
  6.5 11.9 %copy-start.1 = (f32[1,2560]{1,0:T(1,128)S(1)}, f32[1,2560]{1,0:T(1,128)}, u32[]{:S(2)}) copy-start(f32[1,2560]{1,0:T(1,128)} %param.9) | copy-start | bytes 30724
  6.5 83.5 %all-gather.11.cloned.1.call-start = ((), (), s32[]{:S(2)}) async-start(), calls=%async_computation.1 | async-start | bytes 3379200 | tf_op jit(solution)/shard_map/all_gather | solution.py:25
  8.4 161.1 %all-gather.9.cloned.1.call-start = ((), (), s32[]{:S(2)}) async-start(), calls=%async_computation | async-start | bytes 3379200 | tf_op jit(solution)/shard_map/all_gather | solution.py:24
  10.3 238.7 %all-gather.13.cloned.1.call-start = ((), (), s32[]{:S(2)}) async-start(), calls=%async_computation.2 | async-start | bytes 3379200 | tf_op jit(solution)/shard_map/all_gather | solution.py:24
  11.1 317.3 %all-gather.15.cloned.1.call-start = ((), (), s32[]{:S(2)}) async-start(), calls=%async_computation.3 | async-start | bytes 3379200 | tf_op jit(solution)/shard_map/all_gather | solution.py:25
  11.7 396.1 %all-gather.17.cloned.1.call-start = ((), (), s32[]{:S(2)}) async-start(), calls=%async_computation.4 | async-start | bytes 3379200 | tf_op jit(solution)/shard_map/all_gather | solution.py:24
  12.3 474.8 %all-gather.19.cloned.1.call-start = ((), (), s32[]{:S(2)}) async-start(), calls=%async_computation.5 | async-start | bytes 3379200 | tf_op jit(solution)/shard_map/all_gather | solution.py:25
  12.8 553.8 %all-gather.21.cloned.1.call-start = ((), (), s32[]{:S(2)}) async-start(), calls=%async_computation.6 | async-start | bytes 3379200 | tf_op jit(solution)/shard_map/all_gather | solution.py:24
  13.6 632.5 %all-gather.23.cloned.1.call-start = ((), (), s32[]{:S(2)}) async-start(), calls=%async_computation.7 | async-start | bytes 3379200 | tf_op jit(solution)/shard_map/all_gather | solution.py:25
  15.1 5.1 collective-permute-start.3
  653.3 6.5 collective-permute-start.4
  661.2 17.1 %collective-permute-start = (bf16[256,1280]{1,0:T(8,128)(2,1)}, bf16[256,1280]{1,0:T(8,128)(2,1)S(1)}, u32[]{:S(2)}, u32[]{:S(2)}) collective-permute-start(bf16[256,1280]{1,0:T(8,128)(2,1)} %get-tuple-element.504), channel_id=1, source_target_pairs={{0,64},{64,128},{128,192},{1,65},{65,129},{129,193},{2,66},{66,130... | collective-permute-start | bytes 1966088 | tf_op jit(solution)/shard_map/while/body/eval_jaxpr/ppermute | solution.py:12
  678.4 2.9 collective-permute-start.1
  714.8 2.2 collective-permute-start.2
  719.4 17.0 %collective-permute-start = (bf16[256,1280]{1,0:T(8,128)(2,1)}, bf16[256,1280]{1,0:T(8,128)(2,1)S(1)}, u32[]{:S(2)}, u32[]{:S(2)}) collective-permute-start(bf16[256,1280]{1,0:T(8,128)(2,1)} %get-tuple-element.504), channel_id=1, source_target_pairs={{0,64},{64,128},{128,192},{1,65},{65,129},{129,193},{2,66},{66,130... | collective-permute-start | bytes 1966088 | tf_op jit(solution)/shard_map/while/body/eval_jaxpr/ppermute | solution.py:12
  736.4 2.9 collective-permute-start.1
  772.8 2.2 collective-permute-start.2
  777.5 18.2 %collective-permute-start = (bf16[256,1280]{1,0:T(8,128)(2,1)}, bf16[256,1280]{1,0:T(8,128)(2,1)S(1)}, u32[]{:S(2)}, u32[]{:S(2)}) collective-permute-start(bf16[256,1280]{1,0:T(8,128)(2,1)} %get-tuple-element.504), channel_id=1, source_target_pairs={{0,64},{64,128},{128,192},{1,65},{65,129},{129,193},{2,66},{66,130... | collective-permute-start | bytes 1966088 | tf_op jit(solution)/shard_map/while/body/eval_jaxpr/ppermute | solution.py:12
  795.7 2.9 collective-permute-start.1
  832.1 2.2 collective-permute-start.2
Sparse Core Ops, SparseCore 0:
  10.0 80.0 all-gather.10
  92.7 76.8 all-gather.8
  172.2 76.8 all-gather.12
  251.5 76.8 all-gather.14
  330.9 76.8 all-gather.16
  410.2 76.8 all-gather.18
  489.7 76.8 all-gather.20
  569.2 76.8 all-gather.22

commit v4 on v2

--- a/solution.py
+++ b/solution.py
@@ -14,8 +14,10 @@
     segment_count = lax.axis_size("section")
     segment_index = lax.axis_index("section")
     half_index = lax.axis_index("mp")
-    matrix_in = lax.all_gather(weight_in[0], "dp", axis=0, tiled=True)
-    matrix_out_t = lax.all_gather(weight_out[0].T, "dp", axis=0, tiled=True)
+    both = jnp.stack([weight_in[0], weight_out[0].T])
+    gathered = lax.all_gather(both, "dp", axis=1, tiled=True)
+    matrix_in = gathered[0]
+    matrix_out_t = gathered[1]
     gain_row = norm_gain[0]
     local_rows, width_local = frames.shape
     live_count = frame_count[0]
@@ -46,14 +48,16 @@
         summed = keep.astype(jnp.float32) + other.astype(jnp.float32)
         return (current.astype(jnp.float32) + summed).astype(jnp.bfloat16)
 
+    result = apply_layer(first)
+    stored = jnp.where(segment_index == 0, result, jnp.zeros_like(result))
+
     def advance(moment, carry):
-        current, stored = carry
-        result = apply_layer(current)
+        previous, stored = carry
+        result = apply_layer(passed_along(previous, "section", 1))
         stored = jnp.where(segment_index == moment, result, stored)
-        return (passed_along(result, "section", 1), stored)
+        return (result, stored)
 
-    initial = (first, jnp.zeros((local_rows, width_local), jnp.bfloat16))
-    leftover, stored = lax.fori_loop(0, segment_count, advance, initial)
+    leftover, stored = lax.fori_loop(1, segment_count, advance, (result, stored))
     return stored.reshape(1, local_rows, width_local)
 
 

time: 439 us -> 379 us (0.86)
  waiting for transfers between devices: 315 us -> 242 us
  local copies, waits for them, and re-layouts: 1.04 us -> 18.6 us
    all_gather x2 -> x1, waiting for transfers between devices: 248 us -> 188 us  [per_device(): gathered = lax.all_gather(both, 'dp', axis=1, tiled=True)]
    squeeze x0 -> x1, local copies, waits for them, and re-layouts: none -> 17.5 us  [per_device(): matrix_out_t = gathered[1]]
    ppermute x4 -> x3, waiting for transfers between devices: 54.8 us -> 41.5 us  [passed_along(): lax.ppermute(value, axis, [(source, source + steps) for source in range(f...]
    ppermute x4 -> x3, starting transfers between devices: 15.6 us -> 11.4 us  [passed_along(): lax.ppermute(value, axis, [(source, source + steps) for source in range(f...]
  transfers between devices with their start and end apart: 14 -> 12, of which waited for: 14 -> 11; matrix products, arithmetic and copies ran while one was open for 1% -> 5% of each run, Pallas kernels for 0% -> 0%
where the time goes in v4:
time: 379 us; the launch traced here: 378 us
  waiting for transfers between devices  242 us (64%)
  matrix products  73.2 us (19%)
  starting transfers between devices  20.7 us (5%)
  local copies, waits for them, and re-layouts  18.6 us (5%)
  between operations  14.1 us (4%)
  other arithmetic  9.16 us (2%)
    all_gather x1, waiting for transfers between devices, per_device(): gathered = lax.all_gather(both, 'dp', axis=1, tiled=True)  188 us
    dot_general x4, matrix products, apply_layer(): lax.dot_general(hidden, matrix_out_t, (((1,), (1,)), ((), ())), preferred...  73.2 us
    ppermute x3, waiting for transfers between devices, passed_along(): lax.ppermute(value, axis, [(source, source + steps) for source in range(f...  41.5 us
    squeeze x1, local copies, waits for them, and re-layouts, per_device(): matrix_out_t = gathered[1]  17.5 us
    ppermute x3, starting transfers between devices, passed_along(): lax.ppermute(value, axis, [(source, source + steps) for source in range(f...  11.4 us
  transfers between devices with their start and end apart: 12, of which 11 were waited for; matrix products, arithmetic and copies ran while one was open for 5% of the time, Pallas kernels for 0%

profile of v4, /device:TPU:1, one launch (start us, length us, event | category | flops | bytes accessed | tf_op | source)
XLA Modules:
  0.0 378.1 jit_solution(5766570635154216841)
XLA Ops:
  6.5 0.0 copy-start.1
  6.5 0.0 copy-start.2
  6.5 0.0 all-gather.2.cloned.1.call-start
  6.5 2.1 pad_maximum_fusion
  8.7 0.0 all-gather.2.cloned.1.call-update
  9.4 0.0 copy-done.1
  9.4 0.1 broadcast_select_fusion.1
  9.5 3.3 collective-permute-start.3
  12.8 0.0 copy-done.2
  12.9 1.7 collective-permute-done.3
  14.6 0.4 fusion.85
  15.0 188.4 %all-gather.2.cloned.1.call-done = bf16[2,2560,2560]{2,1,0:T(8,128)(2,1)} async-done(((bf16[2,80,2560]{2,1,0:T(8,128)(2,1)}), bf16[2,2560,2560]{2,1,0:T(8,128)(2,1)}) %all-gather.2.cloned.1.call-update) | async-done | bytes 26214416 | tf_op jit(solution)/shard_map/all_gather | solution.py:18
  203.4 18.3 %convolution_convert_fusion.1 = bf16[256,2560]{1,0:T(8,128)(2,1)S(1)} fusion(f32[2560]{0:T(1024)S(1)} %reduce.1, f32[256]{0:T(256)S(1)} %add_rsqrt_fusion.1, bf16[256,1280]{1,0:T(8,128)(2,1)S(1)} %collective-permute-done.3, bf16[256,1280]{1,0:T(8,128)(2,1)S(1)} %broadcast_select_fusion.1, pred[]{:T(512)} %eq.22, ...), kind=kOutput, calls=%fused_computation.97 | convolution fusion | flops 6762659840 | bytes 28847104 | tf_op jit(solution)/shard_map/dot_general | solution.py:40
  221.7 0.1 constant_dynamic-slice_fusion.1
  221.7 1.3 collective-permute-start.4
  223.0 17.5 %slice_bitcast_fusion = (bf16[2560,2560]{1,0:T(8,128)(2,1)}, bf16[2560,2560]{1,0:T(8,128)(2,1)}) fusion(bf16[2,2560,2560]{2,1,0:T(8,128)(2,1)} %all-gather.2.cloned.1.call-done), kind=kLoop, calls=%fused_computation.94 | loop fusion | bytes 52428800 | tf_op jit(solution)/shard_map/squeeze | solution.py:20
  240.5 0.0 collective-permute-done.4
  240.6 0.4 broadcast_select_fusion.2
  241.0 129.4 %while.17 = (s32[]{:T(128)}, bf16[256,1280]{1,0:T(8,128)(2,1)S(1)}, bf16[256,1280]{1,0:T(8,128)(2,1)S(1)}, pred[]{:T(512)}, f32[1,2560]{1,0:T(1,128)S(1)}, /*ind...) while((s32[]{:T(128)}, bf16[256,1280]{1,0:T(8,128)(2,1)S(1)}, ...), condition=%wide.region_3.4_spmd, body=%wide.region_1.3_spmd.sunk | while | flops 6772818432 | bytes 43288832 | solution.py:60
  241.0 3.1 collective-permute-start
  244.1 14.1 %collective-permute-done = bf16[256,1280]{1,0:T(8,128)(2,1)S(1)} collective-permute-done((bf16[256,1280]{1,0:T(8,128)(2,1)S(1)}, bf16[256,1280]{1,0:T(8,128)(2,1)S(1)}, u32[]{:S(2)}, u32[]{:S(2)}) %collective-permute-start) | collective-permute-done | bytes 655392 | tf_op jit(solution)/shard_map/while/body/eval_jaxpr/ppermute | solution.py:10
  258.2 0.8 collective-permute-start.1
  259.0 1.7 collective-permute-done.1
  260.7 0.4 fusion.181
  261.2 18.3 %convolution_convert_fusion.3 = bf16[256,2560]{1,0:T(8,128)(2,1)S(1)} fusion(bf16[2560,2560]{1,0:T(8,128)(2,1)} %get-tuple-element.335, bf16[2560,2560]{1,0:T(8,128)(2,1)} %get-tuple-element.334, f32[2560]{0:T(1024)S(1)} %reduce.3, f32[256]{0:T(256)S(1)} %add_rsqrt_fusion.3, bf16[256,1280]{1,0:T(8,128)(2,1)S(1)} %collective-permute-done.1, ...), kind=kOutput, calls=%fused_computation.1.clone.1 | convolution fusion | flops 6762659840 | bytes 28847104 | tf_op jit(solution)/shard_map/while/body/eval_jaxpr/dot_general | solution.py:40
  279.5 0.1 constant_dynamic-slice_fusion.3
  279.6 0.4 collective-permute-start.2
  280.0 1.9 collective-permute-done.2
  281.9 1.5 broadcast_select_fusion.4
  283.4 4.1 %collective-permute-start = (bf16[256,1280]{1,0:T(8,128)(2,1)S(1)}, bf16[256,1280]{1,0:T(8,128)(2,1)S(1)}, u32[]{:S(2)}, u32[]{:S(2)}) collective-permute-start(bf16[256,1280]{1,0:T(8,128)(2,1)S(1)} %get-tuple-element.318), channel_id=1, source_target_pairs={{0,64},{64,128},{128,192},{1,65},{65,129},{129,193},{2,66},{66,130... | collective-permute-start | bytes 1966088 | tf_op jit(solution)/shard_map/while/body/eval_jaxpr/ppermute | solution.py:10
  287.6 13.7 %collective-permute-done = bf16[256,1280]{1,0:T(8,128)(2,1)S(1)} collective-permute-done((bf16[256,1280]{1,0:T(8,128)(2,1)S(1)}, bf16[256,1280]{1,0:T(8,128)(2,1)S(1)}, u32[]{:S(2)}, u32[]{:S(2)}) %collective-permute-start) | collective-permute-done | bytes 655392 | tf_op jit(solution)/shard_map/while/body/eval_jaxpr/ppermute | solution.py:10
  301.3 1.2 collective-permute-start.1
  302.5 1.7 collective-permute-done.1
  304.2 0.4 fusion.181
  304.6 18.3 %convolution_convert_fusion.3 = bf16[256,2560]{1,0:T(8,128)(2,1)S(1)} fusion(bf16[2560,2560]{1,0:T(8,128)(2,1)} %get-tuple-element.335, bf16[2560,2560]{1,0:T(8,128)(2,1)} %get-tuple-element.334, f32[2560]{0:T(1024)S(1)} %reduce.3, f32[256]{0:T(256)S(1)} %add_rsqrt_fusion.3, bf16[256,1280]{1,0:T(8,128)(2,1)S(1)} %collective-permute-done.1, ...), kind=kOutput, calls=%fused_computation.1.clone.1 | convolution fusion | flops 6762659840 | bytes 28847104 | tf_op jit(solution)/shard_map/while/body/eval_jaxpr/dot_general | solution.py:40
  323.0 0.1 constant_dynamic-slice_fusion.3
  323.0 0.4 collective-permute-start.2
  323.5 1.9 collective-permute-done.2
  325.3 1.5 broadcast_select_fusion.4
  326.9 4.2 %collective-permute-start = (bf16[256,1280]{1,0:T(8,128)(2,1)S(1)}, bf16[256,1280]{1,0:T(8,128)(2,1)S(1)}, u32[]{:S(2)}, u32[]{:S(2)}) collective-permute-start(bf16[256,1280]{1,0:T(8,128)(2,1)S(1)} %get-tuple-element.318), channel_id=1, source_target_pairs={{0,64},{64,128},{128,192},{1,65},{65,129},{129,193},{2,66},{66,130... | collective-permute-start | bytes 1966088 | tf_op jit(solution)/shard_map/while/body/eval_jaxpr/ppermute | solution.py:10
  331.1 13.7 %collective-permute-done = bf16[256,1280]{1,0:T(8,128)(2,1)S(1)} collective-permute-done((bf16[256,1280]{1,0:T(8,128)(2,1)S(1)}, bf16[256,1280]{1,0:T(8,128)(2,1)S(1)}, u32[]{:S(2)}, u32[]{:S(2)}) %collective-permute-start) | collective-permute-done | bytes 655392 | tf_op jit(solution)/shard_map/while/body/eval_jaxpr/ppermute | solution.py:10
  344.8 1.2 collective-permute-start.1
  346.0 1.7 collective-permute-done.1
  347.7 0.4 fusion.181
  348.1 18.3 %convolution_convert_fusion.3 = bf16[256,2560]{1,0:T(8,128)(2,1)S(1)} fusion(bf16[2560,2560]{1,0:T(8,128)(2,1)} %get-tuple-element.335, bf16[2560,2560]{1,0:T(8,128)(2,1)} %get-tuple-element.334, f32[2560]{0:T(1024)S(1)} %reduce.3, f32[256]{0:T(256)S(1)} %add_rsqrt_fusion.3, bf16[256,1280]{1,0:T(8,128)(2,1)S(1)} %collective-permute-done.1, ...), kind=kOutput, calls=%fused_computation.1.clone.1 | convolution fusion | flops 6762659840 | bytes 28847104 | tf_op jit(solution)/shard_map/while/body/eval_jaxpr/dot_general | solution.py:40
  366.4 0.1 constant_dynamic-slice_fusion.3
  366.5 0.5 collective-permute-start.2
  367.0 1.9 collective-permute-done.2
  368.8 1.5 broadcast_select_fusion.4
  370.4 0.0 copy-start
  370.4 0.8 copy-done
  (9 shorter events, 0.2 us)
Async XLA Ops:
  6.5 2.8 copy-start.1
  6.5 6.3 %copy-start.2 = (f32[1,2560]{1,0:T(1,128)S(1)}, f32[1,2560]{1,0:T(1,128)}, u32[]{:S(2)}) copy-start(f32[1,2560]{1,0:T(1,128)} %param.9) | copy-start | bytes 30724
  6.5 196.8 %all-gather.2.cloned.1.call-start = ((), (), s32[]{:S(2)}) async-start(), calls=%async_computation | async-start | bytes 27033600 | tf_op jit(solution)/shard_map/all_gather | solution.py:18
  9.5 5.1 %collective-permute-start.3 = (bf16[256,1280]{1,0:T(8,128)(2,1)S(1)}, bf16[256,1280]{1,0:T(8,128)(2,1)S(1)}, u32[]{:S(2)}, u32[]{:S(2)}) collective-permute-start(bf16[256,1280]{1,0:T(8,128)(2,1)S(1)} %broadcast_select_fusion.1), channel_id=1, source_target_pairs={{0,1},{1,0},{2,3},{3,2},{4,5},{5,4},{6,7},{7,6},{8,9},{9,8},{10,11... | collective-permute-start | bytes 1966088 | tf_op jit(solution)/shard_map/ppermute | solution.py:28
  221.7 18.8 %collective-permute-start.4 = (bf16[256,1280]{1,0:T(8,128)(2,1)S(1)}, bf16[256,1280]{1,0:T(8,128)(2,1)S(1)}, u32[]{:S(2)}, u32[]{:S(2)}) collective-permute-start(bf16[256,1280]{1,0:T(8,128)(2,1)S(1)} %constant_dynamic-slice_fusion.1), channel_id=1, source_target_pairs={{0,1},{1,0},{2,3},{3,2},{4,5},{5,4},{6,7},{7,6},{8,9},{9,8},{10,11... | collective-permute-start | bytes 1966088 | tf_op jit(solution)/shard_map/ppermute | solution.py:47
  241.0 17.2 %collective-permute-start = (bf16[256,1280]{1,0:T(8,128)(2,1)S(1)}, bf16[256,1280]{1,0:T(8,128)(2,1)S(1)}, u32[]{:S(2)}, u32[]{:S(2)}) collective-permute-start(bf16[256,1280]{1,0:T(8,128)(2,1)S(1)} %get-tuple-element.318), channel_id=1, source_target_pairs={{0,64},{64,128},{128,192},{1,65},{65,129},{129,193},{2,66},{66,130... | collective-permute-start | bytes 1966088 | tf_op jit(solution)/shard_map/while/body/eval_jaxpr/ppermute | solution.py:10
  258.2 2.5 collective-permute-start.1
  279.6 2.3 collective-permute-start.2
  283.4 17.8 %collective-permute-start = (bf16[256,1280]{1,0:T(8,128)(2,1)S(1)}, bf16[256,1280]{1,0:T(8,128)(2,1)S(1)}, u32[]{:S(2)}, u32[]{:S(2)}) collective-permute-start(bf16[256,1280]{1,0:T(8,128)(2,1)S(1)} %get-tuple-element.318), channel_id=1, source_target_pairs={{0,64},{64,128},{128,192},{1,65},{65,129},{129,193},{2,66},{66,130... | collective-permute-start | bytes 1966088 | tf_op jit(solution)/shard_map/while/body/eval_jaxpr/ppermute | solution.py:10
  301.3 2.9 collective-permute-start.1
  323.0 2.3 collective-permute-start.2
  326.9 17.9 %collective-permute-start = (bf16[256,1280]{1,0:T(8,128)(2,1)S(1)}, bf16[256,1280]{1,0:T(8,128)(2,1)S(1)}, u32[]{:S(2)}, u32[]{:S(2)}) collective-permute-start(bf16[256,1280]{1,0:T(8,128)(2,1)S(1)} %get-tuple-element.318), channel_id=1, source_target_pairs={{0,64},{64,128},{128,192},{1,65},{65,129},{129,193},{2,66},{66,130... | collective-permute-start | bytes 1966088 | tf_op jit(solution)/shard_map/while/body/eval_jaxpr/ppermute | solution.py:10
  344.8 2.9 collective-permute-start.1
  366.5 2.3 collective-permute-start.2
  370.4 0.8 copy-start
Sparse Core Ops, SparseCore 0:
  9.9 193.3 all-gather.1

commit v5 on v4

--- a/solution.py
+++ b/solution.py
@@ -16,8 +16,6 @@
     half_index = lax.axis_index("mp")
     both = jnp.stack([weight_in[0], weight_out[0].T])
     gathered = lax.all_gather(both, "dp", axis=1, tiled=True)
-    matrix_in = gathered[0]
-    matrix_out_t = gathered[1]
     gain_row = norm_gain[0]
     local_rows, width_local = frames.shape
     live_count = frame_count[0]
@@ -35,10 +33,10 @@
         meansq = jnp.mean(wide * wide, axis=-1, keepdims=True)
         normed = (wide * lax.rsqrt(meansq + 1e-06) * gain_row).astype(jnp.bfloat16)
         hidden = jax.nn.gelu(
-            jnp.dot(normed, matrix_in, preferred_element_type=jnp.float32), approximate=False
+            jnp.dot(normed, gathered[0], preferred_element_type=jnp.float32), approximate=False
         ).astype(jnp.bfloat16)
         partial_term = lax.dot_general(
-            hidden, matrix_out_t, (((1,), (1,)), ((), ())), preferred_element_type=jnp.float32
+            hidden, gathered[1], (((1,), (1,)), ((), ())), preferred_element_type=jnp.float32
         ).astype(jnp.bfloat16)
         keep = lax.dynamic_slice_in_dim(partial_term, half_index * width_local, width_local, axis=1)
         send = lax.dynamic_slice_in_dim(

time: 379 us -> 367 us (0.968)
  local copies, waits for them, and re-layouts: 18.6 us -> 1.05 us
    squeeze x1 -> x0, local copies, waits for them, and re-layouts: 17.5 us -> none  [per_device(): matrix_out_t = gathered[1]]
  transfers between devices with their start and end apart: 12 -> 12, of which waited for: 11 -> 12; matrix products, arithmetic and copies ran while one was open for 5% -> 0% of each run, Pallas kernels for 0% -> 0%
where the time goes in v5:
time: 367 us; the launch traced here: 366 us
  waiting for transfers between devices  244 us (66%)
  matrix products  73.4 us (20%)
  starting transfers between devices  20.8 us (6%)
  between operations  14.1 us (4%)
  other arithmetic  12.5 us (3%)
    all_gather x1, waiting for transfers between devices, per_device(): gathered = lax.all_gather(both, 'dp', axis=1, tiled=True)  188 us
    dot_general x4, matrix products, apply_layer(): lax.dot_general(hidden, gathered[1], (((1,), (1,)), ((), ())), preferred_...  73.4 us
    ppermute x3, waiting for transfers between devices, passed_along(): lax.ppermute(value, axis, [(source, source + steps) for source in range(f...  42 us
    ppermute x3, starting transfers between devices, passed_along(): lax.ppermute(value, axis, [(source, source + steps) for source in range(f...  11.1 us
  transfers between devices with their start and end apart: 12, of which 12 were waited for; matrix products, arithmetic and copies ran while one was open for 0% of the time, Pallas kernels for 0%

profile of v5, /device:TPU:1, one launch (start us, length us, event | category | flops | bytes accessed | tf_op | source)
XLA Modules:
  0.0 366.3 jit_solution(7326993723800943039)
XLA Ops:
  6.5 0.0 copy-start.1
  6.5 0.0 copy-start.2
  6.5 0.0 all-gather.2.cloned.1.call-start
  6.5 2.1 pad_maximum_fusion
  8.7 0.0 all-gather.2.cloned.1.call-update
  9.4 0.0 copy-done.1
  9.4 0.1 broadcast_select_fusion.1
  9.5 3.3 collective-permute-start.3
  12.8 0.0 copy-done.2
  12.9 1.7 collective-permute-done.3
  14.6 0.4 fusion.101
  15.0 188.4 %all-gather.2.cloned.1.call-done = bf16[2,2560,2560]{2,1,0:T(8,128)(2,1)} async-done(((bf16[2,80,2560]{2,1,0:T(8,128)(2,1)}), bf16[2,2560,2560]{2,1,0:T(8,128)(2,1)}) %all-gather.2.cloned.1.call-update) | async-done | bytes 26214416 | tf_op jit(solution)/shard_map/all_gather | solution.py:18
  203.4 18.3 %fusion.100 = bf16[256,2560]{1,0:T(8,128)(2,1)S(1)} fusion(bf16[2,2560,2560]{2,1,0:T(8,128)(2,1)} %all-gather.2.cloned.1.call-done, f32[2560]{0:T(1024)S(1)} %reduce.1, f32[256]{0:T(256)S(1)} %add_rsqrt_fusion.1, bf16[256,1280]{1,0:T(8,128)(2,1)S(1)} %collective-permute-done.3, bf16[256,1280]{1,0:T(8,128)(2,1)S(1)} %broadcast_select_fusion.1, pred[]{:T(512)} %eq.22), kind=kOutput, calls=%fused_computation.104 | convolution fusion | flops 6762659840 | bytes 28847104 | tf_op jit(solution)/shard_map/dot_general | solution.py:38
  221.7 0.1 constant_dynamic-slice_fusion.1
  221.8 1.3 collective-permute-start.4
  223.1 1.7 collective-permute-done.4
  224.8 1.2 broadcast_select_fusion.2
  226.0 132.6 %while.17 = (s32[]{:T(128)}, bf16[256,1280]{1,0:T(8,128)(2,1)}, bf16[256,1280]{1,0:T(8,128)(2,1)S(1)}, pred[]{:T(512)}, f32[1,2560]{1,0:T(1,128)S(1)}, /*index=5...) while((s32[]{:T(128)}, bf16[256,1280]{1,0:T(8,128)(2,1)}, ...), condition=%wide.region_3.4_spmd, body=%wide.region_1.3_spmd.sunk | while | flops 6772818432 | bytes 43288824 | solution.py:58
  226.0 3.1 collective-permute-start
  229.1 14.0 %collective-permute-done = bf16[256,1280]{1,0:T(8,128)(2,1)S(1)} collective-permute-done((bf16[256,1280]{1,0:T(8,128)(2,1)}, bf16[256,1280]{1,0:T(8,128)(2,1)S(1)}, u32[]{:S(2)}, u32[]{:S(2)}) %collective-permute-start) | collective-permute-done | bytes 655392 | tf_op jit(solution)/shard_map/while/body/eval_jaxpr/ppermute | solution.py:10
  243.1 1.2 collective-permute-start.1
  244.4 1.7 collective-permute-done.1
  246.0 0.4 fusion.196
  246.5 18.4 %fusion.197 = bf16[256,2560]{1,0:T(8,128)(2,1)S(1)} fusion(bf16[2,2560,2560]{2,1,0:T(8,128)(2,1)} %get-tuple-element.301, f32[2560]{0:T(1024)S(1)} %reduce.3, f32[256]{0:T(256)S(1)} %add_rsqrt_fusion.3, bf16[256,1280]{1,0:T(8,128)(2,1)S(1)} %collective-permute-done.1, bf16[256,1280]{1,0:T(8,128)(2,1)S(1)} %collective-permute-done, ...), kind=kOutput, calls=%fused_computation.7.clone.1 | convolution fusion | flops 6762659840 | bytes 28847104 | tf_op jit(solution)/shard_map/while/body/eval_jaxpr/dot_general | solution.py:38
  264.9 0.1 constant_dynamic-slice_fusion.3
  264.9 0.4 collective-permute-start.2
  265.4 1.9 collective-permute-done.2
  267.2 2.4 broadcast_select_fusion.4
  269.6 4.0 %collective-permute-start = (bf16[256,1280]{1,0:T(8,128)(2,1)}, bf16[256,1280]{1,0:T(8,128)(2,1)S(1)}, u32[]{:S(2)}, u32[]{:S(2)}) collective-permute-start(bf16[256,1280]{1,0:T(8,128)(2,1)} %get-tuple-element.286), channel_id=1, source_target_pairs={{0,64},{64,128},{128,192},{1,65},{65,129},{129,193},{2,66},{66,130... | collective-permute-start | bytes 1966088 | tf_op jit(solution)/shard_map/while/body/eval_jaxpr/ppermute | solution.py:10
  273.6 14.0 %collective-permute-done = bf16[256,1280]{1,0:T(8,128)(2,1)S(1)} collective-permute-done((bf16[256,1280]{1,0:T(8,128)(2,1)}, bf16[256,1280]{1,0:T(8,128)(2,1)S(1)}, u32[]{:S(2)}, u32[]{:S(2)}) %collective-permute-start) | collective-permute-done | bytes 655392 | tf_op jit(solution)/shard_map/while/body/eval_jaxpr/ppermute | solution.py:10
  287.6 1.2 collective-permute-start.1
  288.9 1.7 collective-permute-done.1
  290.6 0.4 fusion.196
  291.0 18.4 %fusion.197 = bf16[256,2560]{1,0:T(8,128)(2,1)S(1)} fusion(bf16[2,2560,2560]{2,1,0:T(8,128)(2,1)} %get-tuple-element.301, f32[2560]{0:T(1024)S(1)} %reduce.3, f32[256]{0:T(256)S(1)} %add_rsqrt_fusion.3, bf16[256,1280]{1,0:T(8,128)(2,1)S(1)} %collective-permute-done.1, bf16[256,1280]{1,0:T(8,128)(2,1)S(1)} %collective-permute-done, ...), kind=kOutput, calls=%fused_computation.7.clone.1 | convolution fusion | flops 6762659840 | bytes 28847104 | tf_op jit(solution)/shard_map/while/body/eval_jaxpr/dot_general | solution.py:38
  309.4 0.1 constant_dynamic-slice_fusion.3
  309.4 0.5 collective-permute-start.2
  309.9 1.9 collective-permute-done.2
  311.7 2.4 broadcast_select_fusion.4
  314.1 4.0 %collective-permute-start = (bf16[256,1280]{1,0:T(8,128)(2,1)}, bf16[256,1280]{1,0:T(8,128)(2,1)S(1)}, u32[]{:S(2)}, u32[]{:S(2)}) collective-permute-start(bf16[256,1280]{1,0:T(8,128)(2,1)} %get-tuple-element.286), channel_id=1, source_target_pairs={{0,64},{64,128},{128,192},{1,65},{65,129},{129,193},{2,66},{66,130... | collective-permute-start | bytes 1966088 | tf_op jit(solution)/shard_map/while/body/eval_jaxpr/ppermute | solution.py:10
  318.2 14.0 %collective-permute-done = bf16[256,1280]{1,0:T(8,128)(2,1)S(1)} collective-permute-done((bf16[256,1280]{1,0:T(8,128)(2,1)}, bf16[256,1280]{1,0:T(8,128)(2,1)S(1)}, u32[]{:S(2)}, u32[]{:S(2)}) %collective-permute-start) | collective-permute-done | bytes 655392 | tf_op jit(solution)/shard_map/while/body/eval_jaxpr/ppermute | solution.py:10
  332.2 1.2 collective-permute-start.1
  333.4 1.7 collective-permute-done.1
  335.1 0.4 fusion.196
  335.5 18.4 %fusion.197 = bf16[256,2560]{1,0:T(8,128)(2,1)S(1)} fusion(bf16[2,2560,2560]{2,1,0:T(8,128)(2,1)} %get-tuple-element.301, f32[2560]{0:T(1024)S(1)} %reduce.3, f32[256]{0:T(256)S(1)} %add_rsqrt_fusion.3, bf16[256,1280]{1,0:T(8,128)(2,1)S(1)} %collective-permute-done.1, bf16[256,1280]{1,0:T(8,128)(2,1)S(1)} %collective-permute-done, ...), kind=kOutput, calls=%fused_computation.7.clone.1 | convolution fusion | flops 6762659840 | bytes 28847104 | tf_op jit(solution)/shard_map/while/body/eval_jaxpr/dot_general | solution.py:38
  353.9 0.1 constant_dynamic-slice_fusion.3
  354.0 0.5 collective-permute-start.2
  354.4 1.9 collective-permute-done.2
  356.3 2.4 broadcast_select_fusion.4
  358.7 0.0 copy-start
  358.7 0.8 copy-done
  (9 shorter events, 0.2 us)
Async XLA Ops:
  6.5 2.8 copy-start.1
  6.5 6.3 %copy-start.2 = (f32[1,2560]{1,0:T(1,128)S(1)}, f32[1,2560]{1,0:T(1,128)}, u32[]{:S(2)}) copy-start(f32[1,2560]{1,0:T(1,128)} %param.9) | copy-start | bytes 30724
  6.5 196.8 %all-gather.2.cloned.1.call-start = ((), (), s32[]{:S(2)}) async-start(), calls=%async_computation | async-start | bytes 27033600 | tf_op jit(solution)/shard_map/all_gather | solution.py:18
  9.5 5.1 %collective-permute-start.3 = (bf16[256,1280]{1,0:T(8,128)(2,1)S(1)}, bf16[256,1280]{1,0:T(8,128)(2,1)S(1)}, u32[]{:S(2)}, u32[]{:S(2)}) collective-permute-start(bf16[256,1280]{1,0:T(8,128)(2,1)S(1)} %broadcast_select_fusion.1), channel_id=1, source_target_pairs={{0,1},{1,0},{2,3},{3,2},{4,5},{5,4},{6,7},{7,6},{8,9},{9,8},{10,11... | collective-permute-start | bytes 1966088 | tf_op jit(solution)/shard_map/ppermute | solution.py:26
  221.8 3.0 collective-permute-start.4
  226.0 17.1 %collective-permute-start = (bf16[256,1280]{1,0:T(8,128)(2,1)}, bf16[256,1280]{1,0:T(8,128)(2,1)S(1)}, u32[]{:S(2)}, u32[]{:S(2)}) collective-permute-start(bf16[256,1280]{1,0:T(8,128)(2,1)} %get-tuple-element.286), channel_id=1, source_target_pairs={{0,64},{64,128},{128,192},{1,65},{65,129},{129,193},{2,66},{66,130... | collective-permute-start | bytes 1966088 | tf_op jit(solution)/shard_map/while/body/eval_jaxpr/ppermute | solution.py:10
  243.1 2.9 collective-permute-start.1
  264.9 2.3 collective-permute-start.2
  269.6 18.0 %collective-permute-start = (bf16[256,1280]{1,0:T(8,128)(2,1)}, bf16[256,1280]{1,0:T(8,128)(2,1)S(1)}, u32[]{:S(2)}, u32[]{:S(2)}) collective-permute-start(bf16[256,1280]{1,0:T(8,128)(2,1)} %get-tuple-element.286), channel_id=1, source_target_pairs={{0,64},{64,128},{128,192},{1,65},{65,129},{129,193},{2,66},{66,130... | collective-permute-start | bytes 1966088 | tf_op jit(solution)/shard_map/while/body/eval_jaxpr/ppermute | solution.py:10
  287.6 2.9 collective-permute-start.1
  309.4 2.3 collective-permute-start.2
  314.1 18.0 %collective-permute-start = (bf16[256,1280]{1,0:T(8,128)(2,1)}, bf16[256,1280]{1,0:T(8,128)(2,1)S(1)}, u32[]{:S(2)}, u32[]{:S(2)}) collective-permute-start(bf16[256,1280]{1,0:T(8,128)(2,1)} %get-tuple-element.286), channel_id=1, source_target_pairs={{0,64},{64,128},{128,192},{1,65},{65,129},{129,193},{2,66},{66,130... | collective-permute-start | bytes 1966088 | tf_op jit(solution)/shard_map/while/body/eval_jaxpr/ppermute | solution.py:10
  332.2 2.9 collective-permute-start.1
  354.0 2.3 collective-permute-start.2
  358.7 0.8 copy-start
Sparse Core Ops, SparseCore 0:
  9.9 193.3 all-gather.1

commit v6 on v5

--- a/solution.py
+++ b/solution.py
@@ -1,7 +1,48 @@
 import jax
 import jax.numpy as jnp
 from jax import lax
+from jax.experimental import pallas as pl
+from jax.experimental.pallas import tpu as pltpu
 from jax.sharding import PartitionSpec as P
+
+TILE = 512
+
+
+def ffn_body(normed_ref, win_ref, wout_ref, out_ref, acc_ref):
+    step = pl.program_id(0)
+
+    @pl.when(step == 0)
+    def _():
+        acc_ref[...] = jnp.zeros_like(acc_ref)
+
+    pre = jnp.dot(normed_ref[...], win_ref[0], preferred_element_type=jnp.float32)
+    hidden = (0.5 * pre * (1.0 + lax.erf(pre * 0.7071067811865476))).astype(jnp.bfloat16)
+    acc_ref[...] += lax.dot_general(
+        hidden, wout_ref[0], (((1,), (1,)), ((), ())), preferred_element_type=jnp.float32
+    )
+
+    @pl.when(step == pl.num_programs(0) - 1)
+    def _():
+        out_ref[...] = acc_ref[...].astype(out_ref.dtype)
+
+
+def ffn(normed, gathered, interpret=False):
+    rows, width = normed.shape
+    hidden_units = gathered.shape[2]
+    return pl.pallas_call(
+        ffn_body,
+        grid=(hidden_units // TILE,),
+        in_specs=[
+            pl.BlockSpec((rows, width), lambda j: (0, 0)),
+            pl.BlockSpec((1, width, TILE), lambda j: (0, 0, j)),
+            pl.BlockSpec((1, width, TILE), lambda j: (1, 0, j)),
+        ],
+        out_specs=pl.BlockSpec((rows, width), lambda j: (0, 0)),
+        out_shape=jax.ShapeDtypeStruct((rows, width), jnp.bfloat16),
+        scratch_shapes=[pltpu.VMEM((rows, width), jnp.float32)],
+        compiler_params=pltpu.CompilerParams(vmem_limit_bytes=48 << 20),
+        interpret=interpret,
+    )(normed, gathered, gathered)
 
 
 def passed_along(value, axis, steps):
@@ -32,12 +73,7 @@
         wide = whole.astype(jnp.float32)
         meansq = jnp.mean(wide * wide, axis=-1, keepdims=True)
         normed = (wide * lax.rsqrt(meansq + 1e-06) * gain_row).astype(jnp.bfloat16)
-        hidden = jax.nn.gelu(
-            jnp.dot(normed, gathered[0], preferred_element_type=jnp.float32), approximate=False
-        ).astype(jnp.bfloat16)
-        partial_term = lax.dot_general(
-            hidden, gathered[1], (((1,), (1,)), ((), ())), preferred_element_type=jnp.float32
-        ).astype(jnp.bfloat16)
+        partial_term = ffn(normed, gathered)
         keep = lax.dynamic_slice_in_dim(partial_term, half_index * width_local, width_local, axis=1)
         send = lax.dynamic_slice_in_dim(
             partial_term, (1 - half_index) * width_local, width_local, axis=1

time: 367 us -> 347 us (0.946)
  matrix products: 73.4 us -> 0 us
  Pallas kernels: 0 us -> 51.7 us
    dot_general x4 -> x0, matrix products: 73.4 us -> none  [apply_layer(): lax.dot_general(hidden, gathered[1], (((1,), (1,)), ((), ())), preferred_...]
    pallas_call x0 -> x4, Pallas kernels: none -> 51.7 us  [ffn(): pl.pallas_call(ffn_body, grid=(hidden_units // TILE,), in_specs=[pl.Block...]
where the time goes in v6:
time: 347 us; the launch traced here: 346 us
  waiting for transfers between devices  244 us (70%)
  Pallas kernels  51.7 us (15%)
  starting transfers between devices  20.6 us (6%)
  other arithmetic  14.7 us (4%)
  between operations  14.1 us (4%)
    all_gather x1, waiting for transfers between devices, per_device(): gathered = lax.all_gather(both, 'dp', axis=1, tiled=True)  188 us
    pallas_call x4, Pallas kernels, ffn(): pl.pallas_call(ffn_body, grid=(hidden_units // TILE,), in_specs=[pl.Block...  51.7 us
    ppermute x3, waiting for transfers between devices, passed_along(): lax.ppermute(value, axis, [(source, source + steps) for source in range(f...  42 us
    ppermute x3, starting transfers between devices, passed_along(): lax.ppermute(value, axis, [(source, source + steps) for source in range(f...  11.2 us
    ppermute x4, waiting for transfers between devices, apply_layer(): other = lax.ppermute(send, 'mp', [(0, 1), (1, 0)])  7.3 us
    select_n x3, other arithmetic, advance(): stored = jnp.where(segment_index == moment, result, stored)  7.14 us
  transfers between devices with their start and end apart: 12, of which 12 were waited for; matrix products, arithmetic and copies ran while one was open for 0% of the time, Pallas kernels for 0%

profile of v6, /device:TPU:1, one launch (start us, length us, event | category | flops | bytes accessed | tf_op | source)
XLA Modules:
  0.0 346.2 jit_solution(3510448804190517660)
XLA Ops:
  6.5 0.0 copy-start.1
  6.5 0.0 all-gather.2.cloned.1.call-start
  6.5 2.1 pad_maximum_fusion
  8.7 0.0 copy-start.2
  8.7 0.0 all-gather.2.cloned.1.call-update
  9.4 0.0 copy-done.1
  9.4 0.1 broadcast_select_fusion.1
  9.5 3.3 collective-permute-start.3
  12.8 0.0 copy-done.2
  12.9 1.7 collective-permute-done.3
  14.6 0.4 fusion.3
  15.0 0.6 fusion.5.normed_ref
  15.6 187.8 %all-gather.2.cloned.1.call-done.win_ref.wout_ref = bf16[2,2560,2560]{2,1,0:T(8,128)(2,1)} async-done(((bf16[2,80,2560]{2,1,0:T(8,128)(2,1)}), bf16[2,2560,2560]{2,1,0:T(8,128)(2,1)}) %all-gather.2.cloned.1.call-update) | async-done | bytes 26214416 | tf_op jit(solution)/shard_map/all_gather | solution.py:59
  203.4 12.9 %shard_map.55 = bf16[256,2560]{1,0:T(8,128)(2,1)S(1)} custom-call(bf16[256,2560]{1,0:T(8,128)(2,1)S(1)} %fusion.5.normed_ref, bf16[2,2560,2560]{2,1,0:T(8,128)(2,1)} %all-gather.2.cloned.1.call-done.win_ref.wout_ref, bf16[2,2560,2560]{2,1,0:T(8,128)(2,1)} %all-gather.2.cloned.1.call-done.win_ref.wout_ref), custom_call_target="tpu_custom_call" | custom-call | tf_op jit(solution)/shard_map/pallas_call | solution.py:32
  216.3 0.1 constant_dynamic-slice_fusion.1
  216.4 1.1 collective-permute-start.4
  217.5 1.7 collective-permute-done.4
  219.2 1.2 broadcast_select_fusion.2
  220.4 118.1 %while.17 = (s32[]{:T(128)}, bf16[256,1280]{1,0:T(8,128)(2,1)}, bf16[256,1280]{1,0:T(8,128)(2,1)S(1)}, pred[]{:T(512)}, f32[1,2560]{1,0:T(1,128)S(1)}, /*index=5...) while((s32[]{:T(128)}, bf16[256,1280]{1,0:T(8,128)(2,1)}, ...), condition=%wide.region_3.4_spmd, body=%wide.region_1.3_spmd.sunk | while | flops 18678020 | bytes 17074428 | solution.py:94
  220.4 3.1 collective-permute-start
  223.5 14.0 %collective-permute-done = bf16[256,1280]{1,0:T(8,128)(2,1)S(1)} collective-permute-done((bf16[256,1280]{1,0:T(8,128)(2,1)}, bf16[256,1280]{1,0:T(8,128)(2,1)S(1)}, u32[]{:S(2)}, u32[]{:S(2)}) %collective-permute-start) | collective-permute-done | bytes 655392 | tf_op jit(solution)/shard_map/while/body/eval_jaxpr/ppermute | solution.py:51
  237.6 1.2 collective-permute-start.1
  238.8 1.7 collective-permute-done.1
  240.5 0.4 fusion.8
  240.9 0.6 fusion.9.normed_ref
  241.5 12.9 %eval_jaxpr.7 = bf16[256,2560]{1,0:T(8,128)(2,1)S(1)} custom-call(bf16[256,2560]{1,0:T(8,128)(2,1)S(1)} %fusion.9.normed_ref, bf16[2,2560,2560]{2,1,0:T(8,128)(2,1)} %get-tuple-element.299.win_ref.wout_ref, bf16[2,2560,2560]{2,1,0:T(8,128)(2,1)} %get-tuple-element.299.win_ref.wout_ref), custom_call_target="tpu_custom_call" | custom-call | tf_op jit(solution)/shard_map/while/body/eval_jaxpr/pallas_call | solution.py:32
  254.4 0.1 constant_dynamic-slice_fusion.3
  254.5 0.5 collective-permute-start.2
  254.9 1.9 collective-permute-done.2
  256.8 2.4 broadcast_select_fusion.4
  259.2 4.0 %collective-permute-start = (bf16[256,1280]{1,0:T(8,128)(2,1)}, bf16[256,1280]{1,0:T(8,128)(2,1)S(1)}, u32[]{:S(2)}, u32[]{:S(2)}) collective-permute-start(bf16[256,1280]{1,0:T(8,128)(2,1)} %get-tuple-element.284), channel_id=1, source_target_pairs={{0,64},{64,128},{128,192},{1,65},{65,129},{129,193},{2,66},{66,130... | collective-permute-start | bytes 1966088 | tf_op jit(solution)/shard_map/while/body/eval_jaxpr/ppermute | solution.py:51
  263.2 14.0 %collective-permute-done = bf16[256,1280]{1,0:T(8,128)(2,1)S(1)} collective-permute-done((bf16[256,1280]{1,0:T(8,128)(2,1)}, bf16[256,1280]{1,0:T(8,128)(2,1)S(1)}, u32[]{:S(2)}, u32[]{:S(2)}) %collective-permute-start) | collective-permute-done | bytes 655392 | tf_op jit(solution)/shard_map/while/body/eval_jaxpr/ppermute | solution.py:51
  277.2 1.2 collective-permute-start.1
  278.4 1.7 collective-permute-done.1
  280.1 0.4 fusion.8
  280.6 0.6 fusion.9.normed_ref
  281.1 12.9 %eval_jaxpr.7 = bf16[256,2560]{1,0:T(8,128)(2,1)S(1)} custom-call(bf16[256,2560]{1,0:T(8,128)(2,1)S(1)} %fusion.9.normed_ref, bf16[2,2560,2560]{2,1,0:T(8,128)(2,1)} %get-tuple-element.299.win_ref.wout_ref, bf16[2,2560,2560]{2,1,0:T(8,128)(2,1)} %get-tuple-element.299.win_ref.wout_ref), custom_call_target="tpu_custom_call" | custom-call | tf_op jit(solution)/shard_map/while/body/eval_jaxpr/pallas_call | solution.py:32
  294.1 0.1 constant_dynamic-slice_fusion.3
  294.1 0.5 collective-permute-start.2
  294.6 1.9 collective-permute-done.2
  296.4 2.4 broadcast_select_fusion.4
  298.8 4.0 %collective-permute-start = (bf16[256,1280]{1,0:T(8,128)(2,1)}, bf16[256,1280]{1,0:T(8,128)(2,1)S(1)}, u32[]{:S(2)}, u32[]{:S(2)}) collective-permute-start(bf16[256,1280]{1,0:T(8,128)(2,1)} %get-tuple-element.284), channel_id=1, source_target_pairs={{0,64},{64,128},{128,192},{1,65},{65,129},{129,193},{2,66},{66,130... | collective-permute-start | bytes 1966088 | tf_op jit(solution)/shard_map/while/body/eval_jaxpr/ppermute | solution.py:51
  302.9 14.0 %collective-permute-done = bf16[256,1280]{1,0:T(8,128)(2,1)S(1)} collective-permute-done((bf16[256,1280]{1,0:T(8,128)(2,1)}, bf16[256,1280]{1,0:T(8,128)(2,1)S(1)}, u32[]{:S(2)}, u32[]{:S(2)}) %collective-permute-start) | collective-permute-done | bytes 655392 | tf_op jit(solution)/shard_map/while/body/eval_jaxpr/ppermute | solution.py:51
  316.9 1.2 collective-permute-start.1
  318.1 1.7 collective-permute-done.1
  319.8 0.4 fusion.8
  320.2 0.6 fusion.9.normed_ref
  320.8 12.9 %eval_jaxpr.7 = bf16[256,2560]{1,0:T(8,128)(2,1)S(1)} custom-call(bf16[256,2560]{1,0:T(8,128)(2,1)S(1)} %fusion.9.normed_ref, bf16[2,2560,2560]{2,1,0:T(8,128)(2,1)} %get-tuple-element.299.win_ref.wout_ref, bf16[2,2560,2560]{2,1,0:T(8,128)(2,1)} %get-tuple-element.299.win_ref.wout_ref), custom_call_target="tpu_custom_call" | custom-call | tf_op jit(solution)/shard_map/while/body/eval_jaxpr/pallas_call | solution.py:32
  333.7 0.1 constant_dynamic-slice_fusion.3
  333.8 0.5 collective-permute-start.2
  334.2 1.9 collective-permute-done.2
  336.1 2.4 broadcast_select_fusion.4
  338.5 0.0 copy-start
  338.5 0.8 copy-done
  (9 shorter events, 0.2 us)
Async XLA Ops:
  6.5 2.8 copy-start.1
  6.5 196.8 %all-gather.2.cloned.1.call-start = ((), (), s32[]{:S(2)}) async-start(), calls=%async_computation | async-start | bytes 27033600 | tf_op jit(solution)/shard_map/all_gather | solution.py:59
  8.7 4.1 %copy-start.2 = (f32[1,2560]{1,0:T(1,128)S(1)}, f32[1,2560]{1,0:T(1,128)}, u32[]{:S(2)}) copy-start(f32[1,2560]{1,0:T(1,128)} %param.9) | copy-start | bytes 30724
  9.5 5.1 %collective-permute-start.3 = (bf16[256,1280]{1,0:T(8,128)(2,1)S(1)}, bf16[256,1280]{1,0:T(8,128)(2,1)S(1)}, u32[]{:S(2)}, u32[]{:S(2)}) collective-permute-start(bf16[256,1280]{1,0:T(8,128)(2,1)S(1)} %broadcast_select_fusion.1), channel_id=1, source_target_pairs={{0,1},{1,0},{2,3},{3,2},{4,5},{5,4},{6,7},{7,6},{8,9},{9,8},{10,11... | collective-permute-start | bytes 1966088 | tf_op jit(solution)/shard_map/ppermute | solution.py:67
  216.4 2.9 collective-permute-start.4
  220.4 17.1 %collective-permute-start = (bf16[256,1280]{1,0:T(8,128)(2,1)}, bf16[256,1280]{1,0:T(8,128)(2,1)S(1)}, u32[]{:S(2)}, u32[]{:S(2)}) collective-permute-start(bf16[256,1280]{1,0:T(8,128)(2,1)} %get-tuple-element.284), channel_id=1, source_target_pairs={{0,64},{64,128},{128,192},{1,65},{65,129},{129,193},{2,66},{66,130... | collective-permute-start | bytes 1966088 | tf_op jit(solution)/shard_map/while/body/eval_jaxpr/ppermute | solution.py:51
  237.6 2.9 collective-permute-start.1
  254.5 2.3 collective-permute-start.2
  259.2 18.0 %collective-permute-start = (bf16[256,1280]{1,0:T(8,128)(2,1)}, bf16[256,1280]{1,0:T(8,128)(2,1)S(1)}, u32[]{:S(2)}, u32[]{:S(2)}) collective-permute-start(bf16[256,1280]{1,0:T(8,128)(2,1)} %get-tuple-element.284), channel_id=1, source_target_pairs={{0,64},{64,128},{128,192},{1,65},{65,129},{129,193},{2,66},{66,130... | collective-permute-start | bytes 1966088 | tf_op jit(solution)/shard_map/while/body/eval_jaxpr/ppermute | solution.py:51
  277.2 2.9 collective-permute-start.1
  294.1 2.3 collective-permute-start.2
  298.8 18.0 %collective-permute-start = (bf16[256,1280]{1,0:T(8,128)(2,1)}, bf16[256,1280]{1,0:T(8,128)(2,1)S(1)}, u32[]{:S(2)}, u32[]{:S(2)}) collective-permute-start(bf16[256,1280]{1,0:T(8,128)(2,1)} %get-tuple-element.284), channel_id=1, source_target_pairs={{0,64},{64,128},{128,192},{1,65},{65,129},{129,193},{2,66},{66,130... | collective-permute-start | bytes 1966088 | tf_op jit(solution)/shard_map/while/body/eval_jaxpr/ppermute | solution.py:51
  316.9 2.9 collective-permute-start.1
  333.8 2.3 collective-permute-start.2
  338.5 0.8 copy-start
Sparse Core Ops, SparseCore 0:
  9.9 193.3 all-gather.1

commit v7 on v6

--- a/solution.py
+++ b/solution.py
@@ -6,6 +6,7 @@
 from jax.sharding import PartitionSpec as P
 
 TILE = 512
+MICRO = 2
 
 
 def ffn_body(normed_ref, win_ref, wout_ref, out_ref, acc_ref):
@@ -41,6 +42,11 @@
         out_shape=jax.ShapeDtypeStruct((rows, width), jnp.bfloat16),
         scratch_shapes=[pltpu.VMEM((rows, width), jnp.float32)],
         compiler_params=pltpu.CompilerParams(vmem_limit_bytes=48 << 20),
+        cost_estimate=pl.CostEstimate(
+            flops=4 * rows * width * hidden_units,
+            transcendentals=rows * hidden_units,
+            bytes_accessed=2 * (2 * width * hidden_units + 2 * rows * width),
+        ),
         interpret=interpret,
     )(normed, gathered, gathered)
 
@@ -82,16 +88,15 @@
         summed = keep.astype(jnp.float32) + other.astype(jnp.float32)
         return (current.astype(jnp.float32) + summed).astype(jnp.bfloat16)
 
-    result = apply_layer(first)
-    stored = jnp.where(segment_index == 0, result, jnp.zeros_like(result))
-
-    def advance(moment, carry):
-        previous, stored = carry
-        result = apply_layer(passed_along(previous, "section", 1))
-        stored = jnp.where(segment_index == moment, result, stored)
-        return (result, stored)
-
-    leftover, stored = lax.fori_loop(1, segment_count, advance, (result, stored))
+    block_rows = local_rows // MICRO
+    pieces = [first[index * block_rows:(index + 1) * block_rows] for index in range(MICRO)]
+    kept = [jnp.zeros_like(piece) for piece in pieces]
+    for moment in range(segment_count):
+        results = [apply_layer(piece) for piece in pieces]
+        kept = [jnp.where(segment_index == moment, r, k) for r, k in zip(results, kept)]
+        if moment + 1 < segment_count:
+            pieces = [passed_along(r, "section", 1) for r in results]
+    stored = jnp.concatenate(kept, axis=0)
     return stored.reshape(1, local_rows, width_local)
 
 

time: 347 us -> 395 us (1.14)
  Pallas kernels: 51.7 us -> 96.9 us
  starting transfers between devices: 20.6 us -> 36.8 us
  waiting for transfers between devices: 244 us -> 236 us
  other arithmetic: 14.7 us -> 10 us
    pallas_call x4 -> x8, Pallas kernels: 51.7 us -> 96.9 us  [ffn(): pl.pallas_call(ffn_body, grid=(hidden_units // TILE,), in_specs=[pl.Block...]
    ppermute x3 -> x6, starting transfers between devices: 11.2 us -> 22.7 us  [passed_along(): lax.ppermute(value, axis, [(source, source + steps) for source in range(f...]
    select_n x4 -> x2, other arithmetic: 8.35 us -> 0.54 us  [per_device(): jnp.where(segment_index == moment, r, k)]
    ppermute x3 -> x6, waiting for transfers between devices: 42 us -> 36.2 us  [passed_along(): lax.ppermute(value, axis, [(source, source + steps) for source in range(f...]
    ppermute x4 -> x8, starting transfers between devices: 6.92 us -> 10.4 us  [apply_layer(): partner = lax.ppermute(current, 'mp', [(0, 1), (1, 0)])]
  transfers between devices with their start and end apart: 12 -> 23, of which waited for: 12 -> 18; matrix products, arithmetic and copies ran while one was open for 0% -> 1% of each run, Pallas kernels for 0% -> 9%
where the time goes in v7:
time: 395 us
  waiting for transfers between devices  236 us (60%)
  Pallas kernels  96.9 us (25%)
  starting transfers between devices  36.8 us (9%)
  between operations  14.5 us (4%)
  other arithmetic  10 us (3%)
    all_gather x1, waiting for transfers between devices, per_device(): gathered = lax.all_gather(both, 'dp', axis=1, tiled=True)  188 us
    pallas_call x8, Pallas kernels, ffn(): pl.pallas_call(ffn_body, grid=(hidden_units // TILE,), in_specs=[pl.Block...  96.9 us
    ppermute x6, waiting for transfers between devices, passed_along(): lax.ppermute(value, axis, [(source, source + steps) for source in range(f...  36.2 us
    ppermute x6, starting transfers between devices, passed_along(): lax.ppermute(value, axis, [(source, source + steps) for source in range(f...  22.7 us
    ppermute x8, starting transfers between devices, apply_layer(): partner = lax.ppermute(current, 'mp', [(0, 1), (1, 0)])  10.4 us
  transfers between devices with their start and end apart: 23, of which 18 were waited for; matrix products, arithmetic and copies ran while one was open for 1% of the time, Pallas kernels for 9%

profile of v7, /device:TPU:1, one launch (start us, length us, event | category | flops | bytes accessed | tf_op | source)
XLA Modules:
  0.0 395.0 jit_solution(6358222232800845390)
XLA Ops:
  6.5 2.2 pad_maximum_fusion
  9.6 3.3 collective-permute-start.11
  13.0 1.1 collective-permute-done.11
  14.2 0.3 fusion.12
  14.5 0.2 collective-permute-done
  14.6 0.3 fusion
  15.0 0.6 fusion.2
  15.5 187.8 %all-gather.2.cloned.1.call-done.win_ref.wout_ref = bf16[2,2560,2560]{2,1,0:T(8,128)(2,1)} async-done(((bf16[2,80,2560]{2,1,0:T(8,128)(2,1)}), bf16[2,2560,2560]{2,1,0:T(8,128)(2,1)}) %all-gather.2.cloned.1.call-update) | async-done | bytes 26214416 | tf_op jit(solution)/shard_map/all_gather | solution.py:65
  203.4 12.1 %shard_map.59 = bf16[128,2560]{1,0:T(8,128)(2,1)S(1)} custom-call(bf16[128,2560]{1,0:T(8,128)(2,1)S(1)} %get-tuple-element.12.normed_ref, bf16[2,2560,2560]{2,1,0:T(8,128)(2,1)} %all-gather.2.cloned.1.call-done.win_ref.wout_ref, bf16[2,2560,2560]{2,1,0:T(8,128)(2,1)} %all-gather.2.cloned.1.call-done.win_ref.wout_ref), custom_call_target="tpu_custom_call" | custom-call | flops 3355443200 | bytes 27525120 | tf_op jit(solution)/shard_map/pallas_call | solution.py:33
  215.5 1.1 collective-permute-start.12
  216.7 12.1 %shard_map.55 = bf16[128,2560]{1,0:T(8,128)(2,1)S(1)} custom-call(bf16[128,2560]{1,0:T(8,128)(2,1)S(1)} %get-tuple-element.11.normed_ref, bf16[2,2560,2560]{2,1,0:T(8,128)(2,1)} %all-gather.2.cloned.1.call-done.win_ref.wout_ref, bf16[2,2560,2560]{2,1,0:T(8,128)(2,1)} %all-gather.2.cloned.1.call-done.win_ref.wout_ref), custom_call_target="tpu_custom_call" | custom-call | flops 3355443200 | bytes 27525120 | tf_op jit(solution)/shard_map/pallas_call | solution.py:33
  228.9 1.6 collective-permute-done.1
  230.5 1.2 add_convert_fusion.7
  231.7 3.1 collective-permute-start.2
  234.9 6.9 %collective-permute-done.2 = bf16[128,1280]{1,0:T(8,128)(2,1)S(1)} collective-permute-done((bf16[128,1280]{1,0:T(8,128)(2,1)S(1)}, bf16[128,1280]{1,0:T(8,128)(2,1)S(1)}, u32[]{:S(2)}, u32[]{:S(2)}) %collective-permute-start.2) | collective-permute-done | bytes 327712 | tf_op jit(solution)/shard_map/ppermute | solution.py:57
  241.8 0.9 collective-permute-start.3
  242.7 1.3 collective-permute-done.3
  244.0 0.3 fusion.3
  244.3 0.3 fusion.5.normed_ref
  244.6 12.1 %shard_map.56 = bf16[128,2560]{1,0:T(8,128)(2,1)S(1)} custom-call(bf16[128,2560]{1,0:T(8,128)(2,1)S(1)} %fusion.5.normed_ref, bf16[2,2560,2560]{2,1,0:T(8,128)(2,1)} %all-gather.2.cloned.1.call-done.win_ref.wout_ref, bf16[2,2560,2560]{2,1,0:T(8,128)(2,1)} %all-gather.2.cloned.1.call-done.win_ref.wout_ref), custom_call_target="tpu_custom_call" | custom-call | flops 3355443200 | bytes 27525120 | tf_op jit(solution)/shard_map/pallas_call | solution.py:33
  256.8 0.5 collective-permute-start.4
  257.2 1.3 collective-permute-done.4
  258.6 4.1 %collective-permute-start.5 = (bf16[128,1280]{1,0:T(8,128)(2,1)S(1)}, bf16[128,1280]{1,0:T(8,128)(2,1)S(1)}, u32[]{:S(2)}, u32[]{:S(2)}) collective-permute-start(bf16[128,1280]{1,0:T(8,128)(2,1)S(1)} %add_convert_fusion.6), channel_id=1, source_target_pairs={{0,64},{64,128},{128,192},{1,65},{65,129},{129,193},{2,66},{66,130... | collective-permute-start | bytes 983048 | tf_op jit(solution)/shard_map/ppermute | solution.py:57
  262.7 6.7 %collective-permute-done.5 = bf16[128,1280]{1,0:T(8,128)(2,1)S(1)} collective-permute-done((bf16[128,1280]{1,0:T(8,128)(2,1)S(1)}, bf16[128,1280]{1,0:T(8,128)(2,1)S(1)}, u32[]{:S(2)}, u32[]{:S(2)}) %collective-permute-start.5) | collective-permute-done | bytes 327712 | tf_op jit(solution)/shard_map/ppermute | solution.py:57
  269.4 1.2 collective-permute-start.6
  270.6 1.3 collective-permute-done.6
  271.9 0.3 fusion.6
  272.2 0.3 fusion.8.normed_ref
  272.5 12.1 %shard_map.57 = bf16[128,2560]{1,0:T(8,128)(2,1)S(1)} custom-call(bf16[128,2560]{1,0:T(8,128)(2,1)S(1)} %fusion.8.normed_ref, bf16[2,2560,2560]{2,1,0:T(8,128)(2,1)} %all-gather.2.cloned.1.call-done.win_ref.wout_ref, bf16[2,2560,2560]{2,1,0:T(8,128)(2,1)} %all-gather.2.cloned.1.call-done.win_ref.wout_ref), custom_call_target="tpu_custom_call" | custom-call | flops 3355443200 | bytes 27525120 | tf_op jit(solution)/shard_map/pallas_call | solution.py:33
  284.6 0.5 collective-permute-start.7
  285.1 4.1 %collective-permute-start.13 = (bf16[128,1280]{1,0:T(8,128)(2,1)S(1)}, bf16[128,1280]{1,0:T(8,128)(2,1)S(1)}, u32[]{:S(2)}, u32[]{:S(2)}) collective-permute-start(bf16[128,1280]{1,0:T(8,128)(2,1)S(1)} %get-tuple-element.6), channel_id=1, source_target_pairs={{0,64},{64,128},{128,192},{1,65},{65,129},{129,193},{2,66},{66,130... | collective-permute-start | bytes 983048 | tf_op jit(solution)/shard_map/ppermute | solution.py:57
  289.4 3.1 collective-permute-start.8
  292.5 3.7 collective-permute-done.13
  296.1 1.5 collective-permute-start.14
  297.6 5.5 %collective-permute-done.8 = bf16[128,1280]{1,0:T(8,128)(2,1)S(1)} collective-permute-done((bf16[128,1280]{1,0:T(8,128)(2,1)S(1)}, bf16[128,1280]{1,0:T(8,128)(2,1)S(1)}, u32[]{:S(2)}, u32[]{:S(2)}) %collective-permute-start.8) | collective-permute-done | bytes 327712 | tf_op jit(solution)/shard_map/ppermute | solution.py:57
  303.2 0.9 collective-permute-start.9
  304.1 0.3 fusion.15
  304.4 0.9 collective-permute-done.9
  305.4 0.3 fusion.9
  305.7 0.6 fusion.11
  306.3 12.1 %shard_map.60 = bf16[128,2560]{1,0:T(8,128)(2,1)S(1)} custom-call(bf16[128,2560]{1,0:T(8,128)(2,1)S(1)} %get-tuple-element.10.normed_ref, bf16[2,2560,2560]{2,1,0:T(8,128)(2,1)} %all-gather.2.cloned.1.call-done.win_ref.wout_ref, bf16[2,2560,2560]{2,1,0:T(8,128)(2,1)} %all-gather.2.cloned.1.call-done.win_ref.wout_ref), custom_call_target="tpu_custom_call" | custom-call | flops 3355443200 | bytes 27525120 | tf_op jit(solution)/shard_map/pallas_call | solution.py:33
  318.4 0.5 collective-permute-start.15
  318.9 1.3 collective-permute-done.15
  320.3 4.1 %collective-permute-start.16 = (bf16[128,1280]{1,0:T(8,128)(2,1)S(1)}, bf16[128,1280]{1,0:T(8,128)(2,1)S(1)}, u32[]{:S(2)}, u32[]{:S(2)}) collective-permute-start(bf16[128,1280]{1,0:T(8,128)(2,1)S(1)} %add_convert_fusion.2), channel_id=1, source_target_pairs={{0,64},{64,128},{128,192},{1,65},{65,129},{129,193},{2,66},{66,130... | collective-permute-start | bytes 983048 | tf_op jit(solution)/shard_map/ppermute | solution.py:57
  324.4 6.7 %collective-permute-done.16 = bf16[128,1280]{1,0:T(8,128)(2,1)S(1)} collective-permute-done((bf16[128,1280]{1,0:T(8,128)(2,1)S(1)}, bf16[128,1280]{1,0:T(8,128)(2,1)S(1)}, u32[]{:S(2)}, u32[]{:S(2)}) %collective-permute-start.16) | collective-permute-done | bytes 327712 | tf_op jit(solution)/shard_map/ppermute | solution.py:57
  331.1 1.2 collective-permute-start.17
  332.3 1.3 collective-permute-done.17
  333.6 0.3 fusion.18
  333.9 0.3 fusion.20.normed_ref
  334.1 12.1 %shard_map.61 = bf16[128,2560]{1,0:T(8,128)(2,1)S(1)} custom-call(bf16[128,2560]{1,0:T(8,128)(2,1)S(1)} %fusion.20.normed_ref, bf16[2,2560,2560]{2,1,0:T(8,128)(2,1)} %all-gather.2.cloned.1.call-done.win_ref.wout_ref, bf16[2,2560,2560]{2,1,0:T(8,128)(2,1)} %all-gather.2.cloned.1.call-done.win_ref.wout_ref), custom_call_target="tpu_custom_call" | custom-call | flops 3355443200 | bytes 27525120 | tf_op jit(solution)/shard_map/pallas_call | solution.py:33
  346.3 0.5 collective-permute-start.18
  346.8 1.3 collective-permute-done.18
  348.2 4.1 %collective-permute-start.19 = (bf16[128,1280]{1,0:T(8,128)(2,1)S(1)}, bf16[128,1280]{1,0:T(8,128)(2,1)S(1)}, u32[]{:S(2)}, u32[]{:S(2)}) collective-permute-start(bf16[128,1280]{1,0:T(8,128)(2,1)S(1)} %add_convert_fusion.1), channel_id=1, source_target_pairs={{0,64},{64,128},{128,192},{1,65},{65,129},{129,193},{2,66},{66,130... | collective-permute-start | bytes 983048 | tf_op jit(solution)/shard_map/ppermute | solution.py:57
  352.3 6.7 %collective-permute-done.19 = bf16[128,1280]{1,0:T(8,128)(2,1)S(1)} collective-permute-done((bf16[128,1280]{1,0:T(8,128)(2,1)S(1)}, bf16[128,1280]{1,0:T(8,128)(2,1)S(1)}, u32[]{:S(2)}, u32[]{:S(2)}) %collective-permute-start.19) | collective-permute-done | bytes 327712 | tf_op jit(solution)/shard_map/ppermute | solution.py:57
  359.0 1.2 collective-permute-start.20
  360.2 12.1 %shard_map.58 = bf16[128,2560]{1,0:T(8,128)(2,1)S(1)} custom-call(bf16[128,2560]{1,0:T(8,128)(2,1)S(1)} %get-tuple-element.9.normed_ref, bf16[2,2560,2560]{2,1,0:T(8,128)(2,1)} %all-gather.2.cloned.1.call-done.win_ref.wout_ref, bf16[2,2560,2560]{2,1,0:T(8,128)(2,1)} %all-gather.2.cloned.1.call-done.win_ref.wout_ref), custom_call_target="tpu_custom_call" | custom-call | flops 3355443200 | bytes 27525120 | tf_op jit(solution)/shard_map/pallas_call | solution.py:33
  372.4 0.3 fusion.21
  372.8 0.3 fusion.23.normed_ref
  373.0 12.1 %shard_map.62 = bf16[128,2560]{1,0:T(8,128)(2,1)S(1)} custom-call(bf16[128,2560]{1,0:T(8,128)(2,1)S(1)} %fusion.23.normed_ref, bf16[2,2560,2560]{2,1,0:T(8,128)(2,1)} %all-gather.2.cloned.1.call-done.win_ref.wout_ref, bf16[2,2560,2560]{2,1,0:T(8,128)(2,1)} %all-gather.2.cloned.1.call-done.win_ref.wout_ref), custom_call_target="tpu_custom_call" | custom-call | flops 3355443200 | bytes 27525120 | tf_op jit(solution)/shard_map/pallas_call | solution.py:33
  385.2 0.6 collective-permute-start.21
  385.8 0.3 fusion.24
  386.0 1.0 collective-permute-done.21
  387.0 0.3 fusion.25
  387.3 0.9 maximum_bitcast_fusion
  (38 shorter events, 1.4 us)
Async XLA Ops:
  6.5 2.8 copy-start
  6.5 196.8 %all-gather.2.cloned.1.call-start = ((), (), s32[]{:S(2)}) async-start(), calls=%async_computation | async-start | bytes 27033600 | tf_op jit(solution)/shard_map/all_gather | solution.py:65
  9.4 3.6 copy-start.1
  9.6 4.6 %collective-permute-start.11 = (bf16[128,1280]{1,0:T(8,128)(2,1)S(1)}, bf16[128,1280]{1,0:T(8,128)(2,1)S(1)}, u32[]{:S(2)}, u32[]{:S(2)}) collective-permute-start(bf16[128,1280]{1,0:T(8,128)(2,1)S(1)} %get-tuple-element.8), channel_id=1, source_target_pairs={{0,1},{1,0},{2,3},{3,2},{4,5},{5,4},{6,7},{7,6},{8,9},{9,8},{10,11... | collective-permute-start | bytes 983048 | tf_op jit(solution)/shard_map/ppermute | solution.py:73
  12.9 1.7 collective-permute-start
  215.5 13.4 %collective-permute-start.12 = (bf16[128,1280]{1,0:T(8,128)(2,1)S(1)}, bf16[128,1280]{1,0:T(8,128)(2,1)}, u32[]{:S(2)}, u32[]{:S(2)}) collective-permute-start(bf16[128,1280]{1,0:T(8,128)(2,1)S(1)} %constant_dynamic-slice_fusion.3), channel_id=1, source_target_pairs={{0,1},{1,0},{2,3},{3,2},{4,5},{5,4},{6,7},{7,6},{8,9},{9,8},{10,11... | collective-permute-start | bytes 983048 | tf_op jit(solution)/shard_map/ppermute | solution.py:87
  228.8 1.7 collective-permute-start.1
  231.7 10.1 %collective-permute-start.2 = (bf16[128,1280]{1,0:T(8,128)(2,1)S(1)}, bf16[128,1280]{1,0:T(8,128)(2,1)S(1)}, u32[]{:S(2)}, u32[]{:S(2)}) collective-permute-start(bf16[128,1280]{1,0:T(8,128)(2,1)S(1)} %get-tuple-element.5), channel_id=1, source_target_pairs={{0,64},{64,128},{128,192},{1,65},{65,129},{129,193},{2,66},{66,130... | collective-permute-start | bytes 983048 | tf_op jit(solution)/shard_map/ppermute | solution.py:57
  241.8 2.2 collective-permute-start.3
  256.8 1.7 collective-permute-start.4
  258.6 10.8 %collective-permute-start.5 = (bf16[128,1280]{1,0:T(8,128)(2,1)S(1)}, bf16[128,1280]{1,0:T(8,128)(2,1)S(1)}, u32[]{:S(2)}, u32[]{:S(2)}) collective-permute-start(bf16[128,1280]{1,0:T(8,128)(2,1)S(1)} %add_convert_fusion.6), channel_id=1, source_target_pairs={{0,64},{64,128},{128,192},{1,65},{65,129},{129,193},{2,66},{66,130... | collective-permute-start | bytes 983048 | tf_op jit(solution)/shard_map/ppermute | solution.py:57
  269.4 2.5 collective-permute-start.6
  284.6 4.6 %collective-permute-start.7 = (bf16[128,1280]{1,0:T(8,128)(2,1)S(1)}, bf16[128,1280]{1,0:T(8,128)(2,1)S(1)}, u32[]{:S(2)}, u32[]{:S(2)}) collective-permute-start(bf16[128,1280]{1,0:T(8,128)(2,1)S(1)} %constant_dynamic-slice_fusion.5), channel_id=1, source_target_pairs={{0,1},{1,0},{2,3},{3,2},{4,5},{5,4},{6,7},{7,6},{8,9},{9,8},{10,11... | collective-permute-start | bytes 983048 | tf_op jit(solution)/shard_map/ppermute | solution.py:87
  285.1 11.1 %collective-permute-start.13 = (bf16[128,1280]{1,0:T(8,128)(2,1)S(1)}, bf16[128,1280]{1,0:T(8,128)(2,1)S(1)}, u32[]{:S(2)}, u32[]{:S(2)}) collective-permute-start(bf16[128,1280]{1,0:T(8,128)(2,1)S(1)} %get-tuple-element.6), channel_id=1, source_target_pairs={{0,64},{64,128},{128,192},{1,65},{65,129},{129,193},{2,66},{66,130... | collective-permute-start | bytes 983048 | tf_op jit(solution)/shard_map/ppermute | solution.py:57
  289.4 13.8 %collective-permute-start.8 = (bf16[128,1280]{1,0:T(8,128)(2,1)S(1)}, bf16[128,1280]{1,0:T(8,128)(2,1)S(1)}, u32[]{:S(2)}, u32[]{:S(2)}) collective-permute-start(bf16[128,1280]{1,0:T(8,128)(2,1)S(1)} %add_convert_fusion.5), channel_id=1, source_target_pairs={{0,64},{64,128},{128,192},{1,65},{65,129},{129,193},{2,66},{66,130... | collective-permute-start | bytes 983048 | tf_op jit(solution)/shard_map/ppermute | solution.py:57
  296.1 8.0 %collective-permute-start.14 = (bf16[128,1280]{1,0:T(8,128)(2,1)S(1)}, bf16[128,1280]{1,0:T(8,128)(2,1)S(1)}, u32[]{:S(2)}, u32[]{:S(2)}) collective-permute-start(bf16[128,1280]{1,0:T(8,128)(2,1)S(1)} %collective-permute-done.13), channel_id=1, source_target_pairs={{0,1},{1,0},{2,3},{3,2},{4,5},{5,4},{6,7},{7,6},{8,9},{9,8},{10,11... | collective-permute-start | bytes 983048 | tf_op jit(solution)/shard_map/ppermute | solution.py:73
  303.2 2.2 collective-permute-start.9
  318.4 1.7 collective-permute-start.15
  320.3 10.8 %collective-permute-start.16 = (bf16[128,1280]{1,0:T(8,128)(2,1)S(1)}, bf16[128,1280]{1,0:T(8,128)(2,1)S(1)}, u32[]{:S(2)}, u32[]{:S(2)}) collective-permute-start(bf16[128,1280]{1,0:T(8,128)(2,1)S(1)} %add_convert_fusion.2), channel_id=1, source_target_pairs={{0,64},{64,128},{128,192},{1,65},{65,129},{129,193},{2,66},{66,130... | collective-permute-start | bytes 983048 | tf_op jit(solution)/shard_map/ppermute | solution.py:57
  331.1 2.5 collective-permute-start.17
  346.3 1.7 collective-permute-start.18
  348.2 10.8 %collective-permute-start.19 = (bf16[128,1280]{1,0:T(8,128)(2,1)S(1)}, bf16[128,1280]{1,0:T(8,128)(2,1)S(1)}, u32[]{:S(2)}, u32[]{:S(2)}) collective-permute-start(bf16[128,1280]{1,0:T(8,128)(2,1)S(1)} %add_convert_fusion.1), channel_id=1, source_target_pairs={{0,64},{64,128},{128,192},{1,65},{65,129},{129,193},{2,66},{66,130... | collective-permute-start | bytes 983048 | tf_op jit(solution)/shard_map/ppermute | solution.py:57
  359.0 13.5 %collective-permute-start.20 = (bf16[128,1280]{1,0:T(8,128)(2,1)S(1)}, bf16[128,1280]{1,0:T(8,128)(2,1)S(1)}, u32[]{:S(2)}, u32[]{:S(2)}) collective-permute-start(bf16[128,1280]{1,0:T(8,128)(2,1)S(1)} %collective-permute-done.19), channel_id=1, source_target_pairs={{0,1},{1,0},{2,3},{3,2},{4,5},{5,4},{6,7},{7,6},{8,9},{9,8},{10,11... | collective-permute-start | bytes 983048 | tf_op jit(solution)/shard_map/ppermute | solution.py:73
  372.3 13.4 %collective-permute-start.10 = (bf16[128,1280]{1,0:T(8,128)(2,1)S(1)}, bf16[128,1280]{1,0:T(8,128)(2,1)S(1)}, u32[]{:S(2)}, u32[]{:S(2)}) collective-permute-start(bf16[128,1280]{1,0:T(8,128)(2,1)S(1)} %constant_dynamic-slice_fusion.4), channel_id=1, source_target_pairs={{0,1},{1,0},{2,3},{3,2},{4,5},{5,4},{6,7},{7,6},{8,9},{9,8},{10,11... | collective-permute-start | bytes 983048 | tf_op jit(solution)/shard_map/ppermute | solution.py:87
  385.2 1.8 collective-permute-start.21
Sparse Core Ops, SparseCore 0:
  9.9 193.3 all-gather.1

commit v8 on v6

--- a/solution.py
+++ b/solution.py
@@ -85,13 +85,9 @@
     result = apply_layer(first)
     stored = jnp.where(segment_index == 0, result, jnp.zeros_like(result))
 
-    def advance(moment, carry):
-        previous, stored = carry
-        result = apply_layer(passed_along(previous, "section", 1))
+    for moment in range(1, segment_count):
+        result = apply_layer(passed_along(result, "section", 1))
         stored = jnp.where(segment_index == moment, result, stored)
-        return (result, stored)
-
-    leftover, stored = lax.fori_loop(1, segment_count, advance, (result, stored))
     return stored.reshape(1, local_rows, width_local)
 
 

time: 347 us -> 341 us (0.983)
  other arithmetic: 14.7 us -> 9.48 us
    select_n x4 -> x0, other arithmetic: 8.35 us -> none  [the longest x3 7.14 us: advance(): stored = jnp.where(segment_index == moment, result, stored)]
where the time goes in v8:
time: 341 us; the launch traced here: 340 us
  waiting for transfers between devices  243 us (71%)
  Pallas kernels  51.7 us (15%)
  starting transfers between devices  20.9 us (6%)
  between operations  14.2 us (4%)
  other arithmetic  9.48 us (3%)
    all_gather x1, waiting for transfers between devices, per_device(): gathered = lax.all_gather(both, 'dp', axis=1, tiled=True)  188 us
    pallas_call x4, Pallas kernels, ffn(): pl.pallas_call(ffn_body, grid=(hidden_units // TILE,), in_specs=[pl.Block...  51.7 us
    ppermute x3, waiting for transfers between devices, passed_along(): lax.ppermute(value, axis, [(source, source + steps) for source in range(f...  41.1 us
    ppermute x3, starting transfers between devices, passed_along(): lax.ppermute(value, axis, [(source, source + steps) for source in range(f...  11.4 us
    ppermute x4, waiting for transfers between devices, apply_layer(): other = lax.ppermute(send, 'mp', [(0, 1), (1, 0)])  7.24 us
    ppermute x4, starting transfers between devices, apply_layer(): partner = lax.ppermute(current, 'mp', [(0, 1), (1, 0)])  6.91 us
    ppermute x4, waiting for transfers between devices, apply_layer(): partner = lax.ppermute(current, 'mp', [(0, 1), (1, 0)])  6.86 us
  transfers between devices with their start and end apart: 12, of which 12 were waited for; matrix products, arithmetic and copies ran while one was open for 0% of the time, Pallas kernels for 0%

profile of v8, /device:TPU:1, one launch (start us, length us, event | category | flops | bytes accessed | tf_op | source)
XLA Modules:
  0.0 340.4 jit_solution(7114972819182901947)
XLA Ops:
  6.5 0.0 copy-start.1
  6.5 0.0 all-gather.2.cloned.1.call-start
  6.5 2.1 pad_maximum_fusion
  8.7 0.0 copy-start.3
  8.7 0.0 all-gather.2.cloned.1.call-update
  9.4 0.0 copy-done.1
  9.4 0.1 broadcast_select_fusion
  9.5 3.3 collective-permute-start
  12.8 0.0 copy-done.3
  12.9 1.7 collective-permute-done
  14.6 0.4 fusion
  15.0 0.6 fusion.2.normed_ref
  15.5 187.8 %all-gather.2.cloned.1.call-done.win_ref.wout_ref = bf16[2,2560,2560]{2,1,0:T(8,128)(2,1)} async-done(((bf16[2,80,2560]{2,1,0:T(8,128)(2,1)}), bf16[2,2560,2560]{2,1,0:T(8,128)(2,1)}) %all-gather.2.cloned.1.call-update) | async-done | bytes 26214416 | tf_op jit(solution)/shard_map/all_gather | solution.py:59
  203.4 12.9 %shard_map.55 = bf16[256,2560]{1,0:T(8,128)(2,1)S(1)} custom-call(bf16[256,2560]{1,0:T(8,128)(2,1)S(1)} %fusion.2.normed_ref, bf16[2,2560,2560]{2,1,0:T(8,128)(2,1)} %all-gather.2.cloned.1.call-done.win_ref.wout_ref, bf16[2,2560,2560]{2,1,0:T(8,128)(2,1)} %all-gather.2.cloned.1.call-done.win_ref.wout_ref), custom_call_target="tpu_custom_call" | custom-call | tf_op jit(solution)/shard_map/pallas_call | solution.py:32
  216.3 0.0 copy-start.2
  216.3 0.1 constant_dynamic-slice_fusion.3
  216.4 1.1 collective-permute-start.1
  217.5 1.7 collective-permute-done.1
  219.2 0.0 copy-done.2
  219.2 0.3 add_convert_fusion.3
  219.5 3.1 collective-permute-start.2
  222.7 13.7 %collective-permute-done.2 = bf16[256,1280]{1,0:T(8,128)(2,1)S(1)} collective-permute-done((bf16[256,1280]{1,0:T(8,128)(2,1)S(1)}, bf16[256,1280]{1,0:T(8,128)(2,1)S(1)}, u32[]{:S(2)}, u32[]{:S(2)}) %collective-permute-start.2) | collective-permute-done | bytes 655392 | tf_op jit(solution)/shard_map/ppermute | solution.py:51
  236.4 1.2 collective-permute-start.3
  237.6 1.7 collective-permute-done.3
  239.3 0.4 fusion.3
  239.7 0.6 fusion.5.normed_ref
  240.3 12.9 %shard_map.56 = bf16[256,2560]{1,0:T(8,128)(2,1)S(1)} custom-call(bf16[256,2560]{1,0:T(8,128)(2,1)S(1)} %fusion.5.normed_ref, bf16[2,2560,2560]{2,1,0:T(8,128)(2,1)} %all-gather.2.cloned.1.call-done.win_ref.wout_ref, bf16[2,2560,2560]{2,1,0:T(8,128)(2,1)} %all-gather.2.cloned.1.call-done.win_ref.wout_ref), custom_call_target="tpu_custom_call" | custom-call | tf_op jit(solution)/shard_map/pallas_call | solution.py:32
  253.2 0.1 constant_dynamic-slice_fusion.2
  253.3 0.5 collective-permute-start.4
  253.7 1.7 collective-permute-done.4
  255.5 0.2 add_convert_fusion.2
  255.7 4.1 %collective-permute-start.5 = (bf16[256,1280]{1,0:T(8,128)(2,1)S(1)}, bf16[256,1280]{1,0:T(8,128)(2,1)S(1)}, u32[]{:S(2)}, u32[]{:S(2)}) collective-permute-start(bf16[256,1280]{1,0:T(8,128)(2,1)S(1)} %add_convert_fusion.2), channel_id=1, source_target_pairs={{0,64},{64,128},{128,192},{1,65},{65,129},{129,193},{2,66},{66,130... | collective-permute-start | bytes 1966088 | tf_op jit(solution)/shard_map/ppermute | solution.py:51
  259.9 13.7 %collective-permute-done.5 = bf16[256,1280]{1,0:T(8,128)(2,1)S(1)} collective-permute-done((bf16[256,1280]{1,0:T(8,128)(2,1)S(1)}, bf16[256,1280]{1,0:T(8,128)(2,1)S(1)}, u32[]{:S(2)}, u32[]{:S(2)}) %collective-permute-start.5) | collective-permute-done | bytes 655392 | tf_op jit(solution)/shard_map/ppermute | solution.py:51
  273.5 1.2 collective-permute-start.6
  274.7 1.7 collective-permute-done.6
  276.5 0.4 fusion.6
  276.9 0.6 fusion.8.normed_ref
  277.5 12.9 %shard_map.57 = bf16[256,2560]{1,0:T(8,128)(2,1)S(1)} custom-call(bf16[256,2560]{1,0:T(8,128)(2,1)S(1)} %fusion.8.normed_ref, bf16[2,2560,2560]{2,1,0:T(8,128)(2,1)} %all-gather.2.cloned.1.call-done.win_ref.wout_ref, bf16[2,2560,2560]{2,1,0:T(8,128)(2,1)} %all-gather.2.cloned.1.call-done.win_ref.wout_ref), custom_call_target="tpu_custom_call" | custom-call | tf_op jit(solution)/shard_map/pallas_call | solution.py:32
  290.4 0.1 constant_dynamic-slice_fusion.1
  290.5 0.6 collective-permute-start.7
  291.1 1.7 collective-permute-done.7
  292.8 0.2 add_convert_fusion.1
  293.1 0.0 copy-start
  293.1 4.2 %collective-permute-start.8 = (bf16[256,1280]{1,0:T(8,128)(2,1)S(1)}, bf16[256,1280]{1,0:T(8,128)(2,1)S(1)}, u32[]{:S(2)}, u32[]{:S(2)}) collective-permute-start(bf16[256,1280]{1,0:T(8,128)(2,1)S(1)} %add_convert_fusion.1), channel_id=1, source_target_pairs={{0,64},{64,128},{128,192},{1,65},{65,129},{129,193},{2,66},{66,130... | collective-permute-start | bytes 1966088 | tf_op jit(solution)/shard_map/ppermute | solution.py:51
  297.3 13.7 %collective-permute-done.8 = bf16[256,1280]{1,0:T(8,128)(2,1)S(1)} collective-permute-done((bf16[256,1280]{1,0:T(8,128)(2,1)S(1)}, bf16[256,1280]{1,0:T(8,128)(2,1)S(1)}, u32[]{:S(2)}, u32[]{:S(2)}) %collective-permute-start.8) | collective-permute-done | bytes 655392 | tf_op jit(solution)/shard_map/ppermute | solution.py:51
  310.9 1.2 collective-permute-start.9
  312.1 1.7 collective-permute-done.9
  313.9 0.4 fusion.9
  314.3 0.6 fusion.11.normed_ref
  314.9 0.0 copy-done
  314.9 12.9 %shard_map.58 = bf16[256,2560]{1,0:T(8,128)(2,1)S(1)} custom-call(bf16[256,2560]{1,0:T(8,128)(2,1)S(1)} %fusion.11.normed_ref, bf16[2,2560,2560]{2,1,0:T(8,128)(2,1)} %all-gather.2.cloned.1.call-done.win_ref.wout_ref, bf16[2,2560,2560]{2,1,0:T(8,128)(2,1)} %all-gather.2.cloned.1.call-done.win_ref.wout_ref), custom_call_target="tpu_custom_call" | custom-call | tf_op jit(solution)/shard_map/pallas_call | solution.py:32
  327.8 0.9 constant_dynamic-slice_fusion
  328.7 0.4 collective-permute-start.10
  329.1 2.1 collective-permute-done.10
  331.1 2.5 fusion.13
  (6 shorter events, 0.1 us)
Async XLA Ops:
  6.5 2.8 copy-start.1
  6.5 196.8 %all-gather.2.cloned.1.call-start = ((), (), s32[]{:S(2)}) async-start(), calls=%async_computation | async-start | bytes 27033600 | tf_op jit(solution)/shard_map/all_gather | solution.py:59
  8.7 4.1 %copy-start.3 = (f32[1,2560]{1,0:T(1,128)S(1)}, f32[1,2560]{1,0:T(1,128)}, u32[]{:S(2)}) copy-start(f32[1,2560]{1,0:T(1,128)} %param.7) | copy-start | bytes 30724
  9.5 5.1 %collective-permute-start = (bf16[256,1280]{1,0:T(8,128)(2,1)S(1)}, bf16[256,1280]{1,0:T(8,128)(2,1)S(1)}, u32[]{:S(2)}, u32[]{:S(2)}) collective-permute-start(bf16[256,1280]{1,0:T(8,128)(2,1)S(1)} %broadcast_select_fusion), channel_id=1, source_target_pairs={{0,1},{1,0},{2,3},{3,2},{4,5},{5,4},{6,7},{7,6},{8,9},{9,8},{10,11... | collective-permute-start | bytes 1966088 | tf_op jit(solution)/shard_map/ppermute | solution.py:67
  216.3 2.9 copy-start.2
  216.4 2.9 collective-permute-start.1
  219.5 16.8 %collective-permute-start.2 = (bf16[256,1280]{1,0:T(8,128)(2,1)S(1)}, bf16[256,1280]{1,0:T(8,128)(2,1)S(1)}, u32[]{:S(2)}, u32[]{:S(2)}) collective-permute-start(bf16[256,1280]{1,0:T(8,128)(2,1)S(1)} %add_convert_fusion.3), channel_id=1, source_target_pairs={{0,64},{64,128},{128,192},{1,65},{65,129},{129,193},{2,66},{66,130... | collective-permute-start | bytes 1966088 | tf_op jit(solution)/shard_map/ppermute | solution.py:51
  236.4 2.9 collective-permute-start.3
  253.3 2.2 collective-permute-start.4
  255.7 17.8 %collective-permute-start.5 = (bf16[256,1280]{1,0:T(8,128)(2,1)S(1)}, bf16[256,1280]{1,0:T(8,128)(2,1)S(1)}, u32[]{:S(2)}, u32[]{:S(2)}) collective-permute-start(bf16[256,1280]{1,0:T(8,128)(2,1)S(1)} %add_convert_fusion.2), channel_id=1, source_target_pairs={{0,64},{64,128},{128,192},{1,65},{65,129},{129,193},{2,66},{66,130... | collective-permute-start | bytes 1966088 | tf_op jit(solution)/shard_map/ppermute | solution.py:51
  273.5 2.9 collective-permute-start.6
  290.5 2.4 collective-permute-start.7
  293.1 21.8 %copy-start = (bf16[256,1280]{1,0:T(8,128)(2,1)}, bf16[256,1280]{1,0:T(8,128)(2,1)S(1)}, u32[]{:S(2)}) copy-start(bf16[256,1280]{1,0:T(8,128)(2,1)S(1)} %add_convert_fusion.1) | copy-start | bytes 1966084
  293.1 17.9 %collective-permute-start.8 = (bf16[256,1280]{1,0:T(8,128)(2,1)S(1)}, bf16[256,1280]{1,0:T(8,128)(2,1)S(1)}, u32[]{:S(2)}, u32[]{:S(2)}) collective-permute-start(bf16[256,1280]{1,0:T(8,128)(2,1)S(1)} %add_convert_fusion.1), channel_id=1, source_target_pairs={{0,64},{64,128},{128,192},{1,65},{65,129},{129,193},{2,66},{66,130... | collective-permute-start | bytes 1966088 | tf_op jit(solution)/shard_map/ppermute | solution.py:51
  310.9 2.9 collective-permute-start.9
  328.7 2.4 collective-permute-start.10
Sparse Core Ops, SparseCore 0:
  9.9 193.3 all-gather.1

commit v9 on v8

--- a/solution.py
+++ b/solution.py
@@ -8,7 +8,7 @@
 TILE = 512
 
 
-def ffn_body(normed_ref, win_ref, wout_ref, out_ref, acc_ref):
+def ffn_body(normed_ref, win_ref, wout_ref, keep_ref, send_ref, acc_ref):
     step = pl.program_id(0)
 
     @pl.when(step == 0)
@@ -23,12 +23,18 @@
 
     @pl.when(step == pl.num_programs(0) - 1)
     def _():
-        out_ref[...] = acc_ref[...].astype(out_ref.dtype)
+        half = keep_ref.shape[1]
+        own = lax.axis_index("mp")
+        keep_ref[...] = acc_ref[:, pl.ds(pl.multiple_of(own * half, 128), half)].astype(keep_ref.dtype)
+        send_ref[...] = acc_ref[:, pl.ds(pl.multiple_of((1 - own) * half, 128), half)].astype(
+            send_ref.dtype
+        )
 
 
-def ffn(normed, gathered, interpret=False):
+def ffn(normed, gathered):
     rows, width = normed.shape
     hidden_units = gathered.shape[2]
+    half = width // 2
     return pl.pallas_call(
         ffn_body,
         grid=(hidden_units // TILE,),
@@ -37,11 +43,13 @@
             pl.BlockSpec((1, width, TILE), lambda j: (0, 0, j)),
             pl.BlockSpec((1, width, TILE), lambda j: (1, 0, j)),
         ],
-        out_specs=pl.BlockSpec((rows, width), lambda j: (0, 0)),
-        out_shape=jax.ShapeDtypeStruct((rows, width), jnp.bfloat16),
+        out_specs=[
+            pl.BlockSpec((rows, half), lambda j: (0, 0)),
+            pl.BlockSpec((rows, half), lambda j: (0, 0)),
+        ],
+        out_shape=[jax.ShapeDtypeStruct((rows, half), jnp.bfloat16)] * 2,
         scratch_shapes=[pltpu.VMEM((rows, width), jnp.float32)],
         compiler_params=pltpu.CompilerParams(vmem_limit_bytes=48 << 20),
-        interpret=interpret,
     )(normed, gathered, gathered)
 
 
@@ -73,11 +81,7 @@
         wide = whole.astype(jnp.float32)
         meansq = jnp.mean(wide * wide, axis=-1, keepdims=True)
         normed = (wide * lax.rsqrt(meansq + 1e-06) * gain_row).astype(jnp.bfloat16)
-        partial_term = ffn(normed, gathered)
-        keep = lax.dynamic_slice_in_dim(partial_term, half_index * width_local, width_local, axis=1)
-        send = lax.dynamic_slice_in_dim(
-            partial_term, (1 - half_index) * width_local, width_local, axis=1
-        )
+        keep, send = ffn(normed, gathered)
         other = lax.ppermute(send, "mp", [(0, 1), (1, 0)])
         summed = keep.astype(jnp.float32) + other.astype(jnp.float32)
         return (current.astype(jnp.float32) + summed).astype(jnp.bfloat16)
@@ -87,7 +91,7 @@
 
     for moment in range(1, segment_count):
         result = apply_layer(passed_along(result, "section", 1))
-        stored = jnp.where(segment_index == moment, result, stored)
+        stored = lax.optimization_barrier(jnp.where(segment_index == moment, result, stored))
     return stored.reshape(1, local_rows, width_local)
 
 

time: 341 us -> 339 us (level)
  no operation moved by 1% of the time
where the time goes in v9:
time: 339 us
  waiting for transfers between devices  243 us (72%)
  Pallas kernels  51.8 us (15%)
  starting transfers between devices  21 us (6%)
  between operations  14.2 us (4%)
  other arithmetic  9.38 us (3%)
    all_gather x1, waiting for transfers between devices, per_device(): gathered = lax.all_gather(both, 'dp', axis=1, tiled=True)  188 us
    pallas_call x4, Pallas kernels, ffn(): pl.pallas_call(ffn_body, grid=(hidden_units // TILE,), in_specs=[pl.Block...  51.8 us
    ppermute x3, waiting for transfers between devices, passed_along(): lax.ppermute(value, axis, [(source, source + steps) for source in range(f...  41.1 us
    ppermute x3, starting transfers between devices, passed_along(): lax.ppermute(value, axis, [(source, source + steps) for source in range(f...  11.4 us
    ppermute x4, starting transfers between devices, apply_layer(): partner = lax.ppermute(current, 'mp', [(0, 1), (1, 0)])  6.93 us
    ppermute x4, waiting for transfers between devices, apply_layer(): other = lax.ppermute(send, 'mp', [(0, 1), (1, 0)])  6.9 us
    ppermute x4, waiting for transfers between devices, apply_layer(): partner = lax.ppermute(current, 'mp', [(0, 1), (1, 0)])  6.86 us
  transfers between devices with their start and end apart: 12, of which 12 were waited for; matrix products, arithmetic and copies ran while one was open for 0% of the time, Pallas kernels for 0%

profile of v9, /device:TPU:1, one launch (start us, length us, event | category | flops | bytes accessed | tf_op | source)
XLA Modules:
  0.0 339.1 jit_solution(3001183478647159673)
XLA Ops:
  6.5 0.0 copy-start
  6.5 0.0 all-gather.2.cloned.1.call-start
  6.5 2.2 pad_maximum_fusion
  8.7 0.0 copy-start.2
  8.7 0.0 all-gather.2.cloned.1.call-update
  9.4 0.0 copy-done
  9.4 0.1 broadcast_select_fusion
  9.5 3.3 collective-permute-start
  12.9 0.0 copy-done.2
  12.9 1.7 collective-permute-done
  14.6 0.4 fusion
  15.0 0.6 fusion.2.normed_ref
  15.6 187.8 %all-gather.2.cloned.1.call-done.win_ref.wout_ref = bf16[2,2560,2560]{2,1,0:T(8,128)(2,1)} async-done(((bf16[2,80,2560]{2,1,0:T(8,128)(2,1)}), bf16[2,2560,2560]{2,1,0:T(8,128)(2,1)}) %all-gather.2.cloned.1.call-update) | async-done | bytes 26214416 | tf_op jit(solution)/shard_map/all_gather | solution.py:67
  203.4 12.9 %shard_map.55 = (bf16[256,1280]{1,0:T(8,128)(2,1)S(1)}, bf16[256,1280]{1,0:T(8,128)(2,1)S(1)}) custom-call(bf16[256,2560]{1,0:T(8,128)(2,1)S(1)} %fusion.2.normed_ref, bf16[2,2560,2560]{2,1,0:T(8,128)(2,1)} %all-gather.2.cloned.1.call-done.win_ref.wout_ref, bf16[2,2560,2560]{2,1,0:T(8,128)(2,1)} %all-gather.2.cloned.1.call-done.win_ref.wout_ref), custom_call_target="tpu_custom_call" | custom-call | tf_op jit(solution)/shard_map/pallas_call | solution.py:38
  216.3 1.1 collective-permute-start.1
  217.4 1.7 collective-permute-done.1
  219.2 0.3 add_convert_fusion.3
  219.5 3.1 collective-permute-start.2
  222.6 13.7 %collective-permute-done.2 = bf16[256,1280]{1,0:T(8,128)(2,1)S(1)} collective-permute-done((bf16[256,1280]{1,0:T(8,128)(2,1)S(1)}, bf16[256,1280]{1,0:T(8,128)(2,1)S(1)}, u32[]{:S(2)}, u32[]{:S(2)}) %collective-permute-start.2) | collective-permute-done | bytes 655392 | tf_op jit(solution)/shard_map/ppermute | solution.py:59
  236.3 1.2 collective-permute-start.3
  237.5 1.7 collective-permute-done.3
  239.2 0.4 fusion.3
  239.7 0.6 fusion.5.normed_ref
  240.2 12.9 %shard_map.56 = (bf16[256,1280]{1,0:T(8,128)(2,1)S(1)}, bf16[256,1280]{1,0:T(8,128)(2,1)S(1)}) custom-call(bf16[256,2560]{1,0:T(8,128)(2,1)S(1)} %fusion.5.normed_ref, bf16[2,2560,2560]{2,1,0:T(8,128)(2,1)} %all-gather.2.cloned.1.call-done.win_ref.wout_ref, bf16[2,2560,2560]{2,1,0:T(8,128)(2,1)} %all-gather.2.cloned.1.call-done.win_ref.wout_ref), custom_call_target="tpu_custom_call" | custom-call | tf_op jit(solution)/shard_map/pallas_call | solution.py:38
  253.2 0.5 collective-permute-start.4
  253.7 1.7 collective-permute-done.4
  255.4 1.2 select_select_fusion
  256.6 4.1 %collective-permute-start.5 = (bf16[256,1280]{1,0:T(8,128)(2,1)S(1)}, bf16[256,1280]{1,0:T(8,128)(2,1)S(1)}, u32[]{:S(2)}, u32[]{:S(2)}) collective-permute-start(bf16[256,1280]{1,0:T(8,128)(2,1)S(1)} %get-tuple-element.24), channel_id=1, source_target_pairs={{0,64},{64,128},{128,192},{1,65},{65,129},{129,193},{2,66},{66,130... | collective-permute-start | bytes 1966088 | tf_op jit(solution)/shard_map/ppermute | solution.py:59
  260.7 13.7 %collective-permute-done.5 = bf16[256,1280]{1,0:T(8,128)(2,1)S(1)} collective-permute-done((bf16[256,1280]{1,0:T(8,128)(2,1)S(1)}, bf16[256,1280]{1,0:T(8,128)(2,1)S(1)}, u32[]{:S(2)}, u32[]{:S(2)}) %collective-permute-start.5) | collective-permute-done | bytes 655392 | tf_op jit(solution)/shard_map/ppermute | solution.py:59
  274.4 1.2 collective-permute-start.6
  275.6 1.7 collective-permute-done.6
  277.4 0.4 fusion.6
  277.8 0.6 fusion.8.normed_ref
  278.4 0.0 copy-start.1
  278.4 13.0 %shard_map.57 = (bf16[256,1280]{1,0:T(8,128)(2,1)S(1)}, bf16[256,1280]{1,0:T(8,128)(2,1)S(1)}) custom-call(bf16[256,2560]{1,0:T(8,128)(2,1)S(1)} %fusion.8.normed_ref, bf16[2,2560,2560]{2,1,0:T(8,128)(2,1)} %all-gather.2.cloned.1.call-done.win_ref.wout_ref, bf16[2,2560,2560]{2,1,0:T(8,128)(2,1)} %all-gather.2.cloned.1.call-done.win_ref.wout_ref), custom_call_target="tpu_custom_call" | custom-call | tf_op jit(solution)/shard_map/pallas_call | solution.py:38
  291.4 0.6 collective-permute-start.7
  292.0 1.7 collective-permute-done.7
  293.8 0.0 copy-done.1
  293.8 0.3 broadcast_select_fusion.1
  294.1 4.1 %collective-permute-start.8 = (bf16[256,1280]{1,0:T(8,128)(2,1)S(1)}, bf16[256,1280]{1,0:T(8,128)(2,1)S(1)}, u32[]{:S(2)}, u32[]{:S(2)}) collective-permute-start(bf16[256,1280]{1,0:T(8,128)(2,1)S(1)} %get-tuple-element.22), channel_id=1, source_target_pairs={{0,64},{64,128},{128,192},{1,65},{65,129},{129,193},{2,66},{66,130... | collective-permute-start | bytes 1966088 | tf_op jit(solution)/shard_map/ppermute | solution.py:59
  298.3 13.7 %collective-permute-done.8 = bf16[256,1280]{1,0:T(8,128)(2,1)S(1)} collective-permute-done((bf16[256,1280]{1,0:T(8,128)(2,1)S(1)}, bf16[256,1280]{1,0:T(8,128)(2,1)S(1)}, u32[]{:S(2)}, u32[]{:S(2)}) %collective-permute-start.8) | collective-permute-done | bytes 655392 | tf_op jit(solution)/shard_map/ppermute | solution.py:59
  312.0 1.2 collective-permute-start.9
  313.2 1.7 collective-permute-done.9
  314.9 0.4 fusion.9
  315.3 0.6 fusion.11.normed_ref
  315.9 12.9 %shard_map.58 = (bf16[256,1280]{1,0:T(8,128)(2,1)S(1)}, bf16[256,1280]{1,0:T(8,128)(2,1)S(1)}) custom-call(bf16[256,2560]{1,0:T(8,128)(2,1)S(1)} %fusion.11.normed_ref, bf16[2,2560,2560]{2,1,0:T(8,128)(2,1)} %all-gather.2.cloned.1.call-done.win_ref.wout_ref, bf16[2,2560,2560]{2,1,0:T(8,128)(2,1)} %all-gather.2.cloned.1.call-done.win_ref.wout_ref), custom_call_target="tpu_custom_call" | custom-call | tf_op jit(solution)/shard_map/pallas_call | solution.py:38
  328.9 0.5 collective-permute-start.10
  329.3 1.7 collective-permute-done.10
  331.0 1.2 fusion.12
  (6 shorter events, 0.1 us)
Async XLA Ops:
  6.5 2.9 copy-start
  6.5 196.8 %all-gather.2.cloned.1.call-start = ((), (), s32[]{:S(2)}) async-start(), calls=%async_computation | async-start | bytes 27033600 | tf_op jit(solution)/shard_map/all_gather | solution.py:67
  8.7 4.1 %copy-start.2 = (f32[1,2560]{1,0:T(1,128)S(1)}, f32[1,2560]{1,0:T(1,128)}, u32[]{:S(2)}) copy-start(f32[1,2560]{1,0:T(1,128)} %param.7) | copy-start | bytes 30724
  9.5 5.1 %collective-permute-start = (bf16[256,1280]{1,0:T(8,128)(2,1)S(1)}, bf16[256,1280]{1,0:T(8,128)(2,1)S(1)}, u32[]{:S(2)}, u32[]{:S(2)}) collective-permute-start(bf16[256,1280]{1,0:T(8,128)(2,1)S(1)} %broadcast_select_fusion), channel_id=1, source_target_pairs={{0,1},{1,0},{2,3},{3,2},{4,5},{5,4},{6,7},{7,6},{8,9},{9,8},{10,11... | collective-permute-start | bytes 1966088 | tf_op jit(solution)/shard_map/ppermute | solution.py:75
  216.3 2.9 collective-permute-start.1
  219.5 16.8 %collective-permute-start.2 = (bf16[256,1280]{1,0:T(8,128)(2,1)S(1)}, bf16[256,1280]{1,0:T(8,128)(2,1)S(1)}, u32[]{:S(2)}, u32[]{:S(2)}) collective-permute-start(bf16[256,1280]{1,0:T(8,128)(2,1)S(1)} %add_convert_fusion.3), channel_id=1, source_target_pairs={{0,64},{64,128},{128,192},{1,65},{65,129},{129,193},{2,66},{66,130... | collective-permute-start | bytes 1966088 | tf_op jit(solution)/shard_map/ppermute | solution.py:59
  236.3 2.9 collective-permute-start.3
  253.2 2.2 collective-permute-start.4
  256.6 17.8 %collective-permute-start.5 = (bf16[256,1280]{1,0:T(8,128)(2,1)S(1)}, bf16[256,1280]{1,0:T(8,128)(2,1)S(1)}, u32[]{:S(2)}, u32[]{:S(2)}) collective-permute-start(bf16[256,1280]{1,0:T(8,128)(2,1)S(1)} %get-tuple-element.24), channel_id=1, source_target_pairs={{0,64},{64,128},{128,192},{1,65},{65,129},{129,193},{2,66},{66,130... | collective-permute-start | bytes 1966088 | tf_op jit(solution)/shard_map/ppermute | solution.py:59
  274.4 2.9 collective-permute-start.6
  278.4 15.4 %copy-start.1 = (bf16[256,1280]{1,0:T(8,128)(2,1)S(1)}, bf16[256,1280]{1,0:T(8,128)(2,1)}, u32[]{:S(2)}) copy-start(bf16[256,1280]{1,0:T(8,128)(2,1)} %get-tuple-element.23) | copy-start | bytes 1966084
  291.4 2.4 collective-permute-start.7
  294.1 17.8 %collective-permute-start.8 = (bf16[256,1280]{1,0:T(8,128)(2,1)S(1)}, bf16[256,1280]{1,0:T(8,128)(2,1)S(1)}, u32[]{:S(2)}, u32[]{:S(2)}) collective-permute-start(bf16[256,1280]{1,0:T(8,128)(2,1)S(1)} %get-tuple-element.22), channel_id=1, source_target_pairs={{0,64},{64,128},{128,192},{1,65},{65,129},{129,193},{2,66},{66,130... | collective-permute-start | bytes 1966088 | tf_op jit(solution)/shard_map/ppermute | solution.py:59
  312.0 2.9 collective-permute-start.9
  328.9 2.2 collective-permute-start.10
Sparse Core Ops, SparseCore 0:
  9.9 193.3 all-gather.1

commit v10 on v9

--- a/solution.py
+++ b/solution.py
@@ -8,11 +8,25 @@
 TILE = 512
 
 
-def ffn_body(normed_ref, win_ref, wout_ref, keep_ref, send_ref, acc_ref):
+def ffn_body(own_ref, partner_ref, gain_ref, win_ref, wout_ref, keep_ref, send_ref, normed_ref, acc_ref):
     step = pl.program_id(0)
+    half = keep_ref.shape[1]
+    own = lax.axis_index("mp")
+    own_cols = pl.ds(pl.multiple_of(own * half, 128), half)
+    other_cols = pl.ds(pl.multiple_of((1 - own) * half, 128), half)
 
     @pl.when(step == 0)
     def _():
+        mine = own_ref[...].astype(jnp.float32)
+        theirs = partner_ref[...].astype(jnp.float32)
+        total = jnp.sum(mine * mine, axis=-1, keepdims=True) + jnp.sum(
+            theirs * theirs, axis=-1, keepdims=True
+        )
+        scale = lax.rsqrt(total / (2 * half) + 1e-06)
+        normed_ref[:, own_cols] = (mine * scale * gain_ref[:, own_cols]).astype(normed_ref.dtype)
+        normed_ref[:, other_cols] = (theirs * scale * gain_ref[:, other_cols]).astype(
+            normed_ref.dtype
+        )
         acc_ref[...] = jnp.zeros_like(acc_ref)
 
     pre = jnp.dot(normed_ref[...], win_ref[0], preferred_element_type=jnp.float32)
@@ -23,23 +37,21 @@
 
     @pl.when(step == pl.num_programs(0) - 1)
     def _():
-        half = keep_ref.shape[1]
-        own = lax.axis_index("mp")
-        keep_ref[...] = acc_ref[:, pl.ds(pl.multiple_of(own * half, 128), half)].astype(keep_ref.dtype)
-        send_ref[...] = acc_ref[:, pl.ds(pl.multiple_of((1 - own) * half, 128), half)].astype(
-            send_ref.dtype
-        )
+        keep_ref[...] = acc_ref[:, own_cols].astype(keep_ref.dtype)
+        send_ref[...] = acc_ref[:, other_cols].astype(send_ref.dtype)
 
 
-def ffn(normed, gathered):
-    rows, width = normed.shape
+def ffn(current, partner, gain, gathered):
+    rows, half = current.shape
+    width = 2 * half
     hidden_units = gathered.shape[2]
-    half = width // 2
     return pl.pallas_call(
         ffn_body,
         grid=(hidden_units // TILE,),
         in_specs=[
-            pl.BlockSpec((rows, width), lambda j: (0, 0)),
+            pl.BlockSpec((rows, half), lambda j: (0, 0)),
+            pl.BlockSpec((rows, half), lambda j: (0, 0)),
+            pl.BlockSpec((1, width), lambda j: (0, 0)),
             pl.BlockSpec((1, width, TILE), lambda j: (0, 0, j)),
             pl.BlockSpec((1, width, TILE), lambda j: (1, 0, j)),
         ],
@@ -48,9 +60,12 @@
             pl.BlockSpec((rows, half), lambda j: (0, 0)),
         ],
         out_shape=[jax.ShapeDtypeStruct((rows, half), jnp.bfloat16)] * 2,
-        scratch_shapes=[pltpu.VMEM((rows, width), jnp.float32)],
+        scratch_shapes=[
+            pltpu.VMEM((rows, width), jnp.bfloat16),
+            pltpu.VMEM((rows, width), jnp.float32),
+        ],
         compiler_params=pltpu.CompilerParams(vmem_limit_bytes=48 << 20),
-    )(normed, gathered, gathered)
+    )(current, partner, gain, gathered, gathered)
 
 
 def passed_along(value, axis, steps):
@@ -65,7 +80,6 @@
     half_index = lax.axis_index("mp")
     both = jnp.stack([weight_in[0], weight_out[0].T])
     gathered = lax.all_gather(both, "dp", axis=1, tiled=True)
-    gain_row = norm_gain[0]
     local_rows, width_local = frames.shape
     live_count = frame_count[0]
     row_ids = jnp.arange(local_rows, dtype=jnp.int32)
@@ -73,15 +87,7 @@
 
     def apply_layer(current):
         partner = lax.ppermute(current, "mp", [(0, 1), (1, 0)])
-        whole = jnp.where(
-            half_index == 0,
-            jnp.concatenate([current, partner], axis=1),
-            jnp.concatenate([partner, current], axis=1),
-        )
-        wide = whole.astype(jnp.float32)
-        meansq = jnp.mean(wide * wide, axis=-1, keepdims=True)
-        normed = (wide * lax.rsqrt(meansq + 1e-06) * gain_row).astype(jnp.bfloat16)
-        keep, send = ffn(normed, gathered)
+        keep, send = ffn(current, partner, norm_gain, gathered)
         other = lax.ppermute(send, "mp", [(0, 1), (1, 0)])
         summed = keep.astype(jnp.float32) + other.astype(jnp.float32)
         return (current.astype(jnp.float32) + summed).astype(jnp.bfloat16)

time: 339 us -> 337 us (level)
  other arithmetic: 9.38 us -> 4.47 us
where the time goes in v10:
time: 337 us
  waiting for transfers between devices  244 us (72%)
  Pallas kernels  53.7 us (16%)
  starting transfers between devices  20.9 us (6%)
  between operations  14.1 us (4%)
  other arithmetic  4.47 us (1%)
    all_gather x1, waiting for transfers between devices, per_device(): gathered = lax.all_gather(both, 'dp', axis=1, tiled=True)  189 us
    pallas_call x4, Pallas kernels, ffn(): pl.pallas_call(ffn_body, grid=(hidden_units // TILE,), in_specs=[pl.Block...  53.7 us
    ppermute x3, waiting for transfers between devices, passed_along(): lax.ppermute(value, axis, [(source, source + steps) for source in range(f...  41.1 us
    ppermute x3, starting transfers between devices, passed_along(): lax.ppermute(value, axis, [(source, source + steps) for source in range(f...  11.5 us
    ppermute x4, starting transfers between devices, apply_layer(): partner = lax.ppermute(current, 'mp', [(0, 1), (1, 0)])  6.92 us
    ppermute x4, waiting for transfers between devices, apply_layer(): other = lax.ppermute(send, 'mp', [(0, 1), (1, 0)])  6.91 us
    ppermute x4, waiting for transfers between devices, apply_layer(): partner = lax.ppermute(current, 'mp', [(0, 1), (1, 0)])  6.9 us
  transfers between devices with their start and end apart: 12, of which 12 were waited for; matrix products, arithmetic and copies ran while one was open for 0% of the time, Pallas kernels for 0%

profile of v10, /device:TPU:1, one launch (start us, length us, event | category | flops | bytes accessed | tf_op | source)
XLA Modules:
  0.0 336.9 jit_solution(9244591160389024014)
XLA Ops:
  6.5 0.0 copy-start.1
  6.5 0.0 all-gather.2.cloned.1.call-start
  6.5 2.2 pad_maximum_fusion
  8.7 0.0 copy-start
  8.7 0.0 all-gather.2.cloned.1.call-update
  9.4 0.0 copy-done.1
  9.4 0.1 broadcast_select_fusion.own_ref
  9.5 3.3 collective-permute-start
  12.8 1.7 collective-permute-done.partner_ref
  14.6 188.8 %all-gather.2.cloned.1.call-done.win_ref.wout_ref = bf16[2,2560,2560]{2,1,0:T(8,128)(2,1)} async-done(((bf16[2,80,2560]{2,1,0:T(8,128)(2,1)}), bf16[2,2560,2560]{2,1,0:T(8,128)(2,1)}) %all-gather.2.cloned.1.call-update) | async-done | bytes 26214416 | tf_op jit(solution)/shard_map/all_gather | solution.py:82
  203.4 0.0 copy-done
  203.4 13.4 %shard_map.55 = (bf16[256,1280]{1,0:T(8,128)(2,1)S(1)}, bf16[256,1280]{1,0:T(8,128)(2,1)S(1)}) custom-call(bf16[256,1280]{1,0:T(8,128)(2,1)S(1)} %broadcast_select_fusion.own_ref, bf16[256,1280]{1,0:T(8,128)(2,1)S(1)} %collective-permute-done.partner_ref, f32[1,2560]{1,0:T(1,128)S(1)} %copy-done, ...), custom_call_target="tpu_custom_call" | custom-call | tf_op jit(solution)/shard_map/pallas_call | solution.py:48
  216.8 1.1 collective-permute-start.1
  217.9 1.7 collective-permute-done.1
  219.6 0.3 add_convert_fusion.3
  219.9 3.1 collective-permute-start.2
  223.1 13.7 %collective-permute-done.2.own_ref = bf16[256,1280]{1,0:T(8,128)(2,1)S(1)} collective-permute-done((bf16[256,1280]{1,0:T(8,128)(2,1)S(1)}, bf16[256,1280]{1,0:T(8,128)(2,1)S(1)}, u32[]{:S(2)}, u32[]{:S(2)}) %collective-permute-start.2) | collective-permute-done | bytes 655392 | tf_op jit(solution)/shard_map/ppermute | solution.py:74
  236.8 1.2 collective-permute-start.3
  238.0 1.7 collective-permute-done.3.partner_ref
  239.7 13.4 %shard_map.56 = (bf16[256,1280]{1,0:T(8,128)(2,1)S(1)}, bf16[256,1280]{1,0:T(8,128)(2,1)S(1)}) custom-call(bf16[256,1280]{1,0:T(8,128)(2,1)S(1)} %collective-permute-done.2.own_ref, bf16[256,1280]{1,0:T(8,128)(2,1)S(1)} %collective-permute-done.3.partner_ref, f32[1,2560]{1,0:T(1,128)S(1)} %copy-done, ...), custom_call_target="tpu_custom_call" | custom-call | tf_op jit(solution)/shard_map/pallas_call | solution.py:48
  253.1 0.5 collective-permute-start.4
  253.6 1.7 collective-permute-done.4
  255.3 0.4 select_select_fusion
  255.7 4.2 %collective-permute-start.5 = (bf16[256,1280]{1,0:T(8,128)(2,1)S(1)}, bf16[256,1280]{1,0:T(8,128)(2,1)S(1)}, u32[]{:S(2)}, u32[]{:S(2)}) collective-permute-start(bf16[256,1280]{1,0:T(8,128)(2,1)S(1)} %get-tuple-element.24), channel_id=1, source_target_pairs={{0,64},{64,128},{128,192},{1,65},{65,129},{129,193},{2,66},{66,130... | collective-permute-start | bytes 1966088 | tf_op jit(solution)/shard_map/ppermute | solution.py:74
  259.9 13.7 %collective-permute-done.5.own_ref = bf16[256,1280]{1,0:T(8,128)(2,1)S(1)} collective-permute-done((bf16[256,1280]{1,0:T(8,128)(2,1)S(1)}, bf16[256,1280]{1,0:T(8,128)(2,1)S(1)}, u32[]{:S(2)}, u32[]{:S(2)}) %collective-permute-start.5) | collective-permute-done | bytes 655392 | tf_op jit(solution)/shard_map/ppermute | solution.py:74
  273.6 1.2 collective-permute-start.6
  274.8 1.7 collective-permute-done.6.partner_ref
  276.5 13.4 %shard_map.57 = (bf16[256,1280]{1,0:T(8,128)(2,1)S(1)}, bf16[256,1280]{1,0:T(8,128)(2,1)S(1)}) custom-call(bf16[256,1280]{1,0:T(8,128)(2,1)S(1)} %collective-permute-done.5.own_ref, bf16[256,1280]{1,0:T(8,128)(2,1)S(1)} %collective-permute-done.6.partner_ref, f32[1,2560]{1,0:T(1,128)S(1)} %copy-done, ...), custom_call_target="tpu_custom_call" | custom-call | tf_op jit(solution)/shard_map/pallas_call | solution.py:48
  289.9 0.5 collective-permute-start.7
  290.4 1.7 collective-permute-done.7
  292.1 0.4 broadcast_select_fusion.1
  292.5 4.2 %collective-permute-start.8 = (bf16[256,1280]{1,0:T(8,128)(2,1)S(1)}, bf16[256,1280]{1,0:T(8,128)(2,1)S(1)}, u32[]{:S(2)}, u32[]{:S(2)}) collective-permute-start(bf16[256,1280]{1,0:T(8,128)(2,1)S(1)} %get-tuple-element.22), channel_id=1, source_target_pairs={{0,64},{64,128},{128,192},{1,65},{65,129},{129,193},{2,66},{66,130... | collective-permute-start | bytes 1966088 | tf_op jit(solution)/shard_map/ppermute | solution.py:74
  296.6 13.7 %collective-permute-done.8.own_ref = bf16[256,1280]{1,0:T(8,128)(2,1)S(1)} collective-permute-done((bf16[256,1280]{1,0:T(8,128)(2,1)S(1)}, bf16[256,1280]{1,0:T(8,128)(2,1)S(1)}, u32[]{:S(2)}, u32[]{:S(2)}) %collective-permute-start.8) | collective-permute-done | bytes 655392 | tf_op jit(solution)/shard_map/ppermute | solution.py:74
  310.3 1.2 collective-permute-start.9
  311.5 1.7 collective-permute-done.9.partner_ref
  313.2 13.4 %shard_map.58 = (bf16[256,1280]{1,0:T(8,128)(2,1)S(1)}, bf16[256,1280]{1,0:T(8,128)(2,1)S(1)}) custom-call(bf16[256,1280]{1,0:T(8,128)(2,1)S(1)} %collective-permute-done.8.own_ref, bf16[256,1280]{1,0:T(8,128)(2,1)S(1)} %collective-permute-done.9.partner_ref, f32[1,2560]{1,0:T(1,128)S(1)} %copy-done, ...), custom_call_target="tpu_custom_call" | custom-call | tf_op jit(solution)/shard_map/pallas_call | solution.py:48
  326.7 0.5 collective-permute-start.10
  327.1 1.7 collective-permute-done.10
  328.9 1.2 fusion
  (1 shorter events, 0.0 us)
Async XLA Ops:
  6.5 2.9 copy-start.1
  6.5 196.8 %all-gather.2.cloned.1.call-start = ((), (), s32[]{:S(2)}) async-start(), calls=%async_computation | async-start | bytes 27033600 | tf_op jit(solution)/shard_map/all_gather | solution.py:82
  8.7 194.7 %copy-start = (f32[1,2560]{1,0:T(1,128)S(1)}, f32[1,2560]{1,0:T(1,128)}, u32[]{:S(2)}) copy-start(f32[1,2560]{1,0:T(1,128)} %gain_ref.7) | copy-start | bytes 30724
  9.5 5.1 %collective-permute-start = (bf16[256,1280]{1,0:T(8,128)(2,1)S(1)}, bf16[256,1280]{1,0:T(8,128)(2,1)S(1)}, u32[]{:S(2)}, u32[]{:S(2)}) collective-permute-start(bf16[256,1280]{1,0:T(8,128)(2,1)S(1)} %broadcast_select_fusion.own_ref), channel_id=1, source_target_pairs={{0,1},{1,0},{2,3},{3,2},{4,5},{5,4},{6,7},{7,6},{8,9},{9,8},{10,11... | collective-permute-start | bytes 1966088 | tf_op jit(solution)/shard_map/ppermute | solution.py:89
  216.8 2.9 collective-permute-start.1
  219.9 16.8 %collective-permute-start.2 = (bf16[256,1280]{1,0:T(8,128)(2,1)S(1)}, bf16[256,1280]{1,0:T(8,128)(2,1)S(1)}, u32[]{:S(2)}, u32[]{:S(2)}) collective-permute-start(bf16[256,1280]{1,0:T(8,128)(2,1)S(1)} %add_convert_fusion.3), channel_id=1, source_target_pairs={{0,64},{64,128},{128,192},{1,65},{65,129},{129,193},{2,66},{66,130... | collective-permute-start | bytes 1966088 | tf_op jit(solution)/shard_map/ppermute | solution.py:74
  236.8 2.9 collective-permute-start.3
  253.1 2.2 collective-permute-start.4
  255.7 17.9 %collective-permute-start.5 = (bf16[256,1280]{1,0:T(8,128)(2,1)S(1)}, bf16[256,1280]{1,0:T(8,128)(2,1)S(1)}, u32[]{:S(2)}, u32[]{:S(2)}) collective-permute-start(bf16[256,1280]{1,0:T(8,128)(2,1)S(1)} %get-tuple-element.24), channel_id=1, source_target_pairs={{0,64},{64,128},{128,192},{1,65},{65,129},{129,193},{2,66},{66,130... | collective-permute-start | bytes 1966088 | tf_op jit(solution)/shard_map/ppermute | solution.py:74
  273.6 2.9 collective-permute-start.6
  289.9 2.2 collective-permute-start.7
  292.5 17.9 %collective-permute-start.8 = (bf16[256,1280]{1,0:T(8,128)(2,1)S(1)}, bf16[256,1280]{1,0:T(8,128)(2,1)S(1)}, u32[]{:S(2)}, u32[]{:S(2)}) collective-permute-start(bf16[256,1280]{1,0:T(8,128)(2,1)S(1)} %get-tuple-element.22), channel_id=1, source_target_pairs={{0,64},{64,128},{128,192},{1,65},{65,129},{129,193},{2,66},{66,130... | collective-permute-start | bytes 1966088 | tf_op jit(solution)/shard_map/ppermute | solution.py:74
  310.3 2.9 collective-permute-start.9
  326.7 2.2 collective-permute-start.10
Sparse Core Ops, SparseCore 0:
  9.9 193.3 all-gather.1

commit v11 on v10

--- a/solution.py
+++ b/solution.py
@@ -70,8 +70,7 @@
 
 def passed_along(value, axis, steps):
     count = lax.axis_size(axis)
-    first, last = (max(0, -steps), min(count, count - steps))
-    return lax.ppermute(value, axis, [(source, source + steps) for source in range(first, last)])
+    return lax.ppermute(value, axis, [(source, (source + steps) % count) for source in range(count)])
 
 
 def per_device(frames, frame_count, norm_gain, weight_in, weight_out):

time: 337 us -> 336 us (level)
  starting transfers between devices: 20.9 us -> 11.1 us
  waiting for transfers between devices: 244 us -> 253 us
    ppermute x3, starting transfers between devices: 11.5 us -> 1.44 us  [passed_along(): lax.ppermute(value, axis, [(source, (source + steps) % count) for source...]
    ppermute x3, waiting for transfers between devices: 41.1 us -> 50.3 us  [passed_along(): lax.ppermute(value, axis, [(source, (source + steps) % count) for source...]
where the time goes in v11:
time: 336 us
  waiting for transfers between devices  253 us (75%)
  Pallas kernels  53.6 us (16%)
  between operations  14.1 us (4%)
  starting transfers between devices  11.1 us (3%)
  other arithmetic  4.47 us (1%)
    all_gather x1, waiting for transfers between devices, per_device(): gathered = lax.all_gather(both, 'dp', axis=1, tiled=True)  189 us
    pallas_call x4, Pallas kernels, ffn(): pl.pallas_call(ffn_body, grid=(hidden_units // TILE,), in_specs=[pl.Block...  53.6 us
    ppermute x3, waiting for transfers between devices, passed_along(): lax.ppermute(value, axis, [(source, (source + steps) % count) for source...  50.3 us
    ppermute x4, starting transfers between devices, apply_layer(): partner = lax.ppermute(current, 'mp', [(0, 1), (1, 0)])  6.93 us
    ppermute x4, waiting for transfers between devices, apply_layer(): other = lax.ppermute(send, 'mp', [(0, 1), (1, 0)])  6.9 us
    ppermute x4, waiting for transfers between devices, apply_layer(): partner = lax.ppermute(current, 'mp', [(0, 1), (1, 0)])  6.9 us
  transfers between devices with their start and end apart: 12, of which 12 were waited for; matrix products, arithmetic and copies ran while one was open for 0% of the time, Pallas kernels for 0%

profile of v11, /device:TPU:1, one launch (start us, length us, event | category | flops | bytes accessed | tf_op | source)
XLA Modules:
  0.0 336.2 jit_solution(9786930383354108822)
XLA Ops:
  6.5 0.0 copy-start.1
  6.5 0.0 all-gather.2.cloned.1.call-start
  6.5 2.2 pad_maximum_fusion
  8.7 0.0 copy-start
  8.7 0.0 all-gather.2.cloned.1.call-update
  9.4 0.0 copy-done.1
  9.4 0.1 broadcast_select_fusion.own_ref
  9.5 3.3 collective-permute-start
  12.8 1.7 collective-permute-done.partner_ref
  14.6 188.8 %all-gather.2.cloned.1.call-done.win_ref.wout_ref = bf16[2,2560,2560]{2,1,0:T(8,128)(2,1)} async-done(((bf16[2,80,2560]{2,1,0:T(8,128)(2,1)}), bf16[2,2560,2560]{2,1,0:T(8,128)(2,1)}) %all-gather.2.cloned.1.call-update) | async-done | bytes 26214416 | tf_op jit(solution)/shard_map/all_gather | solution.py:81
  203.4 0.0 copy-done
  203.4 13.4 %shard_map.55 = (bf16[256,1280]{1,0:T(8,128)(2,1)S(1)}, bf16[256,1280]{1,0:T(8,128)(2,1)S(1)}) custom-call(bf16[256,1280]{1,0:T(8,128)(2,1)S(1)} %broadcast_select_fusion.own_ref, bf16[256,1280]{1,0:T(8,128)(2,1)S(1)} %collective-permute-done.partner_ref, f32[1,2560]{1,0:T(1,128)S(1)} %copy-done, ...), custom_call_target="tpu_custom_call" | custom-call | tf_op jit(solution)/shard_map/pallas_call | solution.py:48
  216.8 1.1 collective-permute-start.1
  217.9 1.7 collective-permute-done.1
  219.6 0.3 add_convert_fusion.3
  219.9 1.3 collective-permute-start.2
  221.2 16.0 %collective-permute-done.2.own_ref = bf16[256,1280]{1,0:T(8,128)(2,1)S(1)} collective-permute-done((bf16[256,1280]{1,0:T(8,128)(2,1)S(1)}, bf16[256,1280]{1,0:T(8,128)(2,1)S(1)}, u32[]{:S(2)}, u32[]{:S(2)}) %collective-permute-start.2) | collective-permute-done | bytes 655392 | tf_op jit(solution)/shard_map/ppermute | solution.py:73
  237.2 1.2 collective-permute-start.3
  238.4 1.7 collective-permute-done.3.partner_ref
  240.1 13.4 %shard_map.56 = (bf16[256,1280]{1,0:T(8,128)(2,1)S(1)}, bf16[256,1280]{1,0:T(8,128)(2,1)S(1)}) custom-call(bf16[256,1280]{1,0:T(8,128)(2,1)S(1)} %collective-permute-done.2.own_ref, bf16[256,1280]{1,0:T(8,128)(2,1)S(1)} %collective-permute-done.3.partner_ref, f32[1,2560]{1,0:T(1,128)S(1)} %copy-done, ...), custom_call_target="tpu_custom_call" | custom-call | tf_op jit(solution)/shard_map/pallas_call | solution.py:48
  253.5 0.5 collective-permute-start.4
  254.0 1.7 collective-permute-done.4
  255.7 0.4 select_select_fusion
  256.1 0.1 collective-permute-start.5
  256.2 17.1 %collective-permute-done.5.own_ref = bf16[256,1280]{1,0:T(8,128)(2,1)S(1)} collective-permute-done((bf16[256,1280]{1,0:T(8,128)(2,1)S(1)}, bf16[256,1280]{1,0:T(8,128)(2,1)S(1)}, u32[]{:S(2)}, u32[]{:S(2)}) %collective-permute-start.5) | collective-permute-done | bytes 655392 | tf_op jit(solution)/shard_map/ppermute | solution.py:73
  273.3 1.2 collective-permute-start.6
  274.5 1.7 collective-permute-done.6.partner_ref
  276.3 13.4 %shard_map.57 = (bf16[256,1280]{1,0:T(8,128)(2,1)S(1)}, bf16[256,1280]{1,0:T(8,128)(2,1)S(1)}) custom-call(bf16[256,1280]{1,0:T(8,128)(2,1)S(1)} %collective-permute-done.5.own_ref, bf16[256,1280]{1,0:T(8,128)(2,1)S(1)} %collective-permute-done.6.partner_ref, f32[1,2560]{1,0:T(1,128)S(1)} %copy-done, ...), custom_call_target="tpu_custom_call" | custom-call | tf_op jit(solution)/shard_map/pallas_call | solution.py:48
  289.7 0.6 collective-permute-start.7
  290.3 1.7 collective-permute-done.7
  292.1 0.4 broadcast_select_fusion.1
  292.4 0.1 collective-permute-start.8
  292.5 17.1 %collective-permute-done.8.own_ref = bf16[256,1280]{1,0:T(8,128)(2,1)S(1)} collective-permute-done((bf16[256,1280]{1,0:T(8,128)(2,1)S(1)}, bf16[256,1280]{1,0:T(8,128)(2,1)S(1)}, u32[]{:S(2)}, u32[]{:S(2)}) %collective-permute-start.8) | collective-permute-done | bytes 655392 | tf_op jit(solution)/shard_map/ppermute | solution.py:73
  309.6 1.2 collective-permute-start.9
  310.8 1.7 collective-permute-done.9.partner_ref
  312.6 13.4 %shard_map.58 = (bf16[256,1280]{1,0:T(8,128)(2,1)S(1)}, bf16[256,1280]{1,0:T(8,128)(2,1)S(1)}) custom-call(bf16[256,1280]{1,0:T(8,128)(2,1)S(1)} %collective-permute-done.8.own_ref, bf16[256,1280]{1,0:T(8,128)(2,1)S(1)} %collective-permute-done.9.partner_ref, f32[1,2560]{1,0:T(1,128)S(1)} %copy-done, ...), custom_call_target="tpu_custom_call" | custom-call | tf_op jit(solution)/shard_map/pallas_call | solution.py:48
  326.0 0.5 collective-permute-start.10
  326.5 1.7 collective-permute-done.10
  328.2 1.2 fusion
  (1 shorter events, 0.0 us)
Async XLA Ops:
  6.5 2.9 copy-start.1
  6.5 196.8 %all-gather.2.cloned.1.call-start = ((), (), s32[]{:S(2)}) async-start(), calls=%async_computation | async-start | bytes 27033600 | tf_op jit(solution)/shard_map/all_gather | solution.py:81
  8.7 194.7 %copy-start = (f32[1,2560]{1,0:T(1,128)S(1)}, f32[1,2560]{1,0:T(1,128)}, u32[]{:S(2)}) copy-start(f32[1,2560]{1,0:T(1,128)} %gain_ref.7) | copy-start | bytes 30724
  9.5 5.1 %collective-permute-start = (bf16[256,1280]{1,0:T(8,128)(2,1)S(1)}, bf16[256,1280]{1,0:T(8,128)(2,1)S(1)}, u32[]{:S(2)}, u32[]{:S(2)}) collective-permute-start(bf16[256,1280]{1,0:T(8,128)(2,1)S(1)} %broadcast_select_fusion.own_ref), channel_id=1, source_target_pairs={{0,1},{1,0},{2,3},{3,2},{4,5},{5,4},{6,7},{7,6},{8,9},{9,8},{10,11... | collective-permute-start | bytes 1966088 | tf_op jit(solution)/shard_map/ppermute | solution.py:88
  216.8 2.9 collective-permute-start.1
  219.9 17.2 %collective-permute-start.2 = (bf16[256,1280]{1,0:T(8,128)(2,1)S(1)}, bf16[256,1280]{1,0:T(8,128)(2,1)S(1)}, u32[]{:S(2)}, u32[]{:S(2)}) collective-permute-start(bf16[256,1280]{1,0:T(8,128)(2,1)S(1)} %add_convert_fusion.3), channel_id=1, source_target_pairs={{0,64},{64,128},{128,192},{192,0},{1,65},{65,129},{129,193},{193,1... | collective-permute-start | bytes 1966088 | tf_op jit(solution)/shard_map/ppermute | solution.py:73
  237.2 2.9 collective-permute-start.3
  253.5 2.2 collective-permute-start.4
  256.1 17.2 %collective-permute-start.5 = (bf16[256,1280]{1,0:T(8,128)(2,1)S(1)}, bf16[256,1280]{1,0:T(8,128)(2,1)S(1)}, u32[]{:S(2)}, u32[]{:S(2)}) collective-permute-start(bf16[256,1280]{1,0:T(8,128)(2,1)S(1)} %get-tuple-element.24), channel_id=1, source_target_pairs={{0,64},{64,128},{128,192},{192,0},{1,65},{65,129},{129,193},{193,1... | collective-permute-start | bytes 1966088 | tf_op jit(solution)/shard_map/ppermute | solution.py:73
  273.3 2.9 collective-permute-start.6
  289.7 2.4 collective-permute-start.7
  292.4 17.2 %collective-permute-start.8 = (bf16[256,1280]{1,0:T(8,128)(2,1)S(1)}, bf16[256,1280]{1,0:T(8,128)(2,1)S(1)}, u32[]{:S(2)}, u32[]{:S(2)}) collective-permute-start(bf16[256,1280]{1,0:T(8,128)(2,1)S(1)} %get-tuple-element.22), channel_id=1, source_target_pairs={{0,64},{64,128},{128,192},{192,0},{1,65},{65,129},{129,193},{193,1... | collective-permute-start | bytes 1966088 | tf_op jit(solution)/shard_map/ppermute | solution.py:73
  309.6 2.9 collective-permute-start.9
  326.0 2.2 collective-permute-start.10
Sparse Core Ops, SparseCore 0:
  9.9 193.3 all-gather.1

commit v12 on v11

--- a/solution.py
+++ b/solution.py
@@ -68,9 +68,21 @@
     )(current, partner, gain, gathered, gathered)
 
 
-def passed_along(value, axis, steps):
+RELAYED = 32
+
+
+def shifted(value, axis, steps):
     count = lax.axis_size(axis)
     return lax.ppermute(value, axis, [(source, (source + steps) % count) for source in range(count)])
+
+
+def passed_along(value, axis):
+    count = lax.axis_size(axis)
+    direct = shifted(value[:-RELAYED], axis, 1)
+    relayed = value[-RELAYED:]
+    for _ in range(count - 1):
+        relayed = shifted(relayed, axis, -1)
+    return jnp.concatenate([direct, relayed], axis=0)
 
 
 def per_device(frames, frame_count, norm_gain, weight_in, weight_out):
@@ -95,7 +107,7 @@
     stored = jnp.where(segment_index == 0, result, jnp.zeros_like(result))
 
     for moment in range(1, segment_count):
-        result = apply_layer(passed_along(result, "section", 1))
+        result = apply_layer(passed_along(result, "section"))
         stored = lax.optimization_barrier(jnp.where(segment_index == moment, result, stored))
     return stored.reshape(1, local_rows, width_local)
 

time: 336 us -> 333 us (level)
  waiting for transfers between devices: 253 us -> 223 us
  starting transfers between devices: 11.1 us -> 37.4 us
    ppermute x3 -> x12, waiting for transfers between devices: 50.3 us -> 20.4 us  [shifted(): lax.ppermute(value, axis, [(source, (source + steps) % count) for source...]
    ppermute x3 -> x12, starting transfers between devices: 1.44 us -> 27.9 us  [shifted(): lax.ppermute(value, axis, [(source, (source + steps) % count) for source...]
  transfers between devices with their start and end apart: 12 -> 21, of which waited for: 12 -> 18; matrix products, arithmetic and copies ran while one was open for 0% -> 0% of each run, Pallas kernels for 0% -> 0%
where the time goes in v12:
time: 333 us
  waiting for transfers between devices  223 us (67%)
  Pallas kernels  53.6 us (16%)
  starting transfers between devices  37.4 us (11%)
  between operations  14.2 us (4%)
  other arithmetic  4.49 us (1%)
    all_gather x1, waiting for transfers between devices, per_device(): gathered = lax.all_gather(both, 'dp', axis=1, tiled=True)  189 us
    pallas_call x4, Pallas kernels, ffn(): pl.pallas_call(ffn_body, grid=(hidden_units // TILE,), in_specs=[pl.Block...  53.6 us
    ppermute x12, starting transfers between devices, shifted(): lax.ppermute(value, axis, [(source, (source + steps) % count) for source...  27.9 us
    ppermute x12, waiting for transfers between devices, shifted(): lax.ppermute(value, axis, [(source, (source + steps) % count) for source...  20.4 us
    ppermute x4, starting transfers between devices, apply_layer(): partner = lax.ppermute(current, 'mp', [(0, 1), (1, 0)])  6.96 us
    ppermute x4, waiting for transfers between devices, apply_layer(): other = lax.ppermute(send, 'mp', [(0, 1), (1, 0)])  6.9 us
    ppermute x4, waiting for transfers between devices, apply_layer(): partner = lax.ppermute(current, 'mp', [(0, 1), (1, 0)])  6.9 us
  transfers between devices with their start and end apart: 21, of which 18 were waited for; matrix products, arithmetic and copies ran while one was open for 0% of the time, Pallas kernels for 0%

profile of v12, /device:TPU:1, one launch (start us, length us, event | category | flops | bytes accessed | tf_op | source)
XLA Modules:
  0.0 333.0 jit_solution(4156458507938040809)
XLA Ops:
  6.5 0.0 copy-start.1
  6.5 0.0 all-gather.2.cloned.1.call-start
  6.5 2.2 pad_maximum_fusion
  8.7 0.0 copy-start
  8.7 0.0 all-gather.2.cloned.1.call-update
  9.4 0.0 copy-done.1
  9.4 0.1 broadcast_select_fusion.own_ref
  9.5 3.3 collective-permute-start
  12.9 1.7 collective-permute-done.partner_ref
  14.6 188.8 %all-gather.2.cloned.1.call-done.win_ref.wout_ref = bf16[2,2560,2560]{2,1,0:T(8,128)(2,1)} async-done(((bf16[2,80,2560]{2,1,0:T(8,128)(2,1)}), bf16[2,2560,2560]{2,1,0:T(8,128)(2,1)}) %all-gather.2.cloned.1.call-update) | async-done | bytes 26214416 | tf_op jit(solution)/shard_map/all_gather | solution.py:93
  203.4 0.0 copy-done
  203.4 13.4 %shard_map.55 = (bf16[256,1280]{1,0:T(8,128)(2,1)S(1)}, bf16[256,1280]{1,0:T(8,128)(2,1)S(1)}) custom-call(bf16[256,1280]{1,0:T(8,128)(2,1)S(1)} %broadcast_select_fusion.own_ref, bf16[256,1280]{1,0:T(8,128)(2,1)S(1)} %collective-permute-done.partner_ref, f32[1,2560]{1,0:T(1,128)S(1)} %copy-done, ...), custom_call_target="tpu_custom_call" | custom-call | tf_op jit(solution)/shard_map/pallas_call | solution.py:48
  216.8 1.1 collective-permute-start.1
  217.9 1.7 collective-permute-done.1
  219.6 0.3 add_convert_fusion.3
  220.0 1.3 collective-permute-start.2
  221.3 1.5 collective-permute-start.3
  222.8 2.1 collective-permute-done.3
  224.9 2.4 collective-permute-start.4
  227.3 1.5 collective-permute-done.4
  228.7 3.0 collective-permute-start.5
  231.8 3.7 %collective-permute-done.2 = bf16[224,1280]{1,0:T(8,128)(2,1)S(1)} collective-permute-done((bf16[224,1280]{1,0:T(8,128)(2,1)S(1)}, bf16[224,1280]{1,0:T(8,128)(2,1)S(1)}, u32[]{:S(2)}, u32[]{:S(2)}) %collective-permute-start.2) | collective-permute-done | bytes 573472 | tf_op jit(solution)/shard_map/ppermute | solution.py:76
  235.5 0.0 collective-permute-done.5
  235.5 1.5 collective-permute-start.6
  237.1 1.7 collective-permute-done.6.partner_ref
  238.8 13.4 %shard_map.56 = (bf16[256,1280]{1,0:T(8,128)(2,1)S(1)}, bf16[256,1280]{1,0:T(8,128)(2,1)S(1)}) custom-call(bf16[256,1280]{1,0:T(8,128)(2,1)S(1)} %constant_dynamic-update-slice_fusion.own_ref, bf16[256,1280]{1,0:T(8,128)(2,1)S(1)} %collective-permute-done.6.partner_ref, f32[1,2560]{1,0:T(1,128)S(1)} %copy-done, ...), custom_call_target="tpu_custom_call" | custom-call | tf_op jit(solution)/shard_map/pallas_call | solution.py:48
  252.2 0.5 collective-permute-start.7
  252.7 1.7 collective-permute-done.7
  254.4 0.4 select_select_fusion
  254.8 0.1 collective-permute-start.8
  254.9 3.4 %collective-permute-start.9 = (bf16[32,1280]{1,0:T(8,128)(2,1)S(1)}, bf16[32,1280]{1,0:T(8,128)(2,1)S(1)}, u32[]{:S(2)}, u32[]{:S(2)}) collective-permute-start(bf16[32,1280]{1,0:T(8,128)(2,1)S(1)} %slice.27), channel_id=1, source_target_pairs={{0,192},{64,0},{128,64},{192,128},{1,193},{65,1},{129,65},{193,129... | collective-permute-start | bytes 245768 | tf_op jit(solution)/shard_map/ppermute | solution.py:76
  258.3 1.5 collective-permute-done.9
  259.8 3.4 %collective-permute-start.10 = (bf16[32,1280]{1,0:T(8,128)(2,1)S(1)}, bf16[32,1280]{1,0:T(8,128)(2,1)S(1)}, u32[]{:S(2)}, u32[]{:S(2)}) collective-permute-start(bf16[32,1280]{1,0:T(8,128)(2,1)S(1)} %collective-permute-done.9), channel_id=1, source_target_pairs={{0,192},{64,0},{128,64},{192,128},{1,193},{65,1},{129,65},{193,129... | collective-permute-start | bytes 245768 | tf_op jit(solution)/shard_map/ppermute | solution.py:76
  263.2 1.5 collective-permute-done.10
  264.7 3.0 collective-permute-start.11
  267.7 3.6 %collective-permute-done.8 = bf16[224,1280]{1,0:T(8,128)(2,1)S(1)} collective-permute-done((bf16[224,1280]{1,0:T(8,128)(2,1)S(1)}, bf16[224,1280]{1,0:T(8,128)(2,1)S(1)}, u32[]{:S(2)}, u32[]{:S(2)}) %collective-permute-start.8) | collective-permute-done | bytes 573472 | tf_op jit(solution)/shard_map/ppermute | solution.py:76
  271.3 0.0 collective-permute-done.11
  271.3 1.1 collective-permute-start.12
  272.4 1.7 collective-permute-done.12.partner_ref
  274.1 13.4 %shard_map.57 = (bf16[256,1280]{1,0:T(8,128)(2,1)S(1)}, bf16[256,1280]{1,0:T(8,128)(2,1)S(1)}) custom-call(bf16[256,1280]{1,0:T(8,128)(2,1)S(1)} %constant_dynamic-update-slice_fusion.2.own_ref, bf16[256,1280]{1,0:T(8,128)(2,1)S(1)} %collective-permute-done.12.partner_ref, f32[1,2560]{1,0:T(1,128)S(1)} %copy-done, ...), custom_call_target="tpu_custom_call" | custom-call | tf_op jit(solution)/shard_map/pallas_call | solution.py:48
  287.6 0.5 collective-permute-start.13
  288.0 1.7 collective-permute-done.13
  289.7 0.4 broadcast_select_fusion.1
  290.1 0.1 collective-permute-start.14
  290.2 3.4 %collective-permute-start.15 = (bf16[32,1280]{1,0:T(8,128)(2,1)S(1)}, bf16[32,1280]{1,0:T(8,128)(2,1)S(1)}, u32[]{:S(2)}, u32[]{:S(2)}) collective-permute-start(bf16[32,1280]{1,0:T(8,128)(2,1)S(1)} %slice.29), channel_id=1, source_target_pairs={{0,192},{64,0},{128,64},{192,128},{1,193},{65,1},{129,65},{193,129... | collective-permute-start | bytes 245768 | tf_op jit(solution)/shard_map/ppermute | solution.py:76
  293.6 1.5 collective-permute-done.15
  295.1 3.4 %collective-permute-start.16 = (bf16[32,1280]{1,0:T(8,128)(2,1)S(1)}, bf16[32,1280]{1,0:T(8,128)(2,1)S(1)}, u32[]{:S(2)}, u32[]{:S(2)}) collective-permute-start(bf16[32,1280]{1,0:T(8,128)(2,1)S(1)} %collective-permute-done.15), channel_id=1, source_target_pairs={{0,192},{64,0},{128,64},{192,128},{1,193},{65,1},{129,65},{193,129... | collective-permute-start | bytes 245768 | tf_op jit(solution)/shard_map/ppermute | solution.py:76
  298.5 1.5 collective-permute-done.16
  300.0 3.0 collective-permute-start.17
  303.0 3.6 %collective-permute-done.14 = bf16[224,1280]{1,0:T(8,128)(2,1)S(1)} collective-permute-done((bf16[224,1280]{1,0:T(8,128)(2,1)S(1)}, bf16[224,1280]{1,0:T(8,128)(2,1)S(1)}, u32[]{:S(2)}, u32[]{:S(2)}) %collective-permute-start.14) | collective-permute-done | bytes 573472 | tf_op jit(solution)/shard_map/ppermute | solution.py:76
  306.6 0.0 collective-permute-done.17
  306.6 1.1 collective-permute-start.18
  307.7 1.7 collective-permute-done.18.partner_ref
  309.4 13.4 %shard_map.58 = (bf16[256,1280]{1,0:T(8,128)(2,1)S(1)}, bf16[256,1280]{1,0:T(8,128)(2,1)S(1)}) custom-call(bf16[256,1280]{1,0:T(8,128)(2,1)S(1)} %constant_dynamic-update-slice_fusion.4.own_ref, bf16[256,1280]{1,0:T(8,128)(2,1)S(1)} %collective-permute-done.18.partner_ref, f32[1,2560]{1,0:T(1,128)S(1)} %copy-done, ...), custom_call_target="tpu_custom_call" | custom-call | tf_op jit(solution)/shard_map/pallas_call | solution.py:48
  322.8 0.5 collective-permute-start.19
  323.3 1.7 collective-permute-done.19
  325.0 1.2 fusion
  (13 shorter events, 0.3 us)
Async XLA Ops:
  6.5 2.9 copy-start.1
  6.5 196.8 %all-gather.2.cloned.1.call-start = ((), (), s32[]{:S(2)}) async-start(), calls=%async_computation | async-start | bytes 27033600 | tf_op jit(solution)/shard_map/all_gather | solution.py:93
  8.7 194.6 %copy-start = (f32[1,2560]{1,0:T(1,128)S(1)}, f32[1,2560]{1,0:T(1,128)}, u32[]{:S(2)}) copy-start(f32[1,2560]{1,0:T(1,128)} %gain_ref.7) | copy-start | bytes 30724
  9.5 5.1 %collective-permute-start = (bf16[256,1280]{1,0:T(8,128)(2,1)S(1)}, bf16[256,1280]{1,0:T(8,128)(2,1)S(1)}, u32[]{:S(2)}, u32[]{:S(2)}) collective-permute-start(bf16[256,1280]{1,0:T(8,128)(2,1)S(1)} %broadcast_select_fusion.own_ref), channel_id=1, source_target_pairs={{0,1},{1,0},{2,3},{3,2},{4,5},{5,4},{6,7},{7,6},{8,9},{9,8},{10,11... | collective-permute-start | bytes 1966088 | tf_op jit(solution)/shard_map/ppermute | solution.py:100
  216.8 2.9 collective-permute-start.1
  220.0 15.5 %collective-permute-start.2 = (bf16[224,1280]{1,0:T(8,128)(2,1)S(1)}, bf16[224,1280]{1,0:T(8,128)(2,1)S(1)}, u32[]{:S(2)}, u32[]{:S(2)}) collective-permute-start(bf16[224,1280]{1,0:T(8,128)(2,1)S(1)} %slice.24), channel_id=1, source_target_pairs={{0,64},{64,128},{128,192},{192,0},{1,65},{65,129},{129,193},{193,1... | collective-permute-start | bytes 1720328 | tf_op jit(solution)/shard_map/ppermute | solution.py:76
  221.3 3.6 %collective-permute-start.3 = (bf16[32,1280]{1,0:T(8,128)(2,1)S(1)}, bf16[32,1280]{1,0:T(8,128)(2,1)S(1)}, u32[]{:S(2)}, u32[]{:S(2)}) collective-permute-start(bf16[32,1280]{1,0:T(8,128)(2,1)S(1)} %slice.25), channel_id=1, source_target_pairs={{0,192},{64,0},{128,64},{192,128},{1,193},{65,1},{129,65},{193,129... | collective-permute-start | bytes 245768 | tf_op jit(solution)/shard_map/ppermute | solution.py:76
  224.9 3.9 %collective-permute-start.4 = (bf16[32,1280]{1,0:T(8,128)(2,1)S(1)}, bf16[32,1280]{1,0:T(8,128)(2,1)S(1)}, u32[]{:S(2)}, u32[]{:S(2)}) collective-permute-start(bf16[32,1280]{1,0:T(8,128)(2,1)S(1)} %collective-permute-done.3), channel_id=1, source_target_pairs={{0,192},{64,0},{128,64},{192,128},{1,193},{65,1},{129,65},{193,129... | collective-permute-start | bytes 245768 | tf_op jit(solution)/shard_map/ppermute | solution.py:76
  228.7 6.8 %collective-permute-start.5 = (bf16[32,1280]{1,0:T(8,128)(2,1)S(1)}, bf16[32,1280]{1,0:T(8,128)(2,1)S(1)}, u32[]{:S(2)}, u32[]{:S(2)}) collective-permute-start(bf16[32,1280]{1,0:T(8,128)(2,1)S(1)} %collective-permute-done.4), channel_id=1, source_target_pairs={{0,192},{64,0},{128,64},{192,128},{1,193},{65,1},{129,65},{193,129... | collective-permute-start | bytes 245768 | tf_op jit(solution)/shard_map/ppermute | solution.py:76
  235.5 3.2 collective-permute-start.6
  252.2 2.2 collective-permute-start.7
  254.8 16.4 %collective-permute-start.8 = (bf16[224,1280]{1,0:T(8,128)(2,1)S(1)}, bf16[224,1280]{1,0:T(8,128)(2,1)S(1)}, u32[]{:S(2)}, u32[]{:S(2)}) collective-permute-start(bf16[224,1280]{1,0:T(8,128)(2,1)S(1)} %slice.26), channel_id=1, source_target_pairs={{0,64},{64,128},{128,192},{192,0},{1,65},{65,129},{129,193},{193,1... | collective-permute-start | bytes 1720328 | tf_op jit(solution)/shard_map/ppermute | solution.py:76
  254.9 4.9 %collective-permute-start.9 = (bf16[32,1280]{1,0:T(8,128)(2,1)S(1)}, bf16[32,1280]{1,0:T(8,128)(2,1)S(1)}, u32[]{:S(2)}, u32[]{:S(2)}) collective-permute-start(bf16[32,1280]{1,0:T(8,128)(2,1)S(1)} %slice.27), channel_id=1, source_target_pairs={{0,192},{64,0},{128,64},{192,128},{1,193},{65,1},{129,65},{193,129... | collective-permute-start | bytes 245768 | tf_op jit(solution)/shard_map/ppermute | solution.py:76
  259.8 4.9 %collective-permute-start.10 = (bf16[32,1280]{1,0:T(8,128)(2,1)S(1)}, bf16[32,1280]{1,0:T(8,128)(2,1)S(1)}, u32[]{:S(2)}, u32[]{:S(2)}) collective-permute-start(bf16[32,1280]{1,0:T(8,128)(2,1)S(1)} %collective-permute-done.9), channel_id=1, source_target_pairs={{0,192},{64,0},{128,64},{192,128},{1,193},{65,1},{129,65},{193,129... | collective-permute-start | bytes 245768 | tf_op jit(solution)/shard_map/ppermute | solution.py:76
  264.7 6.6 %collective-permute-start.11 = (bf16[32,1280]{1,0:T(8,128)(2,1)S(1)}, bf16[32,1280]{1,0:T(8,128)(2,1)S(1)}, u32[]{:S(2)}, u32[]{:S(2)}) collective-permute-start(bf16[32,1280]{1,0:T(8,128)(2,1)S(1)} %collective-permute-done.10), channel_id=1, source_target_pairs={{0,192},{64,0},{128,64},{192,128},{1,193},{65,1},{129,65},{193,129... | collective-permute-start | bytes 245768 | tf_op jit(solution)/shard_map/ppermute | solution.py:76
  271.3 2.8 collective-permute-start.12
  287.6 2.2 collective-permute-start.13
  290.1 16.4 %collective-permute-start.14 = (bf16[224,1280]{1,0:T(8,128)(2,1)S(1)}, bf16[224,1280]{1,0:T(8,128)(2,1)S(1)}, u32[]{:S(2)}, u32[]{:S(2)}) collective-permute-start(bf16[224,1280]{1,0:T(8,128)(2,1)S(1)} %slice.28), channel_id=1, source_target_pairs={{0,64},{64,128},{128,192},{192,0},{1,65},{65,129},{129,193},{193,1... | collective-permute-start | bytes 1720328 | tf_op jit(solution)/shard_map/ppermute | solution.py:76
  290.2 4.9 %collective-permute-start.15 = (bf16[32,1280]{1,0:T(8,128)(2,1)S(1)}, bf16[32,1280]{1,0:T(8,128)(2,1)S(1)}, u32[]{:S(2)}, u32[]{:S(2)}) collective-permute-start(bf16[32,1280]{1,0:T(8,128)(2,1)S(1)} %slice.29), channel_id=1, source_target_pairs={{0,192},{64,0},{128,64},{192,128},{1,193},{65,1},{129,65},{193,129... | collective-permute-start | bytes 245768 | tf_op jit(solution)/shard_map/ppermute | solution.py:76
  295.1 4.9 %collective-permute-start.16 = (bf16[32,1280]{1,0:T(8,128)(2,1)S(1)}, bf16[32,1280]{1,0:T(8,128)(2,1)S(1)}, u32[]{:S(2)}, u32[]{:S(2)}) collective-permute-start(bf16[32,1280]{1,0:T(8,128)(2,1)S(1)} %collective-permute-done.15), channel_id=1, source_target_pairs={{0,192},{64,0},{128,64},{192,128},{1,193},{65,1},{129,65},{193,129... | collective-permute-start | bytes 245768 | tf_op jit(solution)/shard_map/ppermute | solution.py:76
  300.0 6.6 %collective-permute-start.17 = (bf16[32,1280]{1,0:T(8,128)(2,1)S(1)}, bf16[32,1280]{1,0:T(8,128)(2,1)S(1)}, u32[]{:S(2)}, u32[]{:S(2)}) collective-permute-start(bf16[32,1280]{1,0:T(8,128)(2,1)S(1)} %collective-permute-done.16), channel_id=1, source_target_pairs={{0,192},{64,0},{128,64},{192,128},{1,193},{65,1},{129,65},{193,129... | collective-permute-start | bytes 245768 | tf_op jit(solution)/shard_map/ppermute | solution.py:76
  306.6 2.8 collective-permute-start.18
  322.8 2.2 collective-permute-start.19
Sparse Core Ops, SparseCore 0:
  9.9 193.3 all-gather.1

commit v13 on v12

--- a/solution.py
+++ b/solution.py
@@ -89,7 +89,11 @@
     segment_count = lax.axis_size("section")
     segment_index = lax.axis_index("section")
     half_index = lax.axis_index("mp")
-    both = jnp.stack([weight_in[0], weight_out[0].T])
+    eye = jnp.eye(weight_out.shape[2], dtype=weight_out.dtype)
+    out_t = lax.dot_general(
+        eye, weight_out[0], (((1,), (1,)), ((), ())), preferred_element_type=jnp.float32
+    ).astype(weight_out.dtype)
+    both = jnp.stack([weight_in[0], out_t])
     gathered = lax.all_gather(both, "dp", axis=1, tiled=True)
     local_rows, width_local = frames.shape
     live_count = frame_count[0]

time: 333 us -> 339 us (1.018)
  other arithmetic: 4.49 us -> 9.39 us
    select_n x3, other arithmetic: 1.9 us -> 6.92 us  [per_device(): jnp.where(segment_index == moment, result, stored)]
where the time goes in v13:
time: 339 us
  waiting for transfers between devices  222 us (65%)
  Pallas kernels  53.7 us (16%)
  starting transfers between devices  37.9 us (11%)
  between operations  14.3 us (4%)
  other arithmetic  9.39 us (3%)
    all_gather x1, waiting for transfers between devices, per_device(): gathered = lax.all_gather(both, 'dp', axis=1, tiled=True)  188 us
    pallas_call x4, Pallas kernels, ffn(): pl.pallas_call(ffn_body, grid=(hidden_units // TILE,), in_specs=[pl.Block...  53.7 us
    ppermute x12, starting transfers between devices, shifted(): lax.ppermute(value, axis, [(source, (source + steps) % count) for source...  28.1 us
    ppermute x12, waiting for transfers between devices, shifted(): lax.ppermute(value, axis, [(source, (source + steps) % count) for source...  20.2 us
    ppermute x4, starting transfers between devices, apply_layer(): partner = lax.ppermute(current, 'mp', [(0, 1), (1, 0)])  7.3 us
    ppermute x4, waiting for transfers between devices, apply_layer(): other = lax.ppermute(send, 'mp', [(0, 1), (1, 0)])  7.3 us
    select_n x3, other arithmetic, per_device(): jnp.where(segment_index == moment, result, stored)  6.92 us
    ppermute x4, waiting for transfers between devices, apply_layer(): partner = lax.ppermute(current, 'mp', [(0, 1), (1, 0)])  6.9 us
  transfers between devices with their start and end apart: 21, of which 18 were waited for; matrix products, arithmetic and copies ran while one was open for 0% of the time, Pallas kernels for 0%

profile of v13, /device:TPU:1, one launch (start us, length us, event | category | flops | bytes accessed | tf_op | source)
XLA Modules:
  0.0 338.9 jit_solution(3434794524548126954)
XLA Ops:
  6.5 0.0 copy-start
  6.5 0.0 all-gather.2.cloned.1.call-start
  6.5 1.0 copy-done
  7.5 0.2 fusion
  7.8 0.0 copy-start.2
  7.8 2.0 pad_maximum_fusion
  9.8 0.0 copy-start.1
  9.9 0.0 all-gather.2.cloned.1.call-update
  10.5 0.0 copy-done.2
  10.5 0.1 broadcast_select_fusion.own_ref
  10.7 3.3 collective-permute-start
  14.0 1.7 collective-permute-done.partner_ref
  15.7 187.7 %all-gather.2.cloned.1.call-done.win_ref.wout_ref = bf16[2,2560,2560]{2,1,0:T(8,128)(2,1)} async-done(((bf16[2,80,2560]{2,1,0:T(8,128)(2,1)}), bf16[2,2560,2560]{2,1,0:T(8,128)(2,1)}) %all-gather.2.cloned.1.call-update) | async-done | bytes 26214416 | tf_op jit(solution)/shard_map/all_gather | solution.py:97
  203.4 0.0 copy-done.1
  203.4 13.4 %shard_map.55 = (bf16[256,1280]{1,0:T(8,128)(2,1)S(1)}, bf16[256,1280]{1,0:T(8,128)(2,1)S(1)}) custom-call(bf16[256,1280]{1,0:T(8,128)(2,1)S(1)} %broadcast_select_fusion.own_ref, bf16[256,1280]{1,0:T(8,128)(2,1)S(1)} %collective-permute-done.partner_ref, f32[1,2560]{1,0:T(1,128)S(1)} %copy-done.1, ...), custom_call_target="tpu_custom_call" | custom-call | tf_op jit(solution)/shard_map/pallas_call | solution.py:48
  216.8 1.1 collective-permute-start.1
  218.0 1.7 collective-permute-done.1
  219.7 0.3 add_convert_fusion.3
  220.0 1.3 collective-permute-start.2
  221.3 1.5 collective-permute-start.3
  222.8 2.1 collective-permute-done.3
  224.9 2.4 collective-permute-start.4
  227.3 1.5 collective-permute-done.4
  228.8 3.0 collective-permute-start.5
  231.8 3.7 %collective-permute-done.2 = bf16[224,1280]{1,0:T(8,128)(2,1)S(1)} collective-permute-done((bf16[224,1280]{1,0:T(8,128)(2,1)S(1)}, bf16[224,1280]{1,0:T(8,128)(2,1)S(1)}, u32[]{:S(2)}, u32[]{:S(2)}) %collective-permute-start.2) | collective-permute-done | bytes 573472 | tf_op jit(solution)/shard_map/ppermute | solution.py:76
  235.6 0.0 collective-permute-done.5
  235.6 1.5 collective-permute-start.6
  237.1 1.7 collective-permute-done.6.partner_ref
  238.8 13.4 %shard_map.56 = (bf16[256,1280]{1,0:T(8,128)(2,1)S(1)}, bf16[256,1280]{1,0:T(8,128)(2,1)S(1)}) custom-call(bf16[256,1280]{1,0:T(8,128)(2,1)S(1)} %constant_dynamic-update-slice_fusion.own_ref, bf16[256,1280]{1,0:T(8,128)(2,1)S(1)} %collective-permute-done.6.partner_ref, f32[1,2560]{1,0:T(1,128)S(1)} %copy-done.1, ...), custom_call_target="tpu_custom_call" | custom-call | tf_op jit(solution)/shard_map/pallas_call | solution.py:48
  252.3 0.5 collective-permute-start.7
  252.7 1.9 collective-permute-done.7
  254.6 2.3 select_select_fusion
  257.0 0.1 collective-permute-start.8
  257.1 3.6 %collective-permute-start.9 = (bf16[32,1280]{1,0:T(8,128)(2,1)S(1)}, bf16[32,1280]{1,0:T(8,128)(2,1)S(1)}, u32[]{:S(2)}, u32[]{:S(2)}) collective-permute-start(bf16[32,1280]{1,0:T(8,128)(2,1)S(1)} %slice.27), channel_id=1, source_target_pairs={{0,192},{64,0},{128,64},{192,128},{1,193},{65,1},{129,65},{193,129... | collective-permute-start | bytes 245768 | tf_op jit(solution)/shard_map/ppermute | solution.py:76
  260.6 1.5 collective-permute-done.9
  262.1 3.4 collective-permute-start.10
  265.5 1.5 collective-permute-done.10
  267.0 3.0 collective-permute-start.11
  270.0 3.4 %collective-permute-done.8 = bf16[224,1280]{1,0:T(8,128)(2,1)S(1)} collective-permute-done((bf16[224,1280]{1,0:T(8,128)(2,1)S(1)}, bf16[224,1280]{1,0:T(8,128)(2,1)S(1)}, u32[]{:S(2)}, u32[]{:S(2)}) %collective-permute-start.8) | collective-permute-done | bytes 573472 | tf_op jit(solution)/shard_map/ppermute | solution.py:76
  273.4 0.0 collective-permute-done.11
  273.5 0.0 copy-start.3
  273.5 1.3 collective-permute-start.12
  274.8 1.7 collective-permute-done.12.partner_ref
  276.5 13.4 %shard_map.57 = (bf16[256,1280]{1,0:T(8,128)(2,1)S(1)}, bf16[256,1280]{1,0:T(8,128)(2,1)S(1)}) custom-call(bf16[256,1280]{1,0:T(8,128)(2,1)S(1)} %constant_dynamic-update-slice_fusion.2.own_ref, bf16[256,1280]{1,0:T(8,128)(2,1)S(1)} %collective-permute-done.12.partner_ref, f32[1,2560]{1,0:T(1,128)S(1)} %copy-done.1, ...), custom_call_target="tpu_custom_call" | custom-call | tf_op jit(solution)/shard_map/pallas_call | solution.py:48
  290.0 0.5 collective-permute-start.13
  290.4 1.9 collective-permute-done.13
  292.3 0.0 copy-done.3
  292.3 2.3 broadcast_select_fusion.1
  294.6 0.1 collective-permute-start.14
  294.7 3.4 %collective-permute-start.15 = (bf16[32,1280]{1,0:T(8,128)(2,1)S(1)}, bf16[32,1280]{1,0:T(8,128)(2,1)S(1)}, u32[]{:S(2)}, u32[]{:S(2)}) collective-permute-start(bf16[32,1280]{1,0:T(8,128)(2,1)S(1)} %slice.29), channel_id=1, source_target_pairs={{0,192},{64,0},{128,64},{192,128},{1,193},{65,1},{129,65},{193,129... | collective-permute-start | bytes 245768 | tf_op jit(solution)/shard_map/ppermute | solution.py:76
  298.1 1.5 collective-permute-done.15
  299.6 3.4 collective-permute-start.16
  303.0 1.5 collective-permute-done.16
  304.5 3.0 collective-permute-start.17
  307.5 3.6 %collective-permute-done.14 = bf16[224,1280]{1,0:T(8,128)(2,1)S(1)} collective-permute-done((bf16[224,1280]{1,0:T(8,128)(2,1)S(1)}, bf16[224,1280]{1,0:T(8,128)(2,1)S(1)}, u32[]{:S(2)}, u32[]{:S(2)}) %collective-permute-start.14) | collective-permute-done | bytes 573472 | tf_op jit(solution)/shard_map/ppermute | solution.py:76
  311.1 0.0 collective-permute-done.17
  311.1 0.0 copy-start.4
  311.1 1.1 collective-permute-start.18
  312.3 1.7 collective-permute-done.18.partner_ref
  314.0 13.4 %shard_map.58 = (bf16[256,1280]{1,0:T(8,128)(2,1)S(1)}, bf16[256,1280]{1,0:T(8,128)(2,1)S(1)}) custom-call(bf16[256,1280]{1,0:T(8,128)(2,1)S(1)} %constant_dynamic-update-slice_fusion.4.own_ref, bf16[256,1280]{1,0:T(8,128)(2,1)S(1)} %collective-permute-done.18.partner_ref, f32[1,2560]{1,0:T(1,128)S(1)} %copy-done.1, ...), custom_call_target="tpu_custom_call" | custom-call | tf_op jit(solution)/shard_map/pallas_call | solution.py:48
  327.4 0.5 collective-permute-start.19
  327.9 1.9 collective-permute-done.19
  329.7 0.0 copy-done.4
  329.8 2.3 fusion.1
  (13 shorter events, 0.3 us)
Async XLA Ops:
  6.5 1.0 copy-start
  6.5 196.9 %all-gather.2.cloned.1.call-start = ((), (), s32[]{:S(2)}) async-start(), calls=%async_computation | async-start | bytes 27033600 | tf_op jit(solution)/shard_map/all_gather | solution.py:97
  7.8 2.7 copy-start.2
  9.8 193.6 %copy-start.1 = (f32[1,2560]{1,0:T(1,128)S(1)}, f32[1,2560]{1,0:T(1,128)}, u32[]{:S(2)}) copy-start(f32[1,2560]{1,0:T(1,128)} %gain_ref.7) | copy-start | bytes 30724
  10.7 5.1 %collective-permute-start = (bf16[256,1280]{1,0:T(8,128)(2,1)S(1)}, bf16[256,1280]{1,0:T(8,128)(2,1)S(1)}, u32[]{:S(2)}, u32[]{:S(2)}) collective-permute-start(bf16[256,1280]{1,0:T(8,128)(2,1)S(1)} %broadcast_select_fusion.own_ref), channel_id=1, source_target_pairs={{0,1},{1,0},{2,3},{3,2},{4,5},{5,4},{6,7},{7,6},{8,9},{9,8},{10,11... | collective-permute-start | bytes 1966088 | tf_op jit(solution)/shard_map/ppermute | solution.py:104
  216.8 2.9 collective-permute-start.1
  220.0 15.5 %collective-permute-start.2 = (bf16[224,1280]{1,0:T(8,128)(2,1)S(1)}, bf16[224,1280]{1,0:T(8,128)(2,1)S(1)}, u32[]{:S(2)}, u32[]{:S(2)}) collective-permute-start(bf16[224,1280]{1,0:T(8,128)(2,1)S(1)} %slice.24), channel_id=1, source_target_pairs={{0,64},{64,128},{128,192},{192,0},{1,65},{65,129},{129,193},{193,1... | collective-permute-start | bytes 1720328 | tf_op jit(solution)/shard_map/ppermute | solution.py:76
  221.3 3.6 %collective-permute-start.3 = (bf16[32,1280]{1,0:T(8,128)(2,1)S(1)}, bf16[32,1280]{1,0:T(8,128)(2,1)S(1)}, u32[]{:S(2)}, u32[]{:S(2)}) collective-permute-start(bf16[32,1280]{1,0:T(8,128)(2,1)S(1)} %slice.25), channel_id=1, source_target_pairs={{0,192},{64,0},{128,64},{192,128},{1,193},{65,1},{129,65},{193,129... | collective-permute-start | bytes 245768 | tf_op jit(solution)/shard_map/ppermute | solution.py:76
  224.9 3.9 %collective-permute-start.4 = (bf16[32,1280]{1,0:T(8,128)(2,1)S(1)}, bf16[32,1280]{1,0:T(8,128)(2,1)S(1)}, u32[]{:S(2)}, u32[]{:S(2)}) collective-permute-start(bf16[32,1280]{1,0:T(8,128)(2,1)S(1)} %collective-permute-done.3), channel_id=1, source_target_pairs={{0,192},{64,0},{128,64},{192,128},{1,193},{65,1},{129,65},{193,129... | collective-permute-start | bytes 245768 | tf_op jit(solution)/shard_map/ppermute | solution.py:76
  228.8 6.8 %collective-permute-start.5 = (bf16[32,1280]{1,0:T(8,128)(2,1)S(1)}, bf16[32,1280]{1,0:T(8,128)(2,1)S(1)}, u32[]{:S(2)}, u32[]{:S(2)}) collective-permute-start(bf16[32,1280]{1,0:T(8,128)(2,1)S(1)} %collective-permute-done.4), channel_id=1, source_target_pairs={{0,192},{64,0},{128,64},{192,128},{1,193},{65,1},{129,65},{193,129... | collective-permute-start | bytes 245768 | tf_op jit(solution)/shard_map/ppermute | solution.py:76
  235.6 3.2 collective-permute-start.6
  252.3 2.3 collective-permute-start.7
  257.0 16.4 %collective-permute-start.8 = (bf16[224,1280]{1,0:T(8,128)(2,1)S(1)}, bf16[224,1280]{1,0:T(8,128)(2,1)S(1)}, u32[]{:S(2)}, u32[]{:S(2)}) collective-permute-start(bf16[224,1280]{1,0:T(8,128)(2,1)S(1)} %slice.26), channel_id=1, source_target_pairs={{0,64},{64,128},{128,192},{192,0},{1,65},{65,129},{129,193},{193,1... | collective-permute-start | bytes 1720328 | tf_op jit(solution)/shard_map/ppermute | solution.py:76
  257.1 5.1 %collective-permute-start.9 = (bf16[32,1280]{1,0:T(8,128)(2,1)S(1)}, bf16[32,1280]{1,0:T(8,128)(2,1)S(1)}, u32[]{:S(2)}, u32[]{:S(2)}) collective-permute-start(bf16[32,1280]{1,0:T(8,128)(2,1)S(1)} %slice.27), channel_id=1, source_target_pairs={{0,192},{64,0},{128,64},{192,128},{1,193},{65,1},{129,65},{193,129... | collective-permute-start | bytes 245768 | tf_op jit(solution)/shard_map/ppermute | solution.py:76
  262.1 4.9 %collective-permute-start.10 = (bf16[32,1280]{1,0:T(8,128)(2,1)S(1)}, bf16[32,1280]{1,0:T(8,128)(2,1)S(1)}, u32[]{:S(2)}, u32[]{:S(2)}) collective-permute-start(bf16[32,1280]{1,0:T(8,128)(2,1)S(1)} %collective-permute-done.9), channel_id=1, source_target_pairs={{0,192},{64,0},{128,64},{192,128},{1,193},{65,1},{129,65},{193,129... | collective-permute-start | bytes 245768 | tf_op jit(solution)/shard_map/ppermute | solution.py:76
  267.0 6.5 %collective-permute-start.11 = (bf16[32,1280]{1,0:T(8,128)(2,1)S(1)}, bf16[32,1280]{1,0:T(8,128)(2,1)S(1)}, u32[]{:S(2)}, u32[]{:S(2)}) collective-permute-start(bf16[32,1280]{1,0:T(8,128)(2,1)S(1)} %collective-permute-done.10), channel_id=1, source_target_pairs={{0,192},{64,0},{128,64},{192,128},{1,193},{65,1},{129,65},{193,129... | collective-permute-start | bytes 245768 | tf_op jit(solution)/shard_map/ppermute | solution.py:76
  273.5 18.8 %copy-start.3 = (bf16[256,1280]{1,0:T(8,128)(2,1)S(1)}, bf16[256,1280]{1,0:T(8,128)(2,1)}, u32[]{:S(2)}) copy-start(bf16[256,1280]{1,0:T(8,128)(2,1)} %get-tuple-element.23) | copy-start | bytes 1966084
  273.5 3.0 collective-permute-start.12
  290.0 2.3 collective-permute-start.13
  294.6 16.4 %collective-permute-start.14 = (bf16[224,1280]{1,0:T(8,128)(2,1)S(1)}, bf16[224,1280]{1,0:T(8,128)(2,1)S(1)}, u32[]{:S(2)}, u32[]{:S(2)}) collective-permute-start(bf16[224,1280]{1,0:T(8,128)(2,1)S(1)} %slice.28), channel_id=1, source_target_pairs={{0,64},{64,128},{128,192},{192,0},{1,65},{65,129},{129,193},{193,1... | collective-permute-start | bytes 1720328 | tf_op jit(solution)/shard_map/ppermute | solution.py:76
  294.7 4.9 %collective-permute-start.15 = (bf16[32,1280]{1,0:T(8,128)(2,1)S(1)}, bf16[32,1280]{1,0:T(8,128)(2,1)S(1)}, u32[]{:S(2)}, u32[]{:S(2)}) collective-permute-start(bf16[32,1280]{1,0:T(8,128)(2,1)S(1)} %slice.29), channel_id=1, source_target_pairs={{0,192},{64,0},{128,64},{192,128},{1,193},{65,1},{129,65},{193,129... | collective-permute-start | bytes 245768 | tf_op jit(solution)/shard_map/ppermute | solution.py:76
  299.6 4.9 %collective-permute-start.16 = (bf16[32,1280]{1,0:T(8,128)(2,1)S(1)}, bf16[32,1280]{1,0:T(8,128)(2,1)S(1)}, u32[]{:S(2)}, u32[]{:S(2)}) collective-permute-start(bf16[32,1280]{1,0:T(8,128)(2,1)S(1)} %collective-permute-done.15), channel_id=1, source_target_pairs={{0,192},{64,0},{128,64},{192,128},{1,193},{65,1},{129,65},{193,129... | collective-permute-start | bytes 245768 | tf_op jit(solution)/shard_map/ppermute | solution.py:76
  304.5 6.6 %collective-permute-start.17 = (bf16[32,1280]{1,0:T(8,128)(2,1)S(1)}, bf16[32,1280]{1,0:T(8,128)(2,1)S(1)}, u32[]{:S(2)}, u32[]{:S(2)}) collective-permute-start(bf16[32,1280]{1,0:T(8,128)(2,1)S(1)} %collective-permute-done.16), channel_id=1, source_target_pairs={{0,192},{64,0},{128,64},{192,128},{1,193},{65,1},{129,65},{193,129... | collective-permute-start | bytes 245768 | tf_op jit(solution)/shard_map/ppermute | solution.py:76
  311.1 18.6 %copy-start.4 = (bf16[256,1280]{1,0:T(8,128)(2,1)S(1)}, bf16[256,1280]{1,0:T(8,128)(2,1)}, u32[]{:S(2)}) copy-start(bf16[256,1280]{1,0:T(8,128)(2,1)} %get-tuple-element.21) | copy-start | bytes 1966084
  311.1 2.9 collective-permute-start.18
  327.4 2.3 collective-permute-start.19
Sparse Core Ops, SparseCore 0:
  10.0 193.3 all-gather.1

commit v14 on v12

--- a/solution.py
+++ b/solution.py
@@ -29,10 +29,13 @@
         )
         acc_ref[...] = jnp.zeros_like(acc_ref)
 
-    pre = jnp.dot(normed_ref[...], win_ref[0], preferred_element_type=jnp.float32)
+    blocks, _, piece, tile = win_ref.shape
+    w_in = win_ref[:, 0].reshape(blocks * piece, tile)
+    w_out = wout_ref[:, 0].reshape(blocks * piece, tile)
+    pre = jnp.dot(normed_ref[...], w_in, preferred_element_type=jnp.float32)
     hidden = (0.5 * pre * (1.0 + lax.erf(pre * 0.7071067811865476))).astype(jnp.bfloat16)
     acc_ref[...] += lax.dot_general(
-        hidden, wout_ref[0], (((1,), (1,)), ((), ())), preferred_element_type=jnp.float32
+        hidden, w_out, (((1,), (1,)), ((), ())), preferred_element_type=jnp.float32
     )
 
     @pl.when(step == pl.num_programs(0) - 1)
@@ -44,7 +47,7 @@
 def ffn(current, partner, gain, gathered):
     rows, half = current.shape
     width = 2 * half
-    hidden_units = gathered.shape[2]
+    blocks, _, piece, hidden_units = gathered.shape
     return pl.pallas_call(
         ffn_body,
         grid=(hidden_units // TILE,),
@@ -52,8 +55,8 @@
             pl.BlockSpec((rows, half), lambda j: (0, 0)),
             pl.BlockSpec((rows, half), lambda j: (0, 0)),
             pl.BlockSpec((1, width), lambda j: (0, 0)),
-            pl.BlockSpec((1, width, TILE), lambda j: (0, 0, j)),
-            pl.BlockSpec((1, width, TILE), lambda j: (1, 0, j)),
+            pl.BlockSpec((blocks, 1, piece, TILE), lambda j: (0, 0, 0, j)),
+            pl.BlockSpec((blocks, 1, piece, TILE), lambda j: (0, 1, 0, j)),
         ],
         out_specs=[
             pl.BlockSpec((rows, half), lambda j: (0, 0)),
@@ -89,8 +92,10 @@
     segment_count = lax.axis_size("section")
     segment_index = lax.axis_index("section")
     half_index = lax.axis_index("mp")
-    both = jnp.stack([weight_in[0], weight_out[0].T])
-    gathered = lax.all_gather(both, "dp", axis=1, tiled=True)
+    piece = weight_in.shape[1]
+    both = jnp.concatenate([weight_in[0], weight_out[0].T], axis=0)
+    gathered = lax.all_gather(both, "dp", axis=0, tiled=True)
+    gathered = gathered.reshape(-1, 2, piece, gathered.shape[1])
     local_rows, width_local = frames.shape
     live_count = frame_count[0]
     row_ids = jnp.arange(local_rows, dtype=jnp.int32)

time: 333 us -> 334 us (level)
  no operation moved by 1% of the time
where the time goes in v14:
time: 334 us
  waiting for transfers between devices  223 us (67%)
  Pallas kernels  54.1 us (16%)
  starting transfers between devices  37.4 us (11%)
  between operations  14.2 us (4%)
  other arithmetic  4.47 us (1%)
    all_gather x1, waiting for transfers between devices, per_device(): gathered = lax.all_gather(both, 'dp', axis=0, tiled=True)  189 us
    pallas_call x4, Pallas kernels, ffn(): pl.pallas_call(ffn_body, grid=(hidden_units // TILE,), in_specs=[pl.Block...  54.1 us
    ppermute x12, starting transfers between devices, shifted(): lax.ppermute(value, axis, [(source, (source + steps) % count) for source...  27.9 us
    ppermute x12, waiting for transfers between devices, shifted(): lax.ppermute(value, axis, [(source, (source + steps) % count) for source...  20.4 us
    ppermute x4, starting transfers between devices, apply_layer(): partner = lax.ppermute(current, 'mp', [(0, 1), (1, 0)])  6.96 us
    ppermute x4, waiting for transfers between devices, apply_layer(): partner = lax.ppermute(current, 'mp', [(0, 1), (1, 0)])  6.9 us
    ppermute x4, waiting for transfers between devices, apply_layer(): other = lax.ppermute(send, 'mp', [(0, 1), (1, 0)])  6.9 us
  transfers between devices with their start and end apart: 21, of which 18 were waited for; matrix products, arithmetic and copies ran while one was open for 0% of the time, Pallas kernels for 0%

profile of v14, /device:TPU:1, one launch (start us, length us, event | category | flops | bytes accessed | tf_op | source)
XLA Modules:
  0.0 333.5 jit_solution(9664290069884219660)
XLA Ops:
  6.5 0.0 copy-start.1
  6.5 0.0 all-gather.2.cloned.1.call-start
  6.5 2.2 pad_maximum_fusion
  8.7 0.0 copy-start
  8.7 0.0 all-gather.2.cloned.1.call-update
  9.4 0.0 copy-done.1
  9.4 0.1 broadcast_select_fusion.own_ref
  9.5 3.3 collective-permute-start
  12.8 1.7 collective-permute-done.partner_ref
  14.6 188.8 %all-gather.2.cloned.1.call-done = bf16[5120,2560]{1,0:T(8,128)(2,1)} async-done(((bf16[160,2560]{1,0:T(8,128)(2,1)}), bf16[5120,2560]{1,0:T(8,128)(2,1)}) %all-gather.2.cloned.1.call-update) | async-done | bytes 26214416 | tf_op jit(solution)/shard_map/all_gather | solution.py:97
  203.3 0.0 copy-done
  203.4 13.5 %shard_map.55 = (bf16[256,1280]{1,0:T(8,128)(2,1)S(1)}, bf16[256,1280]{1,0:T(8,128)(2,1)S(1)}) custom-call(bf16[256,1280]{1,0:T(8,128)(2,1)S(1)} %broadcast_select_fusion.own_ref, bf16[256,1280]{1,0:T(8,128)(2,1)S(1)} %collective-permute-done.partner_ref, f32[1,2560]{1,0:T(1,128)S(1)} %copy-done, bf16[32,2,80,2560]{3,2,1,0:T(8,128)(2,1)} %bitcast.8, ...), custom_call_target="tpu_custom_call" | custom-call | tf_op jit(solution)/shard_map/pallas_call | solution.py:51
  216.9 1.1 collective-permute-start.1
  218.0 1.7 collective-permute-done.1
  219.7 0.3 add_convert_fusion.3
  220.1 1.3 collective-permute-start.2
  221.4 1.5 collective-permute-start.3
  222.8 2.1 collective-permute-done.3
  225.0 2.4 collective-permute-start.4
  227.4 1.5 collective-permute-done.4
  228.8 3.0 collective-permute-start.5
  231.9 3.7 %collective-permute-done.2 = bf16[224,1280]{1,0:T(8,128)(2,1)S(1)} collective-permute-done((bf16[224,1280]{1,0:T(8,128)(2,1)S(1)}, bf16[224,1280]{1,0:T(8,128)(2,1)S(1)}, u32[]{:S(2)}, u32[]{:S(2)}) %collective-permute-start.2) | collective-permute-done | bytes 573472 | tf_op jit(solution)/shard_map/ppermute | solution.py:79
  235.6 0.0 collective-permute-done.5
  235.6 1.5 collective-permute-start.6
  237.2 1.7 collective-permute-done.6.partner_ref
  238.9 13.5 %shard_map.56 = (bf16[256,1280]{1,0:T(8,128)(2,1)S(1)}, bf16[256,1280]{1,0:T(8,128)(2,1)S(1)}) custom-call(bf16[256,1280]{1,0:T(8,128)(2,1)S(1)} %constant_dynamic-update-slice_fusion.own_ref, bf16[256,1280]{1,0:T(8,128)(2,1)S(1)} %collective-permute-done.6.partner_ref, f32[1,2560]{1,0:T(1,128)S(1)} %copy-done, bf16[32,2,80,2560]{3,2,1,0:T(8,128)(2,1)} %bitcast.10, ...), custom_call_target="tpu_custom_call" | custom-call | tf_op jit(solution)/shard_map/pallas_call | solution.py:51
  252.4 0.5 collective-permute-start.7
  252.9 1.7 collective-permute-done.7
  254.6 0.4 select_select_fusion
  255.0 0.1 collective-permute-start.8
  255.1 3.4 %collective-permute-start.9 = (bf16[32,1280]{1,0:T(8,128)(2,1)S(1)}, bf16[32,1280]{1,0:T(8,128)(2,1)S(1)}, u32[]{:S(2)}, u32[]{:S(2)}) collective-permute-start(bf16[32,1280]{1,0:T(8,128)(2,1)S(1)} %slice.27), channel_id=1, source_target_pairs={{0,192},{64,0},{128,64},{192,128},{1,193},{65,1},{129,65},{193,129... | collective-permute-start | bytes 245768 | tf_op jit(solution)/shard_map/ppermute | solution.py:79
  258.6 1.5 collective-permute-done.9
  260.0 3.4 %collective-permute-start.10 = (bf16[32,1280]{1,0:T(8,128)(2,1)S(1)}, bf16[32,1280]{1,0:T(8,128)(2,1)S(1)}, u32[]{:S(2)}, u32[]{:S(2)}) collective-permute-start(bf16[32,1280]{1,0:T(8,128)(2,1)S(1)} %collective-permute-done.9), channel_id=1, source_target_pairs={{0,192},{64,0},{128,64},{192,128},{1,193},{65,1},{129,65},{193,129... | collective-permute-start | bytes 245768 | tf_op jit(solution)/shard_map/ppermute | solution.py:79
  263.4 1.5 collective-permute-done.10
  264.9 3.0 collective-permute-start.11
  267.9 3.6 %collective-permute-done.8 = bf16[224,1280]{1,0:T(8,128)(2,1)S(1)} collective-permute-done((bf16[224,1280]{1,0:T(8,128)(2,1)S(1)}, bf16[224,1280]{1,0:T(8,128)(2,1)S(1)}, u32[]{:S(2)}, u32[]{:S(2)}) %collective-permute-start.8) | collective-permute-done | bytes 573472 | tf_op jit(solution)/shard_map/ppermute | solution.py:79
  271.5 0.0 collective-permute-done.11
  271.6 1.1 collective-permute-start.12
  272.6 1.7 collective-permute-done.12.partner_ref
  274.3 13.5 %shard_map.57 = (bf16[256,1280]{1,0:T(8,128)(2,1)S(1)}, bf16[256,1280]{1,0:T(8,128)(2,1)S(1)}) custom-call(bf16[256,1280]{1,0:T(8,128)(2,1)S(1)} %constant_dynamic-update-slice_fusion.2.own_ref, bf16[256,1280]{1,0:T(8,128)(2,1)S(1)} %collective-permute-done.12.partner_ref, f32[1,2560]{1,0:T(1,128)S(1)} %copy-done, bf16[32,2,80,2560]{3,2,1,0:T(8,128)(2,1)} %bitcast.12, ...), custom_call_target="tpu_custom_call" | custom-call | tf_op jit(solution)/shard_map/pallas_call | solution.py:51
  287.9 0.5 collective-permute-start.13
  288.4 1.7 collective-permute-done.13
  290.1 0.4 broadcast_select_fusion.1
  290.5 0.1 collective-permute-start.14
  290.6 3.4 %collective-permute-start.15 = (bf16[32,1280]{1,0:T(8,128)(2,1)S(1)}, bf16[32,1280]{1,0:T(8,128)(2,1)S(1)}, u32[]{:S(2)}, u32[]{:S(2)}) collective-permute-start(bf16[32,1280]{1,0:T(8,128)(2,1)S(1)} %slice.29), channel_id=1, source_target_pairs={{0,192},{64,0},{128,64},{192,128},{1,193},{65,1},{129,65},{193,129... | collective-permute-start | bytes 245768 | tf_op jit(solution)/shard_map/ppermute | solution.py:79
  294.0 1.5 collective-permute-done.15
  295.5 3.4 %collective-permute-start.16 = (bf16[32,1280]{1,0:T(8,128)(2,1)S(1)}, bf16[32,1280]{1,0:T(8,128)(2,1)S(1)}, u32[]{:S(2)}, u32[]{:S(2)}) collective-permute-start(bf16[32,1280]{1,0:T(8,128)(2,1)S(1)} %collective-permute-done.15), channel_id=1, source_target_pairs={{0,192},{64,0},{128,64},{192,128},{1,193},{65,1},{129,65},{193,129... | collective-permute-start | bytes 245768 | tf_op jit(solution)/shard_map/ppermute | solution.py:79
  298.8 1.5 collective-permute-done.16
  300.3 3.0 collective-permute-start.17
  303.3 3.6 %collective-permute-done.14 = bf16[224,1280]{1,0:T(8,128)(2,1)S(1)} collective-permute-done((bf16[224,1280]{1,0:T(8,128)(2,1)S(1)}, bf16[224,1280]{1,0:T(8,128)(2,1)S(1)}, u32[]{:S(2)}, u32[]{:S(2)}) %collective-permute-start.14) | collective-permute-done | bytes 573472 | tf_op jit(solution)/shard_map/ppermute | solution.py:79
  307.0 0.0 collective-permute-done.17
  307.0 1.1 collective-permute-start.18
  308.0 1.7 collective-permute-done.18.partner_ref
  309.8 13.5 %shard_map.58 = (bf16[256,1280]{1,0:T(8,128)(2,1)S(1)}, bf16[256,1280]{1,0:T(8,128)(2,1)S(1)}) custom-call(bf16[256,1280]{1,0:T(8,128)(2,1)S(1)} %constant_dynamic-update-slice_fusion.4.own_ref, bf16[256,1280]{1,0:T(8,128)(2,1)S(1)} %collective-permute-done.18.partner_ref, f32[1,2560]{1,0:T(1,128)S(1)} %copy-done, bf16[32,2,80,2560]{3,2,1,0:T(8,128)(2,1)} %bitcast.14, ...), custom_call_target="tpu_custom_call" | custom-call | tf_op jit(solution)/shard_map/pallas_call | solution.py:51
  323.3 0.5 collective-permute-start.19
  323.8 1.7 collective-permute-done.19
  325.5 1.2 fusion
  (13 shorter events, 0.3 us)
Async XLA Ops:
  6.5 2.8 copy-start.1
  6.5 196.8 %all-gather.2.cloned.1.call-start = ((), (), s32[]{:S(2)}) async-start(), calls=%async_computation | async-start | bytes 27033600 | tf_op jit(solution)/shard_map/all_gather | solution.py:97
  8.7 194.7 %copy-start = (f32[1,2560]{1,0:T(1,128)S(1)}, f32[1,2560]{1,0:T(1,128)}, u32[]{:S(2)}) copy-start(f32[1,2560]{1,0:T(1,128)} %gain_ref.7) | copy-start | bytes 30724
  9.5 5.1 %collective-permute-start = (bf16[256,1280]{1,0:T(8,128)(2,1)S(1)}, bf16[256,1280]{1,0:T(8,128)(2,1)S(1)}, u32[]{:S(2)}, u32[]{:S(2)}) collective-permute-start(bf16[256,1280]{1,0:T(8,128)(2,1)S(1)} %broadcast_select_fusion.own_ref), channel_id=1, source_target_pairs={{0,1},{1,0},{2,3},{3,2},{4,5},{5,4},{6,7},{7,6},{8,9},{9,8},{10,11... | collective-permute-start | bytes 1966088 | tf_op jit(solution)/shard_map/ppermute | solution.py:105
  216.9 2.8 collective-permute-start.1
  220.1 15.5 %collective-permute-start.2 = (bf16[224,1280]{1,0:T(8,128)(2,1)S(1)}, bf16[224,1280]{1,0:T(8,128)(2,1)S(1)}, u32[]{:S(2)}, u32[]{:S(2)}) collective-permute-start(bf16[224,1280]{1,0:T(8,128)(2,1)S(1)} %slice.24), channel_id=1, source_target_pairs={{0,64},{64,128},{128,192},{192,0},{1,65},{65,129},{129,193},{193,1... | collective-permute-start | bytes 1720328 | tf_op jit(solution)/shard_map/ppermute | solution.py:79
  221.4 3.6 %collective-permute-start.3 = (bf16[32,1280]{1,0:T(8,128)(2,1)S(1)}, bf16[32,1280]{1,0:T(8,128)(2,1)S(1)}, u32[]{:S(2)}, u32[]{:S(2)}) collective-permute-start(bf16[32,1280]{1,0:T(8,128)(2,1)S(1)} %slice.25), channel_id=1, source_target_pairs={{0,192},{64,0},{128,64},{192,128},{1,193},{65,1},{129,65},{193,129... | collective-permute-start | bytes 245768 | tf_op jit(solution)/shard_map/ppermute | solution.py:79
  225.0 3.9 %collective-permute-start.4 = (bf16[32,1280]{1,0:T(8,128)(2,1)S(1)}, bf16[32,1280]{1,0:T(8,128)(2,1)S(1)}, u32[]{:S(2)}, u32[]{:S(2)}) collective-permute-start(bf16[32,1280]{1,0:T(8,128)(2,1)S(1)} %collective-permute-done.3), channel_id=1, source_target_pairs={{0,192},{64,0},{128,64},{192,128},{1,193},{65,1},{129,65},{193,129... | collective-permute-start | bytes 245768 | tf_op jit(solution)/shard_map/ppermute | solution.py:79
  228.8 6.8 %collective-permute-start.5 = (bf16[32,1280]{1,0:T(8,128)(2,1)S(1)}, bf16[32,1280]{1,0:T(8,128)(2,1)S(1)}, u32[]{:S(2)}, u32[]{:S(2)}) collective-permute-start(bf16[32,1280]{1,0:T(8,128)(2,1)S(1)} %collective-permute-done.4), channel_id=1, source_target_pairs={{0,192},{64,0},{128,64},{192,128},{1,193},{65,1},{129,65},{193,129... | collective-permute-start | bytes 245768 | tf_op jit(solution)/shard_map/ppermute | solution.py:79
  235.6 3.2 collective-permute-start.6
  252.4 2.2 collective-permute-start.7
  255.0 16.5 %collective-permute-start.8 = (bf16[224,1280]{1,0:T(8,128)(2,1)S(1)}, bf16[224,1280]{1,0:T(8,128)(2,1)S(1)}, u32[]{:S(2)}, u32[]{:S(2)}) collective-permute-start(bf16[224,1280]{1,0:T(8,128)(2,1)S(1)} %slice.26), channel_id=1, source_target_pairs={{0,64},{64,128},{128,192},{192,0},{1,65},{65,129},{129,193},{193,1... | collective-permute-start | bytes 1720328 | tf_op jit(solution)/shard_map/ppermute | solution.py:79
  255.1 4.9 %collective-permute-start.9 = (bf16[32,1280]{1,0:T(8,128)(2,1)S(1)}, bf16[32,1280]{1,0:T(8,128)(2,1)S(1)}, u32[]{:S(2)}, u32[]{:S(2)}) collective-permute-start(bf16[32,1280]{1,0:T(8,128)(2,1)S(1)} %slice.27), channel_id=1, source_target_pairs={{0,192},{64,0},{128,64},{192,128},{1,193},{65,1},{129,65},{193,129... | collective-permute-start | bytes 245768 | tf_op jit(solution)/shard_map/ppermute | solution.py:79
  260.0 4.9 %collective-permute-start.10 = (bf16[32,1280]{1,0:T(8,128)(2,1)S(1)}, bf16[32,1280]{1,0:T(8,128)(2,1)S(1)}, u32[]{:S(2)}, u32[]{:S(2)}) collective-permute-start(bf16[32,1280]{1,0:T(8,128)(2,1)S(1)} %collective-permute-done.9), channel_id=1, source_target_pairs={{0,192},{64,0},{128,64},{192,128},{1,193},{65,1},{129,65},{193,129... | collective-permute-start | bytes 245768 | tf_op jit(solution)/shard_map/ppermute | solution.py:79
  264.9 6.6 %collective-permute-start.11 = (bf16[32,1280]{1,0:T(8,128)(2,1)S(1)}, bf16[32,1280]{1,0:T(8,128)(2,1)S(1)}, u32[]{:S(2)}, u32[]{:S(2)}) collective-permute-start(bf16[32,1280]{1,0:T(8,128)(2,1)S(1)} %collective-permute-done.10), channel_id=1, source_target_pairs={{0,192},{64,0},{128,64},{192,128},{1,193},{65,1},{129,65},{193,129... | collective-permute-start | bytes 245768 | tf_op jit(solution)/shard_map/ppermute | solution.py:79
  271.6 2.8 collective-permute-start.12
  287.9 2.2 collective-permute-start.13
  290.5 16.4 %collective-permute-start.14 = (bf16[224,1280]{1,0:T(8,128)(2,1)S(1)}, bf16[224,1280]{1,0:T(8,128)(2,1)S(1)}, u32[]{:S(2)}, u32[]{:S(2)}) collective-permute-start(bf16[224,1280]{1,0:T(8,128)(2,1)S(1)} %slice.28), channel_id=1, source_target_pairs={{0,64},{64,128},{128,192},{192,0},{1,65},{65,129},{129,193},{193,1... | collective-permute-start | bytes 1720328 | tf_op jit(solution)/shard_map/ppermute | solution.py:79
  290.6 4.9 %collective-permute-start.15 = (bf16[32,1280]{1,0:T(8,128)(2,1)S(1)}, bf16[32,1280]{1,0:T(8,128)(2,1)S(1)}, u32[]{:S(2)}, u32[]{:S(2)}) collective-permute-start(bf16[32,1280]{1,0:T(8,128)(2,1)S(1)} %slice.29), channel_id=1, source_target_pairs={{0,192},{64,0},{128,64},{192,128},{1,193},{65,1},{129,65},{193,129... | collective-permute-start | bytes 245768 | tf_op jit(solution)/shard_map/ppermute | solution.py:79
  295.5 4.9 %collective-permute-start.16 = (bf16[32,1280]{1,0:T(8,128)(2,1)S(1)}, bf16[32,1280]{1,0:T(8,128)(2,1)S(1)}, u32[]{:S(2)}, u32[]{:S(2)}) collective-permute-start(bf16[32,1280]{1,0:T(8,128)(2,1)S(1)} %collective-permute-done.15), channel_id=1, source_target_pairs={{0,192},{64,0},{128,64},{192,128},{1,193},{65,1},{129,65},{193,129... | collective-permute-start | bytes 245768 | tf_op jit(solution)/shard_map/ppermute | solution.py:79
  300.3 6.6 %collective-permute-start.17 = (bf16[32,1280]{1,0:T(8,128)(2,1)S(1)}, bf16[32,1280]{1,0:T(8,128)(2,1)S(1)}, u32[]{:S(2)}, u32[]{:S(2)}) collective-permute-start(bf16[32,1280]{1,0:T(8,128)(2,1)S(1)} %collective-permute-done.16), channel_id=1, source_target_pairs={{0,192},{64,0},{128,64},{192,128},{1,193},{65,1},{129,65},{193,129... | collective-permute-start | bytes 245768 | tf_op jit(solution)/shard_map/ppermute | solution.py:79
  307.0 2.8 collective-permute-start.18
  323.3 2.2 collective-permute-start.19
Sparse Core Ops, SparseCore 0:
  9.9 193.3 all-gather.1

commit v15 on v12

--- a/solution.py
+++ b/solution.py
@@ -6,6 +6,7 @@
 from jax.sharding import PartitionSpec as P
 
 TILE = 512
+MICRO = 2
 
 
 def ffn_body(own_ref, partner_ref, gain_ref, win_ref, wout_ref, keep_ref, send_ref, normed_ref, acc_ref):
@@ -68,7 +69,7 @@
     )(current, partner, gain, gathered, gathered)
 
 
-RELAYED = 32
+RELAYED = 16
 
 
 def shifted(value, axis, steps):
@@ -103,12 +104,22 @@
         summed = keep.astype(jnp.float32) + other.astype(jnp.float32)
         return (current.astype(jnp.float32) + summed).astype(jnp.bfloat16)
 
-    result = apply_layer(first)
-    stored = jnp.where(segment_index == 0, result, jnp.zeros_like(result))
-
-    for moment in range(1, segment_count):
-        result = apply_layer(passed_along(result, "section"))
-        stored = lax.optimization_barrier(jnp.where(segment_index == moment, result, stored))
+    block_rows = local_rows // MICRO
+    pieces = [first[index * block_rows:(index + 1) * block_rows] for index in range(MICRO)]
+    stored = jnp.zeros((MICRO, block_rows, width_local), jnp.bfloat16)
+    result = None
+    for moment in range(MICRO + segment_count - 1):
+        own_piece = pieces[min(moment, MICRO - 1)]
+        if result is None:
+            current = own_piece
+        else:
+            current = jnp.where(segment_index == 0, own_piece, passed_along(result, "section"))
+        result = apply_layer(current)
+        position = moment - segment_index
+        active = jnp.logical_and(position >= 0, position < MICRO)
+        target = jnp.clip(position, 0, MICRO - 1)
+        updated = lax.dynamic_update_index_in_dim(stored, result, target, 0)
+        stored = lax.optimization_barrier(jnp.where(active, updated, stored))
     return stored.reshape(1, local_rows, width_local)
 
 

time: 333 us -> 355 us (1.066)
  starting transfers between devices: 37.4 us -> 57.7 us
  waiting for transfers between devices: 223 us -> 214 us
  Pallas kernels: 53.6 us -> 61.9 us
    ppermute x4 -> x5, starting transfers between devices: 6.96 us -> 18.2 us  [apply_layer(): partner = lax.ppermute(current, 'mp', [(0, 1), (1, 0)])]
    ppermute x12 -> x16, starting transfers between devices: 27.9 us -> 36.4 us  [shifted(): lax.ppermute(value, axis, [(source, (source + steps) % count) for source...]
    pallas_call x4 -> x5, Pallas kernels: 53.6 us -> 61.9 us  [ffn(): pl.pallas_call(ffn_body, grid=(hidden_units // TILE,), in_specs=[pl.Block...]
    ppermute x12 -> x16, waiting for transfers between devices: 20.4 us -> 13.5 us  [shifted(): lax.ppermute(value, axis, [(source, (source + steps) % count) for source...]
  transfers between devices with their start and end apart: 21 -> 27, of which waited for: 18 -> 23; matrix products, arithmetic and copies ran while one was open for 0% -> 0% of each run, Pallas kernels for 0% -> 0%
where the time goes in v15:
time: 355 us; the launch traced here: 354 us
  waiting for transfers between devices  214 us (60%)
  Pallas kernels  61.9 us (17%)
  starting transfers between devices  57.7 us (16%)
  between operations  14.3 us (4%)
  other arithmetic  4.66 us (1%)
    all_gather x1, waiting for transfers between devices, per_device(): gathered = lax.all_gather(both, 'dp', axis=1, tiled=True)  188 us
    pallas_call x5, Pallas kernels, ffn(): pl.pallas_call(ffn_body, grid=(hidden_units // TILE,), in_specs=[pl.Block...  61.9 us
    ppermute x16, starting transfers between devices, shifted(): lax.ppermute(value, axis, [(source, (source + steps) % count) for source...  36.4 us
    ppermute x5, starting transfers between devices, apply_layer(): partner = lax.ppermute(current, 'mp', [(0, 1), (1, 0)])  18.2 us
    ppermute x16, waiting for transfers between devices, shifted(): lax.ppermute(value, axis, [(source, (source + steps) % count) for source...  13.5 us
  transfers between devices with their start and end apart: 27, of which 23 were waited for; matrix products, arithmetic and copies ran while one was open for 0% of the time, Pallas kernels for 0%

profile of v15, /device:TPU:1, one launch (start us, length us, event | category | flops | bytes accessed | tf_op | source)
XLA Modules:
  0.0 354.4 jit_solution(10883042730268534428)
XLA Ops:
  6.5 2.1 pad_maximum_fusion
  9.3 1.2 broadcast_select_fusion
  10.6 3.3 collective-permute-start
  13.9 1.3 collective-permute-done.partner_ref
  15.2 188.2 %all-gather.2.cloned.1.call-done.win_ref.wout_ref = bf16[2,2560,2560]{2,1,0:T(8,128)(2,1)} async-done(((bf16[2,80,2560]{2,1,0:T(8,128)(2,1)}), bf16[2,2560,2560]{2,1,0:T(8,128)(2,1)}) %all-gather.2.cloned.1.call-update) | async-done | bytes 26214416 | tf_op jit(solution)/shard_map/all_gather | solution.py:94
  203.4 0.7 copy-done
  204.1 12.4 %shard_map.55 = (bf16[128,1280]{1,0:T(8,128)(2,1)S(1)}, bf16[128,1280]{1,0:T(8,128)(2,1)S(1)}) custom-call(bf16[128,1280]{1,0:T(8,128)(2,1)S(1)} %slice.40.own_ref, bf16[128,1280]{1,0:T(8,128)(2,1)S(1)} %collective-permute-done.partner_ref, f32[1,2560]{1,0:T(1,128)S(1)} %copy-done, bf16[2,2560,2560]{2,1,0:T(8,128)(2,1)} %all-gather.2.cloned.1.call-done.win_ref.wout_ref, ...), custom_call_target="tpu_custom_call" | custom-call | tf_op jit(solution)/shard_map/pallas_call | solution.py:49
  216.4 1.1 collective-permute-start.1
  217.6 1.3 collective-permute-done.1
  218.9 0.2 bitcast_dynamic-update-slice_fusion
  219.1 1.3 collective-permute-start.2
  220.4 1.5 collective-permute-start.3
  221.9 1.4 collective-permute-done.3
  223.2 2.7 collective-permute-start.4
  225.9 1.1 collective-permute-done.4
  227.0 3.0 collective-permute-start.5
  230.0 1.1 collective-permute-done.5
  231.1 0.1 maximum_select_fusion.own_ref
  231.2 3.9 %collective-permute-start.6 = (bf16[128,1280]{1,0:T(8,128)(2,1)S(1)}, bf16[128,1280]{1,0:T(8,128)(2,1)S(1)}, u32[]{:S(2)}, u32[]{:S(2)}) collective-permute-start(bf16[128,1280]{1,0:T(8,128)(2,1)S(1)} %maximum_select_fusion.own_ref), channel_id=1, source_target_pairs={{0,1},{1,0},{2,3},{3,2},{4,5},{5,4},{6,7},{7,6},{8,9},{9,8},{10,11... | collective-permute-start | bytes 983048 | tf_op jit(solution)/shard_map/ppermute | solution.py:101
  235.1 1.3 collective-permute-done.6.partner_ref
  236.3 12.4 %shard_map.56 = (bf16[128,1280]{1,0:T(8,128)(2,1)S(1)}, bf16[128,1280]{1,0:T(8,128)(2,1)S(1)}) custom-call(bf16[128,1280]{1,0:T(8,128)(2,1)S(1)} %maximum_select_fusion.own_ref, bf16[128,1280]{1,0:T(8,128)(2,1)S(1)} %collective-permute-done.6.partner_ref, f32[1,2560]{1,0:T(1,128)S(1)} %copy-done.1, ...), custom_call_target="tpu_custom_call" | custom-call | tf_op jit(solution)/shard_map/pallas_call | solution.py:49
  248.7 0.5 collective-permute-start.7
  249.2 1.3 collective-permute-done.7
  250.4 0.2 fusion.5
  250.8 3.3 collective-permute-start.9
  254.1 1.1 collective-permute-done.9
  255.2 3.0 collective-permute-start.10
  258.2 1.1 collective-permute-done.10
  259.3 3.0 collective-permute-start.11
  262.2 1.1 collective-permute-done.11
  263.3 0.1 maximum_select_fusion.1.own_ref
  263.4 3.8 %collective-permute-start.12 = (bf16[128,1280]{1,0:T(8,128)(2,1)S(1)}, bf16[128,1280]{1,0:T(8,128)(2,1)S(1)}, u32[]{:S(2)}, u32[]{:S(2)}) collective-permute-start(bf16[128,1280]{1,0:T(8,128)(2,1)S(1)} %maximum_select_fusion.1.own_ref), channel_id=1, source_target_pairs={{0,1},{1,0},{2,3},{3,2},{4,5},{5,4},{6,7},{7,6},{8,9},{9,8},{10,11... | collective-permute-start | bytes 983048 | tf_op jit(solution)/shard_map/ppermute | solution.py:101
  267.2 1.3 collective-permute-done.12.partner_ref
  268.5 12.4 %shard_map.57 = (bf16[128,1280]{1,0:T(8,128)(2,1)S(1)}, bf16[128,1280]{1,0:T(8,128)(2,1)S(1)}) custom-call(bf16[128,1280]{1,0:T(8,128)(2,1)S(1)} %maximum_select_fusion.1.own_ref, bf16[128,1280]{1,0:T(8,128)(2,1)S(1)} %collective-permute-done.12.partner_ref, f32[1,2560]{1,0:T(1,128)S(1)} %copy-done.1, ...), custom_call_target="tpu_custom_call" | custom-call | tf_op jit(solution)/shard_map/pallas_call | solution.py:49
  280.9 0.5 collective-permute-start.13
  281.3 1.3 collective-permute-done.13
  282.6 0.2 fusion.4
  282.9 3.3 collective-permute-start.15
  286.3 1.1 collective-permute-done.15
  287.4 3.0 collective-permute-start.16
  290.3 1.1 collective-permute-done.16
  291.4 3.0 collective-permute-start.17
  294.4 1.1 collective-permute-done.17
  295.5 0.1 maximum_select_fusion.2.own_ref
  295.6 3.6 %collective-permute-start.18 = (bf16[128,1280]{1,0:T(8,128)(2,1)S(1)}, bf16[128,1280]{1,0:T(8,128)(2,1)S(1)}, u32[]{:S(2)}, u32[]{:S(2)}) collective-permute-start(bf16[128,1280]{1,0:T(8,128)(2,1)S(1)} %maximum_select_fusion.2.own_ref), channel_id=1, source_target_pairs={{0,1},{1,0},{2,3},{3,2},{4,5},{5,4},{6,7},{7,6},{8,9},{9,8},{10,11... | collective-permute-start | bytes 983048 | tf_op jit(solution)/shard_map/ppermute | solution.py:101
  299.2 1.3 collective-permute-done.18.partner_ref
  300.5 12.4 %shard_map.58 = (bf16[128,1280]{1,0:T(8,128)(2,1)S(1)}, bf16[128,1280]{1,0:T(8,128)(2,1)S(1)}) custom-call(bf16[128,1280]{1,0:T(8,128)(2,1)S(1)} %maximum_select_fusion.2.own_ref, bf16[128,1280]{1,0:T(8,128)(2,1)S(1)} %collective-permute-done.18.partner_ref, f32[1,2560]{1,0:T(1,128)S(1)} %copy-done.1, ...), custom_call_target="tpu_custom_call" | custom-call | tf_op jit(solution)/shard_map/pallas_call | solution.py:49
  312.8 0.4 collective-permute-start.19
  313.3 1.3 collective-permute-done.19
  314.6 0.2 fusion.3
  314.9 3.3 collective-permute-start.21
  318.2 1.1 collective-permute-done.21
  319.3 3.0 collective-permute-start.22
  322.3 1.1 collective-permute-done.22
  323.4 3.0 collective-permute-start.23
  326.4 1.1 collective-permute-done.23
  327.5 0.1 maximum_select_fusion.3.own_ref
  327.6 3.6 %collective-permute-start.24 = (bf16[128,1280]{1,0:T(8,128)(2,1)S(1)}, bf16[128,1280]{1,0:T(8,128)(2,1)S(1)}, u32[]{:S(2)}, u32[]{:S(2)}) collective-permute-start(bf16[128,1280]{1,0:T(8,128)(2,1)S(1)} %maximum_select_fusion.3.own_ref), channel_id=1, source_target_pairs={{0,1},{1,0},{2,3},{3,2},{4,5},{5,4},{6,7},{7,6},{8,9},{9,8},{10,11... | collective-permute-start | bytes 983048 | tf_op jit(solution)/shard_map/ppermute | solution.py:101
  331.2 1.3 collective-permute-done.24.partner_ref
  332.4 12.4 %shard_map.59 = (bf16[128,1280]{1,0:T(8,128)(2,1)S(1)}, bf16[128,1280]{1,0:T(8,128)(2,1)S(1)}) custom-call(bf16[128,1280]{1,0:T(8,128)(2,1)S(1)} %maximum_select_fusion.3.own_ref, bf16[128,1280]{1,0:T(8,128)(2,1)S(1)} %collective-permute-done.24.partner_ref, f32[1,2560]{1,0:T(1,128)S(1)} %copy-done.1, ...), custom_call_target="tpu_custom_call" | custom-call | tf_op jit(solution)/shard_map/pallas_call | solution.py:49
  344.8 0.5 collective-permute-start.25
  345.3 1.3 collective-permute-done.25
  346.5 0.2 fusion.2
  346.7 0.8 copy-done.2
  (24 shorter events, 0.5 us)
Async XLA Ops:
  6.5 196.8 %all-gather.2.cloned.1.call-start = ((), (), s32[]{:S(2)}) async-start(), calls=%async_computation | async-start | bytes 27033600 | tf_op jit(solution)/shard_map/all_gather | solution.py:94
  10.5 225.8 %copy-start.1 = (f32[1,2560]{1,0:T(1,128)S(1)}, f32[1,2560]{1,0:T(1,128)}, u32[]{:S(2)}) copy-start(f32[1,2560]{1,0:T(1,128)} %gain_ref.9) | copy-start | bytes 30724
  10.6 4.6 %collective-permute-start = (bf16[128,1280]{1,0:T(8,128)(2,1)S(1)}, bf16[128,1280]{1,0:T(8,128)(2,1)S(1)}, u32[]{:S(2)}, u32[]{:S(2)}) collective-permute-start(bf16[128,1280]{1,0:T(8,128)(2,1)S(1)} %slice.40.own_ref), channel_id=1, source_target_pairs={{0,1},{1,0},{2,3},{3,2},{4,5},{5,4},{6,7},{7,6},{8,9},{9,8},{10,11... | collective-permute-start | bytes 983048 | tf_op jit(solution)/shard_map/ppermute | solution.py:101
  203.4 0.7 copy-start
  216.4 2.4 collective-permute-start.1
  219.1 12.0 %collective-permute-start.2 = (bf16[112,1280]{1,0:T(8,128)(2,1)S(1)}, bf16[112,1280]{1,0:T(8,128)(2,1)S(1)}, u32[]{:S(2)}, u32[]{:S(2)}) collective-permute-start(bf16[112,1280]{1,0:T(8,128)(2,1)S(1)} %slice.42), channel_id=1, source_target_pairs={{0,64},{64,128},{128,192},{192,0},{1,65},{65,129},{129,193},{193,1... | collective-permute-start | bytes 860168 | tf_op jit(solution)/shard_map/ppermute | solution.py:77
  220.4 2.9 collective-permute-start.3
  223.2 3.8 %collective-permute-start.4 = (bf16[16,1280]{1,0:T(8,128)(2,1)S(1)}, bf16[16,1280]{1,0:T(8,128)(2,1)S(1)}, u32[]{:S(2)}, u32[]{:S(2)}) collective-permute-start(bf16[16,1280]{1,0:T(8,128)(2,1)S(1)} %collective-permute-done.3), channel_id=1, source_target_pairs={{0,192},{64,0},{128,64},{192,128},{1,193},{65,1},{129,65},{193,129... | collective-permute-start | bytes 122888 | tf_op jit(solution)/shard_map/ppermute | solution.py:77
  227.0 4.1 %collective-permute-start.5 = (bf16[16,1280]{1,0:T(8,128)(2,1)S(1)}, bf16[16,1280]{1,0:T(8,128)(2,1)S(1)}, u32[]{:S(2)}, u32[]{:S(2)}) collective-permute-start(bf16[16,1280]{1,0:T(8,128)(2,1)S(1)} %collective-permute-done.4), channel_id=1, source_target_pairs={{0,192},{64,0},{128,64},{192,128},{1,193},{65,1},{129,65},{193,129... | collective-permute-start | bytes 122888 | tf_op jit(solution)/shard_map/ppermute | solution.py:77
  231.2 5.1 %collective-permute-start.6 = (bf16[128,1280]{1,0:T(8,128)(2,1)S(1)}, bf16[128,1280]{1,0:T(8,128)(2,1)S(1)}, u32[]{:S(2)}, u32[]{:S(2)}) collective-permute-start(bf16[128,1280]{1,0:T(8,128)(2,1)S(1)} %maximum_select_fusion.own_ref), channel_id=1, source_target_pairs={{0,1},{1,0},{2,3},{3,2},{4,5},{5,4},{6,7},{7,6},{8,9},{9,8},{10,11... | collective-permute-start | bytes 983048 | tf_op jit(solution)/shard_map/ppermute | solution.py:101
  248.7 1.7 collective-permute-start.7
  250.7 12.7 %collective-permute-start.8 = (bf16[112,1280]{1,0:T(8,128)(2,1)S(1)}, bf16[112,1280]{1,0:T(8,128)(2,1)S(1)}, u32[]{:S(2)}, u32[]{:S(2)}) collective-permute-start(bf16[112,1280]{1,0:T(8,128)(2,1)S(1)} %slice.44), channel_id=1, source_target_pairs={{0,64},{64,128},{128,192},{192,0},{1,65},{65,129},{129,193},{193,1... | collective-permute-start | bytes 860168 | tf_op jit(solution)/shard_map/ppermute | solution.py:77
  250.8 4.4 %collective-permute-start.9 = (bf16[16,1280]{1,0:T(8,128)(2,1)S(1)}, bf16[16,1280]{1,0:T(8,128)(2,1)S(1)}, u32[]{:S(2)}, u32[]{:S(2)}) collective-permute-start(bf16[16,1280]{1,0:T(8,128)(2,1)S(1)} %slice.45), channel_id=1, source_target_pairs={{0,192},{64,0},{128,64},{192,128},{1,193},{65,1},{129,65},{193,129... | collective-permute-start | bytes 122888 | tf_op jit(solution)/shard_map/ppermute | solution.py:77
  255.2 4.1 %collective-permute-start.10 = (bf16[16,1280]{1,0:T(8,128)(2,1)S(1)}, bf16[16,1280]{1,0:T(8,128)(2,1)S(1)}, u32[]{:S(2)}, u32[]{:S(2)}) collective-permute-start(bf16[16,1280]{1,0:T(8,128)(2,1)S(1)} %collective-permute-done.9), channel_id=1, source_target_pairs={{0,192},{64,0},{128,64},{192,128},{1,193},{65,1},{129,65},{193,129... | collective-permute-start | bytes 122888 | tf_op jit(solution)/shard_map/ppermute | solution.py:77
  259.3 4.1 %collective-permute-start.11 = (bf16[16,1280]{1,0:T(8,128)(2,1)S(1)}, bf16[16,1280]{1,0:T(8,128)(2,1)S(1)}, u32[]{:S(2)}, u32[]{:S(2)}) collective-permute-start(bf16[16,1280]{1,0:T(8,128)(2,1)S(1)} %collective-permute-done.10), channel_id=1, source_target_pairs={{0,192},{64,0},{128,64},{192,128},{1,193},{65,1},{129,65},{193,129... | collective-permute-start | bytes 122888 | tf_op jit(solution)/shard_map/ppermute | solution.py:77
  263.4 5.0 %collective-permute-start.12 = (bf16[128,1280]{1,0:T(8,128)(2,1)S(1)}, bf16[128,1280]{1,0:T(8,128)(2,1)S(1)}, u32[]{:S(2)}, u32[]{:S(2)}) collective-permute-start(bf16[128,1280]{1,0:T(8,128)(2,1)S(1)} %maximum_select_fusion.1.own_ref), channel_id=1, source_target_pairs={{0,1},{1,0},{2,3},{3,2},{4,5},{5,4},{6,7},{7,6},{8,9},{9,8},{10,11... | collective-permute-start | bytes 983048 | tf_op jit(solution)/shard_map/ppermute | solution.py:101
  280.9 1.7 collective-permute-start.13
  282.8 12.7 %collective-permute-start.14 = (bf16[112,1280]{1,0:T(8,128)(2,1)S(1)}, bf16[112,1280]{1,0:T(8,128)(2,1)S(1)}, u32[]{:S(2)}, u32[]{:S(2)}) collective-permute-start(bf16[112,1280]{1,0:T(8,128)(2,1)S(1)} %slice.46), channel_id=1, source_target_pairs={{0,64},{64,128},{128,192},{192,0},{1,65},{65,129},{129,193},{193,1... | collective-permute-start | bytes 860168 | tf_op jit(solution)/shard_map/ppermute | solution.py:77
  282.9 4.4 %collective-permute-start.15 = (bf16[16,1280]{1,0:T(8,128)(2,1)S(1)}, bf16[16,1280]{1,0:T(8,128)(2,1)S(1)}, u32[]{:S(2)}, u32[]{:S(2)}) collective-permute-start(bf16[16,1280]{1,0:T(8,128)(2,1)S(1)} %slice.47), channel_id=1, source_target_pairs={{0,192},{64,0},{128,64},{192,128},{1,193},{65,1},{129,65},{193,129... | collective-permute-start | bytes 122888 | tf_op jit(solution)/shard_map/ppermute | solution.py:77
  287.4 4.1 %collective-permute-start.16 = (bf16[16,1280]{1,0:T(8,128)(2,1)S(1)}, bf16[16,1280]{1,0:T(8,128)(2,1)S(1)}, u32[]{:S(2)}, u32[]{:S(2)}) collective-permute-start(bf16[16,1280]{1,0:T(8,128)(2,1)S(1)} %collective-permute-done.15), channel_id=1, source_target_pairs={{0,192},{64,0},{128,64},{192,128},{1,193},{65,1},{129,65},{193,129... | collective-permute-start | bytes 122888 | tf_op jit(solution)/shard_map/ppermute | solution.py:77
  291.4 4.1 %collective-permute-start.17 = (bf16[16,1280]{1,0:T(8,128)(2,1)S(1)}, bf16[16,1280]{1,0:T(8,128)(2,1)S(1)}, u32[]{:S(2)}, u32[]{:S(2)}) collective-permute-start(bf16[16,1280]{1,0:T(8,128)(2,1)S(1)} %collective-permute-done.16), channel_id=1, source_target_pairs={{0,192},{64,0},{128,64},{192,128},{1,193},{65,1},{129,65},{193,129... | collective-permute-start | bytes 122888 | tf_op jit(solution)/shard_map/ppermute | solution.py:77
  295.6 4.9 %collective-permute-start.18 = (bf16[128,1280]{1,0:T(8,128)(2,1)S(1)}, bf16[128,1280]{1,0:T(8,128)(2,1)S(1)}, u32[]{:S(2)}, u32[]{:S(2)}) collective-permute-start(bf16[128,1280]{1,0:T(8,128)(2,1)S(1)} %maximum_select_fusion.2.own_ref), channel_id=1, source_target_pairs={{0,1},{1,0},{2,3},{3,2},{4,5},{5,4},{6,7},{7,6},{8,9},{9,8},{10,11... | collective-permute-start | bytes 983048 | tf_op jit(solution)/shard_map/ppermute | solution.py:101
  312.8 1.7 collective-permute-start.19
  314.8 12.7 %collective-permute-start.20 = (bf16[112,1280]{1,0:T(8,128)(2,1)S(1)}, bf16[112,1280]{1,0:T(8,128)(2,1)S(1)}, u32[]{:S(2)}, u32[]{:S(2)}) collective-permute-start(bf16[112,1280]{1,0:T(8,128)(2,1)S(1)} %slice.48), channel_id=1, source_target_pairs={{0,64},{64,128},{128,192},{192,0},{1,65},{65,129},{129,193},{193,1... | collective-permute-start | bytes 860168 | tf_op jit(solution)/shard_map/ppermute | solution.py:77
  314.9 4.4 %collective-permute-start.21 = (bf16[16,1280]{1,0:T(8,128)(2,1)S(1)}, bf16[16,1280]{1,0:T(8,128)(2,1)S(1)}, u32[]{:S(2)}, u32[]{:S(2)}) collective-permute-start(bf16[16,1280]{1,0:T(8,128)(2,1)S(1)} %slice.49), channel_id=1, source_target_pairs={{0,192},{64,0},{128,64},{192,128},{1,193},{65,1},{129,65},{193,129... | collective-permute-start | bytes 122888 | tf_op jit(solution)/shard_map/ppermute | solution.py:77
  319.3 4.1 %collective-permute-start.22 = (bf16[16,1280]{1,0:T(8,128)(2,1)S(1)}, bf16[16,1280]{1,0:T(8,128)(2,1)S(1)}, u32[]{:S(2)}, u32[]{:S(2)}) collective-permute-start(bf16[16,1280]{1,0:T(8,128)(2,1)S(1)} %collective-permute-done.21), channel_id=1, source_target_pairs={{0,192},{64,0},{128,64},{192,128},{1,193},{65,1},{129,65},{193,129... | collective-permute-start | bytes 122888 | tf_op jit(solution)/shard_map/ppermute | solution.py:77
  323.4 4.1 %collective-permute-start.23 = (bf16[16,1280]{1,0:T(8,128)(2,1)S(1)}, bf16[16,1280]{1,0:T(8,128)(2,1)S(1)}, u32[]{:S(2)}, u32[]{:S(2)}) collective-permute-start(bf16[16,1280]{1,0:T(8,128)(2,1)S(1)} %collective-permute-done.22), channel_id=1, source_target_pairs={{0,192},{64,0},{128,64},{192,128},{1,193},{65,1},{129,65},{193,129... | collective-permute-start | bytes 122888 | tf_op jit(solution)/shard_map/ppermute | solution.py:77
  327.6 4.9 %collective-permute-start.24 = (bf16[128,1280]{1,0:T(8,128)(2,1)S(1)}, bf16[128,1280]{1,0:T(8,128)(2,1)S(1)}, u32[]{:S(2)}, u32[]{:S(2)}) collective-permute-start(bf16[128,1280]{1,0:T(8,128)(2,1)S(1)} %maximum_select_fusion.3.own_ref), channel_id=1, source_target_pairs={{0,1},{1,0},{2,3},{3,2},{4,5},{5,4},{6,7},{7,6},{8,9},{9,8},{10,11... | collective-permute-start | bytes 983048 | tf_op jit(solution)/shard_map/ppermute | solution.py:101
  344.8 1.7 collective-permute-start.25
  346.7 0.8 copy-start.2
Sparse Core Ops, SparseCore 0:
  9.9 193.3 all-gather.1

commit v16 on v15

--- a/solution.py
+++ b/solution.py
@@ -69,21 +69,9 @@
     )(current, partner, gain, gathered, gathered)
 
 
-RELAYED = 16
-
-
 def shifted(value, axis, steps):
     count = lax.axis_size(axis)
     return lax.ppermute(value, axis, [(source, (source + steps) % count) for source in range(count)])
-
-
-def passed_along(value, axis):
-    count = lax.axis_size(axis)
-    direct = shifted(value[:-RELAYED], axis, 1)
-    relayed = value[-RELAYED:]
-    for _ in range(count - 1):
-        relayed = shifted(relayed, axis, -1)
-    return jnp.concatenate([direct, relayed], axis=0)
 
 
 def per_device(frames, frame_count, norm_gain, weight_in, weight_out):
@@ -113,7 +101,7 @@
         if result is None:
             current = own_piece
         else:
-            current = jnp.where(segment_index == 0, own_piece, passed_along(result, "section"))
+            current = jnp.where(segment_index == 0, own_piece, shifted(result, "section", 1))
         result = apply_layer(current)
         position = moment - segment_index
         active = jnp.logical_and(position >= 0, position < MICRO)

time: 355 us -> 336 us (0.946)
  starting transfers between devices: 57.7 us -> 13.2 us
  waiting for transfers between devices: 214 us -> 240 us
    ppermute x16 -> x4, starting transfers between devices: 36.4 us -> 1.51 us  [shifted(): lax.ppermute(value, axis, [(source, (source + steps) % count) for source...]
    ppermute x16 -> x4, waiting for transfers between devices: 13.5 us -> 39.3 us  [shifted(): lax.ppermute(value, axis, [(source, (source + steps) % count) for source...]
    ppermute x5, starting transfers between devices: 18.2 us -> 8.66 us  [apply_layer(): partner = lax.ppermute(current, 'mp', [(0, 1), (1, 0)])]
  transfers between devices with their start and end apart: 27 -> 15, of which waited for: 23 -> 15; matrix products, arithmetic and copies ran while one was open for 0% -> 0% of each run, Pallas kernels for 0% -> 0%
where the time goes in v16:
time: 336 us; the launch traced here: 335 us
  waiting for transfers between devices  240 us (71%)
  Pallas kernels  61.9 us (18%)
  between operations  14.2 us (4%)
  starting transfers between devices  13.2 us (4%)
  other arithmetic  4.42 us (1%)
    all_gather x1, waiting for transfers between devices, per_device(): gathered = lax.all_gather(both, 'dp', axis=1, tiled=True)  188 us
    pallas_call x5, Pallas kernels, ffn(): pl.pallas_call(ffn_body, grid=(hidden_units // TILE,), in_specs=[pl.Block...  61.9 us
    ppermute x4, waiting for transfers between devices, shifted(): lax.ppermute(value, axis, [(source, (source + steps) % count) for source...  39.3 us
    ppermute x5, starting transfers between devices, apply_layer(): partner = lax.ppermute(current, 'mp', [(0, 1), (1, 0)])  8.66 us
  transfers between devices with their start and end apart: 15, of which 15 were waited for; matrix products, arithmetic and copies ran while one was open for 0% of the time, Pallas kernels for 0%

profile of v16, /device:TPU:1, one launch (start us, length us, event | category | flops | bytes accessed | tf_op | source)
XLA Modules:
  0.0 335.3 jit_solution(14634462400831753210)
XLA Ops:
  6.5 0.0 all-gather.2.cloned.1.call-start
  6.5 2.1 pad_maximum_fusion
  8.6 0.0 all-gather.2.cloned.1.call-update
  9.3 1.2 broadcast_select_fusion
  10.5 0.0 copy-start.1
  10.6 3.3 collective-permute-start
  13.9 1.3 collective-permute-done.partner_ref
  15.1 188.2 %all-gather.2.cloned.1.call-done.win_ref.wout_ref = bf16[2,2560,2560]{2,1,0:T(8,128)(2,1)} async-done(((bf16[2,80,2560]{2,1,0:T(8,128)(2,1)}), bf16[2,2560,2560]{2,1,0:T(8,128)(2,1)}) %all-gather.2.cloned.1.call-update) | async-done | bytes 26214416 | tf_op jit(solution)/shard_map/all_gather | solution.py:82
  203.4 0.0 copy-start
  203.4 0.7 copy-done
  204.1 12.4 %shard_map.55 = (bf16[128,1280]{1,0:T(8,128)(2,1)S(1)}, bf16[128,1280]{1,0:T(8,128)(2,1)S(1)}) custom-call(bf16[128,1280]{1,0:T(8,128)(2,1)S(1)} %slice.8.own_ref, bf16[128,1280]{1,0:T(8,128)(2,1)S(1)} %collective-permute-done.partner_ref, f32[1,2560]{1,0:T(1,128)S(1)} %copy-done, bf16[2,2560,2560]{2,1,0:T(8,128)(2,1)} %all-gather.2.cloned.1.call-done.win_ref.wout_ref, ...), custom_call_target="tpu_custom_call" | custom-call | tf_op jit(solution)/shard_map/pallas_call | solution.py:49
  216.4 1.1 collective-permute-start.1
  217.6 1.3 collective-permute-done.1
  218.9 0.2 bitcast_dynamic-update-slice_fusion
  219.1 1.3 collective-permute-start.2
  220.3 9.0 %collective-permute-done.2 = bf16[128,1280]{1,0:T(8,128)(2,1)S(1)} collective-permute-done((bf16[128,1280]{1,0:T(8,128)(2,1)S(1)}, bf16[128,1280]{1,0:T(8,128)(2,1)S(1)}, u32[]{:S(2)}, u32[]{:S(2)}) %collective-permute-start.2) | collective-permute-done | bytes 327712 | tf_op jit(solution)/shard_map/ppermute | solution.py:74
  229.3 1.3 collective-permute-start.3
  230.6 1.3 collective-permute-done.3.partner_ref
  231.9 0.0 copy-done.1
  231.9 12.4 %shard_map.56 = (bf16[128,1280]{1,0:T(8,128)(2,1)S(1)}, bf16[128,1280]{1,0:T(8,128)(2,1)S(1)}) custom-call(bf16[128,1280]{1,0:T(8,128)(2,1)S(1)} %broadcast_select_fusion.4.own_ref, bf16[128,1280]{1,0:T(8,128)(2,1)S(1)} %collective-permute-done.3.partner_ref, f32[1,2560]{1,0:T(1,128)S(1)} %copy-done.1, ...), custom_call_target="tpu_custom_call" | custom-call | tf_op jit(solution)/shard_map/pallas_call | solution.py:49
  244.2 0.5 collective-permute-start.4
  244.7 1.3 collective-permute-done.4
  246.0 0.2 fusion.5
  246.2 0.1 collective-permute-start.5
  246.3 10.1 %collective-permute-done.5 = bf16[128,1280]{1,0:T(8,128)(2,1)S(1)} collective-permute-done((bf16[128,1280]{1,0:T(8,128)(2,1)S(1)}, bf16[128,1280]{1,0:T(8,128)(2,1)S(1)}, u32[]{:S(2)}, u32[]{:S(2)}) %collective-permute-start.5) | collective-permute-done | bytes 327712 | tf_op jit(solution)/shard_map/ppermute | solution.py:74
  256.4 1.3 collective-permute-start.6
  257.7 1.3 collective-permute-done.6.partner_ref
  259.0 12.4 %shard_map.57 = (bf16[128,1280]{1,0:T(8,128)(2,1)S(1)}, bf16[128,1280]{1,0:T(8,128)(2,1)S(1)}) custom-call(bf16[128,1280]{1,0:T(8,128)(2,1)S(1)} %broadcast_select_fusion.3.own_ref, bf16[128,1280]{1,0:T(8,128)(2,1)S(1)} %collective-permute-done.6.partner_ref, f32[1,2560]{1,0:T(1,128)S(1)} %copy-done.1, ...), custom_call_target="tpu_custom_call" | custom-call | tf_op jit(solution)/shard_map/pallas_call | solution.py:49
  271.4 0.5 collective-permute-start.7
  271.8 1.3 collective-permute-done.7
  273.1 0.2 fusion.4
  273.3 0.1 collective-permute-start.8
  273.4 10.1 %collective-permute-done.8 = bf16[128,1280]{1,0:T(8,128)(2,1)S(1)} collective-permute-done((bf16[128,1280]{1,0:T(8,128)(2,1)S(1)}, bf16[128,1280]{1,0:T(8,128)(2,1)S(1)}, u32[]{:S(2)}, u32[]{:S(2)}) %collective-permute-start.8) | collective-permute-done | bytes 327712 | tf_op jit(solution)/shard_map/ppermute | solution.py:74
  283.5 1.5 collective-permute-start.9
  285.0 1.3 collective-permute-done.9.partner_ref
  286.3 12.4 %shard_map.58 = (bf16[128,1280]{1,0:T(8,128)(2,1)S(1)}, bf16[128,1280]{1,0:T(8,128)(2,1)S(1)}) custom-call(bf16[128,1280]{1,0:T(8,128)(2,1)S(1)} %broadcast_select_fusion.2.own_ref, bf16[128,1280]{1,0:T(8,128)(2,1)S(1)} %collective-permute-done.9.partner_ref, f32[1,2560]{1,0:T(1,128)S(1)} %copy-done.1, ...), custom_call_target="tpu_custom_call" | custom-call | tf_op jit(solution)/shard_map/pallas_call | solution.py:49
  298.6 0.5 collective-permute-start.10
  299.1 1.3 collective-permute-done.10
  300.4 0.2 fusion.3
  300.6 0.1 collective-permute-start.11
  300.7 10.1 %collective-permute-done.11 = bf16[128,1280]{1,0:T(8,128)(2,1)S(1)} collective-permute-done((bf16[128,1280]{1,0:T(8,128)(2,1)S(1)}, bf16[128,1280]{1,0:T(8,128)(2,1)S(1)}, u32[]{:S(2)}, u32[]{:S(2)}) %collective-permute-start.11) | collective-permute-done | bytes 327712 | tf_op jit(solution)/shard_map/ppermute | solution.py:74
  310.8 1.3 collective-permute-start.12
  312.1 1.3 collective-permute-done.12.partner_ref
  313.4 12.4 %shard_map.59 = (bf16[128,1280]{1,0:T(8,128)(2,1)S(1)}, bf16[128,1280]{1,0:T(8,128)(2,1)S(1)}) custom-call(bf16[128,1280]{1,0:T(8,128)(2,1)S(1)} %broadcast_select_fusion.1.own_ref, bf16[128,1280]{1,0:T(8,128)(2,1)S(1)} %collective-permute-done.12.partner_ref, f32[1,2560]{1,0:T(1,128)S(1)} %copy-done.1, ...), custom_call_target="tpu_custom_call" | custom-call | tf_op jit(solution)/shard_map/pallas_call | solution.py:49
  325.8 0.5 collective-permute-start.13
  326.2 1.3 collective-permute-done.13
  327.5 0.2 fusion.2
  327.7 0.0 copy-start.2
  327.7 0.8 copy-done.2
  (7 shorter events, 0.3 us)
Async XLA Ops:
  6.5 196.8 %all-gather.2.cloned.1.call-start = ((), (), s32[]{:S(2)}) async-start(), calls=%async_computation | async-start | bytes 27033600 | tf_op jit(solution)/shard_map/all_gather | solution.py:82
  10.5 221.3 %copy-start.1 = (f32[1,2560]{1,0:T(1,128)S(1)}, f32[1,2560]{1,0:T(1,128)}, u32[]{:S(2)}) copy-start(f32[1,2560]{1,0:T(1,128)} %gain_ref.9) | copy-start | bytes 30724
  10.6 4.6 %collective-permute-start = (bf16[128,1280]{1,0:T(8,128)(2,1)S(1)}, bf16[128,1280]{1,0:T(8,128)(2,1)S(1)}, u32[]{:S(2)}, u32[]{:S(2)}) collective-permute-start(bf16[128,1280]{1,0:T(8,128)(2,1)S(1)} %slice.8.own_ref), channel_id=1, source_target_pairs={{0,1},{1,0},{2,3},{3,2},{4,5},{5,4},{6,7},{7,6},{8,9},{9,8},{10,11... | collective-permute-start | bytes 983048 | tf_op jit(solution)/shard_map/ppermute | solution.py:89
  203.4 0.7 copy-start
  216.4 2.4 collective-permute-start.1
  219.1 10.2 %collective-permute-start.2 = (bf16[128,1280]{1,0:T(8,128)(2,1)S(1)}, bf16[128,1280]{1,0:T(8,128)(2,1)S(1)}, u32[]{:S(2)}, u32[]{:S(2)}) collective-permute-start(bf16[128,1280]{1,0:T(8,128)(2,1)S(1)} %get-tuple-element.32), channel_id=1, source_target_pairs={{0,64},{64,128},{128,192},{192,0},{1,65},{65,129},{129,193},{193,1... | collective-permute-start | bytes 983048 | tf_op jit(solution)/shard_map/ppermute | solution.py:74
  229.3 2.5 collective-permute-start.3
  244.2 1.7 collective-permute-start.4
  246.2 10.2 %collective-permute-start.5 = (bf16[128,1280]{1,0:T(8,128)(2,1)S(1)}, bf16[128,1280]{1,0:T(8,128)(2,1)S(1)}, u32[]{:S(2)}, u32[]{:S(2)}) collective-permute-start(bf16[128,1280]{1,0:T(8,128)(2,1)S(1)} %get-tuple-element.30), channel_id=1, source_target_pairs={{0,64},{64,128},{128,192},{192,0},{1,65},{65,129},{129,193},{193,1... | collective-permute-start | bytes 983048 | tf_op jit(solution)/shard_map/ppermute | solution.py:74
  256.4 2.5 collective-permute-start.6
  271.4 1.7 collective-permute-start.7
  273.3 10.2 %collective-permute-start.8 = (bf16[128,1280]{1,0:T(8,128)(2,1)S(1)}, bf16[128,1280]{1,0:T(8,128)(2,1)S(1)}, u32[]{:S(2)}, u32[]{:S(2)}) collective-permute-start(bf16[128,1280]{1,0:T(8,128)(2,1)S(1)} %get-tuple-element.28), channel_id=1, source_target_pairs={{0,64},{64,128},{128,192},{192,0},{1,65},{65,129},{129,193},{193,1... | collective-permute-start | bytes 983048 | tf_op jit(solution)/shard_map/ppermute | solution.py:74
  283.5 2.7 collective-permute-start.9
  298.6 1.7 collective-permute-start.10
  300.6 10.2 %collective-permute-start.11 = (bf16[128,1280]{1,0:T(8,128)(2,1)S(1)}, bf16[128,1280]{1,0:T(8,128)(2,1)S(1)}, u32[]{:S(2)}, u32[]{:S(2)}) collective-permute-start(bf16[128,1280]{1,0:T(8,128)(2,1)S(1)} %get-tuple-element.26), channel_id=1, source_target_pairs={{0,64},{64,128},{128,192},{192,0},{1,65},{65,129},{129,193},{193,1... | collective-permute-start | bytes 983048 | tf_op jit(solution)/shard_map/ppermute | solution.py:74
  310.8 2.5 collective-permute-start.12
  325.8 1.7 collective-permute-start.13
  327.7 0.8 copy-start.2
Sparse Core Ops, SparseCore 0:
  9.9 193.3 all-gather.1

commit v17 on v12

--- a/solution.py
+++ b/solution.py
@@ -68,7 +68,7 @@
     )(current, partner, gain, gathered, gathered)
 
 
-RELAYED = 32
+RELAYED = 40
 
 
 def shifted(value, axis, steps):
@@ -77,11 +77,9 @@
 
 
 def passed_along(value, axis):
-    count = lax.axis_size(axis)
     direct = shifted(value[:-RELAYED], axis, 1)
     relayed = value[-RELAYED:]
-    for _ in range(count - 1):
-        relayed = shifted(relayed, axis, -1)
+    relayed = shifted(shifted(relayed, axis, -1), axis, 2)
     return jnp.concatenate([direct, relayed], axis=0)
 
 

time: 333 us -> 338 us (1.015)
  waiting for transfers between devices: 223 us -> 240 us
  starting transfers between devices: 37.4 us -> 25 us
    ppermute x12 -> x9, waiting for transfers between devices: 20.4 us -> 37.4 us  [shifted(): lax.ppermute(value, axis, [(source, (source + steps) % count) for source...]
    ppermute x12 -> x9, starting transfers between devices: 27.9 us -> 15.2 us  [shifted(): lax.ppermute(value, axis, [(source, (source + steps) % count) for source...]
  transfers between devices with their start and end apart: 21 -> 18, of which waited for: 18 -> 16; matrix products, arithmetic and copies ran while one was open for 0% -> 0% of each run, Pallas kernels for 0% -> 0%
where the time goes in v17:
time: 338 us
  waiting for transfers between devices  240 us (71%)
  Pallas kernels  53.7 us (16%)
  starting transfers between devices  25 us (7%)
  between operations  14.2 us (4%)
  other arithmetic  4.47 us (1%)
    all_gather x1, waiting for transfers between devices, per_device(): gathered = lax.all_gather(both, 'dp', axis=1, tiled=True)  189 us
    pallas_call x4, Pallas kernels, ffn(): pl.pallas_call(ffn_body, grid=(hidden_units // TILE,), in_specs=[pl.Block...  53.7 us
    ppermute x9, waiting for transfers between devices, shifted(): lax.ppermute(value, axis, [(source, (source + steps) % count) for source...  37.4 us
    ppermute x9, starting transfers between devices, shifted(): lax.ppermute(value, axis, [(source, (source + steps) % count) for source...  15.2 us
    ppermute x4, starting transfers between devices, apply_layer(): partner = lax.ppermute(current, 'mp', [(0, 1), (1, 0)])  7.37 us
    ppermute x4, waiting for transfers between devices, apply_layer(): other = lax.ppermute(send, 'mp', [(0, 1), (1, 0)])  6.91 us
    ppermute x4, waiting for transfers between devices, apply_layer(): partner = lax.ppermute(current, 'mp', [(0, 1), (1, 0)])  6.9 us
  transfers between devices with their start and end apart: 18, of which 16 were waited for; matrix products, arithmetic and copies ran while one was open for 0% of the time, Pallas kernels for 0%

profile of v17, /device:TPU:1, one launch (start us, length us, event | category | flops | bytes accessed | tf_op | source)
XLA Modules:
  0.0 337.7 jit_solution(7000640843611503711)
XLA Ops:
  6.5 0.0 copy-start.1
  6.5 0.0 all-gather.2.cloned.1.call-start
  6.5 2.2 pad_maximum_fusion
  8.7 0.0 copy-start
  8.7 0.0 all-gather.2.cloned.1.call-update
  9.4 0.0 copy-done.1
  9.4 0.1 broadcast_select_fusion.own_ref
  9.5 3.3 collective-permute-start
  12.8 1.7 collective-permute-done.partner_ref
  14.6 188.8 %all-gather.2.cloned.1.call-done.win_ref.wout_ref = bf16[2,2560,2560]{2,1,0:T(8,128)(2,1)} async-done(((bf16[2,80,2560]{2,1,0:T(8,128)(2,1)}), bf16[2,2560,2560]{2,1,0:T(8,128)(2,1)}) %all-gather.2.cloned.1.call-update) | async-done | bytes 26214416 | tf_op jit(solution)/shard_map/all_gather | solution.py:91
  203.4 0.0 copy-done
  203.4 13.4 %shard_map.55 = (bf16[256,1280]{1,0:T(8,128)(2,1)S(1)}, bf16[256,1280]{1,0:T(8,128)(2,1)S(1)}) custom-call(bf16[256,1280]{1,0:T(8,128)(2,1)S(1)} %broadcast_select_fusion.own_ref, bf16[256,1280]{1,0:T(8,128)(2,1)S(1)} %collective-permute-done.partner_ref, f32[1,2560]{1,0:T(1,128)S(1)} %copy-done, ...), custom_call_target="tpu_custom_call" | custom-call | tf_op jit(solution)/shard_map/pallas_call | solution.py:48
  216.8 1.1 collective-permute-start.1
  217.9 1.7 collective-permute-done.1
  219.6 0.3 add_convert_fusion.3
  220.0 1.3 collective-permute-start.2
  221.3 1.6 collective-permute-start.3
  222.8 2.3 collective-permute-done.3
  225.2 2.4 collective-permute-start.4
  227.6 7.5 %collective-permute-done.2 = bf16[216,1280]{1,0:T(8,128)(2,1)S(1)} collective-permute-done((bf16[216,1280]{1,0:T(8,128)(2,1)S(1)}, bf16[216,1280]{1,0:T(8,128)(2,1)S(1)}, u32[]{:S(2)}, u32[]{:S(2)}) %collective-permute-start.2) | collective-permute-done | bytes 552992 | tf_op jit(solution)/shard_map/ppermute | solution.py:76
  235.1 3.1 collective-permute-done.4
  238.2 1.3 collective-permute-start.5
  239.4 1.7 collective-permute-done.5.partner_ref
  241.2 13.4 %shard_map.56 = (bf16[256,1280]{1,0:T(8,128)(2,1)S(1)}, bf16[256,1280]{1,0:T(8,128)(2,1)S(1)}) custom-call(bf16[256,1280]{1,0:T(8,128)(2,1)S(1)} %constant_dynamic-update-slice_fusion.own_ref, bf16[256,1280]{1,0:T(8,128)(2,1)S(1)} %collective-permute-done.5.partner_ref, f32[1,2560]{1,0:T(1,128)S(1)} %copy-done, ...), custom_call_target="tpu_custom_call" | custom-call | tf_op jit(solution)/shard_map/pallas_call | solution.py:48
  254.6 0.5 collective-permute-start.6
  255.1 1.7 collective-permute-done.6
  256.8 0.4 select_select_fusion
  257.2 0.1 collective-permute-start.7
  257.3 2.7 collective-permute-start.8
  260.1 1.7 collective-permute-done.8
  261.7 2.1 collective-permute-start.9
  263.9 10.6 %collective-permute-done.7 = bf16[216,1280]{1,0:T(8,128)(2,1)S(1)} collective-permute-done((bf16[216,1280]{1,0:T(8,128)(2,1)S(1)}, bf16[216,1280]{1,0:T(8,128)(2,1)S(1)}, u32[]{:S(2)}, u32[]{:S(2)}) %collective-permute-start.7) | collective-permute-done | bytes 552992 | tf_op jit(solution)/shard_map/ppermute | solution.py:76
  274.5 0.0 collective-permute-done.9
  274.5 1.5 collective-permute-start.10
  276.0 1.7 collective-permute-done.10.partner_ref
  277.7 13.4 %shard_map.57 = (bf16[256,1280]{1,0:T(8,128)(2,1)S(1)}, bf16[256,1280]{1,0:T(8,128)(2,1)S(1)}) custom-call(bf16[256,1280]{1,0:T(8,128)(2,1)S(1)} %constant_dynamic-update-slice_fusion.2.own_ref, bf16[256,1280]{1,0:T(8,128)(2,1)S(1)} %collective-permute-done.10.partner_ref, f32[1,2560]{1,0:T(1,128)S(1)} %copy-done, ...), custom_call_target="tpu_custom_call" | custom-call | tf_op jit(solution)/shard_map/pallas_call | solution.py:48
  291.2 0.5 collective-permute-start.11
  291.6 1.7 collective-permute-done.11
  293.3 0.4 broadcast_select_fusion.1
  293.7 0.1 collective-permute-start.12
  293.8 2.7 collective-permute-start.13
  296.6 1.7 collective-permute-done.13
  298.3 2.1 collective-permute-start.14
  300.4 10.6 %collective-permute-done.12 = bf16[216,1280]{1,0:T(8,128)(2,1)S(1)} collective-permute-done((bf16[216,1280]{1,0:T(8,128)(2,1)S(1)}, bf16[216,1280]{1,0:T(8,128)(2,1)S(1)}, u32[]{:S(2)}, u32[]{:S(2)}) %collective-permute-start.12) | collective-permute-done | bytes 552992 | tf_op jit(solution)/shard_map/ppermute | solution.py:76
  311.0 0.0 collective-permute-done.14
  311.0 1.3 collective-permute-start.15
  312.3 1.7 collective-permute-done.15.partner_ref
  314.1 13.4 %shard_map.58 = (bf16[256,1280]{1,0:T(8,128)(2,1)S(1)}, bf16[256,1280]{1,0:T(8,128)(2,1)S(1)}) custom-call(bf16[256,1280]{1,0:T(8,128)(2,1)S(1)} %constant_dynamic-update-slice_fusion.4.own_ref, bf16[256,1280]{1,0:T(8,128)(2,1)S(1)} %collective-permute-done.15.partner_ref, f32[1,2560]{1,0:T(1,128)S(1)} %copy-done, ...), custom_call_target="tpu_custom_call" | custom-call | tf_op jit(solution)/shard_map/pallas_call | solution.py:48
  327.5 0.5 collective-permute-start.16
  327.9 1.7 collective-permute-done.16
  329.7 1.2 fusion
  (13 shorter events, 0.3 us)
Async XLA Ops:
  6.5 2.8 copy-start.1
  6.5 196.8 %all-gather.2.cloned.1.call-start = ((), (), s32[]{:S(2)}) async-start(), calls=%async_computation | async-start | bytes 27033600 | tf_op jit(solution)/shard_map/all_gather | solution.py:91
  8.7 194.7 %copy-start = (f32[1,2560]{1,0:T(1,128)S(1)}, f32[1,2560]{1,0:T(1,128)}, u32[]{:S(2)}) copy-start(f32[1,2560]{1,0:T(1,128)} %gain_ref.7) | copy-start | bytes 30724
  9.5 5.1 %collective-permute-start = (bf16[256,1280]{1,0:T(8,128)(2,1)S(1)}, bf16[256,1280]{1,0:T(8,128)(2,1)S(1)}, u32[]{:S(2)}, u32[]{:S(2)}) collective-permute-start(bf16[256,1280]{1,0:T(8,128)(2,1)S(1)} %broadcast_select_fusion.own_ref), channel_id=1, source_target_pairs={{0,1},{1,0},{2,3},{3,2},{4,5},{5,4},{6,7},{7,6},{8,9},{9,8},{10,11... | collective-permute-start | bytes 1966088 | tf_op jit(solution)/shard_map/ppermute | solution.py:98
  216.8 2.9 collective-permute-start.1
  220.0 15.0 %collective-permute-start.2 = (bf16[216,1280]{1,0:T(8,128)(2,1)S(1)}, bf16[216,1280]{1,0:T(8,128)(2,1)S(1)}, u32[]{:S(2)}, u32[]{:S(2)}) collective-permute-start(bf16[216,1280]{1,0:T(8,128)(2,1)S(1)} %slice.24), channel_id=1, source_target_pairs={{0,64},{64,128},{128,192},{192,0},{1,65},{65,129},{129,193},{193,1... | collective-permute-start | bytes 1658888 | tf_op jit(solution)/shard_map/ppermute | solution.py:76
  221.3 3.9 %collective-permute-start.3 = (bf16[40,1280]{1,0:T(8,128)(2,1)S(1)}, bf16[40,1280]{1,0:T(8,128)(2,1)S(1)}, u32[]{:S(2)}, u32[]{:S(2)}) collective-permute-start(bf16[40,1280]{1,0:T(8,128)(2,1)S(1)} %slice.25), channel_id=1, source_target_pairs={{0,192},{64,0},{128,64},{192,128},{1,193},{65,1},{129,65},{193,129... | collective-permute-start | bytes 307208 | tf_op jit(solution)/shard_map/ppermute | solution.py:76
  225.2 13.0 %collective-permute-start.4 = (bf16[40,1280]{1,0:T(8,128)(2,1)S(1)}, bf16[40,1280]{1,0:T(8,128)(2,1)S(1)}, u32[]{:S(2)}, u32[]{:S(2)}) collective-permute-start(bf16[40,1280]{1,0:T(8,128)(2,1)S(1)} %collective-permute-done.3), channel_id=1, source_target_pairs={{0,128},{64,192},{128,0},{192,64},{1,129},{65,193},{129,1},{193,65... | collective-permute-start | bytes 307208 | tf_op jit(solution)/shard_map/ppermute | solution.py:76
  238.2 3.0 collective-permute-start.5
  254.6 2.2 collective-permute-start.6
  257.2 17.2 %collective-permute-start.7 = (bf16[216,1280]{1,0:T(8,128)(2,1)S(1)}, bf16[216,1280]{1,0:T(8,128)(2,1)S(1)}, u32[]{:S(2)}, u32[]{:S(2)}) collective-permute-start(bf16[216,1280]{1,0:T(8,128)(2,1)S(1)} %slice.26), channel_id=1, source_target_pairs={{0,64},{64,128},{128,192},{192,0},{1,65},{65,129},{129,193},{193,1... | collective-permute-start | bytes 1658888 | tf_op jit(solution)/shard_map/ppermute | solution.py:76
  257.3 4.4 %collective-permute-start.8 = (bf16[40,1280]{1,0:T(8,128)(2,1)S(1)}, bf16[40,1280]{1,0:T(8,128)(2,1)S(1)}, u32[]{:S(2)}, u32[]{:S(2)}) collective-permute-start(bf16[40,1280]{1,0:T(8,128)(2,1)S(1)} %slice.27), channel_id=1, source_target_pairs={{0,192},{64,0},{128,64},{192,128},{1,193},{65,1},{129,65},{193,129... | collective-permute-start | bytes 307208 | tf_op jit(solution)/shard_map/ppermute | solution.py:76
  261.7 12.8 %collective-permute-start.9 = (bf16[40,1280]{1,0:T(8,128)(2,1)S(1)}, bf16[40,1280]{1,0:T(8,128)(2,1)S(1)}, u32[]{:S(2)}, u32[]{:S(2)}) collective-permute-start(bf16[40,1280]{1,0:T(8,128)(2,1)S(1)} %collective-permute-done.8), channel_id=1, source_target_pairs={{0,128},{64,192},{128,0},{192,64},{1,129},{65,193},{129,1},{193,65... | collective-permute-start | bytes 307208 | tf_op jit(solution)/shard_map/ppermute | solution.py:76
  274.5 3.2 collective-permute-start.10
  291.2 2.2 collective-permute-start.11
  293.7 17.2 %collective-permute-start.12 = (bf16[216,1280]{1,0:T(8,128)(2,1)S(1)}, bf16[216,1280]{1,0:T(8,128)(2,1)S(1)}, u32[]{:S(2)}, u32[]{:S(2)}) collective-permute-start(bf16[216,1280]{1,0:T(8,128)(2,1)S(1)} %slice.28), channel_id=1, source_target_pairs={{0,64},{64,128},{128,192},{192,0},{1,65},{65,129},{129,193},{193,1... | collective-permute-start | bytes 1658888 | tf_op jit(solution)/shard_map/ppermute | solution.py:76
  293.8 4.4 %collective-permute-start.13 = (bf16[40,1280]{1,0:T(8,128)(2,1)S(1)}, bf16[40,1280]{1,0:T(8,128)(2,1)S(1)}, u32[]{:S(2)}, u32[]{:S(2)}) collective-permute-start(bf16[40,1280]{1,0:T(8,128)(2,1)S(1)} %slice.29), channel_id=1, source_target_pairs={{0,192},{64,0},{128,64},{192,128},{1,193},{65,1},{129,65},{193,129... | collective-permute-start | bytes 307208 | tf_op jit(solution)/shard_map/ppermute | solution.py:76
  298.3 12.8 %collective-permute-start.14 = (bf16[40,1280]{1,0:T(8,128)(2,1)S(1)}, bf16[40,1280]{1,0:T(8,128)(2,1)S(1)}, u32[]{:S(2)}, u32[]{:S(2)}) collective-permute-start(bf16[40,1280]{1,0:T(8,128)(2,1)S(1)} %collective-permute-done.13), channel_id=1, source_target_pairs={{0,128},{64,192},{128,0},{192,64},{1,129},{65,193},{129,1},{193,65... | collective-permute-start | bytes 307208 | tf_op jit(solution)/shard_map/ppermute | solution.py:76
  311.0 3.0 collective-permute-start.15
  327.5 2.2 collective-permute-start.16
Sparse Core Ops, SparseCore 0:
  9.9 193.3 all-gather.1

commit v18 on v12

--- a/solution.py
+++ b/solution.py
@@ -68,7 +68,7 @@
     )(current, partner, gain, gathered, gathered)
 
 
-RELAYED = 32
+RELAYED = 40
 
 
 def shifted(value, axis, steps):

time: 333 us -> 336 us (level)
  starting transfers between devices: 37.4 us -> 41.6 us
    ppermute x4, starting transfers between devices: 6.96 us -> 10.9 us  [apply_layer(): partner = lax.ppermute(current, 'mp', [(0, 1), (1, 0)])]
where the time goes in v18:
time: 336 us
  waiting for transfers between devices  221 us (66%)
  Pallas kernels  53.7 us (16%)
  starting transfers between devices  41.6 us (12%)
  between operations  14.2 us (4%)
  other arithmetic  4.49 us (1%)
    all_gather x1, waiting for transfers between devices, per_device(): gathered = lax.all_gather(both, 'dp', axis=1, tiled=True)  189 us
    pallas_call x4, Pallas kernels, ffn(): pl.pallas_call(ffn_body, grid=(hidden_units // TILE,), in_specs=[pl.Block...  53.7 us
    ppermute x12, starting transfers between devices, shifted(): lax.ppermute(value, axis, [(source, (source + steps) % count) for source...  28.2 us
    ppermute x12, waiting for transfers between devices, shifted(): lax.ppermute(value, axis, [(source, (source + steps) % count) for source...  18.9 us
    ppermute x4, starting transfers between devices, apply_layer(): partner = lax.ppermute(current, 'mp', [(0, 1), (1, 0)])  10.9 us
    ppermute x4, waiting for transfers between devices, apply_layer(): other = lax.ppermute(send, 'mp', [(0, 1), (1, 0)])  6.9 us
    ppermute x4, waiting for transfers between devices, apply_layer(): partner = lax.ppermute(current, 'mp', [(0, 1), (1, 0)])  6.9 us
  transfers between devices with their start and end apart: 21, of which 18 were waited for; matrix products, arithmetic and copies ran while one was open for 0% of the time, Pallas kernels for 0%

profile of v18, /device:TPU:1, one launch (start us, length us, event | category | flops | bytes accessed | tf_op | source)
XLA Modules:
  0.0 335.8 jit_solution(12072436615719696345)
XLA Ops:
  6.5 0.0 copy-start.1
  6.5 0.0 all-gather.2.cloned.1.call-start
  6.5 2.2 pad_maximum_fusion
  8.7 0.0 copy-start
  8.7 0.0 all-gather.2.cloned.1.call-update
  9.4 0.0 copy-done.1
  9.4 0.1 broadcast_select_fusion.own_ref
  9.5 3.3 collective-permute-start
  12.9 1.7 collective-permute-done.partner_ref
  14.6 188.8 %all-gather.2.cloned.1.call-done.win_ref.wout_ref = bf16[2,2560,2560]{2,1,0:T(8,128)(2,1)} async-done(((bf16[2,80,2560]{2,1,0:T(8,128)(2,1)}), bf16[2,2560,2560]{2,1,0:T(8,128)(2,1)}) %all-gather.2.cloned.1.call-update) | async-done | bytes 26214416 | tf_op jit(solution)/shard_map/all_gather | solution.py:93
  203.4 0.0 copy-done
  203.4 13.4 %shard_map.55 = (bf16[256,1280]{1,0:T(8,128)(2,1)S(1)}, bf16[256,1280]{1,0:T(8,128)(2,1)S(1)}) custom-call(bf16[256,1280]{1,0:T(8,128)(2,1)S(1)} %broadcast_select_fusion.own_ref, bf16[256,1280]{1,0:T(8,128)(2,1)S(1)} %collective-permute-done.partner_ref, f32[1,2560]{1,0:T(1,128)S(1)} %copy-done, ...), custom_call_target="tpu_custom_call" | custom-call | tf_op jit(solution)/shard_map/pallas_call | solution.py:48
  216.8 1.1 collective-permute-start.1
  217.9 1.7 collective-permute-done.1
  219.6 0.3 add_convert_fusion.3
  220.0 1.3 collective-permute-start.2
  221.3 1.6 collective-permute-start.3
  222.8 2.3 collective-permute-done.3
  225.2 2.4 collective-permute-start.4
  227.6 1.7 collective-permute-done.4
  229.2 3.0 collective-permute-start.5
  232.3 2.8 collective-permute-done.2
  235.1 0.0 collective-permute-done.5
  235.1 2.8 collective-permute-start.6
  237.9 1.7 collective-permute-done.6.partner_ref
  239.6 13.4 %shard_map.56 = (bf16[256,1280]{1,0:T(8,128)(2,1)S(1)}, bf16[256,1280]{1,0:T(8,128)(2,1)S(1)}) custom-call(bf16[256,1280]{1,0:T(8,128)(2,1)S(1)} %constant_dynamic-update-slice_fusion.own_ref, bf16[256,1280]{1,0:T(8,128)(2,1)S(1)} %collective-permute-done.6.partner_ref, f32[1,2560]{1,0:T(1,128)S(1)} %copy-done, ...), custom_call_target="tpu_custom_call" | custom-call | tf_op jit(solution)/shard_map/pallas_call | solution.py:48
  253.0 0.5 collective-permute-start.7
  253.5 1.7 collective-permute-done.7
  255.2 0.4 select_select_fusion
  255.6 0.1 collective-permute-start.8
  255.7 3.4 %collective-permute-start.9 = (bf16[40,1280]{1,0:T(8,128)(2,1)S(1)}, bf16[40,1280]{1,0:T(8,128)(2,1)S(1)}, u32[]{:S(2)}, u32[]{:S(2)}) collective-permute-start(bf16[40,1280]{1,0:T(8,128)(2,1)S(1)} %slice.27), channel_id=1, source_target_pairs={{0,192},{64,0},{128,64},{192,128},{1,193},{65,1},{129,65},{193,129... | collective-permute-start | bytes 307208 | tf_op jit(solution)/shard_map/ppermute | solution.py:76
  259.2 1.9 collective-permute-done.9
  261.1 3.4 %collective-permute-start.10 = (bf16[40,1280]{1,0:T(8,128)(2,1)S(1)}, bf16[40,1280]{1,0:T(8,128)(2,1)S(1)}, u32[]{:S(2)}, u32[]{:S(2)}) collective-permute-start(bf16[40,1280]{1,0:T(8,128)(2,1)S(1)} %collective-permute-done.9), channel_id=1, source_target_pairs={{0,192},{64,0},{128,64},{192,128},{1,193},{65,1},{129,65},{193,129... | collective-permute-start | bytes 307208 | tf_op jit(solution)/shard_map/ppermute | solution.py:76
  264.5 1.7 collective-permute-done.10
  266.1 3.0 collective-permute-start.11
  269.2 2.5 collective-permute-done.8
  271.7 0.0 collective-permute-done.11
  271.7 2.4 collective-permute-start.12
  274.2 1.7 collective-permute-done.12.partner_ref
  275.9 13.4 %shard_map.57 = (bf16[256,1280]{1,0:T(8,128)(2,1)S(1)}, bf16[256,1280]{1,0:T(8,128)(2,1)S(1)}) custom-call(bf16[256,1280]{1,0:T(8,128)(2,1)S(1)} %constant_dynamic-update-slice_fusion.2.own_ref, bf16[256,1280]{1,0:T(8,128)(2,1)S(1)} %collective-permute-done.12.partner_ref, f32[1,2560]{1,0:T(1,128)S(1)} %copy-done, ...), custom_call_target="tpu_custom_call" | custom-call | tf_op jit(solution)/shard_map/pallas_call | solution.py:48
  289.3 0.5 collective-permute-start.13
  289.8 1.7 collective-permute-done.13
  291.5 0.4 broadcast_select_fusion.1
  291.9 0.1 collective-permute-start.14
  292.0 3.4 %collective-permute-start.15 = (bf16[40,1280]{1,0:T(8,128)(2,1)S(1)}, bf16[40,1280]{1,0:T(8,128)(2,1)S(1)}, u32[]{:S(2)}, u32[]{:S(2)}) collective-permute-start(bf16[40,1280]{1,0:T(8,128)(2,1)S(1)} %slice.29), channel_id=1, source_target_pairs={{0,192},{64,0},{128,64},{192,128},{1,193},{65,1},{129,65},{193,129... | collective-permute-start | bytes 307208 | tf_op jit(solution)/shard_map/ppermute | solution.py:76
  295.4 1.9 collective-permute-done.15
  297.3 3.4 %collective-permute-start.16 = (bf16[40,1280]{1,0:T(8,128)(2,1)S(1)}, bf16[40,1280]{1,0:T(8,128)(2,1)S(1)}, u32[]{:S(2)}, u32[]{:S(2)}) collective-permute-start(bf16[40,1280]{1,0:T(8,128)(2,1)S(1)} %collective-permute-done.15), channel_id=1, source_target_pairs={{0,192},{64,0},{128,64},{192,128},{1,193},{65,1},{129,65},{193,129... | collective-permute-start | bytes 307208 | tf_op jit(solution)/shard_map/ppermute | solution.py:76
  300.7 1.7 collective-permute-done.16
  302.4 3.0 collective-permute-start.17
  305.5 2.5 collective-permute-done.14
  308.0 0.0 collective-permute-done.17
  308.0 2.4 collective-permute-start.18
  310.4 1.7 collective-permute-done.18.partner_ref
  312.2 13.4 %shard_map.58 = (bf16[256,1280]{1,0:T(8,128)(2,1)S(1)}, bf16[256,1280]{1,0:T(8,128)(2,1)S(1)}) custom-call(bf16[256,1280]{1,0:T(8,128)(2,1)S(1)} %constant_dynamic-update-slice_fusion.4.own_ref, bf16[256,1280]{1,0:T(8,128)(2,1)S(1)} %collective-permute-done.18.partner_ref, f32[1,2560]{1,0:T(1,128)S(1)} %copy-done, ...), custom_call_target="tpu_custom_call" | custom-call | tf_op jit(solution)/shard_map/pallas_call | solution.py:48
  325.6 0.5 collective-permute-start.19
  326.0 1.7 collective-permute-done.19
  327.8 1.2 fusion
  (13 shorter events, 0.3 us)
Async XLA Ops:
  6.5 2.9 copy-start.1
  6.5 196.8 %all-gather.2.cloned.1.call-start = ((), (), s32[]{:S(2)}) async-start(), calls=%async_computation | async-start | bytes 27033600 | tf_op jit(solution)/shard_map/all_gather | solution.py:93
  8.7 194.6 %copy-start = (f32[1,2560]{1,0:T(1,128)S(1)}, f32[1,2560]{1,0:T(1,128)}, u32[]{:S(2)}) copy-start(f32[1,2560]{1,0:T(1,128)} %gain_ref.7) | copy-start | bytes 30724
  9.5 5.1 %collective-permute-start = (bf16[256,1280]{1,0:T(8,128)(2,1)S(1)}, bf16[256,1280]{1,0:T(8,128)(2,1)S(1)}, u32[]{:S(2)}, u32[]{:S(2)}) collective-permute-start(bf16[256,1280]{1,0:T(8,128)(2,1)S(1)} %broadcast_select_fusion.own_ref), channel_id=1, source_target_pairs={{0,1},{1,0},{2,3},{3,2},{4,5},{5,4},{6,7},{7,6},{8,9},{9,8},{10,11... | collective-permute-start | bytes 1966088 | tf_op jit(solution)/shard_map/ppermute | solution.py:100
  216.8 2.9 collective-permute-start.1
  220.0 15.0 %collective-permute-start.2 = (bf16[216,1280]{1,0:T(8,128)(2,1)S(1)}, bf16[216,1280]{1,0:T(8,128)(2,1)S(1)}, u32[]{:S(2)}, u32[]{:S(2)}) collective-permute-start(bf16[216,1280]{1,0:T(8,128)(2,1)S(1)} %slice.24), channel_id=1, source_target_pairs={{0,64},{64,128},{128,192},{192,0},{1,65},{65,129},{129,193},{193,1... | collective-permute-start | bytes 1658888 | tf_op jit(solution)/shard_map/ppermute | solution.py:76
  221.3 3.9 %collective-permute-start.3 = (bf16[40,1280]{1,0:T(8,128)(2,1)S(1)}, bf16[40,1280]{1,0:T(8,128)(2,1)S(1)}, u32[]{:S(2)}, u32[]{:S(2)}) collective-permute-start(bf16[40,1280]{1,0:T(8,128)(2,1)S(1)} %slice.25), channel_id=1, source_target_pairs={{0,192},{64,0},{128,64},{192,128},{1,193},{65,1},{129,65},{193,129... | collective-permute-start | bytes 307208 | tf_op jit(solution)/shard_map/ppermute | solution.py:76
  225.2 4.1 %collective-permute-start.4 = (bf16[40,1280]{1,0:T(8,128)(2,1)S(1)}, bf16[40,1280]{1,0:T(8,128)(2,1)S(1)}, u32[]{:S(2)}, u32[]{:S(2)}) collective-permute-start(bf16[40,1280]{1,0:T(8,128)(2,1)S(1)} %collective-permute-done.3), channel_id=1, source_target_pairs={{0,192},{64,0},{128,64},{192,128},{1,193},{65,1},{129,65},{193,129... | collective-permute-start | bytes 307208 | tf_op jit(solution)/shard_map/ppermute | solution.py:76
  229.2 5.8 %collective-permute-start.5 = (bf16[40,1280]{1,0:T(8,128)(2,1)S(1)}, bf16[40,1280]{1,0:T(8,128)(2,1)S(1)}, u32[]{:S(2)}, u32[]{:S(2)}) collective-permute-start(bf16[40,1280]{1,0:T(8,128)(2,1)S(1)} %collective-permute-done.4), channel_id=1, source_target_pairs={{0,192},{64,0},{128,64},{192,128},{1,193},{65,1},{129,65},{193,129... | collective-permute-start | bytes 307208 | tf_op jit(solution)/shard_map/ppermute | solution.py:76
  235.1 4.5 %collective-permute-start.6 = (bf16[256,1280]{1,0:T(8,128)(2,1)S(1)}, bf16[256,1280]{1,0:T(8,128)(2,1)S(1)}, u32[]{:S(2)}, u32[]{:S(2)}) collective-permute-start(bf16[256,1280]{1,0:T(8,128)(2,1)S(1)} %constant_dynamic-update-slice_fusion.own_ref), channel_id=1, source_target_pairs={{0,1},{1,0},{2,3},{3,2},{4,5},{5,4},{6,7},{7,6},{8,9},{9,8},{10,11... | collective-permute-start | bytes 1966088 | tf_op jit(solution)/shard_map/ppermute | solution.py:100
  253.0 2.2 collective-permute-start.7
  255.6 16.0 %collective-permute-start.8 = (bf16[216,1280]{1,0:T(8,128)(2,1)S(1)}, bf16[216,1280]{1,0:T(8,128)(2,1)S(1)}, u32[]{:S(2)}, u32[]{:S(2)}) collective-permute-start(bf16[216,1280]{1,0:T(8,128)(2,1)S(1)} %slice.26), channel_id=1, source_target_pairs={{0,64},{64,128},{128,192},{192,0},{1,65},{65,129},{129,193},{193,1... | collective-permute-start | bytes 1658888 | tf_op jit(solution)/shard_map/ppermute | solution.py:76
  255.7 5.3 %collective-permute-start.9 = (bf16[40,1280]{1,0:T(8,128)(2,1)S(1)}, bf16[40,1280]{1,0:T(8,128)(2,1)S(1)}, u32[]{:S(2)}, u32[]{:S(2)}) collective-permute-start(bf16[40,1280]{1,0:T(8,128)(2,1)S(1)} %slice.27), channel_id=1, source_target_pairs={{0,192},{64,0},{128,64},{192,128},{1,193},{65,1},{129,65},{193,129... | collective-permute-start | bytes 307208 | tf_op jit(solution)/shard_map/ppermute | solution.py:76
  261.1 5.1 %collective-permute-start.10 = (bf16[40,1280]{1,0:T(8,128)(2,1)S(1)}, bf16[40,1280]{1,0:T(8,128)(2,1)S(1)}, u32[]{:S(2)}, u32[]{:S(2)}) collective-permute-start(bf16[40,1280]{1,0:T(8,128)(2,1)S(1)} %collective-permute-done.9), channel_id=1, source_target_pairs={{0,192},{64,0},{128,64},{192,128},{1,193},{65,1},{129,65},{193,129... | collective-permute-start | bytes 307208 | tf_op jit(solution)/shard_map/ppermute | solution.py:76
  266.1 5.6 %collective-permute-start.11 = (bf16[40,1280]{1,0:T(8,128)(2,1)S(1)}, bf16[40,1280]{1,0:T(8,128)(2,1)S(1)}, u32[]{:S(2)}, u32[]{:S(2)}) collective-permute-start(bf16[40,1280]{1,0:T(8,128)(2,1)S(1)} %collective-permute-done.10), channel_id=1, source_target_pairs={{0,192},{64,0},{128,64},{192,128},{1,193},{65,1},{129,65},{193,129... | collective-permute-start | bytes 307208 | tf_op jit(solution)/shard_map/ppermute | solution.py:76
  271.7 4.2 %collective-permute-start.12 = (bf16[256,1280]{1,0:T(8,128)(2,1)S(1)}, bf16[256,1280]{1,0:T(8,128)(2,1)S(1)}, u32[]{:S(2)}, u32[]{:S(2)}) collective-permute-start(bf16[256,1280]{1,0:T(8,128)(2,1)S(1)} %constant_dynamic-update-slice_fusion.2.own_ref), channel_id=1, source_target_pairs={{0,1},{1,0},{2,3},{3,2},{4,5},{5,4},{6,7},{7,6},{8,9},{9,8},{10,11... | collective-permute-start | bytes 1966088 | tf_op jit(solution)/shard_map/ppermute | solution.py:100
  289.3 2.2 collective-permute-start.13
  291.9 16.0 %collective-permute-start.14 = (bf16[216,1280]{1,0:T(8,128)(2,1)S(1)}, bf16[216,1280]{1,0:T(8,128)(2,1)S(1)}, u32[]{:S(2)}, u32[]{:S(2)}) collective-permute-start(bf16[216,1280]{1,0:T(8,128)(2,1)S(1)} %slice.28), channel_id=1, source_target_pairs={{0,64},{64,128},{128,192},{192,0},{1,65},{65,129},{129,193},{193,1... | collective-permute-start | bytes 1658888 | tf_op jit(solution)/shard_map/ppermute | solution.py:76
  292.0 5.3 %collective-permute-start.15 = (bf16[40,1280]{1,0:T(8,128)(2,1)S(1)}, bf16[40,1280]{1,0:T(8,128)(2,1)S(1)}, u32[]{:S(2)}, u32[]{:S(2)}) collective-permute-start(bf16[40,1280]{1,0:T(8,128)(2,1)S(1)} %slice.29), channel_id=1, source_target_pairs={{0,192},{64,0},{128,64},{192,128},{1,193},{65,1},{129,65},{193,129... | collective-permute-start | bytes 307208 | tf_op jit(solution)/shard_map/ppermute | solution.py:76
  297.3 5.1 %collective-permute-start.16 = (bf16[40,1280]{1,0:T(8,128)(2,1)S(1)}, bf16[40,1280]{1,0:T(8,128)(2,1)S(1)}, u32[]{:S(2)}, u32[]{:S(2)}) collective-permute-start(bf16[40,1280]{1,0:T(8,128)(2,1)S(1)} %collective-permute-done.15), channel_id=1, source_target_pairs={{0,192},{64,0},{128,64},{192,128},{1,193},{65,1},{129,65},{193,129... | collective-permute-start | bytes 307208 | tf_op jit(solution)/shard_map/ppermute | solution.py:76
  302.4 5.6 %collective-permute-start.17 = (bf16[40,1280]{1,0:T(8,128)(2,1)S(1)}, bf16[40,1280]{1,0:T(8,128)(2,1)S(1)}, u32[]{:S(2)}, u32[]{:S(2)}) collective-permute-start(bf16[40,1280]{1,0:T(8,128)(2,1)S(1)} %collective-permute-done.16), channel_id=1, source_target_pairs={{0,192},{64,0},{128,64},{192,128},{1,193},{65,1},{129,65},{193,129... | collective-permute-start | bytes 307208 | tf_op jit(solution)/shard_map/ppermute | solution.py:76
  308.0 4.2 %collective-permute-start.18 = (bf16[256,1280]{1,0:T(8,128)(2,1)S(1)}, bf16[256,1280]{1,0:T(8,128)(2,1)S(1)}, u32[]{:S(2)}, u32[]{:S(2)}) collective-permute-start(bf16[256,1280]{1,0:T(8,128)(2,1)S(1)} %constant_dynamic-update-slice_fusion.4.own_ref), channel_id=1, source_target_pairs={{0,1},{1,0},{2,3},{3,2},{4,5},{5,4},{6,7},{7,6},{8,9},{9,8},{10,11... | collective-permute-start | bytes 1966088 | tf_op jit(solution)/shard_map/ppermute | solution.py:100
  325.6 2.2 collective-permute-start.19
Sparse Core Ops, SparseCore 0:
  9.9 193.3 all-gather.1

commit v19 on v18

--- a/solution.py
+++ b/solution.py
@@ -68,7 +68,7 @@
     )(current, partner, gain, gathered, gathered)
 
 
-RELAYED = 40
+RELAYED = 24
 
 
 def shifted(value, axis, steps):

time: 336 us -> 333 us (level)
  starting transfers between devices: 41.6 us -> 35.6 us
    ppermute x4, starting transfers between devices: 10.9 us -> 7.19 us  [apply_layer(): partner = lax.ppermute(current, 'mp', [(0, 1), (1, 0)])]
where the time goes in v19:
time: 333 us
  waiting for transfers between devices  224 us (67%)
  Pallas kernels  53.6 us (16%)
  starting transfers between devices  35.6 us (11%)
  between operations  14.2 us (4%)
  other arithmetic  4.49 us (1%)
    all_gather x1, waiting for transfers between devices, per_device(): gathered = lax.all_gather(both, 'dp', axis=1, tiled=True)  189 us
    pallas_call x4, Pallas kernels, ffn(): pl.pallas_call(ffn_body, grid=(hidden_units // TILE,), in_specs=[pl.Block...  53.6 us
    ppermute x12, starting transfers between devices, shifted(): lax.ppermute(value, axis, [(source, (source + steps) % count) for source...  25.9 us
    ppermute x12, waiting for transfers between devices, shifted(): lax.ppermute(value, axis, [(source, (source + steps) % count) for source...  21.8 us
    ppermute x4, starting transfers between devices, apply_layer(): partner = lax.ppermute(current, 'mp', [(0, 1), (1, 0)])  7.19 us
    ppermute x4, waiting for transfers between devices, apply_layer(): other = lax.ppermute(send, 'mp', [(0, 1), (1, 0)])  6.9 us
    ppermute x4, waiting for transfers between devices, apply_layer(): partner = lax.ppermute(current, 'mp', [(0, 1), (1, 0)])  6.9 us
  transfers between devices with their start and end apart: 21, of which 18 were waited for; matrix products, arithmetic and copies ran while one was open for 0% of the time, Pallas kernels for 0%

profile of v19, /device:TPU:1, one launch (start us, length us, event | category | flops | bytes accessed | tf_op | source)
XLA Modules:
  0.0 332.7 jit_solution(6871692518135594397)
XLA Ops:
  6.5 0.0 copy-start.1
  6.5 0.0 all-gather.2.cloned.1.call-start
  6.5 2.2 pad_maximum_fusion
  8.7 0.0 copy-start
  8.7 0.0 all-gather.2.cloned.1.call-update
  9.4 0.0 copy-done.1
  9.4 0.1 broadcast_select_fusion.own_ref
  9.5 3.3 %collective-permute-start = (bf16[256,1280]{1,0:T(8,128)(2,1)S(1)}, bf16[256,1280]{1,0:T(8,128)(2,1)S(1)}, u32[]{:S(2)}, u32[]{:S(2)}) collective-permute-start(bf16[256,1280]{1,0:T(8,128)(2,1)S(1)} %broadcast_select_fusion.own_ref), channel_id=1, source_target_pairs={{0,1},{1,0},{2,3},{3,2},{4,5},{5,4},{6,7},{7,6},{8,9},{9,8},{10,11... | collective-permute-start | bytes 1966088 | tf_op jit(solution)/shard_map/ppermute | solution.py:100
  12.9 1.7 collective-permute-done.partner_ref
  14.6 188.8 %all-gather.2.cloned.1.call-done.win_ref.wout_ref = bf16[2,2560,2560]{2,1,0:T(8,128)(2,1)} async-done(((bf16[2,80,2560]{2,1,0:T(8,128)(2,1)}), bf16[2,2560,2560]{2,1,0:T(8,128)(2,1)}) %all-gather.2.cloned.1.call-update) | async-done | bytes 26214416 | tf_op jit(solution)/shard_map/all_gather | solution.py:93
  203.4 0.0 copy-done
  203.4 13.4 %shard_map.55 = (bf16[256,1280]{1,0:T(8,128)(2,1)S(1)}, bf16[256,1280]{1,0:T(8,128)(2,1)S(1)}) custom-call(bf16[256,1280]{1,0:T(8,128)(2,1)S(1)} %broadcast_select_fusion.own_ref, bf16[256,1280]{1,0:T(8,128)(2,1)S(1)} %collective-permute-done.partner_ref, f32[1,2560]{1,0:T(1,128)S(1)} %copy-done, ...), custom_call_target="tpu_custom_call" | custom-call | tf_op jit(solution)/shard_map/pallas_call | solution.py:48
  216.8 1.1 collective-permute-start.1
  217.9 1.7 collective-permute-done.1
  219.6 0.3 add_convert_fusion.3
  220.0 1.3 collective-permute-start.2
  221.3 1.5 collective-permute-start.3
  222.8 1.6 collective-permute-done.3
  224.3 2.7 collective-permute-start.4
  227.0 1.3 collective-permute-done.4
  228.3 3.0 collective-permute-start.5
  231.3 4.6 %collective-permute-done.2 = bf16[232,1280]{1,0:T(8,128)(2,1)S(1)} collective-permute-done((bf16[232,1280]{1,0:T(8,128)(2,1)S(1)}, bf16[232,1280]{1,0:T(8,128)(2,1)S(1)}, u32[]{:S(2)}, u32[]{:S(2)}) %collective-permute-start.2) | collective-permute-done | bytes 593952 | tf_op jit(solution)/shard_map/ppermute | solution.py:76
  236.0 0.0 collective-permute-done.5
  236.0 1.3 collective-permute-start.6
  237.3 1.7 collective-permute-done.6.partner_ref
  239.0 13.4 %shard_map.56 = (bf16[256,1280]{1,0:T(8,128)(2,1)S(1)}, bf16[256,1280]{1,0:T(8,128)(2,1)S(1)}) custom-call(bf16[256,1280]{1,0:T(8,128)(2,1)S(1)} %constant_dynamic-update-slice_fusion.own_ref, bf16[256,1280]{1,0:T(8,128)(2,1)S(1)} %collective-permute-done.6.partner_ref, f32[1,2560]{1,0:T(1,128)S(1)} %copy-done, ...), custom_call_target="tpu_custom_call" | custom-call | tf_op jit(solution)/shard_map/pallas_call | solution.py:48
  252.4 0.5 collective-permute-start.7
  252.9 1.7 collective-permute-done.7
  254.6 0.4 select_select_fusion
  255.0 0.1 collective-permute-start.8
  255.1 2.7 collective-permute-start.9
  257.8 1.3 collective-permute-done.9
  259.1 3.0 collective-permute-start.10
  262.1 1.3 collective-permute-done.10
  263.4 3.0 collective-permute-start.11
  266.4 4.6 %collective-permute-done.8 = bf16[232,1280]{1,0:T(8,128)(2,1)S(1)} collective-permute-done((bf16[232,1280]{1,0:T(8,128)(2,1)S(1)}, bf16[232,1280]{1,0:T(8,128)(2,1)S(1)}, u32[]{:S(2)}, u32[]{:S(2)}) %collective-permute-start.8) | collective-permute-done | bytes 593952 | tf_op jit(solution)/shard_map/ppermute | solution.py:76
  271.0 0.0 collective-permute-done.11
  271.0 1.3 collective-permute-start.12
  272.3 1.7 collective-permute-done.12.partner_ref
  274.0 13.4 %shard_map.57 = (bf16[256,1280]{1,0:T(8,128)(2,1)S(1)}, bf16[256,1280]{1,0:T(8,128)(2,1)S(1)}) custom-call(bf16[256,1280]{1,0:T(8,128)(2,1)S(1)} %constant_dynamic-update-slice_fusion.2.own_ref, bf16[256,1280]{1,0:T(8,128)(2,1)S(1)} %collective-permute-done.12.partner_ref, f32[1,2560]{1,0:T(1,128)S(1)} %copy-done, ...), custom_call_target="tpu_custom_call" | custom-call | tf_op jit(solution)/shard_map/pallas_call | solution.py:48
  287.5 0.5 collective-permute-start.13
  287.9 1.7 collective-permute-done.13
  289.6 0.4 broadcast_select_fusion.1
  290.1 0.1 collective-permute-start.14
  290.2 2.7 collective-permute-start.15
  292.8 1.3 collective-permute-done.15
  294.1 3.0 collective-permute-start.16
  297.1 1.3 collective-permute-done.16
  298.4 3.0 collective-permute-start.17
  301.4 4.6 %collective-permute-done.14 = bf16[232,1280]{1,0:T(8,128)(2,1)S(1)} collective-permute-done((bf16[232,1280]{1,0:T(8,128)(2,1)S(1)}, bf16[232,1280]{1,0:T(8,128)(2,1)S(1)}, u32[]{:S(2)}, u32[]{:S(2)}) %collective-permute-start.14) | collective-permute-done | bytes 593952 | tf_op jit(solution)/shard_map/ppermute | solution.py:76
  306.0 0.0 collective-permute-done.17
  306.0 1.3 collective-permute-start.18
  307.3 1.7 collective-permute-done.18.partner_ref
  309.1 13.4 %shard_map.58 = (bf16[256,1280]{1,0:T(8,128)(2,1)S(1)}, bf16[256,1280]{1,0:T(8,128)(2,1)S(1)}) custom-call(bf16[256,1280]{1,0:T(8,128)(2,1)S(1)} %constant_dynamic-update-slice_fusion.4.own_ref, bf16[256,1280]{1,0:T(8,128)(2,1)S(1)} %collective-permute-done.18.partner_ref, f32[1,2560]{1,0:T(1,128)S(1)} %copy-done, ...), custom_call_target="tpu_custom_call" | custom-call | tf_op jit(solution)/shard_map/pallas_call | solution.py:48
  322.5 0.5 collective-permute-start.19
  323.0 1.7 collective-permute-done.19
  324.7 1.2 fusion
  (13 shorter events, 0.3 us)
Async XLA Ops:
  6.5 2.9 copy-start.1
  6.5 196.8 %all-gather.2.cloned.1.call-start = ((), (), s32[]{:S(2)}) async-start(), calls=%async_computation | async-start | bytes 27033600 | tf_op jit(solution)/shard_map/all_gather | solution.py:93
  8.7 194.6 %copy-start = (f32[1,2560]{1,0:T(1,128)S(1)}, f32[1,2560]{1,0:T(1,128)}, u32[]{:S(2)}) copy-start(f32[1,2560]{1,0:T(1,128)} %gain_ref.7) | copy-start | bytes 30724
  9.5 5.1 %collective-permute-start = (bf16[256,1280]{1,0:T(8,128)(2,1)S(1)}, bf16[256,1280]{1,0:T(8,128)(2,1)S(1)}, u32[]{:S(2)}, u32[]{:S(2)}) collective-permute-start(bf16[256,1280]{1,0:T(8,128)(2,1)S(1)} %broadcast_select_fusion.own_ref), channel_id=1, source_target_pairs={{0,1},{1,0},{2,3},{3,2},{4,5},{5,4},{6,7},{7,6},{8,9},{9,8},{10,11... | collective-permute-start | bytes 1966088 | tf_op jit(solution)/shard_map/ppermute | solution.py:100
  216.8 2.9 collective-permute-start.1
  220.0 15.9 %collective-permute-start.2 = (bf16[232,1280]{1,0:T(8,128)(2,1)S(1)}, bf16[232,1280]{1,0:T(8,128)(2,1)S(1)}, u32[]{:S(2)}, u32[]{:S(2)}) collective-permute-start(bf16[232,1280]{1,0:T(8,128)(2,1)S(1)} %slice.24), channel_id=1, source_target_pairs={{0,64},{64,128},{128,192},{192,0},{1,65},{65,129},{129,193},{193,1... | collective-permute-start | bytes 1781768 | tf_op jit(solution)/shard_map/ppermute | solution.py:76
  221.3 3.1 collective-permute-start.3
  224.3 4.0 %collective-permute-start.4 = (bf16[24,1280]{1,0:T(8,128)(2,1)S(1)}, bf16[24,1280]{1,0:T(8,128)(2,1)S(1)}, u32[]{:S(2)}, u32[]{:S(2)}) collective-permute-start(bf16[24,1280]{1,0:T(8,128)(2,1)S(1)} %collective-permute-done.3), channel_id=1, source_target_pairs={{0,192},{64,0},{128,64},{192,128},{1,193},{65,1},{129,65},{193,129... | collective-permute-start | bytes 184328 | tf_op jit(solution)/shard_map/ppermute | solution.py:76
  228.3 7.6 %collective-permute-start.5 = (bf16[24,1280]{1,0:T(8,128)(2,1)S(1)}, bf16[24,1280]{1,0:T(8,128)(2,1)S(1)}, u32[]{:S(2)}, u32[]{:S(2)}) collective-permute-start(bf16[24,1280]{1,0:T(8,128)(2,1)S(1)} %collective-permute-done.4), channel_id=1, source_target_pairs={{0,192},{64,0},{128,64},{192,128},{1,193},{65,1},{129,65},{193,129... | collective-permute-start | bytes 184328 | tf_op jit(solution)/shard_map/ppermute | solution.py:76
  236.0 3.0 collective-permute-start.6
  252.4 2.2 collective-permute-start.7
  255.0 15.9 %collective-permute-start.8 = (bf16[232,1280]{1,0:T(8,128)(2,1)S(1)}, bf16[232,1280]{1,0:T(8,128)(2,1)S(1)}, u32[]{:S(2)}, u32[]{:S(2)}) collective-permute-start(bf16[232,1280]{1,0:T(8,128)(2,1)S(1)} %slice.26), channel_id=1, source_target_pairs={{0,64},{64,128},{128,192},{192,0},{1,65},{65,129},{129,193},{193,1... | collective-permute-start | bytes 1781768 | tf_op jit(solution)/shard_map/ppermute | solution.py:76
  255.1 3.9 %collective-permute-start.9 = (bf16[24,1280]{1,0:T(8,128)(2,1)S(1)}, bf16[24,1280]{1,0:T(8,128)(2,1)S(1)}, u32[]{:S(2)}, u32[]{:S(2)}) collective-permute-start(bf16[24,1280]{1,0:T(8,128)(2,1)S(1)} %slice.27), channel_id=1, source_target_pairs={{0,192},{64,0},{128,64},{192,128},{1,193},{65,1},{129,65},{193,129... | collective-permute-start | bytes 184328 | tf_op jit(solution)/shard_map/ppermute | solution.py:76
  259.1 4.3 %collective-permute-start.10 = (bf16[24,1280]{1,0:T(8,128)(2,1)S(1)}, bf16[24,1280]{1,0:T(8,128)(2,1)S(1)}, u32[]{:S(2)}, u32[]{:S(2)}) collective-permute-start(bf16[24,1280]{1,0:T(8,128)(2,1)S(1)} %collective-permute-done.9), channel_id=1, source_target_pairs={{0,192},{64,0},{128,64},{192,128},{1,193},{65,1},{129,65},{193,129... | collective-permute-start | bytes 184328 | tf_op jit(solution)/shard_map/ppermute | solution.py:76
  263.4 7.6 %collective-permute-start.11 = (bf16[24,1280]{1,0:T(8,128)(2,1)S(1)}, bf16[24,1280]{1,0:T(8,128)(2,1)S(1)}, u32[]{:S(2)}, u32[]{:S(2)}) collective-permute-start(bf16[24,1280]{1,0:T(8,128)(2,1)S(1)} %collective-permute-done.10), channel_id=1, source_target_pairs={{0,192},{64,0},{128,64},{192,128},{1,193},{65,1},{129,65},{193,129... | collective-permute-start | bytes 184328 | tf_op jit(solution)/shard_map/ppermute | solution.py:76
  271.0 3.0 collective-permute-start.12
  287.5 2.2 collective-permute-start.13
  290.1 15.9 %collective-permute-start.14 = (bf16[232,1280]{1,0:T(8,128)(2,1)S(1)}, bf16[232,1280]{1,0:T(8,128)(2,1)S(1)}, u32[]{:S(2)}, u32[]{:S(2)}) collective-permute-start(bf16[232,1280]{1,0:T(8,128)(2,1)S(1)} %slice.28), channel_id=1, source_target_pairs={{0,64},{64,128},{128,192},{192,0},{1,65},{65,129},{129,193},{193,1... | collective-permute-start | bytes 1781768 | tf_op jit(solution)/shard_map/ppermute | solution.py:76
  290.2 3.9 %collective-permute-start.15 = (bf16[24,1280]{1,0:T(8,128)(2,1)S(1)}, bf16[24,1280]{1,0:T(8,128)(2,1)S(1)}, u32[]{:S(2)}, u32[]{:S(2)}) collective-permute-start(bf16[24,1280]{1,0:T(8,128)(2,1)S(1)} %slice.29), channel_id=1, source_target_pairs={{0,192},{64,0},{128,64},{192,128},{1,193},{65,1},{129,65},{193,129... | collective-permute-start | bytes 184328 | tf_op jit(solution)/shard_map/ppermute | solution.py:76
  294.1 4.3 %collective-permute-start.16 = (bf16[24,1280]{1,0:T(8,128)(2,1)S(1)}, bf16[24,1280]{1,0:T(8,128)(2,1)S(1)}, u32[]{:S(2)}, u32[]{:S(2)}) collective-permute-start(bf16[24,1280]{1,0:T(8,128)(2,1)S(1)} %collective-permute-done.15), channel_id=1, source_target_pairs={{0,192},{64,0},{128,64},{192,128},{1,193},{65,1},{129,65},{193,129... | collective-permute-start | bytes 184328 | tf_op jit(solution)/shard_map/ppermute | solution.py:76
  298.4 7.6 %collective-permute-start.17 = (bf16[24,1280]{1,0:T(8,128)(2,1)S(1)}, bf16[24,1280]{1,0:T(8,128)(2,1)S(1)}, u32[]{:S(2)}, u32[]{:S(2)}) collective-permute-start(bf16[24,1280]{1,0:T(8,128)(2,1)S(1)} %collective-permute-done.16), channel_id=1, source_target_pairs={{0,192},{64,0},{128,64},{192,128},{1,193},{65,1},{129,65},{193,129... | collective-permute-start | bytes 184328 | tf_op jit(solution)/shard_map/ppermute | solution.py:76
  306.0 3.0 collective-permute-start.18
  322.5 2.2 collective-permute-start.19
Sparse Core Ops, SparseCore 0:
  9.9 193.3 all-gather.1

commit v20 on v19

--- a/solution.py
+++ b/solution.py
@@ -68,7 +68,7 @@
     )(current, partner, gain, gathered, gathered)
 
 
-RELAYED = 24
+RELAYED = 16
 
 
 def shifted(value, axis, steps):

time: 333 us -> 334 us (level)
  no operation moved by 1% of the time
where the time goes in v20:
time: 334 us
  waiting for transfers between devices  226 us (68%)
  Pallas kernels  53.7 us (16%)
  starting transfers between devices  35.4 us (11%)
  between operations  14.2 us (4%)
  other arithmetic  4.49 us (1%)
    all_gather x1, waiting for transfers between devices, per_device(): gathered = lax.all_gather(both, 'dp', axis=1, tiled=True)  189 us
    pallas_call x4, Pallas kernels, ffn(): pl.pallas_call(ffn_body, grid=(hidden_units // TILE,), in_specs=[pl.Block...  53.7 us
    ppermute x12, starting transfers between devices, shifted(): lax.ppermute(value, axis, [(source, (source + steps) % count) for source...  25.7 us
    ppermute x12, waiting for transfers between devices, shifted(): lax.ppermute(value, axis, [(source, (source + steps) % count) for source...  23.3 us
    ppermute x4, starting transfers between devices, apply_layer(): partner = lax.ppermute(current, 'mp', [(0, 1), (1, 0)])  7.19 us
    ppermute x4, waiting for transfers between devices, apply_layer(): other = lax.ppermute(send, 'mp', [(0, 1), (1, 0)])  6.91 us
    ppermute x4, waiting for transfers between devices, apply_layer(): partner = lax.ppermute(current, 'mp', [(0, 1), (1, 0)])  6.9 us
  transfers between devices with their start and end apart: 21, of which 18 were waited for; matrix products, arithmetic and copies ran while one was open for 0% of the time, Pallas kernels for 0%

profile of v20, /device:TPU:1, one launch (start us, length us, event | category | flops | bytes accessed | tf_op | source)
XLA Modules:
  0.0 334.0 jit_solution(8844311932600581744)
XLA Ops:
  6.5 0.0 copy-start.1
  6.5 0.0 all-gather.2.cloned.1.call-start
  6.5 2.2 pad_maximum_fusion
  8.7 0.0 copy-start
  8.7 0.0 all-gather.2.cloned.1.call-update
  9.4 0.0 copy-done.1
  9.4 0.1 broadcast_select_fusion.own_ref
  9.5 3.3 collective-permute-start
  12.9 1.7 collective-permute-done.partner_ref
  14.6 188.8 %all-gather.2.cloned.1.call-done.win_ref.wout_ref = bf16[2,2560,2560]{2,1,0:T(8,128)(2,1)} async-done(((bf16[2,80,2560]{2,1,0:T(8,128)(2,1)}), bf16[2,2560,2560]{2,1,0:T(8,128)(2,1)}) %all-gather.2.cloned.1.call-update) | async-done | bytes 26214416 | tf_op jit(solution)/shard_map/all_gather | solution.py:93
  203.4 0.0 copy-done
  203.4 13.4 %shard_map.55 = (bf16[256,1280]{1,0:T(8,128)(2,1)S(1)}, bf16[256,1280]{1,0:T(8,128)(2,1)S(1)}) custom-call(bf16[256,1280]{1,0:T(8,128)(2,1)S(1)} %broadcast_select_fusion.own_ref, bf16[256,1280]{1,0:T(8,128)(2,1)S(1)} %collective-permute-done.partner_ref, f32[1,2560]{1,0:T(1,128)S(1)} %copy-done, ...), custom_call_target="tpu_custom_call" | custom-call | tf_op jit(solution)/shard_map/pallas_call | solution.py:48
  216.8 1.1 collective-permute-start.1
  217.9 1.7 collective-permute-done.1
  219.6 0.3 add_convert_fusion.3
  220.0 1.3 collective-permute-start.2
  221.3 1.5 collective-permute-start.3
  222.8 1.4 collective-permute-done.3
  224.1 2.7 collective-permute-start.4
  226.8 1.1 collective-permute-done.4
  227.9 3.0 collective-permute-start.5
  230.9 5.5 %collective-permute-done.2 = bf16[240,1280]{1,0:T(8,128)(2,1)S(1)} collective-permute-done((bf16[240,1280]{1,0:T(8,128)(2,1)S(1)}, bf16[240,1280]{1,0:T(8,128)(2,1)S(1)}, u32[]{:S(2)}, u32[]{:S(2)}) %collective-permute-start.2) | collective-permute-done | bytes 614432 | tf_op jit(solution)/shard_map/ppermute | solution.py:76
  236.4 0.0 collective-permute-done.5
  236.4 1.3 collective-permute-start.6
  237.7 1.7 collective-permute-done.6.partner_ref
  239.4 13.4 %shard_map.56 = (bf16[256,1280]{1,0:T(8,128)(2,1)S(1)}, bf16[256,1280]{1,0:T(8,128)(2,1)S(1)}) custom-call(bf16[256,1280]{1,0:T(8,128)(2,1)S(1)} %constant_dynamic-update-slice_fusion.own_ref, bf16[256,1280]{1,0:T(8,128)(2,1)S(1)} %collective-permute-done.6.partner_ref, f32[1,2560]{1,0:T(1,128)S(1)} %copy-done, ...), custom_call_target="tpu_custom_call" | custom-call | tf_op jit(solution)/shard_map/pallas_call | solution.py:48
  252.9 0.5 collective-permute-start.7
  253.3 1.7 collective-permute-done.7
  255.0 0.4 select_select_fusion
  255.5 0.1 collective-permute-start.8
  255.6 2.7 collective-permute-start.9
  258.2 1.1 collective-permute-done.9
  259.3 3.0 collective-permute-start.10
  262.3 1.1 collective-permute-done.10
  263.4 3.0 collective-permute-start.11
  266.4 5.5 %collective-permute-done.8 = bf16[240,1280]{1,0:T(8,128)(2,1)S(1)} collective-permute-done((bf16[240,1280]{1,0:T(8,128)(2,1)S(1)}, bf16[240,1280]{1,0:T(8,128)(2,1)S(1)}, u32[]{:S(2)}, u32[]{:S(2)}) %collective-permute-start.8) | collective-permute-done | bytes 614432 | tf_op jit(solution)/shard_map/ppermute | solution.py:76
  271.9 0.0 collective-permute-done.11
  271.9 1.3 collective-permute-start.12
  273.2 1.7 collective-permute-done.12.partner_ref
  274.9 13.4 %shard_map.57 = (bf16[256,1280]{1,0:T(8,128)(2,1)S(1)}, bf16[256,1280]{1,0:T(8,128)(2,1)S(1)}) custom-call(bf16[256,1280]{1,0:T(8,128)(2,1)S(1)} %constant_dynamic-update-slice_fusion.2.own_ref, bf16[256,1280]{1,0:T(8,128)(2,1)S(1)} %collective-permute-done.12.partner_ref, f32[1,2560]{1,0:T(1,128)S(1)} %copy-done, ...), custom_call_target="tpu_custom_call" | custom-call | tf_op jit(solution)/shard_map/pallas_call | solution.py:48
  288.3 0.5 collective-permute-start.13
  288.8 1.7 collective-permute-done.13
  290.5 0.4 broadcast_select_fusion.1
  290.9 0.1 collective-permute-start.14
  291.0 2.7 collective-permute-start.15
  293.7 1.1 collective-permute-done.15
  294.8 3.0 collective-permute-start.16
  297.8 1.1 collective-permute-done.16
  298.9 3.0 collective-permute-start.17
  301.8 5.5 %collective-permute-done.14 = bf16[240,1280]{1,0:T(8,128)(2,1)S(1)} collective-permute-done((bf16[240,1280]{1,0:T(8,128)(2,1)S(1)}, bf16[240,1280]{1,0:T(8,128)(2,1)S(1)}, u32[]{:S(2)}, u32[]{:S(2)}) %collective-permute-start.14) | collective-permute-done | bytes 614432 | tf_op jit(solution)/shard_map/ppermute | solution.py:76
  307.3 0.0 collective-permute-done.17
  307.4 1.3 collective-permute-start.18
  308.6 1.7 collective-permute-done.18.partner_ref
  310.4 13.4 %shard_map.58 = (bf16[256,1280]{1,0:T(8,128)(2,1)S(1)}, bf16[256,1280]{1,0:T(8,128)(2,1)S(1)}) custom-call(bf16[256,1280]{1,0:T(8,128)(2,1)S(1)} %constant_dynamic-update-slice_fusion.4.own_ref, bf16[256,1280]{1,0:T(8,128)(2,1)S(1)} %collective-permute-done.18.partner_ref, f32[1,2560]{1,0:T(1,128)S(1)} %copy-done, ...), custom_call_target="tpu_custom_call" | custom-call | tf_op jit(solution)/shard_map/pallas_call | solution.py:48
  323.8 0.5 collective-permute-start.19
  324.3 1.7 collective-permute-done.19
  326.0 1.2 fusion
  (13 shorter events, 0.3 us)
Async XLA Ops:
  6.5 2.9 copy-start.1
  6.5 196.8 %all-gather.2.cloned.1.call-start = ((), (), s32[]{:S(2)}) async-start(), calls=%async_computation | async-start | bytes 27033600 | tf_op jit(solution)/shard_map/all_gather | solution.py:93
  8.7 194.6 %copy-start = (f32[1,2560]{1,0:T(1,128)S(1)}, f32[1,2560]{1,0:T(1,128)}, u32[]{:S(2)}) copy-start(f32[1,2560]{1,0:T(1,128)} %gain_ref.7) | copy-start | bytes 30724
  9.5 5.1 %collective-permute-start = (bf16[256,1280]{1,0:T(8,128)(2,1)S(1)}, bf16[256,1280]{1,0:T(8,128)(2,1)S(1)}, u32[]{:S(2)}, u32[]{:S(2)}) collective-permute-start(bf16[256,1280]{1,0:T(8,128)(2,1)S(1)} %broadcast_select_fusion.own_ref), channel_id=1, source_target_pairs={{0,1},{1,0},{2,3},{3,2},{4,5},{5,4},{6,7},{7,6},{8,9},{9,8},{10,11... | collective-permute-start | bytes 1966088 | tf_op jit(solution)/shard_map/ppermute | solution.py:100
  216.8 2.9 collective-permute-start.1
  220.0 16.4 %collective-permute-start.2 = (bf16[240,1280]{1,0:T(8,128)(2,1)S(1)}, bf16[240,1280]{1,0:T(8,128)(2,1)S(1)}, u32[]{:S(2)}, u32[]{:S(2)}) collective-permute-start(bf16[240,1280]{1,0:T(8,128)(2,1)S(1)} %slice.24), channel_id=1, source_target_pairs={{0,64},{64,128},{128,192},{192,0},{1,65},{65,129},{129,193},{193,1... | collective-permute-start | bytes 1843208 | tf_op jit(solution)/shard_map/ppermute | solution.py:76
  221.3 2.9 collective-permute-start.3
  224.1 3.8 %collective-permute-start.4 = (bf16[16,1280]{1,0:T(8,128)(2,1)S(1)}, bf16[16,1280]{1,0:T(8,128)(2,1)S(1)}, u32[]{:S(2)}, u32[]{:S(2)}) collective-permute-start(bf16[16,1280]{1,0:T(8,128)(2,1)S(1)} %collective-permute-done.3), channel_id=1, source_target_pairs={{0,192},{64,0},{128,64},{192,128},{1,193},{65,1},{129,65},{193,129... | collective-permute-start | bytes 122888 | tf_op jit(solution)/shard_map/ppermute | solution.py:76
  227.9 8.5 %collective-permute-start.5 = (bf16[16,1280]{1,0:T(8,128)(2,1)S(1)}, bf16[16,1280]{1,0:T(8,128)(2,1)S(1)}, u32[]{:S(2)}, u32[]{:S(2)}) collective-permute-start(bf16[16,1280]{1,0:T(8,128)(2,1)S(1)} %collective-permute-done.4), channel_id=1, source_target_pairs={{0,192},{64,0},{128,64},{192,128},{1,193},{65,1},{129,65},{193,129... | collective-permute-start | bytes 122888 | tf_op jit(solution)/shard_map/ppermute | solution.py:76
  236.4 3.0 collective-permute-start.6
  252.9 2.2 collective-permute-start.7
  255.5 16.4 %collective-permute-start.8 = (bf16[240,1280]{1,0:T(8,128)(2,1)S(1)}, bf16[240,1280]{1,0:T(8,128)(2,1)S(1)}, u32[]{:S(2)}, u32[]{:S(2)}) collective-permute-start(bf16[240,1280]{1,0:T(8,128)(2,1)S(1)} %slice.26), channel_id=1, source_target_pairs={{0,64},{64,128},{128,192},{192,0},{1,65},{65,129},{129,193},{193,1... | collective-permute-start | bytes 1843208 | tf_op jit(solution)/shard_map/ppermute | solution.py:76
  255.6 3.8 %collective-permute-start.9 = (bf16[16,1280]{1,0:T(8,128)(2,1)S(1)}, bf16[16,1280]{1,0:T(8,128)(2,1)S(1)}, u32[]{:S(2)}, u32[]{:S(2)}) collective-permute-start(bf16[16,1280]{1,0:T(8,128)(2,1)S(1)} %slice.27), channel_id=1, source_target_pairs={{0,192},{64,0},{128,64},{192,128},{1,193},{65,1},{129,65},{193,129... | collective-permute-start | bytes 122888 | tf_op jit(solution)/shard_map/ppermute | solution.py:76
  259.3 4.1 %collective-permute-start.10 = (bf16[16,1280]{1,0:T(8,128)(2,1)S(1)}, bf16[16,1280]{1,0:T(8,128)(2,1)S(1)}, u32[]{:S(2)}, u32[]{:S(2)}) collective-permute-start(bf16[16,1280]{1,0:T(8,128)(2,1)S(1)} %collective-permute-done.9), channel_id=1, source_target_pairs={{0,192},{64,0},{128,64},{192,128},{1,193},{65,1},{129,65},{193,129... | collective-permute-start | bytes 122888 | tf_op jit(solution)/shard_map/ppermute | solution.py:76
  263.4 8.5 %collective-permute-start.11 = (bf16[16,1280]{1,0:T(8,128)(2,1)S(1)}, bf16[16,1280]{1,0:T(8,128)(2,1)S(1)}, u32[]{:S(2)}, u32[]{:S(2)}) collective-permute-start(bf16[16,1280]{1,0:T(8,128)(2,1)S(1)} %collective-permute-done.10), channel_id=1, source_target_pairs={{0,192},{64,0},{128,64},{192,128},{1,193},{65,1},{129,65},{193,129... | collective-permute-start | bytes 122888 | tf_op jit(solution)/shard_map/ppermute | solution.py:76
  271.9 3.0 collective-permute-start.12
  288.3 2.2 collective-permute-start.13
  290.9 16.4 %collective-permute-start.14 = (bf16[240,1280]{1,0:T(8,128)(2,1)S(1)}, bf16[240,1280]{1,0:T(8,128)(2,1)S(1)}, u32[]{:S(2)}, u32[]{:S(2)}) collective-permute-start(bf16[240,1280]{1,0:T(8,128)(2,1)S(1)} %slice.28), channel_id=1, source_target_pairs={{0,64},{64,128},{128,192},{192,0},{1,65},{65,129},{129,193},{193,1... | collective-permute-start | bytes 1843208 | tf_op jit(solution)/shard_map/ppermute | solution.py:76
  291.0 3.8 %collective-permute-start.15 = (bf16[16,1280]{1,0:T(8,128)(2,1)S(1)}, bf16[16,1280]{1,0:T(8,128)(2,1)S(1)}, u32[]{:S(2)}, u32[]{:S(2)}) collective-permute-start(bf16[16,1280]{1,0:T(8,128)(2,1)S(1)} %slice.29), channel_id=1, source_target_pairs={{0,192},{64,0},{128,64},{192,128},{1,193},{65,1},{129,65},{193,129... | collective-permute-start | bytes 122888 | tf_op jit(solution)/shard_map/ppermute | solution.py:76
  294.8 4.1 %collective-permute-start.16 = (bf16[16,1280]{1,0:T(8,128)(2,1)S(1)}, bf16[16,1280]{1,0:T(8,128)(2,1)S(1)}, u32[]{:S(2)}, u32[]{:S(2)}) collective-permute-start(bf16[16,1280]{1,0:T(8,128)(2,1)S(1)} %collective-permute-done.15), channel_id=1, source_target_pairs={{0,192},{64,0},{128,64},{192,128},{1,193},{65,1},{129,65},{193,129... | collective-permute-start | bytes 122888 | tf_op jit(solution)/shard_map/ppermute | solution.py:76
  298.9 8.5 %collective-permute-start.17 = (bf16[16,1280]{1,0:T(8,128)(2,1)S(1)}, bf16[16,1280]{1,0:T(8,128)(2,1)S(1)}, u32[]{:S(2)}, u32[]{:S(2)}) collective-permute-start(bf16[16,1280]{1,0:T(8,128)(2,1)S(1)} %collective-permute-done.16), channel_id=1, source_target_pairs={{0,192},{64,0},{128,64},{192,128},{1,193},{65,1},{129,65},{193,129... | collective-permute-start | bytes 122888 | tf_op jit(solution)/shard_map/ppermute | solution.py:76
  307.4 3.0 collective-permute-start.18
  323.8 2.2 collective-permute-start.19
Sparse Core Ops, SparseCore 0:
  9.9 193.3 all-gather.1
